TPU v7x, 32 devices: a whole 2x2x4 slice. The times are simulated.
32 devices in a mesh: grp: 2 (over y), dp: 4 (over x, core), sub: 4 (over z).
Axes of the slice: x: 2, y: 2, z: 4, core: 2. Of those that a mesh axis runs over, the one named last changes fastest.
Arguments:
- hidden_in: bfloat16 [128, 5120], P(('grp', 'dp'), 'sub'), parts along dimension 0, may hold values from -76 to 76
- queries: bfloat16 [128, 128, 576], P(('grp', 'dp', 'sub')), parts along dimension 0, may hold values from -260 to 260
- cache_pool: bfloat16 [2048, 128, 576], P(('grp', 'dp', 'sub')), parts along dimension 0, may hold values from -6 to 6
- page_table: int32 [128, 16], P(('grp', 'dp', 'sub')), parts along dimension 0, may hold values from 0 to 63, as said below
- lengths: int32 [128], P(('grp', 'dp', 'sub')), parts along dimension 0, may hold values from 128 to 2048, as said below
- value_up: bfloat16 [128, 512, 128], P(('dp', 'sub')), may hold values from -0.25 to 0.25
- out_proj: bfloat16 [16384, 5120], P('dp', 'sub'), may hold values from -0.125 to 0.125
- norm_gain: bfloat16 [5120], P('sub'), may hold values from 0.099609375 to 1.8984375
- gate_proj: bfloat16 [5120, 12288], P('sub', 'dp'), may hold values from -0.078125 to 0.078125
- up_proj: bfloat16 [5120, 12288], P('sub', 'dp'), may hold values from -0.078125 to 0.078125
- down_proj: bfloat16 [12288, 5120], P('dp', 'sub'), may hold values from -0.21875 to 0.21875
Outputs:
- attn_out: bfloat16 [128, 5120], P(('grp', 'dp'), 'sub'), parts along dimension 0
- next_hidden: bfloat16 [128, 5120], P(('grp', 'dp'), 'sub'), parts along dimension 0
There are 2 independent parts, one for each index of `grp`. A program takes and returns all parts, laid end to end along the dimension named above; an argument that names none is the same for every part. Nothing has to cross between parts.
Inputs may be any that keep to these rules, and one draw needn't show every extreme that they name: `page_table`: row r lists 16 pages of the pool of request r's device; the 4 rows of one device use each of its 64 pages exactly once. `lengths`: some request has exactly 2048 positions and some exactly 128.
All inputs are finite; a program needn't handle non-finite values.
Results may differ from a plain program's by a relative error of at most 0.02.
Values may be sent and summed in bfloat16 or wider, within the bound.
No kernel may reach another device: no remote copies, remote signals or barrier semaphores. Data moves between devices by JAX's collectives and lax.ppermute only.
A program may use at most 192 MiB of HBM per device.

v0:
```python
import functools

import jax
import jax.numpy as jnp
from jax import lax
from jax.experimental import pallas as pl
from jax.experimental.pallas import tpu as pltpu
from jax.sharding import PartitionSpec as P

D = 5120
ROPE = 64
VDIM = 128


masked_score = -1e30


def attend_kernel(page_table, lengths, queries, cache_pool, contexts, keys, scores, weighted, copy_sems,
                  *, latent, score_scale):
    req_dev, pages_req = page_table.shape
    page_size = cache_pool.shape[1]
    head_count = queries.shape[1]

    def page_copy(slot, page):
        return pltpu.make_async_copy(
            cache_pool.at[page_table[slot, page]],
            keys.at[slot * pages_req + page],
            copy_sems.at[slot * pages_req + page],
        )

    def pages_of(slot):
        return (lengths[slot] + page_size - 1) // page_size

    for slot in range(req_dev):
        def start(page, carry, slot=slot):
            page_copy(slot, page).start()
            return carry

        lax.fori_loop(0, pages_of(slot), start, 0)

    positions = lax.broadcasted_iota(jnp.int32, (head_count, page_size), 1)
    for slot in range(req_dev):
        length = lengths[slot]
        query_rows = queries[slot]

        def score_step(page, running_max, slot=slot, length=length, query_rows=query_rows):
            page_copy(slot, page).wait()
            key_rows = keys[slot * pages_req + page]
            block = lax.dot_general(
                query_rows, key_rows, (((1,), (1,)), ((), ())), preferred_element_type=jnp.float32
            ) * score_scale
            block = jnp.where(positions + page * page_size < length, block, masked_score)
            scores[page] = block
            return jnp.maximum(running_max, jnp.max(block, axis=1, keepdims=True))

        row_max = lax.fori_loop(
            0, pages_of(slot), score_step, jnp.full((head_count, 1), masked_score, jnp.float32)
        )
        weighted[...] = jnp.zeros_like(weighted)

        def weight_step(page, denominator, slot=slot, length=length, row_max=row_max):
            live = positions + page * page_size < length
            exponent = jnp.where(live, jnp.exp(scores[page] - row_max), 0.0)
            value_rows = keys[slot * pages_req + page, :, :latent]
            weighted[...] += jnp.dot(
                exponent.astype(jnp.bfloat16), value_rows, preferred_element_type=jnp.float32
            )
            return denominator + jnp.sum(exponent, axis=1, keepdims=True)

        denominator = lax.fori_loop(
            0, pages_of(slot), weight_step, jnp.zeros((head_count, 1), jnp.float32)
        )
        contexts[slot] = (weighted[...] / denominator).astype(contexts.dtype)


def attend_all(queries, page_table, lengths, cache_pool, latent, score_scale):
    req_dev, head_count, width = queries.shape
    pages_req = page_table.shape[1]
    page_size = cache_pool.shape[1]
    kernel = functools.partial(attend_kernel, latent=latent, score_scale=score_scale)
    return pl.pallas_call(
        kernel,
        out_shape=jax.ShapeDtypeStruct((req_dev, head_count, latent), jnp.bfloat16),
        in_specs=[
            pl.BlockSpec(memory_space=pltpu.SMEM),
            pl.BlockSpec(memory_space=pltpu.SMEM),
            pl.BlockSpec(memory_space=pltpu.VMEM),
            pl.BlockSpec(memory_space=pl.ANY),
        ],
        out_specs=pl.BlockSpec(memory_space=pltpu.VMEM),
        scratch_shapes=[
            pltpu.VMEM((req_dev * pages_req, page_size, width), jnp.bfloat16),
            pltpu.VMEM((pages_req, head_count, page_size), jnp.float32),
            pltpu.VMEM((head_count, latent), jnp.float32),
            pltpu.SemaphoreType.DMA((req_dev * pages_req,)),
        ],
        compiler_params=pltpu.CompilerParams(vmem_limit_bytes=48 * 1024 * 1024),
    )(page_table, lengths, queries, cache_pool)


def shards(
    hidden_in,
    queries,
    cache_pool,
    page_table,
    lengths,
    value_up,
    out_proj,
    norm_gain,
    gate_proj,
    up_proj,
    down_proj,
):
    req_dev = queries.shape[0]
    latent = value_up.shape[1]
    value_dim = value_up.shape[2]
    heads_here = value_up.shape[0]
    pages_req = page_table.shape[1]
    score_scale = float(VDIM + ROPE) ** (-0.5)
    units_here = gate_proj.shape[1]
    contexts = attend_all(queries, page_table, lengths, cache_pool, latent, score_scale)
    received = lax.all_to_all(
        contexts[None], ("dp", "sub"), split_axis=2, concat_axis=0, tiled=True
    )
    received = received.reshape(-1, heads_here, latent)
    row_count = received.shape[0]
    values = jnp.einsum("rhc,hcv->rhv", received, value_up, preferred_element_type=jnp.float32)
    values = values.astype(jnp.bfloat16).reshape(row_count, heads_here * value_dim)
    group_values = lax.all_gather(values, "sub", axis=1, tiled=True)
    attention = lax.psum_scatter(
        jnp.dot(group_values, out_proj, preferred_element_type=jnp.float32).astype(jnp.bfloat16),
        "dp",
        scatter_dimension=0,
        tiled=True,
    ).astype(jnp.float32)
    residual = hidden_in.astype(jnp.float32) + attention
    squares = lax.psum(jnp.sum(residual * residual, axis=1), "sub")
    scale_rows = lax.rsqrt(squares / float(D) + 1e-06)
    normed = (residual * scale_rows[:, None] * norm_gain.astype(jnp.float32)).astype(jnp.bfloat16)
    piece = lax.all_gather(normed, "dp", axis=0, tiled=True)
    gate_part = jnp.dot(piece, gate_proj, preferred_element_type=jnp.float32)
    up_part = jnp.dot(piece, up_proj, preferred_element_type=jnp.float32)
    partials = jnp.concatenate([gate_part, up_part], axis=1)
    summed = lax.psum(partials.astype(jnp.bfloat16), "sub").astype(jnp.float32)
    hidden_units = (jax.nn.silu(summed[:, :units_here]) * summed[:, units_here:]).astype(
        jnp.bfloat16
    )
    feed_forward = lax.psum_scatter(
        jnp.dot(hidden_units, down_proj, preferred_element_type=jnp.float32).astype(jnp.bfloat16),
        "dp",
        scatter_dimension=0,
        tiled=True,
    ).astype(jnp.float32)
    return (attention.astype(jnp.bfloat16), (residual + feed_forward).astype(jnp.bfloat16))


def solution(mesh):
    placed = (
        P(("grp", "dp"), "sub"),
        P(("grp", "dp", "sub"), None, None),
        P(("grp", "dp", "sub"), None, None),
        P(("grp", "dp", "sub"), None),
        P(("grp", "dp", "sub")),
        P(("dp", "sub"), None, None),
        P("dp", "sub"),
        P("sub"),
        P("sub", "dp"),
        P("sub", "dp"),
        P("dp", "sub"),
    )
    return jax.shard_map(
        shards,
        mesh=mesh,
        in_specs=placed,
        out_specs=(P(("grp", "dp"), "sub"), P(("grp", "dp"), "sub")),
        check_vma=False,
    )
```

profile of v0, /device:TPU:0, one launch (start us, length us, event | category | flops | bytes accessed | tf_op | source)
XLA Modules:
  0.0 217.7 jit_solution(14189366572653942344)
XLA Ops:
  7.2 0.0 copy-start
  7.2 0.0 copy-start.3
  7.2 0.0 copy-start.1
  7.2 0.0 copy-start.2
  7.2 0.0 reduce-scatter.3.cloned.1.call-start
  7.3 14.1 %copy.21.cache_pool = bf16[64,128,576]{2,1,0:T(8,128)(2,1)} copy(bf16[64,128,576]{1,2,0:T(8,128)(2,1)} %param.13) | data formatting | bytes 18874368 | tf_op args[2]
  21.4 0.0 copy-done.3
  21.4 0.3 copy.20.queries
  21.7 0.0 copy-done.1
  21.7 0.0 copy-done.2
  21.7 20.1 %shard_map.122 = bf16[4,128,512]{2,1,0:T(8,128)(2,1)S(1)} custom-call(s32[4,16]{1,0:T(4,128)S(1)} %copy-done.1, s32[4]{0:T(128)S(1)} %copy-done.2, bf16[4,128,576]{2,1,0:T(8,128)(2,1)S(1)} %copy.20.queries, bf16[64,128,576]{2,1,0:T(8,128)(2,1)} %copy.21.cache_pool), custom_call_target="tpu_custom_call" | custom-call | tf_op jit(solution)/shard_map/pallas_call | solution.py:81
  41.9 0.4 copy.22
  42.3 30.3 %all_to_all.15 = bf16[1,4,128,512]{3,1,0,2:T(4,128)(2,1)S(1)} all-to-all(bf16[1,4,128,512]{3,1,0,2:T(4,128)(2,1)S(1)} %copy.22), channel_id=1, replica_groups=mesh['grp'=2,'dp'=4,'sub'=4] {'dp','sub'}, dimensions={2} | all-to-all | bytes 1048576 | tf_op jit(solution)/shard_map/all_to_all | solution.py:122
  72.6 0.2 copy.28
  72.8 0.1 reshape.13
  72.9 0.0 copy-done
  72.9 0.3 fusion
  73.3 16.1 %all_gather.6 = bf16[64,4096]{1,0:T(8,128)(2,1)S(1)} all-gather(bf16[64,1024]{1,0:T(8,128)(2,1)S(1)} %bitcast.25), channel_id=1, replica_groups=mesh['grp'=2,'dp'=4,'sub'=4] {'sub'}, dimensions={1}, use_global_device_ids=true | all-gather | bytes 655360 | tf_op jit(solution)/shard_map/all_gather | solution.py:129
  89.3 0.0 copy-start.6
  89.3 0.0 copy-start.4
  89.3 6.6 %convolution_convert_fusion.2 = bf16[64,1280]{1,0:T(8,128)(2,1)} fusion(bf16[64,4096]{1,0:T(8,128)(2,1)S(1)} %all_gather.6, bf16[4096,1280]{1,0:T(8,128)(2,1)} %param.17), kind=kOutput, calls=%fused_computation.2 | convolution fusion | flops 671170560 | bytes 11173888 | tf_op jit(solution)/shard_map/dot_general | solution.py:131
  95.9 0.0 reduce-scatter.3.cloned.1.call-update
  95.9 0.0 all-reduce.2.cloned.1.call-start
  96.0 0.0 copy-done.6
  96.0 17.4 %reduce-scatter.3.cloned.1.call-done = bf16[16,1280]{1,0:T(8,128)(2,1)} async-done(((bf16[64,1280]{1,0:T(8,128)(2,1)}), bf16[16,1280]{1,0:T(8,128)(2,1)}) %reduce-scatter.3.cloned.1.call-update) | async-done | bytes 40976 | tf_op jit(solution)/shard_map/reduce_scatter | solution.py:130
  113.4 0.0 copy-done.4
  113.4 0.9 multiply_reduce_fusion
  114.3 11.7 %psum.14 = f32[16]{0:T(128)S(1)} all-reduce(f32[16]{0:T(128)S(1)} %multiply_reduce_fusion), channel_id=1, replica_groups=mesh['grp'=2,'dp'=4,'sub'=4] {'sub'}, use_global_device_ids=true, to_apply=%region_2.0 | all-reduce | flops 16 | bytes 128 | tf_op jit(solution)/shard_map/psum | solution.py:137
  126.0 0.9 multiply_convert_fusion
  126.9 5.5 %all_gather.7 = bf16[64,1280]{1,0:T(8,128)(2,1)S(1)} all-gather(bf16[16,1280]{1,0:T(8,128)(2,1)S(1)} %multiply_convert_fusion), channel_id=1, replica_groups=mesh['grp'=2,'dp'=4,'sub'=4] {'dp'}, dimensions={0}, use_global_device_ids=true | all-gather | bytes 204800 | tf_op jit(solution)/shard_map/all_gather | solution.py:140
  132.4 4.7 %convolution_convert_fusion = bf16[64,3072]{1,0:T(8,128)(2,1)S(1)} fusion(bf16[64,1280]{1,0:T(8,128)(2,1)S(1)} %all_gather.7, bf16[1280,3072]{1,0:T(8,128)(2,1)} %param.20), kind=kOutput, calls=%fused_computation | convolution fusion | flops 503513088 | bytes 8421376 | tf_op jit(solution)/shard_map/dot_general | solution.py:142
  137.2 4.7 %convolution_convert_fusion.1 = bf16[64,3072]{1,0:T(8,128)(2,1)S(1)} fusion(bf16[64,1280]{1,0:T(8,128)(2,1)S(1)} %all_gather.7, bf16[1280,3072]{1,0:T(8,128)(2,1)} %param.19), kind=kOutput, calls=%fused_computation.1 | convolution fusion | flops 503513088 | bytes 8421376 | tf_op jit(solution)/shard_map/dot_general | solution.py:141
  141.9 0.0 copy-start.5
  141.9 0.9 pad_maximum_fusion
  142.9 0.0 all-reduce.2.cloned.1.call-update
  142.9 0.0 reduce-scatter.5.cloned.1.call-start
  142.9 41.0 %all-reduce.2.cloned.1.call-done = bf16[64,6144]{1,0:T(8,128)(2,1)} async-done(((bf16[64,6144]{1,0:T(8,128)(2,1)}), bf16[64,6144]{1,0:T(8,128)(2,1)}) %all-reduce.2.cloned.1.call-update) | async-done | bytes 786448 | tf_op jit(solution)/shard_map/psum | solution.py:144
  184.0 1.2 convert_element_type.45
  185.2 5.4 %convolution_convert_fusion.3 = bf16[64,1280]{1,0:T(8,128)(2,1)} fusion(bf16[3072,1280]{1,0:T(8,128)(2,1)} %param.21, f32[64,6144]{1,0:T(8,128)S(1)} %convert_element_type.45), kind=kOutput, calls=%fused_computation.3 | convolution fusion | flops 504578048 | bytes 9601024 | tf_op jit(solution)/shard_map/dot_general | solution.py:149
  190.6 0.0 reduce-scatter.5.cloned.1.call-update
  190.7 19.1 %reduce-scatter.5.cloned.1.call-done = bf16[16,1280]{1,0:T(8,128)(2,1)} async-done(((bf16[64,1280]{1,0:T(8,128)(2,1)}), bf16[16,1280]{1,0:T(8,128)(2,1)}) %reduce-scatter.5.cloned.1.call-update) | async-done | bytes 40976 | tf_op jit(solution)/shard_map/reduce_scatter | solution.py:148
  209.8 0.0 copy-done.5
  209.8 1.4 add_convert_fusion
  (3 shorter events, 0.0 us)
Async XLA Ops:
  7.2 65.8 %copy-start = (bf16[8,512,128]{2,1,0:T(8,128)(2,1)S(1)}, bf16[8,512,128]{2,1,0:T(8,128)(2,1)}, u32[]{:S(2)}) copy-start(bf16[8,512,128]{2,1,0:T(8,128)(2,1)} %param.16) | copy-start | bytes 3145732
  7.2 14.2 %copy-start.3 = (bf16[4,128,576]{1,2,0:T(8,128)(2,1)S(1)}, bf16[4,128,576]{1,2,0:T(8,128)(2,1)}, u32[]{:S(2)}) copy-start(bf16[4,128,576]{1,2,0:T(8,128)(2,1)} %param.12) | copy-start | bytes 1769476
  7.2 14.5 %copy-start.1 = (s32[4,16]{1,0:T(4,128)S(1)}, s32[4,16]{1,0:T(4,128)}, u32[]{:S(2)}) copy-start(s32[4,16]{1,0:T(4,128)} %page_table.1) | copy-start | bytes 772
  7.2 14.5 %copy-start.2 = (s32[4]{0:T(128)S(1)}, s32[4]{0:T(128)}, u32[]{:S(2)}) copy-start(s32[4]{0:T(128)} %lengths.1) | copy-start | bytes 52
  7.2 106.2 %reduce-scatter.3.cloned.1.call-start = ((), (), s32[]{:S(2)}) async-start(), calls=%async_computation.3 | async-start | bytes 204800 | tf_op jit(solution)/shard_map/reduce_scatter | solution.py:130
  89.3 6.6 %copy-start.6 = (bf16[1280]{0:T(1024)(128)(2,1)S(1)}, bf16[1280]{0:T(1024)(128)(2,1)}, u32[]{:S(2)}) copy-start(bf16[1280]{0:T(1024)(128)(2,1)} %param.18) | copy-start | bytes 7684
  89.3 24.1 %copy-start.4 = (bf16[16,1280]{1,0:T(8,128)(2,1)S(1)}, bf16[16,1280]{1,0:T(8,128)(2,1)}, u32[]{:S(2)}) copy-start(bf16[16,1280]{1,0:T(8,128)(2,1)} %param.11) | copy-start | bytes 122884
  95.9 88.0 %all-reduce.2.cloned.1.call-start = ((), (), s32[]{:S(2)}) async-start(), calls=%async_computation.4 | async-start | bytes 1572864 | tf_op jit(solution)/shard_map/psum | solution.py:144
  141.9 67.9 %copy-start.5 = (bf16[16,1280]{1,0:T(8,128)(2,1)S(1)}, bf16[16,1280]{1,0:T(8,128)(2,1)}, u32[]{:S(2)}) copy-start(bf16[16,1280]{1,0:T(8,128)(2,1)} %reduce-scatter.3.cloned.1.call-done) | copy-start | bytes 122884
  142.9 66.9 %reduce-scatter.5.cloned.1.call-start = ((), (), s32[]{:S(2)}) async-start(), calls=%async_computation.5 | async-start | bytes 204800 | tf_op jit(solution)/shard_map/reduce_scatter | solution.py:148
Sparse Core Ops, SparseCore 0:
  96.1 17.3 reduce-scatter.2
  143.0 40.9 all-reduce.1
  190.8 18.9 reduce-scatter.4
where the time goes:
time: 217 us; the launch traced here: 218 us
  waiting for transfers between devices  77.6 us (36%)
  blocking collectives  63.6 us (29%)
  matrix products  21.8 us (10%)
  Pallas kernels  20.1 us (9%)
  local copies, waits for them, and re-layouts  15.2 us (7%)
  between operations  13.9 us (6%)
  other arithmetic  5.37 us (2%)
    psum x1, waiting for transfers between devices, shards(): summed = lax.psum(partials.astype(jnp.bfloat16), 'sub').astype(jnp.float32)  41 us
    all_to_all x1, blocking collectives, shards(): lax.all_to_all(contexts[None], ('dp', 'sub'), split_axis=2, concat_axis=0...  30.3 us
    pallas_call x1, Pallas kernels, attend_all(): pl.pallas_call(kernel, out_shape=jax.ShapeDtypeStruct((req_dev, head_coun...  20.1 us
    reduce_scatter x1, waiting for transfers between devices, shards(): lax.psum_scatter(jnp.dot(hidden_units, down_proj, preferred_element_type=...  19.1 us
    reduce_scatter x1, waiting for transfers between devices, shards(): lax.psum_scatter(jnp.dot(group_values, out_proj, preferred_element_type=j...  17.4 us
    all_gather x1, blocking collectives, shards(): group_values = lax.all_gather(values, 'sub', axis=1, tiled=True)  16.1 us
    unnamed x16, local copies, waits for them, and re-layouts  14.5 us
    psum x1, blocking collectives, shards(): squares = lax.psum(jnp.sum(residual * residual, axis=1), 'sub')  11.7 us
  transfers between devices with their start and end apart: 3, of which 3 were waited for; matrix products, arithmetic and copies ran while one was open for 0% of the time, Pallas kernels for 0%

commit v1 on v0

--- a/solution.py
+++ b/solution.py
@@ -18,7 +18,7 @@
 def attend_kernel(page_table, lengths, queries, cache_pool, contexts, keys, scores, weighted, copy_sems,
                   *, latent, score_scale):
     req_dev, pages_req = page_table.shape
-    page_size = cache_pool.shape[1]
+    page_size = cache_pool.shape[2]
     head_count = queries.shape[1]
 
     def page_copy(slot, page):
@@ -45,10 +45,8 @@
 
         def score_step(page, running_max, slot=slot, length=length, query_rows=query_rows):
             page_copy(slot, page).wait()
-            key_rows = keys[slot * pages_req + page]
-            block = lax.dot_general(
-                query_rows, key_rows, (((1,), (1,)), ((), ())), preferred_element_type=jnp.float32
-            ) * score_scale
+            key_columns = keys[slot * pages_req + page]
+            block = jnp.dot(query_rows, key_columns, preferred_element_type=jnp.float32) * score_scale
             block = jnp.where(positions + page * page_size < length, block, masked_score)
             scores[page] = block
             return jnp.maximum(running_max, jnp.max(block, axis=1, keepdims=True))
@@ -61,9 +59,12 @@
         def weight_step(page, denominator, slot=slot, length=length, row_max=row_max):
             live = positions + page * page_size < length
             exponent = jnp.where(live, jnp.exp(scores[page] - row_max), 0.0)
-            value_rows = keys[slot * pages_req + page, :, :latent]
-            weighted[...] += jnp.dot(
-                exponent.astype(jnp.bfloat16), value_rows, preferred_element_type=jnp.float32
+            value_columns = keys[slot * pages_req + page, :latent, :]
+            weighted[...] += lax.dot_general(
+                exponent.astype(jnp.bfloat16),
+                value_columns,
+                (((1,), (1,)), ((), ())),
+                preferred_element_type=jnp.float32,
             )
             return denominator + jnp.sum(exponent, axis=1, keepdims=True)
 
@@ -77,6 +78,7 @@
     req_dev, head_count, width = queries.shape
     pages_req = page_table.shape[1]
     page_size = cache_pool.shape[1]
+    cache_columns = jnp.swapaxes(cache_pool, 1, 2)
     kernel = functools.partial(attend_kernel, latent=latent, score_scale=score_scale)
     return pl.pallas_call(
         kernel,
@@ -89,13 +91,13 @@
         ],
         out_specs=pl.BlockSpec(memory_space=pltpu.VMEM),
         scratch_shapes=[
-            pltpu.VMEM((req_dev * pages_req, page_size, width), jnp.bfloat16),
+            pltpu.VMEM((req_dev * pages_req, width, page_size), jnp.bfloat16),
             pltpu.VMEM((pages_req, head_count, page_size), jnp.float32),
             pltpu.VMEM((head_count, latent), jnp.float32),
             pltpu.SemaphoreType.DMA((req_dev * pages_req,)),
         ],
         compiler_params=pltpu.CompilerParams(vmem_limit_bytes=48 * 1024 * 1024),
-    )(page_table, lengths, queries, cache_pool)
+    )(page_table, lengths, queries, cache_columns)
 
 
 def shards(

time: 217 us -> 204 us (0.940)
  local copies, waits for them, and re-layouts: 15.2 us -> 3.53 us
  Pallas kernels: 20.1 us -> 17.3 us
    unnamed x16 -> x13, local copies, waits for them, and re-layouts: 14.5 us -> 2.79 us
    pallas_call x1, Pallas kernels: 20.1 us -> 17.3 us  [attend_all(): pl.pallas_call(kernel, out_shape=jax.ShapeDtypeStruct((req_dev, head_coun...]
where the time goes in v1:
time: 204 us
  waiting for transfers between devices  77.7 us (38%)
  blocking collectives  63.9 us (31%)
  matrix products  21.8 us (11%)
  Pallas kernels  17.3 us (8%)
  between operations  13.9 us (7%)
  other arithmetic  5.38 us (3%)
  local copies, waits for them, and re-layouts  3.53 us (2%)
    psum x1, waiting for transfers between devices, shards(): summed = lax.psum(partials.astype(jnp.bfloat16), 'sub').astype(jnp.float32)  41 us
    all_to_all x1, blocking collectives, shards(): lax.all_to_all(contexts[None], ('dp', 'sub'), split_axis=2, concat_axis=0...  30.7 us
    reduce_scatter x1, waiting for transfers between devices, shards(): lax.psum_scatter(jnp.dot(hidden_units, down_proj, preferred_element_type=...  19.1 us
    reduce_scatter x1, waiting for transfers between devices, shards(): lax.psum_scatter(jnp.dot(group_values, out_proj, preferred_element_type=j...  17.5 us
    pallas_call x1, Pallas kernels, attend_all(): pl.pallas_call(kernel, out_shape=jax.ShapeDtypeStruct((req_dev, head_coun...  17.3 us
    all_gather x1, blocking collectives, shards(): group_values = lax.all_gather(values, 'sub', axis=1, tiled=True)  16.1 us
    psum x1, blocking collectives, shards(): squares = lax.psum(jnp.sum(residual * residual, axis=1), 'sub')  11.7 us
    dot_general x1, matrix products, shards(): jnp.dot(group_values, out_proj, preferred_element_type=jnp.float32)  6.57 us
  transfers between devices with their start and end apart: 3, of which 3 were waited for; matrix products, arithmetic and copies ran while one was open for 0% of the time, Pallas kernels for 0%

profile of v1, /device:TPU:0, one launch (start us, length us, event | category | flops | bytes accessed | tf_op | source)
XLA Modules:
  0.0 203.7 jit_solution(2028636517641284139)
XLA Ops:
  7.2 0.0 copy-start
  7.2 0.0 reduce-scatter.3.cloned.1.call-start
  7.2 1.4 copy.18.queries
  8.7 0.0 copy-start.1
  8.7 0.7 copy-done.1
  9.3 0.0 copy-start.2
  9.4 0.7 copy-done.2
  10.0 17.3 %shard_map.122 = bf16[4,128,512]{2,1,0:T(8,128)(2,1)S(1)} custom-call(s32[4,16]{1,0:T(4,128)S(1)} %copy-done.1, s32[4]{0:T(128)S(1)} %copy-done.2, bf16[4,128,576]{2,1,0:T(8,128)(2,1)S(1)} %copy.18.queries, bf16[64,576,128]{2,1,0:T(8,128)(2,1)} %bitcast.24), custom_call_target="tpu_custom_call" | custom-call | tf_op jit(solution)/shard_map/pallas_call | solution.py:83
  27.3 0.4 copy.19
  27.7 30.7 %all_to_all.15 = bf16[1,4,128,512]{3,1,0,2:T(4,128)(2,1)S(1)} all-to-all(bf16[1,4,128,512]{3,1,0,2:T(4,128)(2,1)S(1)} %copy.19), channel_id=1, replica_groups=mesh['grp'=2,'dp'=4,'sub'=4] {'dp','sub'}, dimensions={2} | all-to-all | bytes 1048576 | tf_op jit(solution)/shard_map/all_to_all | solution.py:124
  58.4 0.2 copy.25
  58.6 0.1 reshape.13
  58.7 0.0 copy-done
  58.7 0.3 fusion
  59.1 16.1 %all_gather.6 = bf16[64,4096]{1,0:T(8,128)(2,1)S(1)} all-gather(bf16[64,1024]{1,0:T(8,128)(2,1)S(1)} %bitcast.27), channel_id=1, replica_groups=mesh['grp'=2,'dp'=4,'sub'=4] {'sub'}, dimensions={1}, use_global_device_ids=true | all-gather | bytes 655360 | tf_op jit(solution)/shard_map/all_gather | solution.py:131
  75.2 0.0 copy-start.5
  75.2 0.0 copy-start.3
  75.2 6.6 %convolution_convert_fusion.2 = bf16[64,1280]{1,0:T(8,128)(2,1)} fusion(bf16[64,4096]{1,0:T(8,128)(2,1)S(1)} %all_gather.6, bf16[4096,1280]{1,0:T(8,128)(2,1)} %param.17), kind=kOutput, calls=%fused_computation.2 | convolution fusion | flops 671170560 | bytes 11173888 | tf_op jit(solution)/shard_map/dot_general | solution.py:133
  81.7 0.0 reduce-scatter.3.cloned.1.call-update
  81.8 0.0 all-reduce.2.cloned.1.call-start
  81.8 0.0 copy-done.5
  81.8 17.5 %reduce-scatter.3.cloned.1.call-done = bf16[16,1280]{1,0:T(8,128)(2,1)} async-done(((bf16[64,1280]{1,0:T(8,128)(2,1)}), bf16[16,1280]{1,0:T(8,128)(2,1)}) %reduce-scatter.3.cloned.1.call-update) | async-done | bytes 40976 | tf_op jit(solution)/shard_map/reduce_scatter | solution.py:132
  99.3 0.0 copy-done.3
  99.3 0.9 multiply_reduce_fusion
  100.3 11.7 %psum.14 = f32[16]{0:T(128)S(1)} all-reduce(f32[16]{0:T(128)S(1)} %multiply_reduce_fusion), channel_id=1, replica_groups=mesh['grp'=2,'dp'=4,'sub'=4] {'sub'}, use_global_device_ids=true, to_apply=%region_2.0 | all-reduce | flops 16 | bytes 128 | tf_op jit(solution)/shard_map/psum | solution.py:139
  111.9 0.9 multiply_convert_fusion
  112.8 5.5 %all_gather.7 = bf16[64,1280]{1,0:T(8,128)(2,1)S(1)} all-gather(bf16[16,1280]{1,0:T(8,128)(2,1)S(1)} %multiply_convert_fusion), channel_id=1, replica_groups=mesh['grp'=2,'dp'=4,'sub'=4] {'dp'}, dimensions={0}, use_global_device_ids=true | all-gather | bytes 204800 | tf_op jit(solution)/shard_map/all_gather | solution.py:142
  118.3 4.7 %convolution_convert_fusion = bf16[64,3072]{1,0:T(8,128)(2,1)S(1)} fusion(bf16[64,1280]{1,0:T(8,128)(2,1)S(1)} %all_gather.7, bf16[1280,3072]{1,0:T(8,128)(2,1)} %param.20), kind=kOutput, calls=%fused_computation | convolution fusion | flops 503513088 | bytes 8421376 | tf_op jit(solution)/shard_map/dot_general | solution.py:144
  123.1 4.7 %convolution_convert_fusion.1 = bf16[64,3072]{1,0:T(8,128)(2,1)S(1)} fusion(bf16[64,1280]{1,0:T(8,128)(2,1)S(1)} %all_gather.7, bf16[1280,3072]{1,0:T(8,128)(2,1)} %param.19), kind=kOutput, calls=%fused_computation.1 | convolution fusion | flops 503513088 | bytes 8421376 | tf_op jit(solution)/shard_map/dot_general | solution.py:143
  127.8 0.0 copy-start.4
  127.8 1.0 pad_maximum_fusion
  128.8 0.0 all-reduce.2.cloned.1.call-update
  128.8 0.0 reduce-scatter.5.cloned.1.call-start
  128.9 41.0 %all-reduce.2.cloned.1.call-done = bf16[64,6144]{1,0:T(8,128)(2,1)} async-done(((bf16[64,6144]{1,0:T(8,128)(2,1)}), bf16[64,6144]{1,0:T(8,128)(2,1)}) %all-reduce.2.cloned.1.call-update) | async-done | bytes 786448 | tf_op jit(solution)/shard_map/psum | solution.py:146
  169.9 1.2 convert_element_type.45
  171.1 5.4 %convolution_convert_fusion.3 = bf16[64,1280]{1,0:T(8,128)(2,1)} fusion(bf16[3072,1280]{1,0:T(8,128)(2,1)} %param.21, f32[64,6144]{1,0:T(8,128)S(1)} %convert_element_type.45), kind=kOutput, calls=%fused_computation.3 | convolution fusion | flops 504578048 | bytes 9601024 | tf_op jit(solution)/shard_map/dot_general | solution.py:151
  176.6 0.0 reduce-scatter.5.cloned.1.call-update
  176.6 19.1 %reduce-scatter.5.cloned.1.call-done = bf16[16,1280]{1,0:T(8,128)(2,1)} async-done(((bf16[64,1280]{1,0:T(8,128)(2,1)}), bf16[16,1280]{1,0:T(8,128)(2,1)}) %reduce-scatter.5.cloned.1.call-update) | async-done | bytes 40976 | tf_op jit(solution)/shard_map/reduce_scatter | solution.py:150
  195.7 0.0 copy-done.4
  195.7 1.4 add_convert_fusion
  (3 shorter events, 0.0 us)
Async XLA Ops:
  7.2 51.6 %copy-start = (bf16[8,512,128]{2,1,0:T(8,128)(2,1)S(1)}, bf16[8,512,128]{2,1,0:T(8,128)(2,1)}, u32[]{:S(2)}) copy-start(bf16[8,512,128]{2,1,0:T(8,128)(2,1)} %param.16) | copy-start | bytes 3145732
  7.2 92.2 %reduce-scatter.3.cloned.1.call-start = ((), (), s32[]{:S(2)}) async-start(), calls=%async_computation.3 | async-start | bytes 204800 | tf_op jit(solution)/shard_map/reduce_scatter | solution.py:132
  8.7 0.7 copy-start.1
  9.3 0.7 copy-start.2
  75.2 6.7 %copy-start.5 = (bf16[1280]{0:T(1024)(128)(2,1)S(1)}, bf16[1280]{0:T(1024)(128)(2,1)}, u32[]{:S(2)}) copy-start(bf16[1280]{0:T(1024)(128)(2,1)} %param.18) | copy-start | bytes 7684
  75.2 24.2 %copy-start.3 = (bf16[16,1280]{1,0:T(8,128)(2,1)S(1)}, bf16[16,1280]{1,0:T(8,128)(2,1)}, u32[]{:S(2)}) copy-start(bf16[16,1280]{1,0:T(8,128)(2,1)} %param.11) | copy-start | bytes 122884
  81.8 88.1 %all-reduce.2.cloned.1.call-start = ((), (), s32[]{:S(2)}) async-start(), calls=%async_computation.4 | async-start | bytes 1572864 | tf_op jit(solution)/shard_map/psum | solution.py:146
  127.8 67.9 %copy-start.4 = (bf16[16,1280]{1,0:T(8,128)(2,1)S(1)}, bf16[16,1280]{1,0:T(8,128)(2,1)}, u32[]{:S(2)}) copy-start(bf16[16,1280]{1,0:T(8,128)(2,1)} %reduce-scatter.3.cloned.1.call-done) | copy-start | bytes 122884
  128.8 66.9 %reduce-scatter.5.cloned.1.call-start = ((), (), s32[]{:S(2)}) async-start(), calls=%async_computation.5 | async-start | bytes 204800 | tf_op jit(solution)/shard_map/reduce_scatter | solution.py:150
Sparse Core Ops, SparseCore 0:
  81.9 17.4 reduce-scatter.2
  128.9 40.9 all-reduce.1
  176.7 18.9 reduce-scatter.4

commit v2 on v1

--- a/solution.py
+++ b/solution.py
@@ -100,7 +100,28 @@
     )(page_table, lengths, queries, cache_columns)
 
 
+def swap_with(x, axis, distance, size):
+    return lax.ppermute(x, axis, [(i, i ^ distance) for i in range(size)])
+
+
+def halving_scatter(x, axis, size, dim=0):
+    index = lax.axis_index(axis)
+    x = x.astype(jnp.float32)
+    distance = size // 2
+    while distance >= 1:
+        half = x.shape[dim] // 2
+        low = lax.slice_in_dim(x, 0, half, axis=dim)
+        high = lax.slice_in_dim(x, half, 2 * half, axis=dim)
+        upper = (index & distance) != 0
+        keep = jnp.where(upper, high, low)
+        send = jnp.where(upper, low, high)
+        x = keep + swap_with(send.astype(jnp.bfloat16), axis, distance, size).astype(jnp.float32)
+        distance //= 2
+    return x
+
+
 def shards(
+    axis_sizes,
     hidden_in,
     queries,
     cache_pool,
@@ -129,12 +150,9 @@
     values = jnp.einsum("rhc,hcv->rhv", received, value_up, preferred_element_type=jnp.float32)
     values = values.astype(jnp.bfloat16).reshape(row_count, heads_here * value_dim)
     group_values = lax.all_gather(values, "sub", axis=1, tiled=True)
-    attention = lax.psum_scatter(
-        jnp.dot(group_values, out_proj, preferred_element_type=jnp.float32).astype(jnp.bfloat16),
-        "dp",
-        scatter_dimension=0,
-        tiled=True,
-    ).astype(jnp.float32)
+    attention = halving_scatter(
+        jnp.dot(group_values, out_proj, preferred_element_type=jnp.float32), "dp", axis_sizes["dp"]
+    )
     residual = hidden_in.astype(jnp.float32) + attention
     squares = lax.psum(jnp.sum(residual * residual, axis=1), "sub")
     scale_rows = lax.rsqrt(squares / float(D) + 1e-06)
@@ -147,12 +165,9 @@
     hidden_units = (jax.nn.silu(summed[:, :units_here]) * summed[:, units_here:]).astype(
         jnp.bfloat16
     )
-    feed_forward = lax.psum_scatter(
-        jnp.dot(hidden_units, down_proj, preferred_element_type=jnp.float32).astype(jnp.bfloat16),
-        "dp",
-        scatter_dimension=0,
-        tiled=True,
-    ).astype(jnp.float32)
+    feed_forward = halving_scatter(
+        jnp.dot(hidden_units, down_proj, preferred_element_type=jnp.float32), "dp", axis_sizes["dp"]
+    )
     return (attention.astype(jnp.bfloat16), (residual + feed_forward).astype(jnp.bfloat16))
 
 
@@ -171,7 +186,7 @@
         P("dp", "sub"),
     )
     return jax.shard_map(
-        shards,
+        functools.partial(shards, dict(mesh.shape)),
         mesh=mesh,
         in_specs=placed,
         out_specs=(P(("grp", "dp"), "sub"), P(("grp", "dp"), "sub")),

time: 204 us -> 175 us (0.86)
  blocking collectives: 63.9 us -> 30.6 us
  starting transfers between devices: 0.12 us -> 15.3 us
  waiting for transfers between devices: 77.7 us -> 73.3 us
  Pallas kernels: 17.3 us -> 14.9 us
  other arithmetic: 5.38 us -> 3.2 us
    reduce_scatter x2 -> x0, waiting for transfers between devices: 36.7 us -> none  [the longest x1 19.1 us: shards(): lax.psum_scatter(jnp.dot(hidden_units, down_proj, preferred_element_type=...]
    all_to_all x1 -> x0, blocking collectives: 30.7 us -> none  [shards(): lax.all_to_all(contexts[None], ('dp', 'sub'), split_axis=2, concat_axis=0...]
    all_to_all x0 -> x1, waiting for transfers between devices: none -> 15.6 us  [shards(): lax.all_to_all(contexts[None], ('dp', 'sub'), split_axis=2, concat_axis=0...]
    all_to_all x0 -> x1, starting transfers between devices: none -> 12.9 us  [shards(): lax.all_to_all(contexts[None], ('dp', 'sub'), split_axis=2, concat_axis=0...]
    ppermute x0 -> x4, waiting for transfers between devices: none -> 9.19 us  [swap_with(): return lax.ppermute(x, axis, [(i, i ^ distance) for i in range(size)])]
    psum x1, waiting for transfers between devices: 41 us -> 48.4 us  [shards(): summed = lax.psum(partials.astype(jnp.bfloat16), 'sub').astype(jnp.float32)]
    psum x1, blocking collectives: 11.7 us -> 8.84 us  [shards(): squares = lax.psum(jnp.sum(residual * residual, axis=1), 'sub')]
    ppermute x0 -> x4, starting transfers between devices: none -> 2.35 us  [swap_with(): return lax.ppermute(x, axis, [(i, i ^ distance) for i in range(size)])]
  transfers between devices with their start and end apart: 3 -> 6, of which waited for: 3 -> 6; matrix products, arithmetic and copies ran while one was open for 0% -> 0% of each run, Pallas kernels for 0% -> 0%
where the time goes in v2:
time: 175 us; the launch traced here: 176 us
  waiting for transfers between devices  73.3 us (42%)
  blocking collectives  30.6 us (17%)
  matrix products  20.5 us (12%)
  starting transfers between devices  15.3 us (9%)
  Pallas kernels  14.9 us (9%)
  between operations  14.2 us (8%)
  local copies, waits for them, and re-layouts  4.32 us (2%)
  other arithmetic  3.2 us (2%)
    psum x1, waiting for transfers between devices, shards(): summed = lax.psum(partials.astype(jnp.bfloat16), 'sub').astype(jnp.float32)  48.4 us
    all_gather x1, blocking collectives, shards(): group_values = lax.all_gather(values, 'sub', axis=1, tiled=True)  16.1 us
    all_to_all x1, waiting for transfers between devices, shards(): lax.all_to_all(contexts[None], ('dp', 'sub'), split_axis=2, concat_axis=0...  15.6 us
    pallas_call x1, Pallas kernels, attend_all(): pl.pallas_call(kernel, out_shape=jax.ShapeDtypeStruct((req_dev, head_coun...  14.9 us
    all_to_all x1, starting transfers between devices, shards(): lax.all_to_all(contexts[None], ('dp', 'sub'), split_axis=2, concat_axis=0...  12.9 us
    ppermute x4, waiting for transfers between devices, swap_with(): return lax.ppermute(x, axis, [(i, i ^ distance) for i in range(size)])  9.19 us
    psum x1, blocking collectives, shards(): squares = lax.psum(jnp.sum(residual * residual, axis=1), 'sub')  8.84 us
    dot_general x1, matrix products, shards(): jnp.dot(group_values, out_proj, preferred_element_type=jnp.float32)  5.9 us
  transfers between devices with their start and end apart: 6, of which 6 were waited for; matrix products, arithmetic and copies ran while one was open for 0% of the time, Pallas kernels for 0%

profile of v2, /device:TPU:0, one launch (start us, length us, event | category | flops | bytes accessed | tf_op | source)
XLA Modules:
  0.0 176.4 jit_solution(2948266706225502374)
XLA Ops:
  7.2 0.0 copy-start
  7.2 1.4 copy.18.queries
  8.6 0.0 copy-start.1
  8.6 0.7 copy-done.1
  9.3 0.0 copy-start.2
  9.3 0.7 copy-done.2
  10.0 14.9 %shard_map.122 = bf16[4,128,512]{2,1,0:T(8,128)(2,1)S(1)} custom-call(s32[4,16]{1,0:T(4,128)S(1)} %copy-done.1, s32[4]{0:T(128)S(1)} %copy-done.2, bf16[4,128,576]{2,1,0:T(8,128)(2,1)S(1)} %copy.18.queries, bf16[64,576,128]{2,1,0:T(8,128)(2,1)} %bitcast.24), custom_call_target="tpu_custom_call" | custom-call | tf_op jit(solution)/shard_map/pallas_call | solution.py:83
  24.9 1.2 copy.19
  26.1 12.9 %all-to-all-start = ((bf16[1,4,128,512]{3,1,0,2:T(4,128)(2,1)}), bf16[1,4,128,512]{3,1,0,2:T(4,128)(2,1)S(1)}, u32[]{:S(2)}, u32[]{:S(2)}) async-start(bf16[1,4,128,512]{3,1,0,2:T(4,128)(2,1)} %copy.19), calls=%async_computation | async-start | bytes 1048576 | tf_op jit(solution)/shard_map/all_to_all | solution.py:145
  39.1 0.0 all-reduce.2.cloned.1.call-start
  39.1 15.6 %all-to-all-done = bf16[1,4,128,512]{3,1,0,2:T(4,128)(2,1)S(1)} async-done(((bf16[1,4,128,512]{3,1,0,2:T(4,128)(2,1)}), bf16[1,4,128,512]{3,1,0,2:T(4,128)(2,1)S(1)}, u32[]{:S(2)}, u32[]{:S(2)}) %all-to-all-start) | async-done | bytes 524320 | tf_op jit(solution)/shard_map/all_to_all | solution.py:145
  54.7 0.2 copy.25
  54.9 0.1 reshape.13
  55.1 0.0 copy-done
  55.1 0.3 fusion
  55.4 16.1 %all_gather.6 = bf16[64,4096]{1,0:T(8,128)(2,1)S(1)} all-gather(bf16[64,1024]{1,0:T(8,128)(2,1)S(1)} %bitcast.27), channel_id=1, replica_groups=mesh['grp'=2,'dp'=4,'sub'=4] {'sub'}, dimensions={1}, use_global_device_ids=true | all-gather | bytes 655360 | tf_op jit(solution)/shard_map/all_gather | solution.py:152
  71.5 0.0 copy-start.4
  71.5 0.0 copy-start.3
  71.5 5.9 %fusion.6 = f32[64,1280]{1,0:T(8,128)S(1)} fusion(bf16[64,4096]{1,0:T(8,128)(2,1)S(1)} %all_gather.6, bf16[4096,1280]{1,0:T(8,128)(2,1)} %param.17), kind=kOutput, calls=%fused_computation.24 | convolution fusion | flops 671088640 | bytes 11337728 | tf_op jit(solution)/shard_map/dot_general | solution.py:154
  77.4 0.7 collective-permute-start
  78.1 3.8 %collective-permute-done = bf16[32,1280]{1,0:T(8,128)(2,1)S(1)} collective-permute-done((bf16[32,1280]{1,0:T(8,128)(2,1)S(1)}, bf16[32,1280]{1,0:T(8,128)(2,1)S(1)}, u32[]{:S(2)}, u32[]{:S(2)}) %collective-permute-start) | collective-permute-done | bytes 81952 | tf_op jit(solution)/shard_map/ppermute | solution.py:104
  82.0 0.1 collective-permute-start.1
  82.1 0.0 copy-done.4
  82.1 1.2 collective-permute-done.1
  83.3 0.0 copy-done.3
  83.3 0.1 multiply_reduce_fusion
  83.4 8.8 %psum.14 = f32[16]{0:T(128)S(1)} all-reduce(f32[16]{0:T(128)S(1)} %get-tuple-element.2), channel_id=1, replica_groups=mesh['grp'=2,'dp'=4,'sub'=4] {'sub'}, use_global_device_ids=true, to_apply=%region_1.2 | all-reduce | flops 16 | bytes 128 | tf_op jit(solution)/shard_map/psum | solution.py:157
  92.2 0.1 multiply_convert_fusion
  92.3 5.7 %all_gather.7 = bf16[64,1280]{1,0:T(8,128)(2,1)S(1)} all-gather(bf16[16,1280]{1,0:T(8,128)(2,1)S(1)} %multiply_convert_fusion), channel_id=1, replica_groups=mesh['grp'=2,'dp'=4,'sub'=4] {'dp'}, dimensions={0}, use_global_device_ids=true | all-gather | bytes 204800 | tf_op jit(solution)/shard_map/all_gather | solution.py:160
  98.1 4.7 %convolution_convert_fusion = bf16[64,3072]{1,0:T(8,128)(2,1)S(1)} fusion(bf16[64,1280]{1,0:T(8,128)(2,1)S(1)} %all_gather.7, bf16[1280,3072]{1,0:T(8,128)(2,1)} %param.20), kind=kOutput, calls=%fused_computation | convolution fusion | flops 503513088 | bytes 8421376 | tf_op jit(solution)/shard_map/dot_general | solution.py:162
  102.8 4.7 %convolution_convert_fusion.1 = bf16[64,3072]{1,0:T(8,128)(2,1)S(1)} fusion(bf16[64,1280]{1,0:T(8,128)(2,1)S(1)} %all_gather.7, bf16[1280,3072]{1,0:T(8,128)(2,1)} %param.19), kind=kOutput, calls=%fused_computation.1 | convolution fusion | flops 503513088 | bytes 8421376 | tf_op jit(solution)/shard_map/dot_general | solution.py:161
  107.6 1.0 pad_maximum_fusion
  108.5 0.0 all-reduce.2.cloned.1.call-update
  108.5 48.4 %all-reduce.2.cloned.1.call-done = bf16[64,6144]{1,0:T(8,128)(2,1)} async-done(((bf16[64,6144]{1,0:T(8,128)(2,1)}), bf16[64,6144]{1,0:T(8,128)(2,1)}) %all-reduce.2.cloned.1.call-update) | async-done | bytes 786448 | tf_op jit(solution)/shard_map/psum | solution.py:164
  157.0 1.2 convert_element_type.62
  158.2 4.8 %fusion.2 = f32[64,1280]{1,0:T(8,128)S(1)} fusion(bf16[3072,1280]{1,0:T(8,128)(2,1)} %param.21, f32[64,6144]{1,0:T(8,128)S(1)} %convert_element_type.62), kind=kOutput, calls=%fused_computation.8 | convolution fusion | flops 504496128 | bytes 9764864 | tf_op jit(solution)/shard_map/dot_general | solution.py:169
  163.0 1.5 collective-permute-start.2
  164.6 3.0 %collective-permute-done.2 = bf16[32,1280]{1,0:T(8,128)(2,1)S(1)} collective-permute-done((bf16[32,1280]{1,0:T(8,128)(2,1)S(1)}, bf16[32,1280]{1,0:T(8,128)(2,1)S(1)}, u32[]{:S(2)}, u32[]{:S(2)}) %collective-permute-start.2) | collective-permute-done | bytes 81952 | tf_op jit(solution)/shard_map/ppermute | solution.py:104
  167.6 0.1 collective-permute-start.3
  167.7 1.2 collective-permute-done.3
  168.9 0.7 add_convert_fusion
  (9 shorter events, 0.2 us)
Async XLA Ops:
  7.2 47.9 %copy-start = (bf16[8,512,128]{2,1,0:T(8,128)(2,1)S(1)}, bf16[8,512,128]{2,1,0:T(8,128)(2,1)}, u32[]{:S(2)}) copy-start(bf16[8,512,128]{2,1,0:T(8,128)(2,1)} %param.16) | copy-start | bytes 3145732
  8.6 0.7 copy-start.1
  9.3 0.7 copy-start.2
  26.1 28.6 %all-to-all-start = ((bf16[1,4,128,512]{3,1,0,2:T(4,128)(2,1)}), bf16[1,4,128,512]{3,1,0,2:T(4,128)(2,1)S(1)}, u32[]{:S(2)}, u32[]{:S(2)}) async-start(bf16[1,4,128,512]{3,1,0,2:T(4,128)(2,1)} %copy.19), calls=%async_computation | async-start | bytes 1048576 | tf_op jit(solution)/shard_map/all_to_all | solution.py:145
  39.1 117.9 %all-reduce.2.cloned.1.call-start = ((), (), s32[]{:S(2)}) async-start(), calls=%async_computation.1 | async-start | bytes 1572864 | tf_op jit(solution)/shard_map/psum | solution.py:164
  71.5 10.6 %copy-start.4 = (bf16[1280]{0:T(1024)(128)(2,1)S(1)}, bf16[1280]{0:T(1024)(128)(2,1)}, u32[]{:S(2)}) copy-start(bf16[1280]{0:T(1024)(128)(2,1)} %param.18) | copy-start | bytes 7684
  71.5 11.8 %copy-start.3 = (bf16[16,1280]{1,0:T(8,128)(2,1)S(1)}, bf16[16,1280]{1,0:T(8,128)(2,1)}, u32[]{:S(2)}) copy-start(bf16[16,1280]{1,0:T(8,128)(2,1)} %param.11) | copy-start | bytes 122884
  77.4 4.5 %collective-permute-start = (bf16[32,1280]{1,0:T(8,128)(2,1)S(1)}, bf16[32,1280]{1,0:T(8,128)(2,1)S(1)}, u32[]{:S(2)}, u32[]{:S(2)}) collective-permute-start(bf16[32,1280]{1,0:T(8,128)(2,1)S(1)} %select_convert_fusion.1), channel_id=1, source_target_pairs={{0,8},{4,12},{8,0},{12,4},{1,9},{5,13},{9,1},{13,5},{2,10},{6,14},... | collective-permute-start | bytes 245768 | tf_op jit(solution)/shard_map/ppermute | solution.py:104
  82.0 1.3 collective-permute-start.1
  163.0 4.5 %collective-permute-start.2 = (bf16[32,1280]{1,0:T(8,128)(2,1)S(1)}, bf16[32,1280]{1,0:T(8,128)(2,1)S(1)}, u32[]{:S(2)}, u32[]{:S(2)}) collective-permute-start(bf16[32,1280]{1,0:T(8,128)(2,1)S(1)} %select_convert_fusion), channel_id=1, source_target_pairs={{0,8},{4,12},{8,0},{12,4},{1,9},{5,13},{9,1},{13,5},{2,10},{6,14},... | collective-permute-start | bytes 245768 | tf_op jit(solution)/shard_map/ppermute | solution.py:104
  167.6 1.3 collective-permute-start.3
Sparse Core Ops, SparseCore 0:
  108.7 48.2 all-reduce.1

commit v3 on v2

--- a/solution.py
+++ b/solution.py
@@ -120,6 +120,35 @@
     return x
 
 
+def nearest_first_scatter(x, axis, size):
+    index = lax.axis_index(axis)
+    x = x.astype(jnp.float32)
+    distance = 1
+    while distance < size:
+        pairs = x.reshape(x.shape[:1] + (x.shape[1] // 2, 2) + x.shape[2:])
+        even = pairs[:, :, 0]
+        odd = pairs[:, :, 1]
+        upper = (index & distance) != 0
+        keep = jnp.where(upper, odd, even)
+        send = jnp.where(upper, even, odd)
+        x = keep + swap_with(send.astype(jnp.bfloat16), axis, distance, size).astype(jnp.float32)
+        distance *= 2
+    return x[:, 0]
+
+
+def doubling_gather(x, axis, size, dim):
+    index = lax.axis_index(axis)
+    distance = 1
+    while distance < size:
+        got = swap_with(x, axis, distance, size)
+        upper = (index & distance) != 0
+        x = jnp.where(
+            upper, jnp.concatenate([got, x], axis=dim), jnp.concatenate([x, got], axis=dim)
+        )
+        distance *= 2
+    return x
+
+
 def shards(
     axis_sizes,
     hidden_in,
@@ -160,11 +189,19 @@
     piece = lax.all_gather(normed, "dp", axis=0, tiled=True)
     gate_part = jnp.dot(piece, gate_proj, preferred_element_type=jnp.float32)
     up_part = jnp.dot(piece, up_proj, preferred_element_type=jnp.float32)
-    partials = jnp.concatenate([gate_part, up_part], axis=1)
-    summed = lax.psum(partials.astype(jnp.bfloat16), "sub").astype(jnp.float32)
-    hidden_units = (jax.nn.silu(summed[:, :units_here]) * summed[:, units_here:]).astype(
-        jnp.bfloat16
-    )
+    sub_size = axis_sizes["sub"]
+    row_count = piece.shape[0]
+    unit_chunk = units_here // sub_size
+    partials = jnp.stack(
+        [
+            gate_part.reshape(row_count, sub_size, unit_chunk),
+            up_part.reshape(row_count, sub_size, unit_chunk),
+        ],
+        axis=2,
+    )
+    summed = nearest_first_scatter(partials, "sub", sub_size)
+    hidden_chunk = (jax.nn.silu(summed[:, 0]) * summed[:, 1]).astype(jnp.bfloat16)
+    hidden_units = doubling_gather(hidden_chunk, "sub", sub_size, 1)
     feed_forward = halving_scatter(
         jnp.dot(hidden_units, down_proj, preferred_element_type=jnp.float32), "dp", axis_sizes["dp"]
     )

time: 175 us -> 162 us (0.926); the launches traced: 176 us -> 160 us
  between operations: 14.2 us -> 0.87 us
  waiting for transfers between devices: 73.3 us -> 60.1 us
  Pallas kernels: 14.9 us -> 20.1 us
  local copies, waits for them, and re-layouts: 4.32 us -> 9.08 us
  other arithmetic: 3.2 us -> 1.4 us
    psum x1 -> x0, waiting for transfers between devices: 48.4 us -> none  [shards(): summed = lax.psum(partials.astype(jnp.bfloat16), 'sub').astype(jnp.float32)]
    ppermute x4 -> x8, waiting for transfers between devices: 9.19 us -> 44.4 us  [swap_with(): return lax.ppermute(x, axis, [(i, i ^ distance) for i in range(size)])]
    pallas_call x1, Pallas kernels: 14.9 us -> 20.1 us  [attend_all(): pl.pallas_call(kernel, out_shape=jax.ShapeDtypeStruct((req_dev, head_coun...]
    ppermute x4 -> x8, starting transfers between devices: 2.35 us -> 5.87 us  [swap_with(): return lax.ppermute(x, axis, [(i, i ^ distance) for i in range(size)])]
    another operation x0 -> x3, local copies, waits for them, and re-layouts: none -> 3.48 us  [shards(): jnp.stack([gate_part.reshape(row_count, sub_size, unit_chunk), up_part.re...]
    all_to_all x1, starting transfers between devices: 12.9 us -> 11.1 us  [shards(): lax.all_to_all(contexts[None], ('dp', 'sub'), split_axis=2, concat_axis=0...]
    unnamed x11 -> x12, local copies, waits for them, and re-layouts: 2.79 us -> 4.08 us
  transfers between devices with their start and end apart: 6 -> 9, of which waited for: 6 -> 9; matrix products, arithmetic and copies ran while one was open for 0% -> 0% of each run, Pallas kernels for 0% -> 0%
where the time goes in v3:
time: 162 us; the launch traced here: 160 us
  waiting for transfers between devices  60.1 us (37%)
  blocking collectives  30.7 us (19%)
  matrix products  21.2 us (13%)
  Pallas kernels  20.1 us (12%)
  starting transfers between devices  17 us (10%)
  local copies, waits for them, and re-layouts  9.08 us (6%)
    ppermute x8, waiting for transfers between devices, swap_with(): return lax.ppermute(x, axis, [(i, i ^ distance) for i in range(size)])  44.4 us
    pallas_call x1, Pallas kernels, attend_all(): pl.pallas_call(kernel, out_shape=jax.ShapeDtypeStruct((req_dev, head_coun...  20.1 us
    all_gather x1, blocking collectives, shards(): group_values = lax.all_gather(values, 'sub', axis=1, tiled=True)  16.1 us
    all_to_all x1, waiting for transfers between devices, shards(): lax.all_to_all(contexts[None], ('dp', 'sub'), split_axis=2, concat_axis=0...  15.7 us
    all_to_all x1, starting transfers between devices, shards(): lax.all_to_all(contexts[None], ('dp', 'sub'), split_axis=2, concat_axis=0...  11.1 us
    psum x1, blocking collectives, shards(): squares = lax.psum(jnp.sum(residual * residual, axis=1), 'sub')  8.86 us
    dot_general x1, matrix products, shards(): jnp.dot(group_values, out_proj, preferred_element_type=jnp.float32)  5.9 us
    ppermute x8, starting transfers between devices, swap_with(): return lax.ppermute(x, axis, [(i, i ^ distance) for i in range(size)])  5.87 us
  transfers between devices with their start and end apart: 9, of which 9 were waited for; matrix products, arithmetic and copies ran while one was open for 0% of the time, Pallas kernels for 0%

profile of v3, /device:TPU:0, one launch (start us, length us, event | category | flops | bytes accessed | tf_op | source)
XLA Modules:
  0.0 160.5 jit_solution(105758133128900624)
XLA Ops:
  0.6 0.0 copy-start
  0.6 1.4 copy.28.queries
  2.1 0.0 copy-start.1
  2.1 0.7 copy-done.1
  2.8 0.0 copy-start.2
  2.8 0.7 copy-done.2
  3.4 20.1 %shard_map.122 = bf16[4,128,512]{2,1,0:T(8,128)(2,1)S(1)} custom-call(s32[4,16]{1,0:T(4,128)S(1)} %copy-done.1, s32[4]{0:T(128)S(1)} %copy-done.2, bf16[4,128,576]{2,1,0:T(8,128)(2,1)S(1)} %copy.28.queries, bf16[64,576,128]{2,1,0:T(8,128)(2,1)} %bitcast.50), custom_call_target="tpu_custom_call" | custom-call | tf_op jit(solution)/shard_map/pallas_call | solution.py:83
  23.5 1.2 copy.29
  24.7 11.1 %all-to-all-start = ((bf16[1,4,128,512]{3,1,0,2:T(4,128)(2,1)}), bf16[1,4,128,512]{3,1,0,2:T(4,128)(2,1)S(1)}, u32[]{:S(2)}, u32[]{:S(2)}) async-start(bf16[1,4,128,512]{3,1,0,2:T(4,128)(2,1)} %copy.29), calls=%async_computation | async-start | bytes 1048576 | tf_op jit(solution)/shard_map/all_to_all | solution.py:174
  35.9 15.7 %all-to-all-done = bf16[1,4,128,512]{3,1,0,2:T(4,128)(2,1)S(1)} async-done(((bf16[1,4,128,512]{3,1,0,2:T(4,128)(2,1)}), bf16[1,4,128,512]{3,1,0,2:T(4,128)(2,1)S(1)}, u32[]{:S(2)}, u32[]{:S(2)}) %all-to-all-start) | async-done | bytes 524320 | tf_op jit(solution)/shard_map/all_to_all | solution.py:174
  51.6 0.2 copy.39
  51.7 0.1 reshape.75
  51.9 0.0 copy-done
  51.9 0.3 fusion
  52.2 16.1 %all_gather.6 = bf16[64,4096]{1,0:T(8,128)(2,1)S(1)} all-gather(bf16[64,1024]{1,0:T(8,128)(2,1)S(1)} %bitcast.53), channel_id=1, replica_groups=mesh['grp'=2,'dp'=4,'sub'=4] {'sub'}, dimensions={1}, use_global_device_ids=true | all-gather | bytes 655360 | tf_op jit(solution)/shard_map/all_gather | solution.py:181
  68.3 0.0 copy-start.4
  68.3 0.0 copy-start.3
  68.3 5.9 %fusion.15 = f32[64,1280]{1,0:T(8,128)S(1)} fusion(bf16[64,4096]{1,0:T(8,128)(2,1)S(1)} %all_gather.6, bf16[4096,1280]{1,0:T(8,128)(2,1)} %param.17), kind=kOutput, calls=%fused_computation.40 | convolution fusion | flops 671088640 | bytes 11337728 | tf_op jit(solution)/shard_map/dot_general | solution.py:183
  74.2 0.7 collective-permute-start
  74.9 3.8 %collective-permute-done = bf16[32,1280]{1,0:T(8,128)(2,1)S(1)} collective-permute-done((bf16[32,1280]{1,0:T(8,128)(2,1)S(1)}, bf16[32,1280]{1,0:T(8,128)(2,1)S(1)}, u32[]{:S(2)}, u32[]{:S(2)}) %collective-permute-start) | collective-permute-done | bytes 81952 | tf_op jit(solution)/shard_map/ppermute | solution.py:104
  78.8 0.1 collective-permute-start.1
  78.9 0.0 copy-done.4
  78.9 1.2 collective-permute-done.1
  80.1 0.0 copy-done.3
  80.1 0.1 multiply_reduce_fusion
  80.2 8.9 %psum.7 = f32[16]{0:T(128)S(1)} all-reduce(f32[16]{0:T(128)S(1)} %get-tuple-element.2), channel_id=1, replica_groups=mesh['grp'=2,'dp'=4,'sub'=4] {'sub'}, use_global_device_ids=true, to_apply=%region_1.2 | all-reduce | flops 16 | bytes 128 | tf_op jit(solution)/shard_map/psum | solution.py:186
  89.1 0.1 multiply_convert_fusion
  89.2 5.7 %all_gather.7 = bf16[64,1280]{1,0:T(8,128)(2,1)S(1)} all-gather(bf16[16,1280]{1,0:T(8,128)(2,1)S(1)} %multiply_convert_fusion), channel_id=1, replica_groups=mesh['grp'=2,'dp'=4,'sub'=4] {'dp'}, dimensions={0}, use_global_device_ids=true | all-gather | bytes 204800 | tf_op jit(solution)/shard_map/all_gather | solution.py:189
  94.9 4.7 %fusion.16 = f32[64,3072]{1,0:T(8,128)S(1)} fusion(bf16[64,1280]{1,0:T(8,128)(2,1)S(1)} %all_gather.7, bf16[1280,3072]{1,0:T(8,128)(2,1)} %param.19), kind=kOutput, calls=%fused_computation.41 | convolution fusion | flops 503316480 | bytes 8814592 | tf_op jit(solution)/shard_map/dot_general | solution.py:190
  99.6 1.6 stack.7
  101.2 1.3 copy_dynamic-update-slice_fusion.1
  102.5 5.6 %fusion.17 = f32[64,3072]{1,0:T(8,128)} fusion(bf16[64,1280]{1,0:T(8,128)(2,1)S(1)} %all_gather.7, bf16[1280,3072]{1,0:T(8,128)(2,1)} %param.20), kind=kOutput, calls=%fused_computation.42 | convolution fusion | flops 503316480 | bytes 8814592 | tf_op jit(solution)/shard_map/dot_general | solution.py:191
  108.1 1.8 %stack.8 = f32[64,2,2,1,768]{4,2,1,0,3:T(2,128)S(1)} reshape(f32[64,3072]{1,0:T(8,128)} %fusion.17) | data formatting | bytes 1572864 | tf_op jit(solution)/shard_map/stack | solution.py:195
  109.9 0.1 copy_dynamic-update-slice_fusion
  110.0 0.1 fusion.2
  110.1 1.3 collective-permute-start.2
  111.4 10.1 %collective-permute-done.2 = bf16[64,2,2,768]{3,0,2,1:T(8,128)(2,1)S(1)} collective-permute-done((bf16[64,2,2,768]{3,0,2,1:T(8,128)(2,1)S(1)}, bf16[64,2,2,768]{3,0,2,1:T(8,128)(2,1)S(1)}, u32[]{:S(2)}, u32[]{:S(2)}) %collective-permute-start.2) | collective-permute-done | bytes 393248 | tf_op jit(solution)/shard_map/ppermute | solution.py:104
  121.5 0.1 fusion.1
  121.7 0.2 collective-permute-start.3
  121.9 11.3 %collective-permute-done.3 = bf16[64,1,2,768]{3,0,2,1:T(8,128)(2,1)S(1)} collective-permute-done((bf16[64,1,2,768]{3,0,2,1:T(8,128)(2,1)S(1)}, bf16[64,1,2,768]{3,0,2,1:T(8,128)(2,1)S(1)}, u32[]{:S(2)}, u32[]{:S(2)}) %collective-permute-start.3) | collective-permute-done | bytes 196640 | tf_op jit(solution)/shard_map/ppermute | solution.py:104
  133.2 0.1 fusion.9
  133.3 0.1 fusion.13
  133.3 0.1 collective-permute-start.4
  133.4 4.6 %collective-permute-done.4 = bf16[64,768]{1,0:T(8,128)(2,1)S(1)} collective-permute-done((bf16[64,768]{1,0:T(8,128)(2,1)S(1)}, bf16[64,768]{1,0:T(8,128)(2,1)S(1)}, u32[]{:S(2)}, u32[]{:S(2)}) %collective-permute-start.4) | collective-permute-done | bytes 98336 | tf_op jit(solution)/shard_map/ppermute | solution.py:104
  138.1 0.2 collective-permute-start.5
  138.3 9.6 %collective-permute-done.5 = bf16[64,1536]{1,0:T(8,128)(2,1)S(1)} collective-permute-done((bf16[64,1536]{1,0:T(8,128)(2,1)S(1)}, bf16[64,1536]{1,0:T(8,128)(2,1)S(1)}, u32[]{:S(2)}, u32[]{:S(2)}) %collective-permute-start.5) | collective-permute-done | bytes 196640 | tf_op jit(solution)/shard_map/ppermute | solution.py:104
  147.9 4.7 %fusion.3 = f32[64,1280]{1,0:T(8,128)S(1)} fusion(bf16[3072,1280]{1,0:T(8,128)(2,1)} %param.21, bf16[64,1536]{1,0:T(8,128)(2,1)S(1)} %maximum_select_fusion.2, bf16[64,1536]{1,0:T(8,128)(2,1)S(1)} %collective-permute-done.5, pred[]{:T(512)S(6)} %ne.18), kind=kOutput, calls=%fused_computation.10 | convolution fusion | flops 505085952 | bytes 8585217 | tf_op jit(solution)/shard_map/dot_general | solution.py:206
  152.7 3.2 %collective-permute-start.6 = (bf16[32,1280]{1,0:T(8,128)(2,1)S(1)}, bf16[32,1280]{1,0:T(8,128)(2,1)S(1)}, u32[]{:S(2)}, u32[]{:S(2)}) collective-permute-start(bf16[32,1280]{1,0:T(8,128)(2,1)S(1)} %select_convert_fusion.2), channel_id=1, source_target_pairs={{0,8},{4,12},{8,0},{12,4},{1,9},{5,13},{9,1},{13,5},{2,10},{6,14},... | collective-permute-start | bytes 245768 | tf_op jit(solution)/shard_map/ppermute | solution.py:104
  155.9 2.6 %collective-permute-done.6 = bf16[32,1280]{1,0:T(8,128)(2,1)S(1)} collective-permute-done((bf16[32,1280]{1,0:T(8,128)(2,1)S(1)}, bf16[32,1280]{1,0:T(8,128)(2,1)S(1)}, u32[]{:S(2)}, u32[]{:S(2)}) %collective-permute-start.6) | collective-permute-done | bytes 81952 | tf_op jit(solution)/shard_map/ppermute | solution.py:104
  158.5 0.1 collective-permute-start.7
  158.6 1.2 collective-permute-done.7
  159.8 0.7 add_convert_fusion
  (11 shorter events, 0.2 us)
Async XLA Ops:
  0.6 51.2 %copy-start = (bf16[8,512,128]{2,1,0:T(8,128)(2,1)S(1)}, bf16[8,512,128]{2,1,0:T(8,128)(2,1)}, u32[]{:S(2)}) copy-start(bf16[8,512,128]{2,1,0:T(8,128)(2,1)} %param.16) | copy-start | bytes 3145732
  2.1 0.7 copy-start.1
  2.8 0.7 copy-start.2
  24.7 26.8 %all-to-all-start = ((bf16[1,4,128,512]{3,1,0,2:T(4,128)(2,1)}), bf16[1,4,128,512]{3,1,0,2:T(4,128)(2,1)S(1)}, u32[]{:S(2)}, u32[]{:S(2)}) async-start(bf16[1,4,128,512]{3,1,0,2:T(4,128)(2,1)} %copy.29), calls=%async_computation | async-start | bytes 1048576 | tf_op jit(solution)/shard_map/all_to_all | solution.py:174
  68.3 10.6 %copy-start.4 = (bf16[1280]{0:T(1024)(128)(2,1)S(1)}, bf16[1280]{0:T(1024)(128)(2,1)}, u32[]{:S(2)}) copy-start(bf16[1280]{0:T(1024)(128)(2,1)} %param.18) | copy-start | bytes 7684
  68.3 11.8 %copy-start.3 = (bf16[16,1280]{1,0:T(8,128)(2,1)S(1)}, bf16[16,1280]{1,0:T(8,128)(2,1)}, u32[]{:S(2)}) copy-start(bf16[16,1280]{1,0:T(8,128)(2,1)} %param.11) | copy-start | bytes 122884
  74.2 4.5 %collective-permute-start = (bf16[32,1280]{1,0:T(8,128)(2,1)S(1)}, bf16[32,1280]{1,0:T(8,128)(2,1)S(1)}, u32[]{:S(2)}, u32[]{:S(2)}) collective-permute-start(bf16[32,1280]{1,0:T(8,128)(2,1)S(1)} %select_convert_fusion.3), channel_id=1, source_target_pairs={{0,8},{4,12},{8,0},{12,4},{1,9},{5,13},{9,1},{13,5},{2,10},{6,14},... | collective-permute-start | bytes 245768 | tf_op jit(solution)/shard_map/ppermute | solution.py:104
  78.8 1.3 collective-permute-start.1
  110.1 11.4 %collective-permute-start.2 = (bf16[64,2,2,768]{3,0,2,1:T(8,128)(2,1)S(1)}, bf16[64,2,2,768]{3,0,2,1:T(8,128)(2,1)S(1)}, u32[]{:S(2)}, u32[]{:S(2)}) collective-permute-start(bf16[64,2,2,768]{3,0,2,1:T(8,128)(2,1)S(1)} %fusion.2), channel_id=1, source_target_pairs={{0,1},{1,0},{2,3},{3,2},{4,5},{5,4},{6,7},{7,6},{8,9},{9,8},{10,11... | collective-permute-start | bytes 1179656 | tf_op jit(solution)/shard_map/ppermute | solution.py:104
  121.7 11.5 %collective-permute-start.3 = (bf16[64,1,2,768]{3,0,2,1:T(8,128)(2,1)S(1)}, bf16[64,1,2,768]{3,0,2,1:T(8,128)(2,1)S(1)}, u32[]{:S(2)}, u32[]{:S(2)}) collective-permute-start(bf16[64,1,2,768]{3,0,2,1:T(8,128)(2,1)S(1)} %fusion.11), channel_id=1, source_target_pairs={{0,2},{1,3},{2,0},{3,1},{4,6},{5,7},{6,4},{7,5},{8,10},{9,11},{10,... | collective-permute-start | bytes 589832 | tf_op jit(solution)/shard_map/ppermute | solution.py:104
  133.3 4.7 %collective-permute-start.4 = (bf16[64,768]{1,0:T(8,128)(2,1)S(1)}, bf16[64,768]{1,0:T(8,128)(2,1)S(1)}, u32[]{:S(2)}, u32[]{:S(2)}) collective-permute-start(bf16[64,768]{1,0:T(8,128)(2,1)S(1)} %fusion.13), channel_id=1, source_target_pairs={{0,1},{1,0},{2,3},{3,2},{4,5},{5,4},{6,7},{7,6},{8,9},{9,8},{10,11... | collective-permute-start | bytes 294920 | tf_op jit(solution)/shard_map/ppermute | solution.py:104
  138.1 9.8 %collective-permute-start.5 = (bf16[64,1536]{1,0:T(8,128)(2,1)S(1)}, bf16[64,1536]{1,0:T(8,128)(2,1)S(1)}, u32[]{:S(2)}, u32[]{:S(2)}) collective-permute-start(bf16[64,1536]{1,0:T(8,128)(2,1)S(1)} %maximum_select_fusion.2), channel_id=1, source_target_pairs={{0,2},{1,3},{2,0},{3,1},{4,6},{5,7},{6,4},{7,5},{8,10},{9,11},{10,... | collective-permute-start | bytes 589832 | tf_op jit(solution)/shard_map/ppermute | solution.py:104
  152.7 5.8 %collective-permute-start.6 = (bf16[32,1280]{1,0:T(8,128)(2,1)S(1)}, bf16[32,1280]{1,0:T(8,128)(2,1)S(1)}, u32[]{:S(2)}, u32[]{:S(2)}) collective-permute-start(bf16[32,1280]{1,0:T(8,128)(2,1)S(1)} %select_convert_fusion.2), channel_id=1, source_target_pairs={{0,8},{4,12},{8,0},{12,4},{1,9},{5,13},{9,1},{13,5},{2,10},{6,14},... | collective-permute-start | bytes 245768 | tf_op jit(solution)/shard_map/ppermute | solution.py:104
  158.5 1.3 collective-permute-start.7

commit v4 on v3

--- a/solution.py
+++ b/solution.py
@@ -120,20 +120,34 @@
     return x
 
 
-def nearest_first_scatter(x, axis, size):
-    index = lax.axis_index(axis)
-    x = x.astype(jnp.float32)
+def nearest_first_scatter(parts, axis, size):
+    index = lax.axis_index(axis)
+    parts = tuple(part.astype(jnp.float32) for part in parts)
     distance = 1
     while distance < size:
-        pairs = x.reshape(x.shape[:1] + (x.shape[1] // 2, 2) + x.shape[2:])
-        even = pairs[:, :, 0]
-        odd = pairs[:, :, 1]
-        upper = (index & distance) != 0
-        keep = jnp.where(upper, odd, even)
-        send = jnp.where(upper, even, odd)
-        x = keep + swap_with(send.astype(jnp.bfloat16), axis, distance, size).astype(jnp.float32)
+        half = parts[0].shape[1] // 2
+        upper = (index & distance) != 0
+        keeps = tuple(jnp.where(upper, part[:, half:], part[:, :half]) for part in parts)
+        sends = tuple(
+            jnp.where(upper, part[:, :half], part[:, half:]).astype(jnp.bfloat16) for part in parts
+        )
+        got = swap_with(sends, axis, distance, size)
+        parts = tuple(keep + more.astype(jnp.float32) for keep, more in zip(keeps, got))
         distance *= 2
-    return x[:, 0]
+    return parts
+
+
+def farthest_first_gather(x, axis, size, dim):
+    index = lax.axis_index(axis)
+    distance = size // 2
+    while distance >= 1:
+        got = swap_with(x, axis, distance, size)
+        upper = (index & distance) != 0
+        x = jnp.where(
+            upper, jnp.concatenate([got, x], axis=dim), jnp.concatenate([x, got], axis=dim)
+        )
+        distance //= 2
+    return x
 
 
 def doubling_gather(x, axis, size, dim):
@@ -145,6 +159,14 @@
         x = jnp.where(
             upper, jnp.concatenate([got, x], axis=dim), jnp.concatenate([x, got], axis=dim)
         )
+        distance *= 2
+    return x
+
+
+def doubling_sum(x, axis, size):
+    distance = 1
+    while distance < size:
+        x = x + swap_with(x, axis, distance, size)
         distance *= 2
     return x
 
@@ -183,25 +205,16 @@
         jnp.dot(group_values, out_proj, preferred_element_type=jnp.float32), "dp", axis_sizes["dp"]
     )
     residual = hidden_in.astype(jnp.float32) + attention
-    squares = lax.psum(jnp.sum(residual * residual, axis=1), "sub")
-    scale_rows = lax.rsqrt(squares / float(D) + 1e-06)
-    normed = (residual * scale_rows[:, None] * norm_gain.astype(jnp.float32)).astype(jnp.bfloat16)
-    piece = lax.all_gather(normed, "dp", axis=0, tiled=True)
-    gate_part = jnp.dot(piece, gate_proj, preferred_element_type=jnp.float32)
-    up_part = jnp.dot(piece, up_proj, preferred_element_type=jnp.float32)
     sub_size = axis_sizes["sub"]
-    row_count = piece.shape[0]
-    unit_chunk = units_here // sub_size
-    partials = jnp.stack(
-        [
-            gate_part.reshape(row_count, sub_size, unit_chunk),
-            up_part.reshape(row_count, sub_size, unit_chunk),
-        ],
-        axis=2,
-    )
-    summed = nearest_first_scatter(partials, "sub", sub_size)
-    hidden_chunk = (jax.nn.silu(summed[:, 0]) * summed[:, 1]).astype(jnp.bfloat16)
-    hidden_units = doubling_gather(hidden_chunk, "sub", sub_size, 1)
+    all_residual = doubling_gather(residual, "dp", axis_sizes["dp"], 0)
+    squares = doubling_sum(jnp.sum(all_residual * all_residual, axis=1), "sub", sub_size)
+    gained = (all_residual * norm_gain.astype(jnp.float32)).astype(jnp.bfloat16)
+    gate_part = jnp.dot(gained, gate_proj, preferred_element_type=jnp.float32)
+    up_part = jnp.dot(gained, up_proj, preferred_element_type=jnp.float32)
+    gate_sum, up_sum = nearest_first_scatter((gate_part, up_part), "sub", sub_size)
+    scale_rows = lax.rsqrt(squares / float(D) + 1e-06)[:, None]
+    hidden_chunk = (jax.nn.silu(gate_sum * scale_rows) * (up_sum * scale_rows)).astype(jnp.bfloat16)
+    hidden_units = farthest_first_gather(hidden_chunk, "sub", sub_size, 1)
     feed_forward = halving_scatter(
         jnp.dot(hidden_units, down_proj, preferred_element_type=jnp.float32), "dp", axis_sizes["dp"]
     )

time: 162 us -> 137 us (0.85); the launches traced: 160 us -> 137 us
  blocking collectives: 30.7 us -> 16.1 us
  starting transfers between devices: 17 us -> 30.8 us
  waiting for transfers between devices: 60.1 us -> 52.2 us
  matrix products: 21.2 us -> 14 us
  local copies, waits for them, and re-layouts: 9.08 us -> 4.37 us
  Pallas kernels: 20.1 us -> 16.8 us
    psum x1 -> x0, blocking collectives: 8.86 us -> none  [shards(): squares = lax.psum(jnp.sum(residual * residual, axis=1), 'sub')]
    ppermute x8 -> x14, waiting for transfers between devices: 44.4 us -> 36.5 us  [swap_with(): return lax.ppermute(x, axis, [(i, i ^ distance) for i in range(size)])]
    all_to_all x1, starting transfers between devices: 11.1 us -> 18.2 us  [shards(): lax.all_to_all(contexts[None], ('dp', 'sub'), split_axis=2, concat_axis=0...]
    ppermute x8 -> x14, starting transfers between devices: 5.87 us -> 12.6 us  [swap_with(): return lax.ppermute(x, axis, [(i, i ^ distance) for i in range(size)])]
    all_gather x1 -> x0, blocking collectives: 5.74 us -> none  [shards(): piece = lax.all_gather(normed, 'dp', axis=0, tiled=True)]
    dot_general x2, matrix products: 10.3 us -> 6.34 us  [the longest x1 4.86 us: shards(): up_part = jnp.dot(gained, up_proj, preferred_element_type=jnp.float32)]
    another operation x3 -> x0, local copies, waits for them, and re-layouts: 3.48 us -> none  [shards(): jnp.stack([gate_part.reshape(row_count, sub_size, unit_chunk), up_part.re...]
    pallas_call x1, Pallas kernels: 20.1 us -> 16.8 us  [attend_all(): pl.pallas_call(kernel, out_shape=jax.ShapeDtypeStruct((req_dev, head_coun...]
  transfers between devices with their start and end apart: 9 -> 15, of which waited for: 9 -> 12; matrix products, arithmetic and copies ran while one was open for 0% -> 5% of each run, Pallas kernels for 0% -> 0%
where the time goes in v4:
time: 137 us
  waiting for transfers between devices  52.2 us (38%)
  starting transfers between devices  30.8 us (22%)
  Pallas kernels  16.8 us (12%)
  blocking collectives  16.1 us (12%)
  matrix products  14 us (10%)
  local copies, waits for them, and re-layouts  4.37 us (3%)
  other arithmetic  2 us (1%)
    ppermute x14, waiting for transfers between devices, swap_with(): return lax.ppermute(x, axis, [(i, i ^ distance) for i in range(size)])  36.5 us
    all_to_all x1, starting transfers between devices, shards(): lax.all_to_all(contexts[None], ('dp', 'sub'), split_axis=2, concat_axis=0...  18.2 us
    pallas_call x1, Pallas kernels, attend_all(): pl.pallas_call(kernel, out_shape=jax.ShapeDtypeStruct((req_dev, head_coun...  16.8 us
    all_gather x1, blocking collectives, shards(): group_values = lax.all_gather(values, 'sub', axis=1, tiled=True)  16.1 us
    all_to_all x1, waiting for transfers between devices, shards(): lax.all_to_all(contexts[None], ('dp', 'sub'), split_axis=2, concat_axis=0...  15.7 us
    ppermute x14, starting transfers between devices, swap_with(): return lax.ppermute(x, axis, [(i, i ^ distance) for i in range(size)])  12.6 us
    dot_general x1, matrix products, shards(): jnp.dot(group_values, out_proj, preferred_element_type=jnp.float32)  5.89 us
    dot_general x1, matrix products, shards(): up_part = jnp.dot(gained, up_proj, preferred_element_type=jnp.float32)  4.86 us
  transfers between devices with their start and end apart: 15, of which 12 were waited for; matrix products, arithmetic and copies ran while one was open for 5% of the time, Pallas kernels for 0%

profile of v4, /device:TPU:0, one launch (start us, length us, event | category | flops | bytes accessed | tf_op | source)
XLA Modules:
  0.0 137.2 jit_solution(9291053953097130196)
XLA Ops:
  0.6 0.0 copy-start
  0.6 1.4 %copy.18.queries = bf16[4,128,576]{2,1,0:T(8,128)(2,1)S(1)} copy(bf16[4,128,576]{1,2,0:T(8,128)(2,1)} %param.12) | data formatting | bytes 1179648 | tf_op args[1]
  2.1 0.0 copy-start.1
  2.1 0.7 copy-done.1
  2.8 0.0 copy-start.2
  2.8 0.7 copy-done.2
  3.4 16.8 %shard_map.122 = bf16[4,128,512]{2,1,0:T(8,128)(2,1)S(1)} custom-call(s32[4,16]{1,0:T(4,128)S(1)} %copy-done.1, s32[4]{0:T(128)S(1)} %copy-done.2, bf16[4,128,576]{2,1,0:T(8,128)(2,1)S(1)} %copy.18.queries, bf16[64,576,128]{2,1,0:T(8,128)(2,1)} %bitcast.24), custom_call_target="tpu_custom_call" | custom-call | tf_op jit(solution)/shard_map/pallas_call | solution.py:83
  20.3 1.2 copy.19
  21.5 18.2 %all-to-all-start = ((bf16[1,4,128,512]{3,1,0,2:T(4,128)(2,1)}), bf16[1,4,128,512]{3,1,0,2:T(4,128)(2,1)S(1)}, u32[]{:S(2)}, u32[]{:S(2)}) async-start(bf16[1,4,128,512]{3,1,0,2:T(4,128)(2,1)} %copy.19), calls=%async_computation | async-start | bytes 1048576 | tf_op jit(solution)/shard_map/all_to_all | solution.py:196
  39.7 15.7 %all-to-all-done = bf16[1,4,128,512]{3,1,0,2:T(4,128)(2,1)S(1)} async-done(((bf16[1,4,128,512]{3,1,0,2:T(4,128)(2,1)}), bf16[1,4,128,512]{3,1,0,2:T(4,128)(2,1)S(1)}, u32[]{:S(2)}, u32[]{:S(2)}) %all-to-all-start) | async-done | bytes 524320 | tf_op jit(solution)/shard_map/all_to_all | solution.py:196
  55.3 0.2 copy.25
  55.5 0.1 reshape.13
  55.7 0.0 copy-done
  55.7 0.3 fusion
  56.0 16.1 %all_gather.3 = bf16[64,4096]{1,0:T(8,128)(2,1)S(1)} all-gather(bf16[64,1024]{1,0:T(8,128)(2,1)S(1)} %bitcast.29), channel_id=1, replica_groups=mesh['grp'=2,'dp'=4,'sub'=4] {'sub'}, dimensions={1}, use_global_device_ids=true | all-gather | bytes 655360 | tf_op jit(solution)/shard_map/all_gather | solution.py:203
  72.1 0.0 copy-start.3
  72.1 0.0 copy-start.4
  72.1 5.9 %fusion.12 = f32[64,1280]{1,0:T(8,128)S(1)} fusion(bf16[64,4096]{1,0:T(8,128)(2,1)S(1)} %all_gather.3, bf16[4096,1280]{1,0:T(8,128)(2,1)} %param.17), kind=kOutput, calls=%fused_computation.38 | convolution fusion | flops 671088640 | bytes 11337728 | tf_op jit(solution)/shard_map/dot_general | solution.py:205
  78.0 0.7 collective-permute-start
  78.7 3.8 %collective-permute-done = bf16[32,1280]{1,0:T(8,128)(2,1)S(1)} collective-permute-done((bf16[32,1280]{1,0:T(8,128)(2,1)S(1)}, bf16[32,1280]{1,0:T(8,128)(2,1)S(1)}, u32[]{:S(2)}, u32[]{:S(2)}) %collective-permute-start) | collective-permute-done | bytes 81952 | tf_op jit(solution)/shard_map/ppermute | solution.py:104
  82.6 0.1 collective-permute-start.1
  82.6 1.2 collective-permute-done.1
  83.8 0.0 copy-done.3
  83.8 0.6 convert_add_fusion.4
  84.5 0.2 collective-permute-start.2
  84.7 1.1 collective-permute-done.2
  85.8 0.7 collective-permute-start.3
  86.5 0.0 copy-done.4
  86.5 5.6 %collective-permute-done.3 = f32[32,1280]{1,0:T(8,128)S(1)} collective-permute-done((f32[32,1280]{1,0:T(8,128)S(1)}, f32[32,1280]{1,0:T(8,128)S(1)}, u32[]{:S(2)}, u32[]{:S(2)}) %collective-permute-start.3) | collective-permute-done | bytes 163872 | tf_op jit(solution)/shard_map/ppermute | solution.py:104
  92.1 0.0 slice-start
  92.1 0.1 multiply_reduce_fusion
  92.3 0.1 collective-permute-start.6
  92.3 4.9 %fusion.10 = f32[64,3072]{1,0:T(8,128)S(1)} fusion(bf16[1280,3072]{1,0:T(8,128)(2,1)} %param.20, f32[32,1280]{1,0:T(8,128)S(1)} %collective-permute-done.3, f32[32,1280]{1,0:T(8,128)S(1)} %maximum_select_fusion.4, f32[1280]{0:T(1024)S(1)} %convert_element_type.80, pred[]{:T(512)S(6)} %ne.9), kind=kOutput, calls=%fused_computation.36 | convolution fusion | flops 503726080 | bytes 8983553 | tf_op jit(solution)/shard_map/dot_general | solution.py:213
  97.2 0.0 slice-start.2
  97.3 0.0 slice-start.3
  97.3 1.9 %collective-permute-start.8 = (bf16[64,1536]{1,0:T(8,128)(2,1)S(1)}, bf16[64,1536]{1,0:T(8,128)(2,1)S(1)}, u32[]{:S(2)}, u32[]{:S(2)}) collective-permute-start(bf16[64,1536]{1,0:T(8,128)(2,1)S(1)} %select_convert_fusion), channel_id=1, source_target_pairs={{0,1},{1,0},{2,3},{3,2},{4,5},{5,4},{6,7},{7,6},{8,9},{9,8},{10,11... | collective-permute-start | bytes 589832 | tf_op jit(solution)/shard_map/ppermute | solution.py:104
  99.2 0.0 slice-done
  99.2 0.0 slice-done.1
  99.2 1.5 %fusion.11 = f32[64,3072]{1,0:T(8,128)S(1)} fusion(bf16[1280,3072]{1,0:T(8,128)(2,1)S(1)} %bitcast.23, f32[32,1280]{1,0:T(8,128)S(1)} %collective-permute-done.3, f32[32,1280]{1,0:T(8,128)S(1)} %maximum_select_fusion.4, f32[1280]{0:T(1024)S(1)} %convert_element_type.80, pred[]{:T(512)S(6)} %ne.9), kind=kOutput, calls=%fused_computation.37 | convolution fusion | flops 503726080 | bytes 8983553 | tf_op jit(solution)/shard_map/dot_general | solution.py:212
  100.8 0.2 collective-permute-start.4
  101.0 0.0 collective-permute-done.6
  101.0 1.6 %collective-permute-start.7 = (f32[64]{0:T(128)S(1)}, f32[64]{0:T(128)S(1)}, u32[]{:S(2)}, u32[]{:S(2)}) collective-permute-start(f32[64]{0:T(128)S(1)} %add.51), channel_id=1, source_target_pairs={{0,2},{1,3},{2,0},{3,1},{4,6},{5,7},{6,4},{7,5},{8,10},{9,11},{10,... | collective-permute-start | bytes 776 | tf_op jit(solution)/shard_map/ppermute | solution.py:104
  102.5 2.2 %collective-permute-done.8 = bf16[64,1536]{1,0:T(8,128)(2,1)S(1)} collective-permute-done((bf16[64,1536]{1,0:T(8,128)(2,1)S(1)}, bf16[64,1536]{1,0:T(8,128)(2,1)S(1)}, u32[]{:S(2)}, u32[]{:S(2)}) %collective-permute-start.8) | collective-permute-done | bytes 196640 | tf_op jit(solution)/shard_map/ppermute | solution.py:104
  104.8 0.1 convert_add_fusion
  104.9 2.1 %collective-permute-start.9 = (bf16[64,768]{1,0:T(8,128)(2,1)S(1)}, bf16[64,768]{1,0:T(8,128)(2,1)S(1)}, u32[]{:S(2)}, u32[]{:S(2)}) collective-permute-start(bf16[64,768]{1,0:T(8,128)(2,1)S(1)} %select_convert_fusion.2), channel_id=1, source_target_pairs={{0,2},{1,3},{2,0},{3,1},{4,6},{5,7},{6,4},{7,5},{8,10},{9,11},{10,... | collective-permute-start | bytes 294920 | tf_op jit(solution)/shard_map/ppermute | solution.py:104
  106.9 1.8 %collective-permute-done.4 = bf16[64,1536]{1,0:T(8,128)(2,1)S(1)} collective-permute-done((bf16[64,1536]{1,0:T(8,128)(2,1)S(1)}, bf16[64,1536]{1,0:T(8,128)(2,1)S(1)}, u32[]{:S(2)}, u32[]{:S(2)}) %collective-permute-start.4) | collective-permute-done | bytes 196640 | tf_op jit(solution)/shard_map/ppermute | solution.py:104
  108.8 0.1 convert_add_fusion.1
  108.9 1.7 %collective-permute-start.5 = (bf16[64,768]{1,0:T(8,128)(2,1)S(1)}, bf16[64,768]{1,0:T(8,128)(2,1)S(1)}, u32[]{:S(2)}, u32[]{:S(2)}) collective-permute-start(bf16[64,768]{1,0:T(8,128)(2,1)S(1)} %select_convert_fusion.3), channel_id=1, source_target_pairs={{0,2},{1,3},{2,0},{3,1},{4,6},{5,7},{6,4},{7,5},{8,10},{9,11},{10,... | collective-permute-start | bytes 294920 | tf_op jit(solution)/shard_map/ppermute | solution.py:104
  110.5 0.0 collective-permute-done.7
  110.5 0.0 collective-permute-done.9
  110.6 5.2 %collective-permute-done.5 = bf16[64,768]{1,0:T(8,128)(2,1)S(1)} collective-permute-done((bf16[64,768]{1,0:T(8,128)(2,1)S(1)}, bf16[64,768]{1,0:T(8,128)(2,1)S(1)}, u32[]{:S(2)}, u32[]{:S(2)}) %collective-permute-start.5) | collective-permute-done | bytes 98336 | tf_op jit(solution)/shard_map/ppermute | solution.py:104
  115.8 0.1 multiply_convert_fusion.1
  115.9 0.4 collective-permute-start.10
  116.4 6.2 %collective-permute-done.10 = bf16[64,768]{1,0:T(8,128)(2,1)S(1)} collective-permute-done((bf16[64,768]{1,0:T(8,128)(2,1)S(1)}, bf16[64,768]{1,0:T(8,128)(2,1)S(1)}, u32[]{:S(2)}, u32[]{:S(2)}) %collective-permute-start.10) | collective-permute-done | bytes 98336 | tf_op jit(solution)/shard_map/ppermute | solution.py:104
  122.6 0.1 collective-permute-start.11
  122.7 5.7 %collective-permute-done.11 = bf16[64,1536]{1,0:T(8,128)(2,1)S(1)} collective-permute-done((bf16[64,1536]{1,0:T(8,128)(2,1)S(1)}, bf16[64,1536]{1,0:T(8,128)(2,1)S(1)}, u32[]{:S(2)}, u32[]{:S(2)}) %collective-permute-start.11) | collective-permute-done | bytes 196640 | tf_op jit(solution)/shard_map/ppermute | solution.py:104
  128.4 0.0 slice-done.2
  128.4 0.0 slice-done.3
  128.4 1.5 %fusion.1 = f32[64,1280]{1,0:T(8,128)S(1)} fusion(bf16[3072,1280]{1,0:T(8,128)(2,1)S(1)} %bitcast.26, bf16[64,1536]{1,0:T(8,128)(2,1)S(1)} %maximum_select_fusion.3, bf16[64,1536]{1,0:T(8,128)(2,1)S(1)} %collective-permute-done.11, pred[]{:T(512)S(6)} %ne.20), kind=kOutput, calls=%fused_computation.4 | convolution fusion | flops 505085952 | bytes 8585217 | tf_op jit(solution)/shard_map/dot_general | solution.py:219
  129.9 2.9 %collective-permute-start.12 = (bf16[32,1280]{1,0:T(8,128)(2,1)S(1)}, bf16[32,1280]{1,0:T(8,128)(2,1)S(1)}, u32[]{:S(2)}, u32[]{:S(2)}) collective-permute-start(bf16[32,1280]{1,0:T(8,128)(2,1)S(1)} %select_convert_fusion.4), channel_id=1, source_target_pairs={{0,8},{4,12},{8,0},{12,4},{1,9},{5,13},{9,1},{13,5},{2,10},{6,14},... | collective-permute-start | bytes 245768 | tf_op jit(solution)/shard_map/ppermute | solution.py:104
  132.8 2.4 %collective-permute-done.12 = bf16[32,1280]{1,0:T(8,128)(2,1)S(1)} collective-permute-done((bf16[32,1280]{1,0:T(8,128)(2,1)S(1)}, bf16[32,1280]{1,0:T(8,128)(2,1)S(1)}, u32[]{:S(2)}, u32[]{:S(2)}) %collective-permute-start.12) | collective-permute-done | bytes 81952 | tf_op jit(solution)/shard_map/ppermute | solution.py:104
  135.2 0.1 collective-permute-start.13
  135.3 1.2 collective-permute-done.13
  136.5 0.6 add_convert_fusion
  (19 shorter events, 0.3 us)
Async XLA Ops:
  0.6 55.0 %copy-start = (bf16[8,512,128]{2,1,0:T(8,128)(2,1)S(1)}, bf16[8,512,128]{2,1,0:T(8,128)(2,1)}, u32[]{:S(2)}) copy-start(bf16[8,512,128]{2,1,0:T(8,128)(2,1)} %param.16) | copy-start | bytes 3145732
  2.1 0.7 copy-start.1
  2.8 0.7 copy-start.2
  21.5 33.9 %all-to-all-start = ((bf16[1,4,128,512]{3,1,0,2:T(4,128)(2,1)}), bf16[1,4,128,512]{3,1,0,2:T(4,128)(2,1)S(1)}, u32[]{:S(2)}, u32[]{:S(2)}) async-start(bf16[1,4,128,512]{3,1,0,2:T(4,128)(2,1)} %copy.19), calls=%async_computation | async-start | bytes 1048576 | tf_op jit(solution)/shard_map/all_to_all | solution.py:196
  72.1 11.8 %copy-start.3 = (bf16[16,1280]{1,0:T(8,128)(2,1)S(1)}, bf16[16,1280]{1,0:T(8,128)(2,1)}, u32[]{:S(2)}) copy-start(bf16[16,1280]{1,0:T(8,128)(2,1)} %param.11) | copy-start | bytes 122884
  72.1 14.4 %copy-start.4 = (bf16[1280]{0:T(1024)(128)(2,1)S(1)}, bf16[1280]{0:T(1024)(128)(2,1)}, u32[]{:S(2)}) copy-start(bf16[1280]{0:T(1024)(128)(2,1)} %param.18) | copy-start | bytes 7684
  78.0 4.5 %collective-permute-start = (bf16[32,1280]{1,0:T(8,128)(2,1)S(1)}, bf16[32,1280]{1,0:T(8,128)(2,1)S(1)}, u32[]{:S(2)}, u32[]{:S(2)}) collective-permute-start(bf16[32,1280]{1,0:T(8,128)(2,1)S(1)} %select_convert_fusion.5), channel_id=1, source_target_pairs={{0,8},{4,12},{8,0},{12,4},{1,9},{5,13},{9,1},{13,5},{2,10},{6,14},... | collective-permute-start | bytes 245768 | tf_op jit(solution)/shard_map/ppermute | solution.py:104
  82.6 1.3 collective-permute-start.1
  84.5 1.3 collective-permute-start.2
  85.8 6.3 %collective-permute-start.3 = (f32[32,1280]{1,0:T(8,128)S(1)}, f32[32,1280]{1,0:T(8,128)S(1)}, u32[]{:S(2)}, u32[]{:S(2)}) collective-permute-start(f32[32,1280]{1,0:T(8,128)S(1)} %maximum_select_fusion.4), channel_id=1, source_target_pairs={{0,8},{4,12},{8,0},{12,4},{1,9},{5,13},{9,1},{13,5},{2,10},{6,14},... | collective-permute-start | bytes 491528 | tf_op jit(solution)/shard_map/ppermute | solution.py:104
  92.1 7.1 %slice-start = ((s8[7864320]{0:T(1024)(128)(4,1)}), s8[4194304]{0:T(1024)(128)(4,1)S(1)}, s32[]{:S(2)}) async-start(s8[7864320]{0:T(1024)(128)(4,1)} %bitcast.22), calls=%async_computation.1 | async-start | bytes 8388608
  92.3 7.0 %slice-start.1 = ((s8[7864320]{0:T(1024)(128)(4,1)}), s8[3670016]{0:T(1024)(128)(4,1)S(1)}, s32[]{:S(2)}) async-start(s8[7864320]{0:T(1024)(128)(4,1)} %bitcast.22), calls=%async_computation.2 | async-start | bytes 7340032
  92.3 8.7 %collective-permute-start.6 = (f32[64]{0:T(128)S(1)}, f32[64]{0:T(128)S(1)}, u32[]{:S(2)}, u32[]{:S(2)}) collective-permute-start(f32[64]{0:T(128)S(1)} %multiply_reduce_fusion), channel_id=1, source_target_pairs={{0,1},{1,0},{2,3},{3,2},{4,5},{5,4},{6,7},{7,6},{8,9},{9,8},{10,11... | collective-permute-start | bytes 776 | tf_op jit(solution)/shard_map/ppermute | solution.py:104
  97.2 31.2 %slice-start.2 = ((s8[7864320]{0:T(1024)(128)(4,1)}), s8[4194304]{0:T(1024)(128)(4,1)S(1)}, s32[]{:S(2)}) async-start(s8[7864320]{0:T(1024)(128)(4,1)} %bitcast.25), calls=%async_computation.3 | async-start | bytes 8388608
  97.3 31.1 %slice-start.3 = ((s8[7864320]{0:T(1024)(128)(4,1)}), s8[3670016]{0:T(1024)(128)(4,1)S(1)}, s32[]{:S(2)}) async-start(s8[7864320]{0:T(1024)(128)(4,1)} %bitcast.25), calls=%async_computation.4 | async-start | bytes 7340032
  97.3 7.5 %collective-permute-start.8 = (bf16[64,1536]{1,0:T(8,128)(2,1)S(1)}, bf16[64,1536]{1,0:T(8,128)(2,1)S(1)}, u32[]{:S(2)}, u32[]{:S(2)}) collective-permute-start(bf16[64,1536]{1,0:T(8,128)(2,1)S(1)} %select_convert_fusion), channel_id=1, source_target_pairs={{0,1},{1,0},{2,3},{3,2},{4,5},{5,4},{6,7},{7,6},{8,9},{9,8},{10,11... | collective-permute-start | bytes 589832 | tf_op jit(solution)/shard_map/ppermute | solution.py:104
  100.8 8.0 %collective-permute-start.4 = (bf16[64,1536]{1,0:T(8,128)(2,1)S(1)}, bf16[64,1536]{1,0:T(8,128)(2,1)S(1)}, u32[]{:S(2)}, u32[]{:S(2)}) collective-permute-start(bf16[64,1536]{1,0:T(8,128)(2,1)S(1)} %select_convert_fusion.1), channel_id=1, source_target_pairs={{0,1},{1,0},{2,3},{3,2},{4,5},{5,4},{6,7},{7,6},{8,9},{9,8},{10,11... | collective-permute-start | bytes 589832 | tf_op jit(solution)/shard_map/ppermute | solution.py:104
  101.0 9.5 %collective-permute-start.7 = (f32[64]{0:T(128)S(1)}, f32[64]{0:T(128)S(1)}, u32[]{:S(2)}, u32[]{:S(2)}) collective-permute-start(f32[64]{0:T(128)S(1)} %add.51), channel_id=1, source_target_pairs={{0,2},{1,3},{2,0},{3,1},{4,6},{5,7},{6,4},{7,5},{8,10},{9,11},{10,... | collective-permute-start | bytes 776 | tf_op jit(solution)/shard_map/ppermute | solution.py:104
  104.9 5.7 %collective-permute-start.9 = (bf16[64,768]{1,0:T(8,128)(2,1)S(1)}, bf16[64,768]{1,0:T(8,128)(2,1)S(1)}, u32[]{:S(2)}, u32[]{:S(2)}) collective-permute-start(bf16[64,768]{1,0:T(8,128)(2,1)S(1)} %select_convert_fusion.2), channel_id=1, source_target_pairs={{0,2},{1,3},{2,0},{3,1},{4,6},{5,7},{6,4},{7,5},{8,10},{9,11},{10,... | collective-permute-start | bytes 294920 | tf_op jit(solution)/shard_map/ppermute | solution.py:104
  108.9 6.9 %collective-permute-start.5 = (bf16[64,768]{1,0:T(8,128)(2,1)S(1)}, bf16[64,768]{1,0:T(8,128)(2,1)S(1)}, u32[]{:S(2)}, u32[]{:S(2)}) collective-permute-start(bf16[64,768]{1,0:T(8,128)(2,1)S(1)} %select_convert_fusion.3), channel_id=1, source_target_pairs={{0,2},{1,3},{2,0},{3,1},{4,6},{5,7},{6,4},{7,5},{8,10},{9,11},{10,... | collective-permute-start | bytes 294920 | tf_op jit(solution)/shard_map/ppermute | solution.py:104
  115.9 6.7 %collective-permute-start.10 = (bf16[64,768]{1,0:T(8,128)(2,1)S(1)}, bf16[64,768]{1,0:T(8,128)(2,1)S(1)}, u32[]{:S(2)}, u32[]{:S(2)}) collective-permute-start(bf16[64,768]{1,0:T(8,128)(2,1)S(1)} %multiply_convert_fusion.1), channel_id=1, source_target_pairs={{0,2},{1,3},{2,0},{3,1},{4,6},{5,7},{6,4},{7,5},{8,10},{9,11},{10,... | collective-permute-start | bytes 294920 | tf_op jit(solution)/shard_map/ppermute | solution.py:104
  122.6 5.7 %collective-permute-start.11 = (bf16[64,1536]{1,0:T(8,128)(2,1)S(1)}, bf16[64,1536]{1,0:T(8,128)(2,1)S(1)}, u32[]{:S(2)}, u32[]{:S(2)}) collective-permute-start(bf16[64,1536]{1,0:T(8,128)(2,1)S(1)} %maximum_select_fusion.3), channel_id=1, source_target_pairs={{0,1},{1,0},{2,3},{3,2},{4,5},{5,4},{6,7},{7,6},{8,9},{9,8},{10,11... | collective-permute-start | bytes 589832 | tf_op jit(solution)/shard_map/ppermute | solution.py:104
  129.9 5.3 %collective-permute-start.12 = (bf16[32,1280]{1,0:T(8,128)(2,1)S(1)}, bf16[32,1280]{1,0:T(8,128)(2,1)S(1)}, u32[]{:S(2)}, u32[]{:S(2)}) collective-permute-start(bf16[32,1280]{1,0:T(8,128)(2,1)S(1)} %select_convert_fusion.4), channel_id=1, source_target_pairs={{0,8},{4,12},{8,0},{12,4},{1,9},{5,13},{9,1},{13,5},{2,10},{6,14},... | collective-permute-start | bytes 245768 | tf_op jit(solution)/shard_map/ppermute | solution.py:104
  135.2 1.3 collective-permute-start.13

commit v5 on v4

--- a/solution.py
+++ b/solution.py
@@ -15,7 +15,7 @@
 masked_score = -1e30
 
 
-def attend_kernel(page_table, lengths, queries, cache_pool, contexts, keys, scores, weighted, copy_sems,
+def attend_kernel(page_table, lengths, queries, cache_pool, contexts, keys, copy_sems,
                   *, latent, score_scale):
     req_dev, pages_req = page_table.shape
     page_size = cache_pool.shape[2]
@@ -24,54 +24,38 @@
     def page_copy(slot, page):
         return pltpu.make_async_copy(
             cache_pool.at[page_table[slot, page]],
-            keys.at[slot * pages_req + page],
+            keys.at[slot, :, pl.ds(pl.multiple_of(page * page_size, page_size), page_size)],
             copy_sems.at[slot * pages_req + page],
         )
-
-    def pages_of(slot):
-        return (lengths[slot] + page_size - 1) // page_size
 
     for slot in range(req_dev):
         def start(page, carry, slot=slot):
             page_copy(slot, page).start()
             return carry
 
-        lax.fori_loop(0, pages_of(slot), start, 0)
-
-    positions = lax.broadcasted_iota(jnp.int32, (head_count, page_size), 1)
+        lax.fori_loop(0, pages_req, start, 0)
+
+    span = pages_req * page_size
+    positions = lax.broadcasted_iota(jnp.int32, (head_count, span), 1)
     for slot in range(req_dev):
-        length = lengths[slot]
-        query_rows = queries[slot]
-
-        def score_step(page, running_max, slot=slot, length=length, query_rows=query_rows):
+        def finish(page, carry, slot=slot):
             page_copy(slot, page).wait()
-            key_columns = keys[slot * pages_req + page]
-            block = jnp.dot(query_rows, key_columns, preferred_element_type=jnp.float32) * score_scale
-            block = jnp.where(positions + page * page_size < length, block, masked_score)
-            scores[page] = block
-            return jnp.maximum(running_max, jnp.max(block, axis=1, keepdims=True))
-
-        row_max = lax.fori_loop(
-            0, pages_of(slot), score_step, jnp.full((head_count, 1), masked_score, jnp.float32)
-        )
-        weighted[...] = jnp.zeros_like(weighted)
-
-        def weight_step(page, denominator, slot=slot, length=length, row_max=row_max):
-            live = positions + page * page_size < length
-            exponent = jnp.where(live, jnp.exp(scores[page] - row_max), 0.0)
-            value_columns = keys[slot * pages_req + page, :latent, :]
-            weighted[...] += lax.dot_general(
-                exponent.astype(jnp.bfloat16),
-                value_columns,
-                (((1,), (1,)), ((), ())),
-                preferred_element_type=jnp.float32,
-            )
-            return denominator + jnp.sum(exponent, axis=1, keepdims=True)
-
-        denominator = lax.fori_loop(
-            0, pages_of(slot), weight_step, jnp.zeros((head_count, 1), jnp.float32)
-        )
-        contexts[slot] = (weighted[...] / denominator).astype(contexts.dtype)
+            return carry
+
+        lax.fori_loop(0, pages_req, finish, 0)
+        live = positions < lengths[slot]
+        scores = jnp.dot(queries[slot], keys[slot], preferred_element_type=jnp.float32) * score_scale
+        scores = jnp.where(live, scores, masked_score)
+        row_max = jnp.max(scores, axis=1, keepdims=True)
+        exponent = jnp.where(live, jnp.exp(scores - row_max), 0.0)
+        denominator = jnp.sum(exponent, axis=1, keepdims=True)
+        weighted = lax.dot_general(
+            exponent.astype(jnp.bfloat16),
+            keys[slot, :latent, :],
+            (((1,), (1,)), ((), ())),
+            preferred_element_type=jnp.float32,
+        )
+        contexts[slot] = (weighted / denominator).astype(contexts.dtype)
 
 
 def attend_all(queries, page_table, lengths, cache_pool, latent, score_scale):
@@ -91,9 +75,7 @@
         ],
         out_specs=pl.BlockSpec(memory_space=pltpu.VMEM),
         scratch_shapes=[
-            pltpu.VMEM((req_dev * pages_req, width, page_size), jnp.bfloat16),
-            pltpu.VMEM((pages_req, head_count, page_size), jnp.float32),
-            pltpu.VMEM((head_count, latent), jnp.float32),
+            pltpu.VMEM((req_dev, width, pages_req * page_size), jnp.bfloat16),
             pltpu.SemaphoreType.DMA((req_dev * pages_req,)),
         ],
         compiler_params=pltpu.CompilerParams(vmem_limit_bytes=48 * 1024 * 1024),

time: 137 us -> 119 us (0.87)
  starting transfers between devices: 30.8 us -> 20 us
  Pallas kernels: 16.8 us -> 9.28 us
    all_to_all x1, starting transfers between devices: 18.2 us -> 7.35 us  [shards(): lax.all_to_all(contexts[None], ('dp', 'sub'), split_axis=2, concat_axis=0...]
    pallas_call x1, Pallas kernels: 16.8 us -> 9.28 us  [attend_all(): pl.pallas_call(kernel, out_shape=jax.ShapeDtypeStruct((req_dev, head_coun...]
  transfers between devices with their start and end apart: 15 -> 15, of which waited for: 12 -> 12; matrix products, arithmetic and copies ran while one was open for 5% -> 6% of each run, Pallas kernels for 0% -> 0%
where the time goes in v5:
time: 119 us
  waiting for transfers between devices  52.2 us (44%)
  starting transfers between devices  20 us (17%)
  blocking collectives  16.2 us (14%)
  matrix products  14 us (12%)
  Pallas kernels  9.28 us (8%)
  local copies, waits for them, and re-layouts  4.37 us (4%)
  other arithmetic  2 us (2%)
    ppermute x14, waiting for transfers between devices, swap_with(): return lax.ppermute(x, axis, [(i, i ^ distance) for i in range(size)])  36.5 us
    all_gather x1, blocking collectives, shards(): group_values = lax.all_gather(values, 'sub', axis=1, tiled=True)  16.2 us
    all_to_all x1, waiting for transfers between devices, shards(): lax.all_to_all(contexts[None], ('dp', 'sub'), split_axis=2, concat_axis=0...  15.7 us
    ppermute x14, starting transfers between devices, swap_with(): return lax.ppermute(x, axis, [(i, i ^ distance) for i in range(size)])  12.6 us
    pallas_call x1, Pallas kernels, attend_all(): pl.pallas_call(kernel, out_shape=jax.ShapeDtypeStruct((req_dev, head_coun...  9.28 us
    all_to_all x1, starting transfers between devices, shards(): lax.all_to_all(contexts[None], ('dp', 'sub'), split_axis=2, concat_axis=0...  7.35 us
    dot_general x1, matrix products, shards(): jnp.dot(group_values, out_proj, preferred_element_type=jnp.float32)  5.89 us
    dot_general x1, matrix products, shards(): up_part = jnp.dot(gained, up_proj, preferred_element_type=jnp.float32)  4.86 us
  transfers between devices with their start and end apart: 15, of which 12 were waited for; matrix products, arithmetic and copies ran while one was open for 6% of the time, Pallas kernels for 0%

profile of v5, /device:TPU:0, one launch (start us, length us, event | category | flops | bytes accessed | tf_op | source)
XLA Modules:
  0.0 119.0 jit_solution(12085329726482706026)
XLA Ops:
  0.6 0.0 copy-start
  0.6 1.4 %copy.18.queries = bf16[4,128,576]{2,1,0:T(8,128)(2,1)S(1)} copy(bf16[4,128,576]{1,2,0:T(8,128)(2,1)} %param.12) | data formatting | bytes 1179648 | tf_op args[1]
  2.1 0.0 copy-start.1
  2.1 0.7 copy-done.1
  2.8 0.0 copy-start.2
  2.8 0.7 copy-done.2
  3.4 9.3 %shard_map.122 = bf16[4,128,512]{2,1,0:T(8,128)(2,1)S(1)} custom-call(s32[4,16]{1,0:T(4,128)S(1)} %copy-done.1, s32[4]{0:T(128)S(1)} %copy-done.2, bf16[4,128,576]{2,1,0:T(8,128)(2,1)S(1)} %copy.18.queries, bf16[64,576,128]{2,1,0:T(8,128)(2,1)} %bitcast.24), custom_call_target="tpu_custom_call" | custom-call | tf_op jit(solution)/shard_map/pallas_call | solution.py:67
  12.7 1.2 %copy.19 = bf16[1,4,128,512]{3,1,0,2:T(4,128)(2,1)} copy(bf16[1,4,128,512]{3,2,1,0:T(8,128)(2,1)S(1)} %bitcast.21) | data formatting | bytes 1048576 | tf_op jit(solution)/shard_map/broadcast_in_dim | solution.py:179
  13.9 7.4 %all-to-all-start = ((bf16[1,4,128,512]{3,1,0,2:T(4,128)(2,1)}), bf16[1,4,128,512]{3,1,0,2:T(4,128)(2,1)S(1)}, u32[]{:S(2)}, u32[]{:S(2)}) async-start(bf16[1,4,128,512]{3,1,0,2:T(4,128)(2,1)} %copy.19), calls=%async_computation | async-start | bytes 1048576 | tf_op jit(solution)/shard_map/all_to_all | solution.py:178
  21.3 15.7 %all-to-all-done = bf16[1,4,128,512]{3,1,0,2:T(4,128)(2,1)S(1)} async-done(((bf16[1,4,128,512]{3,1,0,2:T(4,128)(2,1)}), bf16[1,4,128,512]{3,1,0,2:T(4,128)(2,1)S(1)}, u32[]{:S(2)}, u32[]{:S(2)}) %all-to-all-start) | async-done | bytes 524320 | tf_op jit(solution)/shard_map/all_to_all | solution.py:178
  37.0 0.2 copy.25
  37.2 0.1 reshape.13
  37.3 0.0 copy-done
  37.3 0.3 fusion
  37.7 16.2 %all_gather.3 = bf16[64,4096]{1,0:T(8,128)(2,1)S(1)} all-gather(bf16[64,1024]{1,0:T(8,128)(2,1)S(1)} %bitcast.29), channel_id=1, replica_groups=mesh['grp'=2,'dp'=4,'sub'=4] {'sub'}, dimensions={1}, use_global_device_ids=true | all-gather | bytes 655360 | tf_op jit(solution)/shard_map/all_gather | solution.py:185
  53.9 0.0 copy-start.3
  53.9 0.0 copy-start.4
  53.9 5.9 %fusion.12 = f32[64,1280]{1,0:T(8,128)S(1)} fusion(bf16[64,4096]{1,0:T(8,128)(2,1)S(1)} %all_gather.3, bf16[4096,1280]{1,0:T(8,128)(2,1)} %param.17), kind=kOutput, calls=%fused_computation.38 | convolution fusion | flops 671088640 | bytes 11337728 | tf_op jit(solution)/shard_map/dot_general | solution.py:187
  59.8 0.7 collective-permute-start
  60.5 3.8 %collective-permute-done = bf16[32,1280]{1,0:T(8,128)(2,1)S(1)} collective-permute-done((bf16[32,1280]{1,0:T(8,128)(2,1)S(1)}, bf16[32,1280]{1,0:T(8,128)(2,1)S(1)}, u32[]{:S(2)}, u32[]{:S(2)}) %collective-permute-start) | collective-permute-done | bytes 81952 | tf_op jit(solution)/shard_map/ppermute | solution.py:86
  64.4 0.1 collective-permute-start.1
  64.5 1.2 %collective-permute-done.1 = bf16[16,1280]{1,0:T(8,128)(2,1)S(1)} collective-permute-done((bf16[16,1280]{1,0:T(8,128)(2,1)S(1)}, bf16[16,1280]{1,0:T(8,128)(2,1)S(1)}, u32[]{:S(2)}, u32[]{:S(2)}) %collective-permute-start.1) | collective-permute-done | bytes 40992 | tf_op jit(solution)/shard_map/ppermute | solution.py:86
  65.7 0.0 copy-done.3
  65.7 0.6 convert_add_fusion.4
  66.3 0.2 collective-permute-start.2
  66.5 1.1 collective-permute-done.2
  67.6 0.7 collective-permute-start.3
  68.3 0.0 copy-done.4
  68.3 5.7 %collective-permute-done.3 = f32[32,1280]{1,0:T(8,128)S(1)} collective-permute-done((f32[32,1280]{1,0:T(8,128)S(1)}, f32[32,1280]{1,0:T(8,128)S(1)}, u32[]{:S(2)}, u32[]{:S(2)}) %collective-permute-start.3) | collective-permute-done | bytes 163872 | tf_op jit(solution)/shard_map/ppermute | solution.py:86
  74.0 0.0 slice-start
  74.0 0.1 multiply_reduce_fusion
  74.1 0.1 collective-permute-start.6
  74.2 4.9 %fusion.10 = f32[64,3072]{1,0:T(8,128)S(1)} fusion(bf16[1280,3072]{1,0:T(8,128)(2,1)} %param.20, f32[32,1280]{1,0:T(8,128)S(1)} %collective-permute-done.3, f32[32,1280]{1,0:T(8,128)S(1)} %maximum_select_fusion.4, f32[1280]{0:T(1024)S(1)} %convert_element_type.80, pred[]{:T(512)S(6)} %ne.9), kind=kOutput, calls=%fused_computation.36 | convolution fusion | flops 503726080 | bytes 8983553 | tf_op jit(solution)/shard_map/dot_general | solution.py:195
  79.0 0.0 slice-start.2
  79.1 0.0 slice-start.3
  79.1 1.9 %collective-permute-start.8 = (bf16[64,1536]{1,0:T(8,128)(2,1)S(1)}, bf16[64,1536]{1,0:T(8,128)(2,1)S(1)}, u32[]{:S(2)}, u32[]{:S(2)}) collective-permute-start(bf16[64,1536]{1,0:T(8,128)(2,1)S(1)} %select_convert_fusion), channel_id=1, source_target_pairs={{0,1},{1,0},{2,3},{3,2},{4,5},{5,4},{6,7},{7,6},{8,9},{9,8},{10,11... | collective-permute-start | bytes 589832 | tf_op jit(solution)/shard_map/ppermute | solution.py:86
  81.0 0.0 slice-done
  81.0 0.0 slice-done.1
  81.0 1.5 %fusion.11 = f32[64,3072]{1,0:T(8,128)S(1)} fusion(bf16[1280,3072]{1,0:T(8,128)(2,1)S(1)} %bitcast.23, f32[32,1280]{1,0:T(8,128)S(1)} %collective-permute-done.3, f32[32,1280]{1,0:T(8,128)S(1)} %maximum_select_fusion.4, f32[1280]{0:T(1024)S(1)} %convert_element_type.80, pred[]{:T(512)S(6)} %ne.9), kind=kOutput, calls=%fused_computation.37 | convolution fusion | flops 503726080 | bytes 8983553 | tf_op jit(solution)/shard_map/dot_general | solution.py:194
  82.6 0.2 collective-permute-start.4
  82.8 0.0 collective-permute-done.6
  82.8 1.6 %collective-permute-start.7 = (f32[64]{0:T(128)S(1)}, f32[64]{0:T(128)S(1)}, u32[]{:S(2)}, u32[]{:S(2)}) collective-permute-start(f32[64]{0:T(128)S(1)} %add.51), channel_id=1, source_target_pairs={{0,2},{1,3},{2,0},{3,1},{4,6},{5,7},{6,4},{7,5},{8,10},{9,11},{10,... | collective-permute-start | bytes 776 | tf_op jit(solution)/shard_map/ppermute | solution.py:86
  84.4 2.2 %collective-permute-done.8 = bf16[64,1536]{1,0:T(8,128)(2,1)S(1)} collective-permute-done((bf16[64,1536]{1,0:T(8,128)(2,1)S(1)}, bf16[64,1536]{1,0:T(8,128)(2,1)S(1)}, u32[]{:S(2)}, u32[]{:S(2)}) %collective-permute-start.8) | collective-permute-done | bytes 196640 | tf_op jit(solution)/shard_map/ppermute | solution.py:86
  86.6 0.1 convert_add_fusion
  86.7 2.1 %collective-permute-start.9 = (bf16[64,768]{1,0:T(8,128)(2,1)S(1)}, bf16[64,768]{1,0:T(8,128)(2,1)S(1)}, u32[]{:S(2)}, u32[]{:S(2)}) collective-permute-start(bf16[64,768]{1,0:T(8,128)(2,1)S(1)} %select_convert_fusion.2), channel_id=1, source_target_pairs={{0,2},{1,3},{2,0},{3,1},{4,6},{5,7},{6,4},{7,5},{8,10},{9,11},{10,... | collective-permute-start | bytes 294920 | tf_op jit(solution)/shard_map/ppermute | solution.py:86
  88.8 1.8 %collective-permute-done.4 = bf16[64,1536]{1,0:T(8,128)(2,1)S(1)} collective-permute-done((bf16[64,1536]{1,0:T(8,128)(2,1)S(1)}, bf16[64,1536]{1,0:T(8,128)(2,1)S(1)}, u32[]{:S(2)}, u32[]{:S(2)}) %collective-permute-start.4) | collective-permute-done | bytes 196640 | tf_op jit(solution)/shard_map/ppermute | solution.py:86
  90.6 0.1 convert_add_fusion.1
  90.7 1.7 %collective-permute-start.5 = (bf16[64,768]{1,0:T(8,128)(2,1)S(1)}, bf16[64,768]{1,0:T(8,128)(2,1)S(1)}, u32[]{:S(2)}, u32[]{:S(2)}) collective-permute-start(bf16[64,768]{1,0:T(8,128)(2,1)S(1)} %select_convert_fusion.3), channel_id=1, source_target_pairs={{0,2},{1,3},{2,0},{3,1},{4,6},{5,7},{6,4},{7,5},{8,10},{9,11},{10,... | collective-permute-start | bytes 294920 | tf_op jit(solution)/shard_map/ppermute | solution.py:86
  92.4 0.0 collective-permute-done.7
  92.4 0.0 collective-permute-done.9
  92.4 5.2 %collective-permute-done.5 = bf16[64,768]{1,0:T(8,128)(2,1)S(1)} collective-permute-done((bf16[64,768]{1,0:T(8,128)(2,1)S(1)}, bf16[64,768]{1,0:T(8,128)(2,1)S(1)}, u32[]{:S(2)}, u32[]{:S(2)}) %collective-permute-start.5) | collective-permute-done | bytes 98336 | tf_op jit(solution)/shard_map/ppermute | solution.py:86
  97.6 0.1 multiply_convert_fusion.1
  97.7 0.5 collective-permute-start.10
  98.2 6.2 %collective-permute-done.10 = bf16[64,768]{1,0:T(8,128)(2,1)S(1)} collective-permute-done((bf16[64,768]{1,0:T(8,128)(2,1)S(1)}, bf16[64,768]{1,0:T(8,128)(2,1)S(1)}, u32[]{:S(2)}, u32[]{:S(2)}) %collective-permute-start.10) | collective-permute-done | bytes 98336 | tf_op jit(solution)/shard_map/ppermute | solution.py:86
  104.5 0.1 collective-permute-start.11
  104.5 5.7 %collective-permute-done.11 = bf16[64,1536]{1,0:T(8,128)(2,1)S(1)} collective-permute-done((bf16[64,1536]{1,0:T(8,128)(2,1)S(1)}, bf16[64,1536]{1,0:T(8,128)(2,1)S(1)}, u32[]{:S(2)}, u32[]{:S(2)}) %collective-permute-start.11) | collective-permute-done | bytes 196640 | tf_op jit(solution)/shard_map/ppermute | solution.py:86
  110.2 0.0 slice-done.2
  110.2 0.0 slice-done.3
  110.2 1.5 %fusion.1 = f32[64,1280]{1,0:T(8,128)S(1)} fusion(bf16[3072,1280]{1,0:T(8,128)(2,1)S(1)} %bitcast.26, bf16[64,1536]{1,0:T(8,128)(2,1)S(1)} %maximum_select_fusion.3, bf16[64,1536]{1,0:T(8,128)(2,1)S(1)} %collective-permute-done.11, pred[]{:T(512)S(6)} %ne.20), kind=kOutput, calls=%fused_computation.4 | convolution fusion | flops 505085952 | bytes 8585217 | tf_op jit(solution)/shard_map/dot_general | solution.py:201
  111.7 2.9 %collective-permute-start.12 = (bf16[32,1280]{1,0:T(8,128)(2,1)S(1)}, bf16[32,1280]{1,0:T(8,128)(2,1)S(1)}, u32[]{:S(2)}, u32[]{:S(2)}) collective-permute-start(bf16[32,1280]{1,0:T(8,128)(2,1)S(1)} %select_convert_fusion.4), channel_id=1, source_target_pairs={{0,8},{4,12},{8,0},{12,4},{1,9},{5,13},{9,1},{13,5},{2,10},{6,14},... | collective-permute-start | bytes 245768 | tf_op jit(solution)/shard_map/ppermute | solution.py:86
  114.6 2.4 %collective-permute-done.12 = bf16[32,1280]{1,0:T(8,128)(2,1)S(1)} collective-permute-done((bf16[32,1280]{1,0:T(8,128)(2,1)S(1)}, bf16[32,1280]{1,0:T(8,128)(2,1)S(1)}, u32[]{:S(2)}, u32[]{:S(2)}) %collective-permute-start.12) | collective-permute-done | bytes 81952 | tf_op jit(solution)/shard_map/ppermute | solution.py:86
  117.1 0.1 collective-permute-start.13
  117.1 1.2 %collective-permute-done.13 = bf16[16,1280]{1,0:T(8,128)(2,1)S(1)} collective-permute-done((bf16[16,1280]{1,0:T(8,128)(2,1)S(1)}, bf16[16,1280]{1,0:T(8,128)(2,1)S(1)}, u32[]{:S(2)}, u32[]{:S(2)}) %collective-permute-start.13) | collective-permute-done | bytes 40992 | tf_op jit(solution)/shard_map/ppermute | solution.py:86
  118.3 0.6 add_convert_fusion
  (19 shorter events, 0.3 us)
Async XLA Ops:
  0.6 36.7 %copy-start = (bf16[8,512,128]{2,1,0:T(8,128)(2,1)S(1)}, bf16[8,512,128]{2,1,0:T(8,128)(2,1)}, u32[]{:S(2)}) copy-start(bf16[8,512,128]{2,1,0:T(8,128)(2,1)} %param.16) | copy-start | bytes 3145732
  2.1 0.7 copy-start.1
  2.8 0.7 copy-start.2
  13.9 23.0 %all-to-all-start = ((bf16[1,4,128,512]{3,1,0,2:T(4,128)(2,1)}), bf16[1,4,128,512]{3,1,0,2:T(4,128)(2,1)S(1)}, u32[]{:S(2)}, u32[]{:S(2)}) async-start(bf16[1,4,128,512]{3,1,0,2:T(4,128)(2,1)} %copy.19), calls=%async_computation | async-start | bytes 1048576 | tf_op jit(solution)/shard_map/all_to_all | solution.py:178
  53.9 11.8 %copy-start.3 = (bf16[16,1280]{1,0:T(8,128)(2,1)S(1)}, bf16[16,1280]{1,0:T(8,128)(2,1)}, u32[]{:S(2)}) copy-start(bf16[16,1280]{1,0:T(8,128)(2,1)} %param.11) | copy-start | bytes 122884
  53.9 14.4 %copy-start.4 = (bf16[1280]{0:T(1024)(128)(2,1)S(1)}, bf16[1280]{0:T(1024)(128)(2,1)}, u32[]{:S(2)}) copy-start(bf16[1280]{0:T(1024)(128)(2,1)} %param.18) | copy-start | bytes 7684
  59.8 4.5 %collective-permute-start = (bf16[32,1280]{1,0:T(8,128)(2,1)S(1)}, bf16[32,1280]{1,0:T(8,128)(2,1)S(1)}, u32[]{:S(2)}, u32[]{:S(2)}) collective-permute-start(bf16[32,1280]{1,0:T(8,128)(2,1)S(1)} %select_convert_fusion.5), channel_id=1, source_target_pairs={{0,8},{4,12},{8,0},{12,4},{1,9},{5,13},{9,1},{13,5},{2,10},{6,14},... | collective-permute-start | bytes 245768 | tf_op jit(solution)/shard_map/ppermute | solution.py:86
  64.4 1.3 %collective-permute-start.1 = (bf16[16,1280]{1,0:T(8,128)(2,1)S(1)}, bf16[16,1280]{1,0:T(8,128)(2,1)S(1)}, u32[]{:S(2)}, u32[]{:S(2)}) collective-permute-start(bf16[16,1280]{1,0:T(8,128)(2,1)S(1)} %select_convert_fusion.7), channel_id=1, source_target_pairs={{0,4},{4,0},{8,12},{12,8},{1,5},{5,1},{9,13},{13,9},{2,6},{6,2},{1... | collective-permute-start | bytes 122888 | tf_op jit(solution)/shard_map/ppermute | solution.py:86
  66.3 1.3 %collective-permute-start.2 = (f32[16,1280]{1,0:T(8,128)S(1)}, f32[16,1280]{1,0:T(8,128)S(1)}, u32[]{:S(2)}, u32[]{:S(2)}) collective-permute-start(f32[16,1280]{1,0:T(8,128)S(1)} %get-tuple-element.2), channel_id=1, source_target_pairs={{0,4},{4,0},{8,12},{12,8},{1,5},{5,1},{9,13},{13,9},{2,6},{6,2},{1... | collective-permute-start | bytes 245768 | tf_op jit(solution)/shard_map/ppermute | solution.py:86
  67.6 6.3 %collective-permute-start.3 = (f32[32,1280]{1,0:T(8,128)S(1)}, f32[32,1280]{1,0:T(8,128)S(1)}, u32[]{:S(2)}, u32[]{:S(2)}) collective-permute-start(f32[32,1280]{1,0:T(8,128)S(1)} %maximum_select_fusion.4), channel_id=1, source_target_pairs={{0,8},{4,12},{8,0},{12,4},{1,9},{5,13},{9,1},{13,5},{2,10},{6,14},... | collective-permute-start | bytes 491528 | tf_op jit(solution)/shard_map/ppermute | solution.py:86
  74.0 7.1 %slice-start = ((s8[7864320]{0:T(1024)(128)(4,1)}), s8[4194304]{0:T(1024)(128)(4,1)S(1)}, s32[]{:S(2)}) async-start(s8[7864320]{0:T(1024)(128)(4,1)} %bitcast.22), calls=%async_computation.1 | async-start | bytes 8388608
  74.1 7.0 %slice-start.1 = ((s8[7864320]{0:T(1024)(128)(4,1)}), s8[3670016]{0:T(1024)(128)(4,1)S(1)}, s32[]{:S(2)}) async-start(s8[7864320]{0:T(1024)(128)(4,1)} %bitcast.22), calls=%async_computation.2 | async-start | bytes 7340032
  74.1 8.7 %collective-permute-start.6 = (f32[64]{0:T(128)S(1)}, f32[64]{0:T(128)S(1)}, u32[]{:S(2)}, u32[]{:S(2)}) collective-permute-start(f32[64]{0:T(128)S(1)} %multiply_reduce_fusion), channel_id=1, source_target_pairs={{0,1},{1,0},{2,3},{3,2},{4,5},{5,4},{6,7},{7,6},{8,9},{9,8},{10,11... | collective-permute-start | bytes 776 | tf_op jit(solution)/shard_map/ppermute | solution.py:86
  79.0 31.2 %slice-start.2 = ((s8[7864320]{0:T(1024)(128)(4,1)}), s8[4194304]{0:T(1024)(128)(4,1)S(1)}, s32[]{:S(2)}) async-start(s8[7864320]{0:T(1024)(128)(4,1)} %bitcast.25), calls=%async_computation.3 | async-start | bytes 8388608
  79.1 31.1 %slice-start.3 = ((s8[7864320]{0:T(1024)(128)(4,1)}), s8[3670016]{0:T(1024)(128)(4,1)S(1)}, s32[]{:S(2)}) async-start(s8[7864320]{0:T(1024)(128)(4,1)} %bitcast.25), calls=%async_computation.4 | async-start | bytes 7340032
  79.1 7.5 %collective-permute-start.8 = (bf16[64,1536]{1,0:T(8,128)(2,1)S(1)}, bf16[64,1536]{1,0:T(8,128)(2,1)S(1)}, u32[]{:S(2)}, u32[]{:S(2)}) collective-permute-start(bf16[64,1536]{1,0:T(8,128)(2,1)S(1)} %select_convert_fusion), channel_id=1, source_target_pairs={{0,1},{1,0},{2,3},{3,2},{4,5},{5,4},{6,7},{7,6},{8,9},{9,8},{10,11... | collective-permute-start | bytes 589832 | tf_op jit(solution)/shard_map/ppermute | solution.py:86
  82.6 8.0 %collective-permute-start.4 = (bf16[64,1536]{1,0:T(8,128)(2,1)S(1)}, bf16[64,1536]{1,0:T(8,128)(2,1)S(1)}, u32[]{:S(2)}, u32[]{:S(2)}) collective-permute-start(bf16[64,1536]{1,0:T(8,128)(2,1)S(1)} %select_convert_fusion.1), channel_id=1, source_target_pairs={{0,1},{1,0},{2,3},{3,2},{4,5},{5,4},{6,7},{7,6},{8,9},{9,8},{10,11... | collective-permute-start | bytes 589832 | tf_op jit(solution)/shard_map/ppermute | solution.py:86
  82.8 9.5 %collective-permute-start.7 = (f32[64]{0:T(128)S(1)}, f32[64]{0:T(128)S(1)}, u32[]{:S(2)}, u32[]{:S(2)}) collective-permute-start(f32[64]{0:T(128)S(1)} %add.51), channel_id=1, source_target_pairs={{0,2},{1,3},{2,0},{3,1},{4,6},{5,7},{6,4},{7,5},{8,10},{9,11},{10,... | collective-permute-start | bytes 776 | tf_op jit(solution)/shard_map/ppermute | solution.py:86
  86.7 5.7 %collective-permute-start.9 = (bf16[64,768]{1,0:T(8,128)(2,1)S(1)}, bf16[64,768]{1,0:T(8,128)(2,1)S(1)}, u32[]{:S(2)}, u32[]{:S(2)}) collective-permute-start(bf16[64,768]{1,0:T(8,128)(2,1)S(1)} %select_convert_fusion.2), channel_id=1, source_target_pairs={{0,2},{1,3},{2,0},{3,1},{4,6},{5,7},{6,4},{7,5},{8,10},{9,11},{10,... | collective-permute-start | bytes 294920 | tf_op jit(solution)/shard_map/ppermute | solution.py:86
  90.7 6.9 %collective-permute-start.5 = (bf16[64,768]{1,0:T(8,128)(2,1)S(1)}, bf16[64,768]{1,0:T(8,128)(2,1)S(1)}, u32[]{:S(2)}, u32[]{:S(2)}) collective-permute-start(bf16[64,768]{1,0:T(8,128)(2,1)S(1)} %select_convert_fusion.3), channel_id=1, source_target_pairs={{0,2},{1,3},{2,0},{3,1},{4,6},{5,7},{6,4},{7,5},{8,10},{9,11},{10,... | collective-permute-start | bytes 294920 | tf_op jit(solution)/shard_map/ppermute | solution.py:86
  97.7 6.7 %collective-permute-start.10 = (bf16[64,768]{1,0:T(8,128)(2,1)S(1)}, bf16[64,768]{1,0:T(8,128)(2,1)S(1)}, u32[]{:S(2)}, u32[]{:S(2)}) collective-permute-start(bf16[64,768]{1,0:T(8,128)(2,1)S(1)} %multiply_convert_fusion.1), channel_id=1, source_target_pairs={{0,2},{1,3},{2,0},{3,1},{4,6},{5,7},{6,4},{7,5},{8,10},{9,11},{10,... | collective-permute-start | bytes 294920 | tf_op jit(solution)/shard_map/ppermute | solution.py:86
  104.5 5.7 %collective-permute-start.11 = (bf16[64,1536]{1,0:T(8,128)(2,1)S(1)}, bf16[64,1536]{1,0:T(8,128)(2,1)S(1)}, u32[]{:S(2)}, u32[]{:S(2)}) collective-permute-start(bf16[64,1536]{1,0:T(8,128)(2,1)S(1)} %maximum_select_fusion.3), channel_id=1, source_target_pairs={{0,1},{1,0},{2,3},{3,2},{4,5},{5,4},{6,7},{7,6},{8,9},{9,8},{10,11... | collective-permute-start | bytes 589832 | tf_op jit(solution)/shard_map/ppermute | solution.py:86
  111.7 5.3 %collective-permute-start.12 = (bf16[32,1280]{1,0:T(8,128)(2,1)S(1)}, bf16[32,1280]{1,0:T(8,128)(2,1)S(1)}, u32[]{:S(2)}, u32[]{:S(2)}) collective-permute-start(bf16[32,1280]{1,0:T(8,128)(2,1)S(1)} %select_convert_fusion.4), channel_id=1, source_target_pairs={{0,8},{4,12},{8,0},{12,4},{1,9},{5,13},{9,1},{13,5},{2,10},{6,14},... | collective-permute-start | bytes 245768 | tf_op jit(solution)/shard_map/ppermute | solution.py:86
  117.1 1.3 %collective-permute-start.13 = (bf16[16,1280]{1,0:T(8,128)(2,1)S(1)}, bf16[16,1280]{1,0:T(8,128)(2,1)S(1)}, u32[]{:S(2)}, u32[]{:S(2)}) collective-permute-start(bf16[16,1280]{1,0:T(8,128)(2,1)S(1)} %select_convert_fusion.6), channel_id=1, source_target_pairs={{0,4},{4,0},{8,12},{12,8},{1,5},{5,1},{9,13},{13,9},{2,6},{6,2},{1... | collective-permute-start | bytes 122888 | tf_op jit(solution)/shard_map/ppermute | solution.py:86

commit v6 on v5

--- a/solution.py
+++ b/solution.py
@@ -151,6 +151,34 @@
         x = x + swap_with(x, axis, distance, size)
         distance *= 2
     return x
+
+
+def nearest_first_rows_scatter(x, axis, size):
+    index = lax.axis_index(axis)
+    x = x.astype(jnp.float32)
+    x = x.reshape((size, x.shape[0] // size) + x.shape[1:])
+    distance = 1
+    while distance < size:
+        pairs = x.reshape((x.shape[0] // 2, 2) + x.shape[1:])
+        upper = (index & distance) != 0
+        keep = jnp.where(upper, pairs[:, 1], pairs[:, 0])
+        send = jnp.where(upper, pairs[:, 0], pairs[:, 1])
+        x = keep + swap_with(send.astype(jnp.bfloat16), axis, distance, size).astype(jnp.float32)
+        distance *= 2
+    return x[0]
+
+
+def farthest_first_rows_gather(x, axis, size):
+    index = lax.axis_index(axis)
+    x = x[None]
+    distance = size // 2
+    while distance >= 1:
+        got = swap_with(x, axis, distance, size)
+        upper = (index & distance) != 0
+        x = jnp.where(upper, jnp.stack([got, x], axis=1), jnp.stack([x, got], axis=1))
+        x = x.reshape((-1,) + x.shape[2:])
+        distance //= 2
+    return x.reshape((-1,) + x.shape[2:])
 
 
 def shards(
@@ -183,12 +211,12 @@
     values = jnp.einsum("rhc,hcv->rhv", received, value_up, preferred_element_type=jnp.float32)
     values = values.astype(jnp.bfloat16).reshape(row_count, heads_here * value_dim)
     group_values = lax.all_gather(values, "sub", axis=1, tiled=True)
-    attention = halving_scatter(
+    attention = nearest_first_rows_scatter(
         jnp.dot(group_values, out_proj, preferred_element_type=jnp.float32), "dp", axis_sizes["dp"]
     )
     residual = hidden_in.astype(jnp.float32) + attention
     sub_size = axis_sizes["sub"]
-    all_residual = doubling_gather(residual, "dp", axis_sizes["dp"], 0)
+    all_residual = farthest_first_rows_gather(residual, "dp", axis_sizes["dp"])
     squares = doubling_sum(jnp.sum(all_residual * all_residual, axis=1), "sub", sub_size)
     gained = (all_residual * norm_gain.astype(jnp.float32)).astype(jnp.bfloat16)
     gate_part = jnp.dot(gained, gate_proj, preferred_element_type=jnp.float32)
@@ -197,7 +225,7 @@
     scale_rows = lax.rsqrt(squares / float(D) + 1e-06)[:, None]
     hidden_chunk = (jax.nn.silu(gate_sum * scale_rows) * (up_sum * scale_rows)).astype(jnp.bfloat16)
     hidden_units = farthest_first_gather(hidden_chunk, "sub", sub_size, 1)
-    feed_forward = halving_scatter(
+    feed_forward = nearest_first_rows_scatter(
         jnp.dot(hidden_units, down_proj, preferred_element_type=jnp.float32), "dp", axis_sizes["dp"]
     )
     return (attention.astype(jnp.bfloat16), (residual + feed_forward).astype(jnp.bfloat16))

time: 119 us -> 119 us (level)
  starting transfers between devices: 20 us -> 14.4 us
  matrix products: 14 us -> 17.3 us
  waiting for transfers between devices: 52.2 us -> 54.2 us
    ppermute x14, starting transfers between devices: 12.6 us -> 7.06 us  [swap_with(): return lax.ppermute(x, axis, [(i, i ^ distance) for i in range(size)])]
    dot_general x1, matrix products: 1.48 us -> 4.75 us  [shards(): gate_part = jnp.dot(gained, gate_proj, preferred_element_type=jnp.float32)]
    ppermute x14, waiting for transfers between devices: 36.5 us -> 38.5 us  [swap_with(): return lax.ppermute(x, axis, [(i, i ^ distance) for i in range(size)])]
    unnamed x19 -> x15, local copies, waits for them, and re-layouts: 2.82 us -> 2.81 us
  transfers between devices with their start and end apart: 15 -> 15, of which waited for: 12 -> 11; matrix products, arithmetic and copies ran while one was open for 6% -> 9% of each run, Pallas kernels for 0% -> 0%
where the time goes in v6:
time: 119 us
  waiting for transfers between devices  54.2 us (46%)
  matrix products  17.3 us (15%)
  blocking collectives  16.2 us (14%)
  starting transfers between devices  14.4 us (12%)
  Pallas kernels  9.28 us (8%)
  local copies, waits for them, and re-layouts  4.44 us (4%)
  other arithmetic  2.04 us (2%)
    ppermute x14, waiting for transfers between devices, swap_with(): return lax.ppermute(x, axis, [(i, i ^ distance) for i in range(size)])  38.5 us
    all_gather x1, blocking collectives, shards(): group_values = lax.all_gather(values, 'sub', axis=1, tiled=True)  16.2 us
    all_to_all x1, waiting for transfers between devices, shards(): lax.all_to_all(contexts[None], ('dp', 'sub'), split_axis=2, concat_axis=0...  15.7 us
    pallas_call x1, Pallas kernels, attend_all(): pl.pallas_call(kernel, out_shape=jax.ShapeDtypeStruct((req_dev, head_coun...  9.28 us
    all_to_all x1, starting transfers between devices, shards(): lax.all_to_all(contexts[None], ('dp', 'sub'), split_axis=2, concat_axis=0...  7.35 us
    ppermute x14, starting transfers between devices, swap_with(): return lax.ppermute(x, axis, [(i, i ^ distance) for i in range(size)])  7.06 us
    dot_general x1, matrix products, shards(): jnp.dot(group_values, out_proj, preferred_element_type=jnp.float32)  5.9 us
    dot_general x1, matrix products, shards(): up_part = jnp.dot(gained, up_proj, preferred_element_type=jnp.float32)  4.89 us
  transfers between devices with their start and end apart: 15, of which 11 were waited for; matrix products, arithmetic and copies ran while one was open for 9% of the time, Pallas kernels for 0%

profile of v6, /device:TPU:0, one launch (start us, length us, event | category | flops | bytes accessed | tf_op | source)
XLA Modules:
  0.0 118.9 jit_solution(1308077726343885463)
XLA Ops:
  0.6 0.0 copy-start
  0.6 1.4 %copy.26.queries = bf16[4,128,576]{2,1,0:T(8,128)(2,1)S(1)} copy(bf16[4,128,576]{1,2,0:T(8,128)(2,1)} %param.12) | data formatting | bytes 1179648 | tf_op args[1]
  2.1 0.0 copy-start.1
  2.1 0.7 copy-done.1
  2.8 0.0 copy-start.2
  2.8 0.7 copy-done.2
  3.4 9.3 %shard_map.122 = bf16[4,128,512]{2,1,0:T(8,128)(2,1)S(1)} custom-call(s32[4,16]{1,0:T(4,128)S(1)} %copy-done.1, s32[4]{0:T(128)S(1)} %copy-done.2, bf16[4,128,576]{2,1,0:T(8,128)(2,1)S(1)} %copy.26.queries, bf16[64,576,128]{2,1,0:T(8,128)(2,1)} %bitcast.108), custom_call_target="tpu_custom_call" | custom-call | tf_op jit(solution)/shard_map/pallas_call | solution.py:67
  12.7 1.2 %copy.27 = bf16[1,4,128,512]{3,1,0,2:T(4,128)(2,1)} copy(bf16[1,4,128,512]{3,2,1,0:T(8,128)(2,1)S(1)} %bitcast.107) | data formatting | bytes 1048576 | tf_op jit(solution)/shard_map/broadcast_in_dim | solution.py:207
  13.9 7.4 %all-to-all-start = ((bf16[1,4,128,512]{3,1,0,2:T(4,128)(2,1)}), bf16[1,4,128,512]{3,1,0,2:T(4,128)(2,1)S(1)}, u32[]{:S(2)}, u32[]{:S(2)}) async-start(bf16[1,4,128,512]{3,1,0,2:T(4,128)(2,1)} %copy.27), calls=%async_computation | async-start | bytes 1048576 | tf_op jit(solution)/shard_map/all_to_all | solution.py:206
  21.3 15.7 %all-to-all-done = bf16[1,4,128,512]{3,1,0,2:T(4,128)(2,1)S(1)} async-done(((bf16[1,4,128,512]{3,1,0,2:T(4,128)(2,1)}), bf16[1,4,128,512]{3,1,0,2:T(4,128)(2,1)S(1)}, u32[]{:S(2)}, u32[]{:S(2)}) %all-to-all-start) | async-done | bytes 524320 | tf_op jit(solution)/shard_map/all_to_all | solution.py:206
  37.0 0.2 copy.41
  37.2 0.1 reshape.213
  37.3 0.0 copy-done
  37.3 0.3 fusion
  37.7 16.2 %all_gather.3 = bf16[64,4096]{1,0:T(8,128)(2,1)S(1)} all-gather(bf16[64,1024]{1,0:T(8,128)(2,1)S(1)} %bitcast.117), channel_id=1, replica_groups=mesh['grp'=2,'dp'=4,'sub'=4] {'sub'}, dimensions={1}, use_global_device_ids=true | all-gather | bytes 655360 | tf_op jit(solution)/shard_map/all_gather | solution.py:213
  53.9 0.0 copy-start.4
  53.9 0.0 copy-start.3
  53.9 5.9 %fusion.19 = f32[64,1280]{1,0:T(8,128)S(1)} fusion(bf16[64,4096]{1,0:T(8,128)(2,1)S(1)} %all_gather.3, bf16[4096,1280]{1,0:T(8,128)(2,1)} %param.17), kind=kOutput, calls=%fused_computation.52 | convolution fusion | flops 671088640 | bytes 11337728 | tf_op jit(solution)/shard_map/dot_general | solution.py:215
  59.8 0.1 collective-permute-start
  59.9 1.3 %collective-permute-done = bf16[2,16,1280]{2,1,0:T(8,128)(2,1)S(1)} collective-permute-done((bf16[2,16,1280]{2,1,0:T(8,128)(2,1)S(1)}, bf16[2,16,1280]{2,1,0:T(8,128)(2,1)S(1)}, u32[]{:S(2)}, u32[]{:S(2)}) %collective-permute-start) | collective-permute-done | bytes 81952 | tf_op jit(solution)/shard_map/ppermute | solution.py:86
  61.2 0.7 collective-permute-start.1
  61.9 0.0 copy-done.4
  61.9 3.4 %collective-permute-done.1 = bf16[1,16,1280]{2,1,0:T(8,128)(2,1)S(1)} collective-permute-done((bf16[1,16,1280]{2,1,0:T(8,128)(2,1)S(1)}, bf16[1,16,1280]{2,1,0:T(8,128)(2,1)S(1)}, u32[]{:S(2)}, u32[]{:S(2)}) %collective-permute-start.1) | collective-permute-done | bytes 40992 | tf_op jit(solution)/shard_map/ppermute | solution.py:86
  65.3 0.0 copy-done.3
  65.3 0.7 collective-permute-start.2
  66.0 3.8 %collective-permute-done.2 = f32[1,16,1280]{2,1,0:T(8,128)S(1)} collective-permute-done((f32[1,16,1280]{2,1,0:T(8,128)S(1)}, f32[1,16,1280]{2,1,0:T(8,128)S(1)}, u32[]{:S(2)}, u32[]{:S(2)}) %collective-permute-start.2) | collective-permute-done | bytes 81952 | tf_op jit(solution)/shard_map/ppermute | solution.py:86
  69.9 0.1 collective-permute-start.3
  70.0 1.4 %collective-permute-done.3 = f32[2,16,1280]{2,1,0:T(8,128)S(1)} collective-permute-done((f32[2,16,1280]{2,1,0:T(8,128)S(1)}, f32[2,16,1280]{2,1,0:T(8,128)S(1)}, u32[]{:S(2)}, u32[]{:S(2)}) %collective-permute-start.3) | collective-permute-done | bytes 163872 | tf_op jit(solution)/shard_map/ppermute | solution.py:86
  71.3 0.1 multiply_reduce_fusion
  71.4 0.1 reduce_sum.12
  71.5 0.0 collective-permute-start.6
  71.6 4.7 %fusion.20 = f32[64,3072]{1,0:T(8,128)S(1)} fusion(bf16[64,1280]{1,0:T(8,128)(2,1)S(1)} %fusion.8, bf16[1280,3072]{1,0:T(8,128)(2,1)} %param.19), kind=kOutput, calls=%fused_computation.53 | convolution fusion | flops 503316480 | bytes 8814592 | tf_op jit(solution)/shard_map/dot_general | solution.py:222
  76.3 0.0 slice-start
  76.4 0.0 slice-start.1
  76.4 2.1 %collective-permute-start.4 = (bf16[64,1536]{1,0:T(8,128)(2,1)S(1)}, bf16[64,1536]{1,0:T(8,128)(2,1)S(1)}, u32[]{:S(2)}, u32[]{:S(2)}) collective-permute-start(bf16[64,1536]{1,0:T(8,128)(2,1)S(1)} %select_convert_fusion.1), channel_id=1, source_target_pairs={{0,1},{1,0},{2,3},{3,2},{4,5},{5,4},{6,7},{7,6},{8,9},{9,8},{10,11... | collective-permute-start | bytes 589832 | tf_op jit(solution)/shard_map/ppermute | solution.py:86
  78.5 4.9 %fusion.21 = f32[64,3072]{1,0:T(8,128)S(1)} fusion(bf16[64,1280]{1,0:T(8,128)(2,1)S(1)} %fusion.8, bf16[1280,3072]{1,0:T(8,128)(2,1)} %param.20), kind=kOutput, calls=%fused_computation.54 | convolution fusion | flops 503316480 | bytes 8814592 | tf_op jit(solution)/shard_map/dot_general | solution.py:223
  83.4 0.1 collective-permute-start.8
  83.5 0.0 collective-permute-done.6
  83.5 1.1 collective-permute-start.7
  84.7 0.0 collective-permute-done.4
  84.7 0.1 convert_add_fusion.1
  84.7 1.9 %collective-permute-start.5 = (bf16[64,768]{1,0:T(8,128)(2,1)S(1)}, bf16[64,768]{1,0:T(8,128)(2,1)S(1)}, u32[]{:S(2)}, u32[]{:S(2)}) collective-permute-start(bf16[64,768]{1,0:T(8,128)(2,1)S(1)} %select_convert_fusion.3), channel_id=1, source_target_pairs={{0,2},{1,3},{2,0},{3,1},{4,6},{5,7},{6,4},{7,5},{8,10},{9,11},{10,... | collective-permute-start | bytes 294920 | tf_op jit(solution)/shard_map/ppermute | solution.py:86
  86.7 5.9 %collective-permute-done.8 = bf16[64,1536]{1,0:T(8,128)(2,1)S(1)} collective-permute-done((bf16[64,1536]{1,0:T(8,128)(2,1)S(1)}, bf16[64,1536]{1,0:T(8,128)(2,1)S(1)}, u32[]{:S(2)}, u32[]{:S(2)}) %collective-permute-start.8) | collective-permute-done | bytes 196640 | tf_op jit(solution)/shard_map/ppermute | solution.py:86
  92.6 0.1 convert_add_fusion
  92.7 0.1 collective-permute-start.9
  92.7 0.0 collective-permute-done.7
  92.8 0.0 collective-permute-done.5
  92.8 5.9 %collective-permute-done.9 = bf16[64,768]{1,0:T(8,128)(2,1)S(1)} collective-permute-done((bf16[64,768]{1,0:T(8,128)(2,1)S(1)}, bf16[64,768]{1,0:T(8,128)(2,1)S(1)}, u32[]{:S(2)}, u32[]{:S(2)}) %collective-permute-start.9) | collective-permute-done | bytes 98336 | tf_op jit(solution)/shard_map/ppermute | solution.py:86
  98.7 0.1 multiply_convert_fusion
  98.8 0.1 collective-permute-start.10
  98.9 6.0 %collective-permute-done.10 = bf16[64,768]{1,0:T(8,128)(2,1)S(1)} collective-permute-done((bf16[64,768]{1,0:T(8,128)(2,1)S(1)}, bf16[64,768]{1,0:T(8,128)(2,1)S(1)}, u32[]{:S(2)}, u32[]{:S(2)}) %collective-permute-start.10) | collective-permute-done | bytes 98336 | tf_op jit(solution)/shard_map/ppermute | solution.py:86
  104.9 0.1 collective-permute-start.11
  105.0 6.2 %collective-permute-done.11 = bf16[64,1536]{1,0:T(8,128)(2,1)S(1)} collective-permute-done((bf16[64,1536]{1,0:T(8,128)(2,1)S(1)}, bf16[64,1536]{1,0:T(8,128)(2,1)S(1)}, u32[]{:S(2)}, u32[]{:S(2)}) %collective-permute-start.11) | collective-permute-done | bytes 196640 | tf_op jit(solution)/shard_map/ppermute | solution.py:86
  111.2 0.0 slice-done
  111.2 0.0 slice-done.1
  111.3 1.5 %fusion.1 = f32[64,1280]{1,0:T(8,128)S(1)} fusion(bf16[3072,1280]{1,0:T(8,128)(2,1)S(1)} %bitcast.110, bf16[64,1536]{1,0:T(8,128)(2,1)S(1)} %maximum_select_fusion.3, bf16[64,1536]{1,0:T(8,128)(2,1)S(1)} %collective-permute-done.11, pred[]{:T(512)S(6)} %ne.20), kind=kOutput, calls=%fused_computation.4 | convolution fusion | flops 505085952 | bytes 8585217 | tf_op jit(solution)/shard_map/dot_general | solution.py:229
  112.8 0.1 collective-permute-start.12
  112.8 1.3 %collective-permute-done.12 = bf16[2,16,1280]{2,1,0:T(8,128)(2,1)S(1)} collective-permute-done((bf16[2,16,1280]{2,1,0:T(8,128)(2,1)S(1)}, bf16[2,16,1280]{2,1,0:T(8,128)(2,1)S(1)}, u32[]{:S(2)}, u32[]{:S(2)}) %collective-permute-start.12) | collective-permute-done | bytes 81952 | tf_op jit(solution)/shard_map/ppermute | solution.py:86
  114.1 0.1 collective-permute-start.13
  114.2 0.6 bitcast_convert_fusion
  114.9 3.4 %collective-permute-done.13 = bf16[1,16,1280]{2,1,0:T(8,128)(2,1)S(1)} collective-permute-done((bf16[1,16,1280]{2,1,0:T(8,128)(2,1)S(1)}, bf16[1,16,1280]{2,1,0:T(8,128)(2,1)S(1)}, u32[]{:S(2)}, u32[]{:S(2)}) %collective-permute-start.13) | collective-permute-done | bytes 40992 | tf_op jit(solution)/shard_map/ppermute | solution.py:86
  118.2 0.6 fusion.13
  (21 shorter events, 0.4 us)
Async XLA Ops:
  0.6 36.7 %copy-start = (bf16[8,512,128]{2,1,0:T(8,128)(2,1)S(1)}, bf16[8,512,128]{2,1,0:T(8,128)(2,1)}, u32[]{:S(2)}) copy-start(bf16[8,512,128]{2,1,0:T(8,128)(2,1)} %param.16) | copy-start | bytes 3145732
  2.1 0.7 copy-start.1
  2.8 0.7 copy-start.2
  13.9 23.0 %all-to-all-start = ((bf16[1,4,128,512]{3,1,0,2:T(4,128)(2,1)}), bf16[1,4,128,512]{3,1,0,2:T(4,128)(2,1)S(1)}, u32[]{:S(2)}, u32[]{:S(2)}) async-start(bf16[1,4,128,512]{3,1,0,2:T(4,128)(2,1)} %copy.27), calls=%async_computation | async-start | bytes 1048576 | tf_op jit(solution)/shard_map/all_to_all | solution.py:206
  53.9 8.0 %copy-start.4 = (bf16[1280]{0:T(1024)(128)(2,1)S(1)}, bf16[1280]{0:T(1024)(128)(2,1)}, u32[]{:S(2)}) copy-start(bf16[1280]{0:T(1024)(128)(2,1)} %param.18) | copy-start | bytes 7684
  53.9 11.4 %copy-start.3 = (bf16[16,1280]{1,0:T(8,128)(2,1)S(1)}, bf16[16,1280]{1,0:T(8,128)(2,1)}, u32[]{:S(2)}) copy-start(bf16[16,1280]{1,0:T(8,128)(2,1)} %param.11) | copy-start | bytes 122884
  59.8 1.3 %collective-permute-start = (bf16[2,16,1280]{2,1,0:T(8,128)(2,1)S(1)}, bf16[2,16,1280]{2,1,0:T(8,128)(2,1)S(1)}, u32[]{:S(2)}, u32[]{:S(2)}) collective-permute-start(bf16[2,16,1280]{2,1,0:T(8,128)(2,1)S(1)} %fusion.11), channel_id=1, source_target_pairs={{0,4},{4,0},{8,12},{12,8},{1,5},{5,1},{9,13},{13,9},{2,6},{6,2},{1... | collective-permute-start | bytes 245768 | tf_op jit(solution)/shard_map/ppermute | solution.py:86
  61.2 4.1 %collective-permute-start.1 = (bf16[1,16,1280]{2,1,0:T(8,128)(2,1)S(1)}, bf16[1,16,1280]{2,1,0:T(8,128)(2,1)S(1)}, u32[]{:S(2)}, u32[]{:S(2)}) collective-permute-start(bf16[1,16,1280]{2,1,0:T(8,128)(2,1)S(1)} %fusion.14), channel_id=1, source_target_pairs={{0,8},{4,12},{8,0},{12,4},{1,9},{5,13},{9,1},{13,5},{2,10},{6,14},... | collective-permute-start | bytes 122888 | tf_op jit(solution)/shard_map/ppermute | solution.py:86
  65.3 4.5 %collective-permute-start.2 = (f32[1,16,1280]{2,1,0:T(8,128)S(1)}, f32[1,16,1280]{2,1,0:T(8,128)S(1)}, u32[]{:S(2)}, u32[]{:S(2)}) collective-permute-start(f32[1,16,1280]{2,1,0:T(8,128)S(1)} %get-tuple-element.4), channel_id=1, source_target_pairs={{0,8},{4,12},{8,0},{12,4},{1,9},{5,13},{9,1},{13,5},{2,10},{6,14},... | collective-permute-start | bytes 245768 | tf_op jit(solution)/shard_map/ppermute | solution.py:86
  69.9 1.5 %collective-permute-start.3 = (f32[2,16,1280]{2,1,0:T(8,128)S(1)}, f32[2,16,1280]{2,1,0:T(8,128)S(1)}, u32[]{:S(2)}, u32[]{:S(2)}) collective-permute-start(f32[2,16,1280]{2,1,0:T(8,128)S(1)} %maximum_select_fusion.4), channel_id=1, source_target_pairs={{0,4},{4,0},{8,12},{12,8},{1,5},{5,1},{9,13},{13,9},{2,6},{6,2},{1... | collective-permute-start | bytes 491528 | tf_op jit(solution)/shard_map/ppermute | solution.py:86
  71.5 12.0 %collective-permute-start.6 = (f32[64]{0:T(128)S(1)}, f32[64]{0:T(128)S(1)}, u32[]{:S(2)}, u32[]{:S(2)}) collective-permute-start(f32[64]{0:T(128)S(1)} %reduce_sum.12), channel_id=1, source_target_pairs={{0,1},{1,0},{2,3},{3,2},{4,5},{5,4},{6,7},{7,6},{8,9},{9,8},{10,11... | collective-permute-start | bytes 776 | tf_op jit(solution)/shard_map/ppermute | solution.py:86
  76.3 34.9 %slice-start = ((s8[7864320]{0:T(1024)(128)(4,1)}), s8[4194304]{0:T(1024)(128)(4,1)S(1)}, s32[]{:S(2)}) async-start(s8[7864320]{0:T(1024)(128)(4,1)} %bitcast.109), calls=%async_computation.1 | async-start | bytes 8388608
  76.4 34.9 %slice-start.1 = ((s8[7864320]{0:T(1024)(128)(4,1)}), s8[3670016]{0:T(1024)(128)(4,1)S(1)}, s32[]{:S(2)}) async-start(s8[7864320]{0:T(1024)(128)(4,1)} %bitcast.109), calls=%async_computation.2 | async-start | bytes 7340032
  76.4 8.3 %collective-permute-start.4 = (bf16[64,1536]{1,0:T(8,128)(2,1)S(1)}, bf16[64,1536]{1,0:T(8,128)(2,1)S(1)}, u32[]{:S(2)}, u32[]{:S(2)}) collective-permute-start(bf16[64,1536]{1,0:T(8,128)(2,1)S(1)} %select_convert_fusion.1), channel_id=1, source_target_pairs={{0,1},{1,0},{2,3},{3,2},{4,5},{5,4},{6,7},{7,6},{8,9},{9,8},{10,11... | collective-permute-start | bytes 589832 | tf_op jit(solution)/shard_map/ppermute | solution.py:86
  83.4 9.1 %collective-permute-start.8 = (bf16[64,1536]{1,0:T(8,128)(2,1)S(1)}, bf16[64,1536]{1,0:T(8,128)(2,1)S(1)}, u32[]{:S(2)}, u32[]{:S(2)}) collective-permute-start(bf16[64,1536]{1,0:T(8,128)(2,1)S(1)} %select_convert_fusion), channel_id=1, source_target_pairs={{0,1},{1,0},{2,3},{3,2},{4,5},{5,4},{6,7},{7,6},{8,9},{9,8},{10,11... | collective-permute-start | bytes 589832 | tf_op jit(solution)/shard_map/ppermute | solution.py:86
  83.5 9.2 %collective-permute-start.7 = (f32[64]{0:T(128)S(1)}, f32[64]{0:T(128)S(1)}, u32[]{:S(2)}, u32[]{:S(2)}) collective-permute-start(f32[64]{0:T(128)S(1)} %add.51), channel_id=1, source_target_pairs={{0,2},{1,3},{2,0},{3,1},{4,6},{5,7},{6,4},{7,5},{8,10},{9,11},{10,... | collective-permute-start | bytes 776 | tf_op jit(solution)/shard_map/ppermute | solution.py:86
  84.7 8.0 %collective-permute-start.5 = (bf16[64,768]{1,0:T(8,128)(2,1)S(1)}, bf16[64,768]{1,0:T(8,128)(2,1)S(1)}, u32[]{:S(2)}, u32[]{:S(2)}) collective-permute-start(bf16[64,768]{1,0:T(8,128)(2,1)S(1)} %select_convert_fusion.3), channel_id=1, source_target_pairs={{0,2},{1,3},{2,0},{3,1},{4,6},{5,7},{6,4},{7,5},{8,10},{9,11},{10,... | collective-permute-start | bytes 294920 | tf_op jit(solution)/shard_map/ppermute | solution.py:86
  92.7 6.0 %collective-permute-start.9 = (bf16[64,768]{1,0:T(8,128)(2,1)S(1)}, bf16[64,768]{1,0:T(8,128)(2,1)S(1)}, u32[]{:S(2)}, u32[]{:S(2)}) collective-permute-start(bf16[64,768]{1,0:T(8,128)(2,1)S(1)} %select_convert_fusion.2), channel_id=1, source_target_pairs={{0,2},{1,3},{2,0},{3,1},{4,6},{5,7},{6,4},{7,5},{8,10},{9,11},{10,... | collective-permute-start | bytes 294920 | tf_op jit(solution)/shard_map/ppermute | solution.py:86
  98.8 6.0 %collective-permute-start.10 = (bf16[64,768]{1,0:T(8,128)(2,1)S(1)}, bf16[64,768]{1,0:T(8,128)(2,1)S(1)}, u32[]{:S(2)}, u32[]{:S(2)}) collective-permute-start(bf16[64,768]{1,0:T(8,128)(2,1)S(1)} %multiply_convert_fusion), channel_id=1, source_target_pairs={{0,2},{1,3},{2,0},{3,1},{4,6},{5,7},{6,4},{7,5},{8,10},{9,11},{10,... | collective-permute-start | bytes 294920 | tf_op jit(solution)/shard_map/ppermute | solution.py:86
  104.9 6.3 %collective-permute-start.11 = (bf16[64,1536]{1,0:T(8,128)(2,1)S(1)}, bf16[64,1536]{1,0:T(8,128)(2,1)S(1)}, u32[]{:S(2)}, u32[]{:S(2)}) collective-permute-start(bf16[64,1536]{1,0:T(8,128)(2,1)S(1)} %maximum_select_fusion.3), channel_id=1, source_target_pairs={{0,1},{1,0},{2,3},{3,2},{4,5},{5,4},{6,7},{7,6},{8,9},{9,8},{10,11... | collective-permute-start | bytes 589832 | tf_op jit(solution)/shard_map/ppermute | solution.py:86
  112.8 1.3 %collective-permute-start.12 = (bf16[2,16,1280]{2,1,0:T(8,128)(2,1)S(1)}, bf16[2,16,1280]{2,1,0:T(8,128)(2,1)S(1)}, u32[]{:S(2)}, u32[]{:S(2)}) collective-permute-start(bf16[2,16,1280]{2,1,0:T(8,128)(2,1)S(1)} %fusion.12), channel_id=1, source_target_pairs={{0,4},{4,0},{8,12},{12,8},{1,5},{5,1},{9,13},{13,9},{2,6},{6,2},{1... | collective-permute-start | bytes 245768 | tf_op jit(solution)/shard_map/ppermute | solution.py:86
  114.1 4.1 %collective-permute-start.13 = (bf16[1,16,1280]{2,1,0:T(8,128)(2,1)S(1)}, bf16[1,16,1280]{2,1,0:T(8,128)(2,1)S(1)}, u32[]{:S(2)}, u32[]{:S(2)}) collective-permute-start(bf16[1,16,1280]{2,1,0:T(8,128)(2,1)S(1)} %fusion.15), channel_id=1, source_target_pairs={{0,8},{4,12},{8,0},{12,4},{1,9},{5,13},{9,1},{13,5},{2,10},{6,14},... | collective-permute-start | bytes 122888 | tf_op jit(solution)/shard_map/ppermute | solution.py:86

commit v7 on v6

--- a/solution.py
+++ b/solution.py
@@ -47,7 +47,7 @@
         scores = jnp.dot(queries[slot], keys[slot], preferred_element_type=jnp.float32) * score_scale
         scores = jnp.where(live, scores, masked_score)
         row_max = jnp.max(scores, axis=1, keepdims=True)
-        exponent = jnp.where(live, jnp.exp(scores - row_max), 0.0)
+        exponent = jnp.exp(scores - row_max)
         denominator = jnp.sum(exponent, axis=1, keepdims=True)
         weighted = lax.dot_general(
             exponent.astype(jnp.bfloat16),
@@ -179,6 +179,16 @@
         x = x.reshape((-1,) + x.shape[2:])
         distance //= 2
     return x.reshape((-1,) + x.shape[2:])
+
+
+def matched_sum(x, axis, size):
+    x = x.astype(jnp.float32)
+    distance = 1
+    while distance < size:
+        mine = x.astype(jnp.bfloat16)
+        x = mine.astype(jnp.float32) + swap_with(mine, axis, distance, size).astype(jnp.float32)
+        distance *= 2
+    return x
 
 
 def shards(
@@ -211,12 +221,13 @@
     values = jnp.einsum("rhc,hcv->rhv", received, value_up, preferred_element_type=jnp.float32)
     values = values.astype(jnp.bfloat16).reshape(row_count, heads_here * value_dim)
     group_values = lax.all_gather(values, "sub", axis=1, tiled=True)
-    attention = nearest_first_rows_scatter(
-        jnp.dot(group_values, out_proj, preferred_element_type=jnp.float32), "dp", axis_sizes["dp"]
-    )
-    residual = hidden_in.astype(jnp.float32) + attention
+    dp_size = axis_sizes["dp"]
     sub_size = axis_sizes["sub"]
-    all_residual = farthest_first_rows_gather(residual, "dp", axis_sizes["dp"])
+    attention_all = matched_sum(
+        jnp.dot(group_values, out_proj, preferred_element_type=jnp.float32), "dp", dp_size
+    )
+    hidden_all = farthest_first_rows_gather(hidden_in, "dp", dp_size)
+    all_residual = hidden_all.astype(jnp.float32) + attention_all
     squares = doubling_sum(jnp.sum(all_residual * all_residual, axis=1), "sub", sub_size)
     gained = (all_residual * norm_gain.astype(jnp.float32)).astype(jnp.bfloat16)
     gate_part = jnp.dot(gained, gate_proj, preferred_element_type=jnp.float32)
@@ -228,6 +239,10 @@
     feed_forward = nearest_first_rows_scatter(
         jnp.dot(hidden_units, down_proj, preferred_element_type=jnp.float32), "dp", axis_sizes["dp"]
     )
+    own_rows = hidden_in.shape[0]
+    first_row = lax.axis_index("dp") * own_rows
+    attention = lax.dynamic_slice_in_dim(attention_all, first_row, own_rows, 0)
+    residual = lax.dynamic_slice_in_dim(all_residual, first_row, own_rows, 0)
     return (attention.astype(jnp.bfloat16), (residual + feed_forward).astype(jnp.bfloat16))
 
 

time: 119 us -> 112 us (0.941)
  waiting for transfers between devices: 54.2 us -> 46.8 us
  matrix products: 17.3 us -> 14 us
  starting transfers between devices: 14.4 us -> 17.7 us
    all_to_all x1, waiting for transfers between devices: 15.7 us -> 8.35 us  [shards(): lax.all_to_all(contexts[None], ('dp', 'sub'), split_axis=2, concat_axis=0...]
    dot_general x1, matrix products: 4.89 us -> 1.49 us  [shards(): up_part = jnp.dot(gained, up_proj, preferred_element_type=jnp.float32)]
    ppermute x14, starting transfers between devices: 7.06 us -> 10.4 us  [swap_with(): return lax.ppermute(x, axis, [(i, i ^ distance) for i in range(size)])]
    dot_general x1, matrix products: 4.75 us -> 1.48 us  [shards(): gate_part = jnp.dot(gained, gate_proj, preferred_element_type=jnp.float32)]
    dot_general x1, matrix products: 1.47 us -> 4.7 us  [shards(): jnp.dot(hidden_units, down_proj, preferred_element_type=jnp.float32)]
    unnamed x15 -> x19, local copies, waits for them, and re-layouts: 2.81 us -> 2.81 us
  transfers between devices with their start and end apart: 15 -> 15, of which waited for: 11 -> 12; matrix products, arithmetic and copies ran while one was open for 9% -> 10% of each run, Pallas kernels for 0% -> 0%
where the time goes in v7:
time: 112 us; the launch traced here: 111 us
  waiting for transfers between devices  46.8 us (42%)
  starting transfers between devices  17.7 us (16%)
  blocking collectives  16.4 us (15%)
  matrix products  14 us (12%)
  Pallas kernels  9.13 us (8%)
  local copies, waits for them, and re-layouts  4.98 us (4%)
  other arithmetic  1.46 us (1%)
    ppermute x14, waiting for transfers between devices, swap_with(): return lax.ppermute(x, axis, [(i, i ^ distance) for i in range(size)])  38.4 us
    all_gather x1, blocking collectives, shards(): group_values = lax.all_gather(values, 'sub', axis=1, tiled=True)  16.4 us
    ppermute x14, starting transfers between devices, swap_with(): return lax.ppermute(x, axis, [(i, i ^ distance) for i in range(size)])  10.4 us
    pallas_call x1, Pallas kernels, attend_all(): pl.pallas_call(kernel, out_shape=jax.ShapeDtypeStruct((req_dev, head_coun...  9.13 us
    all_to_all x1, waiting for transfers between devices, shards(): lax.all_to_all(contexts[None], ('dp', 'sub'), split_axis=2, concat_axis=0...  8.35 us
    all_to_all x1, starting transfers between devices, shards(): lax.all_to_all(contexts[None], ('dp', 'sub'), split_axis=2, concat_axis=0...  7.37 us
    dot_general x1, matrix products, shards(): jnp.dot(group_values, out_proj, preferred_element_type=jnp.float32)  6.04 us
    dot_general x1, matrix products, shards(): jnp.dot(hidden_units, down_proj, preferred_element_type=jnp.float32)  4.7 us
  transfers between devices with their start and end apart: 15, of which 12 were waited for; matrix products, arithmetic and copies ran while one was open for 10% of the time, Pallas kernels for 0%

profile of v7, /device:TPU:0, one launch (start us, length us, event | category | flops | bytes accessed | tf_op | source)
XLA Modules:
  0.0 111.4 jit_solution(531647799930229087)
XLA Ops:
  0.6 0.0 copy-start
  0.6 0.0 copy-start.3
  0.7 0.0 copy-start.4
  0.7 1.4 %copy.20.queries = bf16[4,128,576]{2,1,0:T(8,128)(2,1)S(1)} copy(bf16[4,128,576]{1,2,0:T(8,128)(2,1)} %param.12) | data formatting | bytes 1179648 | tf_op args[1]
  2.1 0.0 copy-start.1
  2.1 0.7 copy-done.1
  2.8 0.0 copy-start.2
  2.8 0.7 copy-done.2
  3.5 9.1 %shard_map.122 = bf16[4,128,512]{2,1,0:T(8,128)(2,1)S(1)} custom-call(s32[4,16]{1,0:T(4,128)S(1)} %copy-done.1, s32[4]{0:T(128)S(1)} %copy-done.2, bf16[4,128,576]{2,1,0:T(8,128)(2,1)S(1)} %copy.20.queries, bf16[64,576,128]{2,1,0:T(8,128)(2,1)} %bitcast.69), custom_call_target="tpu_custom_call" | custom-call | tf_op jit(solution)/shard_map/pallas_call | solution.py:67
  12.6 1.2 %copy.21 = bf16[1,4,128,512]{3,1,0,2:T(4,128)(2,1)} copy(bf16[1,4,128,512]{3,2,1,0:T(8,128)(2,1)S(1)} %bitcast.64) | data formatting | bytes 1048576 | tf_op jit(solution)/shard_map/broadcast_in_dim | solution.py:217
  13.8 7.4 %all-to-all-start = ((bf16[1,4,128,512]{3,1,0,2:T(4,128)(2,1)}), bf16[1,4,128,512]{3,1,0,2:T(4,128)(2,1)S(1)}, u32[]{:S(2)}, u32[]{:S(2)}) async-start(bf16[1,4,128,512]{3,1,0,2:T(4,128)(2,1)} %copy.21), calls=%async_computation | async-start | bytes 1048576 | tf_op jit(solution)/shard_map/all_to_all | solution.py:216
  21.2 0.0 copy-done.3
  21.2 2.0 %collective-permute-start.2 = (bf16[1,16,1280]{2,1,0:T(8,128)(2,1)S(1)}, bf16[1,16,1280]{2,1,0:T(8,128)(2,1)S(1)}, u32[]{:S(2)}, u32[]{:S(2)}) collective-permute-start(bf16[1,16,1280]{2,1,0:T(8,128)(2,1)S(1)} %bitcast.75), channel_id=1, source_target_pairs={{0,8},{4,12},{8,0},{12,4},{1,9},{5,13},{9,1},{13,5},{2,10},{6,14},... | collective-permute-start | bytes 122888 | tf_op jit(solution)/shard_map/ppermute | solution.py:86
  23.2 0.0 copy-done.4
  23.2 5.2 %collective-permute-done.2 = bf16[1,16,1280]{2,1,0:T(8,128)(2,1)S(1)} collective-permute-done((bf16[1,16,1280]{2,1,0:T(8,128)(2,1)S(1)}, bf16[1,16,1280]{2,1,0:T(8,128)(2,1)S(1)}, u32[]{:S(2)}, u32[]{:S(2)}) %collective-permute-start.2) | collective-permute-done | bytes 40992 | tf_op jit(solution)/shard_map/ppermute | solution.py:86
  28.4 0.1 collective-permute-start.3
  28.5 8.3 %all-to-all-done = bf16[1,4,128,512]{3,1,0,2:T(4,128)(2,1)S(1)} async-done(((bf16[1,4,128,512]{3,1,0,2:T(4,128)(2,1)}), bf16[1,4,128,512]{3,1,0,2:T(4,128)(2,1)S(1)}, u32[]{:S(2)}, u32[]{:S(2)}) %all-to-all-start) | async-done | bytes 524320 | tf_op jit(solution)/shard_map/all_to_all | solution.py:216
  36.9 0.2 copy.31
  37.1 0.1 reshape.157
  37.2 0.0 copy-done
  37.2 0.3 fusion
  37.5 0.0 slice-start
  37.6 16.4 %all_gather.3 = bf16[64,4096]{1,0:T(8,128)(2,1)S(1)} all-gather(bf16[64,1024]{1,0:T(8,128)(2,1)S(1)} %bitcast.74), channel_id=1, replica_groups=mesh['grp'=2,'dp'=4,'sub'=4] {'sub'}, dimensions={1}, use_global_device_ids=true | all-gather | bytes 655360 | tf_op jit(solution)/shard_map/all_gather | solution.py:223
  53.9 0.0 slice-start.1
  53.9 6.0 %convolution_convert_fusion = bf16[64,1280]{1,0:T(8,128)(2,1)S(1)} fusion(bf16[64,4096]{1,0:T(8,128)(2,1)S(1)} %all_gather.3, bf16[4096,1280]{1,0:T(8,128)(2,1)} %param.17), kind=kOutput, calls=%fused_computation | convolution fusion | flops 671170560 | bytes 11173888 | tf_op jit(solution)/shard_map/dot_general | solution.py:227
  60.0 0.1 collective-permute-start
  60.1 1.4 %collective-permute-done = bf16[64,1280]{1,0:T(8,128)(2,1)S(1)} collective-permute-done((bf16[64,1280]{1,0:T(8,128)(2,1)S(1)}, bf16[64,1280]{1,0:T(8,128)(2,1)S(1)}, u32[]{:S(2)}, u32[]{:S(2)}) %collective-permute-start) | collective-permute-done | bytes 163872 | tf_op jit(solution)/shard_map/ppermute | solution.py:86
  61.5 0.7 collective-permute-start.1
  62.1 0.0 collective-permute-done.3
  62.2 5.6 %collective-permute-done.1 = bf16[64,1280]{1,0:T(8,128)(2,1)S(1)} collective-permute-done((bf16[64,1280]{1,0:T(8,128)(2,1)S(1)}, bf16[64,1280]{1,0:T(8,128)(2,1)S(1)}, u32[]{:S(2)}, u32[]{:S(2)}) %collective-permute-start.1) | collective-permute-done | bytes 163872 | tf_op jit(solution)/shard_map/ppermute | solution.py:86
  67.8 0.2 multiply_reduce_fusion
  68.0 0.1 collective-permute-start.6
  68.1 0.0 slice-done
  68.1 0.0 slice-done.1
  68.1 0.0 slice-start.3
  68.1 1.5 %fusion.11 = f32[64,3072]{1,0:T(8,128)S(1)} fusion(bf16[1280,3072]{1,0:T(8,128)(2,1)S(1)} %bitcast.66, f32[64,1280]{1,0:T(8,128)S(1)} %get-tuple-element.3, f32[1280]{0:T(1024)S(1)} %convert_element_type.106), kind=kOutput, calls=%fused_computation.40 | convolution fusion | flops 503480320 | bytes 8983552 | tf_op jit(solution)/shard_map/dot_general | solution.py:234
  69.6 2.0 %collective-permute-start.8 = (bf16[64,1536]{1,0:T(8,128)(2,1)S(1)}, bf16[64,1536]{1,0:T(8,128)(2,1)S(1)}, u32[]{:S(2)}, u32[]{:S(2)}) collective-permute-start(bf16[64,1536]{1,0:T(8,128)(2,1)S(1)} %select_convert_fusion), channel_id=1, source_target_pairs={{0,1},{1,0},{2,3},{3,2},{4,5},{5,4},{6,7},{7,6},{8,9},{9,8},{10,11... | collective-permute-start | bytes 589832 | tf_op jit(solution)/shard_map/ppermute | solution.py:86
  71.7 0.0 slice-done.2
  71.7 0.0 slice-done.3
  71.7 1.5 %fusion.12 = f32[64,3072]{1,0:T(8,128)S(1)} fusion(bf16[1280,3072]{1,0:T(8,128)(2,1)S(1)} %bitcast.68, f32[64,1280]{1,0:T(8,128)S(1)} %get-tuple-element.3, f32[1280]{0:T(1024)S(1)} %convert_element_type.106), kind=kOutput, calls=%fused_computation.41 | convolution fusion | flops 503480320 | bytes 8983552 | tf_op jit(solution)/shard_map/dot_general | solution.py:233
  73.2 0.5 collective-permute-start.4
  73.7 0.0 collective-permute-done.6
  73.7 0.9 collective-permute-start.7
  74.6 2.4 %collective-permute-done.8 = bf16[64,1536]{1,0:T(8,128)(2,1)S(1)} collective-permute-done((bf16[64,1536]{1,0:T(8,128)(2,1)S(1)}, bf16[64,1536]{1,0:T(8,128)(2,1)S(1)}, u32[]{:S(2)}, u32[]{:S(2)}) %collective-permute-start.8) | collective-permute-done | bytes 196640 | tf_op jit(solution)/shard_map/ppermute | solution.py:86
  77.0 0.1 convert_add_fusion
  77.1 1.7 %collective-permute-start.9 = (bf16[64,768]{1,0:T(8,128)(2,1)S(1)}, bf16[64,768]{1,0:T(8,128)(2,1)S(1)}, u32[]{:S(2)}, u32[]{:S(2)}) collective-permute-start(bf16[64,768]{1,0:T(8,128)(2,1)S(1)} %select_convert_fusion.2), channel_id=1, source_target_pairs={{0,2},{1,3},{2,0},{3,1},{4,6},{5,7},{6,4},{7,5},{8,10},{9,11},{10,... | collective-permute-start | bytes 294920 | tf_op jit(solution)/shard_map/ppermute | solution.py:86
  78.9 2.2 %collective-permute-done.4 = bf16[64,1536]{1,0:T(8,128)(2,1)S(1)} collective-permute-done((bf16[64,1536]{1,0:T(8,128)(2,1)S(1)}, bf16[64,1536]{1,0:T(8,128)(2,1)S(1)}, u32[]{:S(2)}, u32[]{:S(2)}) %collective-permute-start.4) | collective-permute-done | bytes 196640 | tf_op jit(solution)/shard_map/ppermute | solution.py:86
  81.1 0.1 convert_add_fusion.1
  81.2 1.4 %collective-permute-start.5 = (bf16[64,768]{1,0:T(8,128)(2,1)S(1)}, bf16[64,768]{1,0:T(8,128)(2,1)S(1)}, u32[]{:S(2)}, u32[]{:S(2)}) collective-permute-start(bf16[64,768]{1,0:T(8,128)(2,1)S(1)} %select_convert_fusion.3), channel_id=1, source_target_pairs={{0,2},{1,3},{2,0},{3,1},{4,6},{5,7},{6,4},{7,5},{8,10},{9,11},{10,... | collective-permute-start | bytes 294920 | tf_op jit(solution)/shard_map/ppermute | solution.py:86
  82.6 0.0 collective-permute-done.7
  82.6 0.1 collective-permute-done.9
  82.7 5.5 %collective-permute-done.5 = bf16[64,768]{1,0:T(8,128)(2,1)S(1)} collective-permute-done((bf16[64,768]{1,0:T(8,128)(2,1)S(1)}, bf16[64,768]{1,0:T(8,128)(2,1)S(1)}, u32[]{:S(2)}, u32[]{:S(2)}) %collective-permute-start.5) | collective-permute-done | bytes 98336 | tf_op jit(solution)/shard_map/ppermute | solution.py:86
  88.2 0.1 multiply_convert_fusion.1
  88.4 0.1 collective-permute-start.10
  88.4 6.4 %collective-permute-done.10 = bf16[64,768]{1,0:T(8,128)(2,1)S(1)} collective-permute-done((bf16[64,768]{1,0:T(8,128)(2,1)S(1)}, bf16[64,768]{1,0:T(8,128)(2,1)S(1)}, u32[]{:S(2)}, u32[]{:S(2)}) %collective-permute-start.10) | collective-permute-done | bytes 98336 | tf_op jit(solution)/shard_map/ppermute | solution.py:86
  94.8 0.1 collective-permute-start.11
  94.9 5.7 %collective-permute-done.11 = bf16[64,1536]{1,0:T(8,128)(2,1)S(1)} collective-permute-done((bf16[64,1536]{1,0:T(8,128)(2,1)S(1)}, bf16[64,1536]{1,0:T(8,128)(2,1)S(1)}, u32[]{:S(2)}, u32[]{:S(2)}) %collective-permute-start.11) | collective-permute-done | bytes 196640 | tf_op jit(solution)/shard_map/ppermute | solution.py:86
  100.6 4.7 %fusion.1 = f32[64,1280]{1,0:T(8,128)S(1)} fusion(bf16[3072,1280]{1,0:T(8,128)(2,1)} %param.21, bf16[64,1536]{1,0:T(8,128)(2,1)S(1)} %maximum_select_fusion.2, bf16[64,1536]{1,0:T(8,128)(2,1)S(1)} %collective-permute-done.11, pred[]{:T(512)S(6)} %ne.18), kind=kOutput, calls=%fused_computation.5 | convolution fusion | flops 505085952 | bytes 8585217 | tf_op jit(solution)/shard_map/dot_general | solution.py:240
  105.3 0.1 collective-permute-start.12
  105.4 1.2 %collective-permute-done.12 = bf16[2,16,1280]{2,1,0:T(8,128)(2,1)S(1)} collective-permute-done((bf16[2,16,1280]{2,1,0:T(8,128)(2,1)S(1)}, bf16[2,16,1280]{2,1,0:T(8,128)(2,1)S(1)}, u32[]{:S(2)}, u32[]{:S(2)}) %collective-permute-start.12) | collective-permute-done | bytes 81952 | tf_op jit(solution)/shard_map/ppermute | solution.py:86
  106.7 0.7 collective-permute-start.13
  107.4 0.6 dynamic-slice_convert_fusion
  108.0 2.7 %collective-permute-done.13 = bf16[1,16,1280]{2,1,0:T(8,128)(2,1)S(1)} collective-permute-done((bf16[1,16,1280]{2,1,0:T(8,128)(2,1)S(1)}, bf16[1,16,1280]{2,1,0:T(8,128)(2,1)S(1)}, u32[]{:S(2)}, u32[]{:S(2)}) %collective-permute-start.13) | collective-permute-done | bytes 40992 | tf_op jit(solution)/shard_map/ppermute | solution.py:86
  110.8 0.6 fusion.10
  (20 shorter events, 0.4 us)
Async XLA Ops:
  0.6 36.6 %copy-start = (bf16[8,512,128]{2,1,0:T(8,128)(2,1)S(1)}, bf16[8,512,128]{2,1,0:T(8,128)(2,1)}, u32[]{:S(2)}) copy-start(bf16[8,512,128]{2,1,0:T(8,128)(2,1)} %param.16) | copy-start | bytes 3145732
  0.6 20.5 %copy-start.3 = (bf16[16,1280]{1,0:T(8,128)(2,1)S(1)}, bf16[16,1280]{1,0:T(8,128)(2,1)}, u32[]{:S(2)}) copy-start(bf16[16,1280]{1,0:T(8,128)(2,1)} %param.11) | copy-start | bytes 122884
  0.7 22.5 %copy-start.4 = (bf16[1280]{0:T(1024)(128)(2,1)S(1)}, bf16[1280]{0:T(1024)(128)(2,1)}, u32[]{:S(2)}) copy-start(bf16[1280]{0:T(1024)(128)(2,1)} %param.18) | copy-start | bytes 7684
  2.1 0.7 copy-start.1
  2.8 0.7 copy-start.2
  13.8 23.1 %all-to-all-start = ((bf16[1,4,128,512]{3,1,0,2:T(4,128)(2,1)}), bf16[1,4,128,512]{3,1,0,2:T(4,128)(2,1)S(1)}, u32[]{:S(2)}, u32[]{:S(2)}) async-start(bf16[1,4,128,512]{3,1,0,2:T(4,128)(2,1)} %copy.21), calls=%async_computation | async-start | bytes 1048576 | tf_op jit(solution)/shard_map/all_to_all | solution.py:216
  21.2 7.2 %collective-permute-start.2 = (bf16[1,16,1280]{2,1,0:T(8,128)(2,1)S(1)}, bf16[1,16,1280]{2,1,0:T(8,128)(2,1)S(1)}, u32[]{:S(2)}, u32[]{:S(2)}) collective-permute-start(bf16[1,16,1280]{2,1,0:T(8,128)(2,1)S(1)} %bitcast.75), channel_id=1, source_target_pairs={{0,8},{4,12},{8,0},{12,4},{1,9},{5,13},{9,1},{13,5},{2,10},{6,14},... | collective-permute-start | bytes 122888 | tf_op jit(solution)/shard_map/ppermute | solution.py:86
  28.4 33.7 %collective-permute-start.3 = (bf16[2,16,1280]{2,1,0:T(8,128)(2,1)S(1)}, bf16[2,16,1280]{2,1,0:T(8,128)(2,1)S(1)}, u32[]{:S(2)}, u32[]{:S(2)}) collective-permute-start(bf16[2,16,1280]{2,1,0:T(8,128)(2,1)S(1)} %maximum_select_fusion.4), channel_id=1, source_target_pairs={{0,4},{4,0},{8,12},{12,8},{1,5},{5,1},{9,13},{13,9},{2,6},{6,2},{1... | collective-permute-start | bytes 245768 | tf_op jit(solution)/shard_map/ppermute | solution.py:86
  37.5 30.5 %slice-start = ((s8[7864320]{0:T(1024)(128)(4,1)}), s8[4194304]{0:T(1024)(128)(4,1)S(1)}, s32[]{:S(2)}) async-start(s8[7864320]{0:T(1024)(128)(4,1)} %bitcast.65), calls=%async_computation.1 | async-start | bytes 8388608
  53.9 14.1 %slice-start.1 = ((s8[7864320]{0:T(1024)(128)(4,1)}), s8[3670016]{0:T(1024)(128)(4,1)S(1)}, s32[]{:S(2)}) async-start(s8[7864320]{0:T(1024)(128)(4,1)} %bitcast.65), calls=%async_computation.2 | async-start | bytes 7340032
  60.0 1.5 %collective-permute-start = (bf16[64,1280]{1,0:T(8,128)(2,1)S(1)}, bf16[64,1280]{1,0:T(8,128)(2,1)S(1)}, u32[]{:S(2)}, u32[]{:S(2)}) collective-permute-start(bf16[64,1280]{1,0:T(8,128)(2,1)S(1)} %convolution_convert_fusion), channel_id=1, source_target_pairs={{0,4},{4,0},{8,12},{12,8},{1,5},{5,1},{9,13},{13,9},{2,6},{6,2},{1... | collective-permute-start | bytes 491528 | tf_op jit(solution)/shard_map/ppermute | solution.py:86
  61.5 6.3 %collective-permute-start.1 = (bf16[64,1280]{1,0:T(8,128)(2,1)S(1)}, bf16[64,1280]{1,0:T(8,128)(2,1)S(1)}, u32[]{:S(2)}, u32[]{:S(2)}) collective-permute-start(bf16[64,1280]{1,0:T(8,128)(2,1)S(1)} %add_convert_fusion), channel_id=1, source_target_pairs={{0,8},{4,12},{8,0},{12,4},{1,9},{5,13},{9,1},{13,5},{2,10},{6,14},... | collective-permute-start | bytes 491528 | tf_op jit(solution)/shard_map/ppermute | solution.py:86
  67.8 3.9 %slice-start.2 = ((s8[7864320]{0:T(1024)(128)(4,1)}), s8[4194304]{0:T(1024)(128)(4,1)S(1)}, s32[]{:S(2)}) async-start(s8[7864320]{0:T(1024)(128)(4,1)} %bitcast.67), calls=%async_computation.3 | async-start | bytes 8388608
  68.0 5.7 %collective-permute-start.6 = (f32[64]{0:T(128)S(1)}, f32[64]{0:T(128)S(1)}, u32[]{:S(2)}, u32[]{:S(2)}) collective-permute-start(f32[64]{0:T(128)S(1)} %get-tuple-element.2), channel_id=1, source_target_pairs={{0,1},{1,0},{2,3},{3,2},{4,5},{5,4},{6,7},{7,6},{8,9},{9,8},{10,11... | collective-permute-start | bytes 776 | tf_op jit(solution)/shard_map/ppermute | solution.py:86
  68.1 3.6 %slice-start.3 = ((s8[7864320]{0:T(1024)(128)(4,1)}), s8[3670016]{0:T(1024)(128)(4,1)S(1)}, s32[]{:S(2)}) async-start(s8[7864320]{0:T(1024)(128)(4,1)} %bitcast.67), calls=%async_computation.4 | async-start | bytes 7340032
  69.6 7.4 %collective-permute-start.8 = (bf16[64,1536]{1,0:T(8,128)(2,1)S(1)}, bf16[64,1536]{1,0:T(8,128)(2,1)S(1)}, u32[]{:S(2)}, u32[]{:S(2)}) collective-permute-start(bf16[64,1536]{1,0:T(8,128)(2,1)S(1)} %select_convert_fusion), channel_id=1, source_target_pairs={{0,1},{1,0},{2,3},{3,2},{4,5},{5,4},{6,7},{7,6},{8,9},{9,8},{10,11... | collective-permute-start | bytes 589832 | tf_op jit(solution)/shard_map/ppermute | solution.py:86
  73.2 7.9 %collective-permute-start.4 = (bf16[64,1536]{1,0:T(8,128)(2,1)S(1)}, bf16[64,1536]{1,0:T(8,128)(2,1)S(1)}, u32[]{:S(2)}, u32[]{:S(2)}) collective-permute-start(bf16[64,1536]{1,0:T(8,128)(2,1)S(1)} %select_convert_fusion.1), channel_id=1, source_target_pairs={{0,1},{1,0},{2,3},{3,2},{4,5},{5,4},{6,7},{7,6},{8,9},{9,8},{10,11... | collective-permute-start | bytes 589832 | tf_op jit(solution)/shard_map/ppermute | solution.py:86
  73.7 8.9 %collective-permute-start.7 = (f32[64]{0:T(128)S(1)}, f32[64]{0:T(128)S(1)}, u32[]{:S(2)}, u32[]{:S(2)}) collective-permute-start(f32[64]{0:T(128)S(1)} %add.56), channel_id=1, source_target_pairs={{0,2},{1,3},{2,0},{3,1},{4,6},{5,7},{6,4},{7,5},{8,10},{9,11},{10,... | collective-permute-start | bytes 776 | tf_op jit(solution)/shard_map/ppermute | solution.py:86
  77.1 5.6 %collective-permute-start.9 = (bf16[64,768]{1,0:T(8,128)(2,1)S(1)}, bf16[64,768]{1,0:T(8,128)(2,1)S(1)}, u32[]{:S(2)}, u32[]{:S(2)}) collective-permute-start(bf16[64,768]{1,0:T(8,128)(2,1)S(1)} %select_convert_fusion.2), channel_id=1, source_target_pairs={{0,2},{1,3},{2,0},{3,1},{4,6},{5,7},{6,4},{7,5},{8,10},{9,11},{10,... | collective-permute-start | bytes 294920 | tf_op jit(solution)/shard_map/ppermute | solution.py:86
  81.2 7.0 %collective-permute-start.5 = (bf16[64,768]{1,0:T(8,128)(2,1)S(1)}, bf16[64,768]{1,0:T(8,128)(2,1)S(1)}, u32[]{:S(2)}, u32[]{:S(2)}) collective-permute-start(bf16[64,768]{1,0:T(8,128)(2,1)S(1)} %select_convert_fusion.3), channel_id=1, source_target_pairs={{0,2},{1,3},{2,0},{3,1},{4,6},{5,7},{6,4},{7,5},{8,10},{9,11},{10,... | collective-permute-start | bytes 294920 | tf_op jit(solution)/shard_map/ppermute | solution.py:86
  88.4 6.4 %collective-permute-start.10 = (bf16[64,768]{1,0:T(8,128)(2,1)S(1)}, bf16[64,768]{1,0:T(8,128)(2,1)S(1)}, u32[]{:S(2)}, u32[]{:S(2)}) collective-permute-start(bf16[64,768]{1,0:T(8,128)(2,1)S(1)} %multiply_convert_fusion.1), channel_id=1, source_target_pairs={{0,2},{1,3},{2,0},{3,1},{4,6},{5,7},{6,4},{7,5},{8,10},{9,11},{10,... | collective-permute-start | bytes 294920 | tf_op jit(solution)/shard_map/ppermute | solution.py:86
  94.8 5.7 %collective-permute-start.11 = (bf16[64,1536]{1,0:T(8,128)(2,1)S(1)}, bf16[64,1536]{1,0:T(8,128)(2,1)S(1)}, u32[]{:S(2)}, u32[]{:S(2)}) collective-permute-start(bf16[64,1536]{1,0:T(8,128)(2,1)S(1)} %maximum_select_fusion.2), channel_id=1, source_target_pairs={{0,1},{1,0},{2,3},{3,2},{4,5},{5,4},{6,7},{7,6},{8,9},{9,8},{10,11... | collective-permute-start | bytes 589832 | tf_op jit(solution)/shard_map/ppermute | solution.py:86
  105.3 1.3 %collective-permute-start.12 = (bf16[2,16,1280]{2,1,0:T(8,128)(2,1)S(1)}, bf16[2,16,1280]{2,1,0:T(8,128)(2,1)S(1)}, u32[]{:S(2)}, u32[]{:S(2)}) collective-permute-start(bf16[2,16,1280]{2,1,0:T(8,128)(2,1)S(1)} %fusion.9), channel_id=1, source_target_pairs={{0,4},{4,0},{8,12},{12,8},{1,5},{5,1},{9,13},{13,9},{2,6},{6,2},{1... | collective-permute-start | bytes 245768 | tf_op jit(solution)/shard_map/ppermute | solution.py:86
  106.7 4.1 %collective-permute-start.13 = (bf16[1,16,1280]{2,1,0:T(8,128)(2,1)S(1)}, bf16[1,16,1280]{2,1,0:T(8,128)(2,1)S(1)}, u32[]{:S(2)}, u32[]{:S(2)}) collective-permute-start(bf16[1,16,1280]{2,1,0:T(8,128)(2,1)S(1)} %fusion.13), channel_id=1, source_target_pairs={{0,8},{4,12},{8,0},{12,4},{1,9},{5,13},{9,1},{13,5},{2,10},{6,14},... | collective-permute-start | bytes 122888 | tf_op jit(solution)/shard_map/ppermute | solution.py:86

commit v8 on v7

--- a/solution.py
+++ b/solution.py
@@ -19,7 +19,7 @@
                   *, latent, score_scale):
     req_dev, pages_req = page_table.shape
     page_size = cache_pool.shape[2]
-    head_count = queries.shape[1]
+    head_count = queries.shape[2]
 
     def page_copy(slot, page):
         return pltpu.make_async_copy(
@@ -44,7 +44,8 @@
 
         lax.fori_loop(0, pages_req, finish, 0)
         live = positions < lengths[slot]
-        scores = jnp.dot(queries[slot], keys[slot], preferred_element_type=jnp.float32) * score_scale
+        query_rows = jnp.transpose(queries[slot])
+        scores = jnp.dot(query_rows, keys[slot], preferred_element_type=jnp.float32) * score_scale
         scores = jnp.where(live, scores, masked_score)
         row_max = jnp.max(scores, axis=1, keepdims=True)
         exponent = jnp.exp(scores - row_max)
@@ -61,6 +62,7 @@
 def attend_all(queries, page_table, lengths, cache_pool, latent, score_scale):
     req_dev, head_count, width = queries.shape
     pages_req = page_table.shape[1]
+    query_columns = jnp.swapaxes(queries, 1, 2)
     page_size = cache_pool.shape[1]
     cache_columns = jnp.swapaxes(cache_pool, 1, 2)
     kernel = functools.partial(attend_kernel, latent=latent, score_scale=score_scale)
@@ -79,7 +81,7 @@
             pltpu.SemaphoreType.DMA((req_dev * pages_req,)),
         ],
         compiler_params=pltpu.CompilerParams(vmem_limit_bytes=48 * 1024 * 1024),
-    )(page_table, lengths, queries, cache_columns)
+    )(page_table, lengths, query_columns, cache_columns)
 
 
 def swap_with(x, axis, distance, size):

time: 112 us -> 112 us (level)
    unnamed x19 -> x20, local copies, waits for them, and re-layouts: 2.81 us -> 2.52 us
where the time goes in v8:
time: 112 us; the launch traced here: 111 us
  waiting for transfers between devices  46.8 us (42%)
  starting transfers between devices  17.7 us (16%)
  blocking collectives  16.4 us (15%)
  matrix products  14 us (12%)
  Pallas kernels  9.23 us (8%)
  local copies, waits for them, and re-layouts  4.69 us (4%)
  other arithmetic  1.46 us (1%)
    ppermute x14, waiting for transfers between devices, swap_with(): return lax.ppermute(x, axis, [(i, i ^ distance) for i in range(size)])  38.4 us
    all_gather x1, blocking collectives, shards(): group_values = lax.all_gather(values, 'sub', axis=1, tiled=True)  16.4 us
    ppermute x14, starting transfers between devices, swap_with(): return lax.ppermute(x, axis, [(i, i ^ distance) for i in range(size)])  10.4 us
    pallas_call x1, Pallas kernels, attend_all(): pl.pallas_call(kernel, out_shape=jax.ShapeDtypeStruct((req_dev, head_coun...  9.23 us
    all_to_all x1, waiting for transfers between devices, shards(): lax.all_to_all(contexts[None], ('dp', 'sub'), split_axis=2, concat_axis=0...  8.35 us
    all_to_all x1, starting transfers between devices, shards(): lax.all_to_all(contexts[None], ('dp', 'sub'), split_axis=2, concat_axis=0...  7.35 us
    dot_general x1, matrix products, shards(): jnp.dot(group_values, out_proj, preferred_element_type=jnp.float32)  6.04 us
    dot_general x1, matrix products, shards(): jnp.dot(hidden_units, down_proj, preferred_element_type=jnp.float32)  4.7 us
  transfers between devices with their start and end apart: 15, of which 12 were waited for; matrix products, arithmetic and copies ran while one was open for 10% of the time, Pallas kernels for 0%

profile of v8, /device:TPU:0, one launch (start us, length us, event | category | flops | bytes accessed | tf_op | source)
XLA Modules:
  0.0 111.2 jit_solution(16016769811629361561)
XLA Ops:
  0.6 0.0 copy-start
  0.6 0.0 copy-start.1
  0.7 1.1 %copy-done.1 = bf16[4,128,576]{1,2,0:T(8,128)(2,1)S(1)} copy-done((bf16[4,128,576]{1,2,0:T(8,128)(2,1)S(1)}, bf16[4,128,576]{1,2,0:T(8,128)(2,1)}, u32[]{:S(2)}) %copy-start.1) | copy-done | bytes 589848
  1.8 0.0 copy-start.2
  1.8 0.7 copy-done.2
  2.5 0.0 copy-start.3
  2.5 0.7 copy-done.3
  3.1 0.0 copy-start.4
  3.1 0.0 copy-start.5
  3.1 9.2 %shard_map.122 = bf16[4,128,512]{2,1,0:T(8,128)(2,1)S(1)} custom-call(s32[4,16]{1,0:T(4,128)S(1)} %copy-done.2, s32[4]{0:T(128)S(1)} %copy-done.3, bf16[4,576,128]{2,1,0:T(8,128)(2,1)S(1)} %bitcast.66, bf16[64,576,128]{2,1,0:T(8,128)(2,1)} %bitcast.71), custom_call_target="tpu_custom_call" | custom-call | tf_op jit(solution)/shard_map/pallas_call | solution.py:69
  12.4 1.2 %copy.18 = bf16[1,4,128,512]{3,1,0,2:T(4,128)(2,1)} copy(bf16[1,4,128,512]{3,2,1,0:T(8,128)(2,1)S(1)} %bitcast.65) | data formatting | bytes 1048576 | tf_op jit(solution)/shard_map/broadcast_in_dim | solution.py:219
  13.6 7.4 %all-to-all-start = ((bf16[1,4,128,512]{3,1,0,2:T(4,128)(2,1)}), bf16[1,4,128,512]{3,1,0,2:T(4,128)(2,1)S(1)}, u32[]{:S(2)}, u32[]{:S(2)}) async-start(bf16[1,4,128,512]{3,1,0,2:T(4,128)(2,1)} %copy.18), calls=%async_computation | async-start | bytes 1048576 | tf_op jit(solution)/shard_map/all_to_all | solution.py:218
  21.0 0.0 copy-done.4
  21.0 2.0 %collective-permute-start.2 = (bf16[1,16,1280]{2,1,0:T(8,128)(2,1)S(1)}, bf16[1,16,1280]{2,1,0:T(8,128)(2,1)S(1)}, u32[]{:S(2)}, u32[]{:S(2)}) collective-permute-start(bf16[1,16,1280]{2,1,0:T(8,128)(2,1)S(1)} %bitcast.77), channel_id=1, source_target_pairs={{0,8},{4,12},{8,0},{12,4},{1,9},{5,13},{9,1},{13,5},{2,10},{6,14},... | collective-permute-start | bytes 122888 | tf_op jit(solution)/shard_map/ppermute | solution.py:88
  23.0 0.0 copy-done.5
  23.0 5.2 %collective-permute-done.2 = bf16[1,16,1280]{2,1,0:T(8,128)(2,1)S(1)} collective-permute-done((bf16[1,16,1280]{2,1,0:T(8,128)(2,1)S(1)}, bf16[1,16,1280]{2,1,0:T(8,128)(2,1)S(1)}, u32[]{:S(2)}, u32[]{:S(2)}) %collective-permute-start.2) | collective-permute-done | bytes 40992 | tf_op jit(solution)/shard_map/ppermute | solution.py:88
  28.2 0.1 collective-permute-start.3
  28.3 8.3 %all-to-all-done = bf16[1,4,128,512]{3,1,0,2:T(4,128)(2,1)S(1)} async-done(((bf16[1,4,128,512]{3,1,0,2:T(4,128)(2,1)}), bf16[1,4,128,512]{3,1,0,2:T(4,128)(2,1)S(1)}, u32[]{:S(2)}, u32[]{:S(2)}) %all-to-all-start) | async-done | bytes 524320 | tf_op jit(solution)/shard_map/all_to_all | solution.py:218
  36.6 0.2 copy.28
  36.8 0.1 reshape.157
  37.0 0.0 copy-done
  37.0 0.3 fusion
  37.3 0.0 slice-start
  37.3 16.4 %all_gather.3 = bf16[64,4096]{1,0:T(8,128)(2,1)S(1)} all-gather(bf16[64,1024]{1,0:T(8,128)(2,1)S(1)} %bitcast.76), channel_id=1, replica_groups=mesh['grp'=2,'dp'=4,'sub'=4] {'sub'}, dimensions={1}, use_global_device_ids=true | all-gather | bytes 655360 | tf_op jit(solution)/shard_map/all_gather | solution.py:225
  53.7 6.0 %convolution_convert_fusion = bf16[64,1280]{1,0:T(8,128)(2,1)S(1)} fusion(bf16[64,4096]{1,0:T(8,128)(2,1)S(1)} %all_gather.3, bf16[4096,1280]{1,0:T(8,128)(2,1)} %param.17), kind=kOutput, calls=%fused_computation | convolution fusion | flops 671170560 | bytes 11173888 | tf_op jit(solution)/shard_map/dot_general | solution.py:229
  59.8 0.1 collective-permute-start
  59.9 1.4 %collective-permute-done = bf16[64,1280]{1,0:T(8,128)(2,1)S(1)} collective-permute-done((bf16[64,1280]{1,0:T(8,128)(2,1)S(1)}, bf16[64,1280]{1,0:T(8,128)(2,1)S(1)}, u32[]{:S(2)}, u32[]{:S(2)}) %collective-permute-start) | collective-permute-done | bytes 163872 | tf_op jit(solution)/shard_map/ppermute | solution.py:88
  61.3 0.7 collective-permute-start.1
  61.9 0.0 collective-permute-done.3
  61.9 5.6 %collective-permute-done.1 = bf16[64,1280]{1,0:T(8,128)(2,1)S(1)} collective-permute-done((bf16[64,1280]{1,0:T(8,128)(2,1)S(1)}, bf16[64,1280]{1,0:T(8,128)(2,1)S(1)}, u32[]{:S(2)}, u32[]{:S(2)}) %collective-permute-start.1) | collective-permute-done | bytes 163872 | tf_op jit(solution)/shard_map/ppermute | solution.py:88
  67.6 0.2 multiply_reduce_fusion
  67.8 0.1 collective-permute-start.6
  67.8 0.0 slice-done
  67.8 0.0 slice-done.1
  67.9 0.0 slice-start.3
  67.9 1.5 %fusion.11 = f32[64,3072]{1,0:T(8,128)S(1)} fusion(bf16[1280,3072]{1,0:T(8,128)(2,1)S(1)} %bitcast.68, f32[64,1280]{1,0:T(8,128)S(1)} %get-tuple-element.3, f32[1280]{0:T(1024)S(1)} %convert_element_type.106), kind=kOutput, calls=%fused_computation.40 | convolution fusion | flops 503480320 | bytes 8983552 | tf_op jit(solution)/shard_map/dot_general | solution.py:236
  69.4 2.0 %collective-permute-start.8 = (bf16[64,1536]{1,0:T(8,128)(2,1)S(1)}, bf16[64,1536]{1,0:T(8,128)(2,1)S(1)}, u32[]{:S(2)}, u32[]{:S(2)}) collective-permute-start(bf16[64,1536]{1,0:T(8,128)(2,1)S(1)} %select_convert_fusion), channel_id=1, source_target_pairs={{0,1},{1,0},{2,3},{3,2},{4,5},{5,4},{6,7},{7,6},{8,9},{9,8},{10,11... | collective-permute-start | bytes 589832 | tf_op jit(solution)/shard_map/ppermute | solution.py:88
  71.5 0.0 slice-done.2
  71.5 0.0 slice-done.3
  71.5 1.5 %fusion.12 = f32[64,3072]{1,0:T(8,128)S(1)} fusion(bf16[1280,3072]{1,0:T(8,128)(2,1)S(1)} %bitcast.70, f32[64,1280]{1,0:T(8,128)S(1)} %get-tuple-element.3, f32[1280]{0:T(1024)S(1)} %convert_element_type.106), kind=kOutput, calls=%fused_computation.41 | convolution fusion | flops 503480320 | bytes 8983552 | tf_op jit(solution)/shard_map/dot_general | solution.py:235
  73.0 0.5 collective-permute-start.4
  73.5 0.0 collective-permute-done.6
  73.5 0.9 collective-permute-start.7
  74.4 2.4 %collective-permute-done.8 = bf16[64,1536]{1,0:T(8,128)(2,1)S(1)} collective-permute-done((bf16[64,1536]{1,0:T(8,128)(2,1)S(1)}, bf16[64,1536]{1,0:T(8,128)(2,1)S(1)}, u32[]{:S(2)}, u32[]{:S(2)}) %collective-permute-start.8) | collective-permute-done | bytes 196640 | tf_op jit(solution)/shard_map/ppermute | solution.py:88
  76.8 0.1 convert_add_fusion
  76.9 1.7 %collective-permute-start.9 = (bf16[64,768]{1,0:T(8,128)(2,1)S(1)}, bf16[64,768]{1,0:T(8,128)(2,1)S(1)}, u32[]{:S(2)}, u32[]{:S(2)}) collective-permute-start(bf16[64,768]{1,0:T(8,128)(2,1)S(1)} %select_convert_fusion.2), channel_id=1, source_target_pairs={{0,2},{1,3},{2,0},{3,1},{4,6},{5,7},{6,4},{7,5},{8,10},{9,11},{10,... | collective-permute-start | bytes 294920 | tf_op jit(solution)/shard_map/ppermute | solution.py:88
  78.7 2.2 %collective-permute-done.4 = bf16[64,1536]{1,0:T(8,128)(2,1)S(1)} collective-permute-done((bf16[64,1536]{1,0:T(8,128)(2,1)S(1)}, bf16[64,1536]{1,0:T(8,128)(2,1)S(1)}, u32[]{:S(2)}, u32[]{:S(2)}) %collective-permute-start.4) | collective-permute-done | bytes 196640 | tf_op jit(solution)/shard_map/ppermute | solution.py:88
  80.9 0.1 convert_add_fusion.1
  81.0 1.4 %collective-permute-start.5 = (bf16[64,768]{1,0:T(8,128)(2,1)S(1)}, bf16[64,768]{1,0:T(8,128)(2,1)S(1)}, u32[]{:S(2)}, u32[]{:S(2)}) collective-permute-start(bf16[64,768]{1,0:T(8,128)(2,1)S(1)} %select_convert_fusion.3), channel_id=1, source_target_pairs={{0,2},{1,3},{2,0},{3,1},{4,6},{5,7},{6,4},{7,5},{8,10},{9,11},{10,... | collective-permute-start | bytes 294920 | tf_op jit(solution)/shard_map/ppermute | solution.py:88
  82.4 0.0 collective-permute-done.7
  82.4 0.1 collective-permute-done.9
  82.5 5.5 %collective-permute-done.5 = bf16[64,768]{1,0:T(8,128)(2,1)S(1)} collective-permute-done((bf16[64,768]{1,0:T(8,128)(2,1)S(1)}, bf16[64,768]{1,0:T(8,128)(2,1)S(1)}, u32[]{:S(2)}, u32[]{:S(2)}) %collective-permute-start.5) | collective-permute-done | bytes 98336 | tf_op jit(solution)/shard_map/ppermute | solution.py:88
  88.0 0.1 multiply_convert_fusion.1
  88.1 0.1 collective-permute-start.10
  88.2 6.4 %collective-permute-done.10 = bf16[64,768]{1,0:T(8,128)(2,1)S(1)} collective-permute-done((bf16[64,768]{1,0:T(8,128)(2,1)S(1)}, bf16[64,768]{1,0:T(8,128)(2,1)S(1)}, u32[]{:S(2)}, u32[]{:S(2)}) %collective-permute-start.10) | collective-permute-done | bytes 98336 | tf_op jit(solution)/shard_map/ppermute | solution.py:88
  94.6 0.1 collective-permute-start.11
  94.7 5.7 %collective-permute-done.11 = bf16[64,1536]{1,0:T(8,128)(2,1)S(1)} collective-permute-done((bf16[64,1536]{1,0:T(8,128)(2,1)S(1)}, bf16[64,1536]{1,0:T(8,128)(2,1)S(1)}, u32[]{:S(2)}, u32[]{:S(2)}) %collective-permute-start.11) | collective-permute-done | bytes 196640 | tf_op jit(solution)/shard_map/ppermute | solution.py:88
  100.4 4.7 %fusion.1 = f32[64,1280]{1,0:T(8,128)S(1)} fusion(bf16[3072,1280]{1,0:T(8,128)(2,1)} %param.21, bf16[64,1536]{1,0:T(8,128)(2,1)S(1)} %maximum_select_fusion.2, bf16[64,1536]{1,0:T(8,128)(2,1)S(1)} %collective-permute-done.11, pred[]{:T(512)S(6)} %ne.18), kind=kOutput, calls=%fused_computation.5 | convolution fusion | flops 505085952 | bytes 8585217 | tf_op jit(solution)/shard_map/dot_general | solution.py:242
  105.1 0.1 collective-permute-start.12
  105.2 1.2 %collective-permute-done.12 = bf16[2,16,1280]{2,1,0:T(8,128)(2,1)S(1)} collective-permute-done((bf16[2,16,1280]{2,1,0:T(8,128)(2,1)S(1)}, bf16[2,16,1280]{2,1,0:T(8,128)(2,1)S(1)}, u32[]{:S(2)}, u32[]{:S(2)}) %collective-permute-start.12) | collective-permute-done | bytes 81952 | tf_op jit(solution)/shard_map/ppermute | solution.py:88
  106.5 0.7 collective-permute-start.13
  107.2 0.6 dynamic-slice_convert_fusion
  107.8 2.7 %collective-permute-done.13 = bf16[1,16,1280]{2,1,0:T(8,128)(2,1)S(1)} collective-permute-done((bf16[1,16,1280]{2,1,0:T(8,128)(2,1)S(1)}, bf16[1,16,1280]{2,1,0:T(8,128)(2,1)S(1)}, u32[]{:S(2)}, u32[]{:S(2)}) %collective-permute-start.13) | collective-permute-done | bytes 40992 | tf_op jit(solution)/shard_map/ppermute | solution.py:88
  110.5 0.6 fusion.10
  (21 shorter events, 0.4 us)
Async XLA Ops:
  0.6 36.3 %copy-start = (bf16[8,512,128]{2,1,0:T(8,128)(2,1)S(1)}, bf16[8,512,128]{2,1,0:T(8,128)(2,1)}, u32[]{:S(2)}) copy-start(bf16[8,512,128]{2,1,0:T(8,128)(2,1)} %param.16) | copy-start | bytes 3145732
  0.6 1.2 %copy-start.1 = (bf16[4,128,576]{1,2,0:T(8,128)(2,1)S(1)}, bf16[4,128,576]{1,2,0:T(8,128)(2,1)}, u32[]{:S(2)}) copy-start(bf16[4,128,576]{1,2,0:T(8,128)(2,1)} %param.12) | copy-start | bytes 1769476
  1.8 0.7 copy-start.2
  2.5 0.7 copy-start.3
  3.1 17.8 %copy-start.4 = (bf16[16,1280]{1,0:T(8,128)(2,1)S(1)}, bf16[16,1280]{1,0:T(8,128)(2,1)}, u32[]{:S(2)}) copy-start(bf16[16,1280]{1,0:T(8,128)(2,1)} %param.11) | copy-start | bytes 122884
  3.1 19.8 %copy-start.5 = (bf16[1280]{0:T(1024)(128)(2,1)S(1)}, bf16[1280]{0:T(1024)(128)(2,1)}, u32[]{:S(2)}) copy-start(bf16[1280]{0:T(1024)(128)(2,1)} %param.18) | copy-start | bytes 7684
  13.6 23.0 %all-to-all-start = ((bf16[1,4,128,512]{3,1,0,2:T(4,128)(2,1)}), bf16[1,4,128,512]{3,1,0,2:T(4,128)(2,1)S(1)}, u32[]{:S(2)}, u32[]{:S(2)}) async-start(bf16[1,4,128,512]{3,1,0,2:T(4,128)(2,1)} %copy.18), calls=%async_computation | async-start | bytes 1048576 | tf_op jit(solution)/shard_map/all_to_all | solution.py:218
  21.0 7.2 %collective-permute-start.2 = (bf16[1,16,1280]{2,1,0:T(8,128)(2,1)S(1)}, bf16[1,16,1280]{2,1,0:T(8,128)(2,1)S(1)}, u32[]{:S(2)}, u32[]{:S(2)}) collective-permute-start(bf16[1,16,1280]{2,1,0:T(8,128)(2,1)S(1)} %bitcast.77), channel_id=1, source_target_pairs={{0,8},{4,12},{8,0},{12,4},{1,9},{5,13},{9,1},{13,5},{2,10},{6,14},... | collective-permute-start | bytes 122888 | tf_op jit(solution)/shard_map/ppermute | solution.py:88
  28.2 33.7 %collective-permute-start.3 = (bf16[2,16,1280]{2,1,0:T(8,128)(2,1)S(1)}, bf16[2,16,1280]{2,1,0:T(8,128)(2,1)S(1)}, u32[]{:S(2)}, u32[]{:S(2)}) collective-permute-start(bf16[2,16,1280]{2,1,0:T(8,128)(2,1)S(1)} %maximum_select_fusion.4), channel_id=1, source_target_pairs={{0,4},{4,0},{8,12},{12,8},{1,5},{5,1},{9,13},{13,9},{2,6},{6,2},{1... | collective-permute-start | bytes 245768 | tf_op jit(solution)/shard_map/ppermute | solution.py:88
  37.3 30.5 %slice-start = ((s8[7864320]{0:T(1024)(128)(4,1)}), s8[4194304]{0:T(1024)(128)(4,1)S(1)}, s32[]{:S(2)}) async-start(s8[7864320]{0:T(1024)(128)(4,1)} %bitcast.67), calls=%async_computation.1 | async-start | bytes 8388608
  53.7 14.1 %slice-start.1 = ((s8[7864320]{0:T(1024)(128)(4,1)}), s8[3670016]{0:T(1024)(128)(4,1)S(1)}, s32[]{:S(2)}) async-start(s8[7864320]{0:T(1024)(128)(4,1)} %bitcast.67), calls=%async_computation.2 | async-start | bytes 7340032
  59.8 1.5 %collective-permute-start = (bf16[64,1280]{1,0:T(8,128)(2,1)S(1)}, bf16[64,1280]{1,0:T(8,128)(2,1)S(1)}, u32[]{:S(2)}, u32[]{:S(2)}) collective-permute-start(bf16[64,1280]{1,0:T(8,128)(2,1)S(1)} %convolution_convert_fusion), channel_id=1, source_target_pairs={{0,4},{4,0},{8,12},{12,8},{1,5},{5,1},{9,13},{13,9},{2,6},{6,2},{1... | collective-permute-start | bytes 491528 | tf_op jit(solution)/shard_map/ppermute | solution.py:88
  61.3 6.3 %collective-permute-start.1 = (bf16[64,1280]{1,0:T(8,128)(2,1)S(1)}, bf16[64,1280]{1,0:T(8,128)(2,1)S(1)}, u32[]{:S(2)}, u32[]{:S(2)}) collective-permute-start(bf16[64,1280]{1,0:T(8,128)(2,1)S(1)} %add_convert_fusion), channel_id=1, source_target_pairs={{0,8},{4,12},{8,0},{12,4},{1,9},{5,13},{9,1},{13,5},{2,10},{6,14},... | collective-permute-start | bytes 491528 | tf_op jit(solution)/shard_map/ppermute | solution.py:88
  67.6 3.9 %slice-start.2 = ((s8[7864320]{0:T(1024)(128)(4,1)}), s8[4194304]{0:T(1024)(128)(4,1)S(1)}, s32[]{:S(2)}) async-start(s8[7864320]{0:T(1024)(128)(4,1)} %bitcast.69), calls=%async_computation.3 | async-start | bytes 8388608
  67.8 5.7 %collective-permute-start.6 = (f32[64]{0:T(128)S(1)}, f32[64]{0:T(128)S(1)}, u32[]{:S(2)}, u32[]{:S(2)}) collective-permute-start(f32[64]{0:T(128)S(1)} %get-tuple-element.2), channel_id=1, source_target_pairs={{0,1},{1,0},{2,3},{3,2},{4,5},{5,4},{6,7},{7,6},{8,9},{9,8},{10,11... | collective-permute-start | bytes 776 | tf_op jit(solution)/shard_map/ppermute | solution.py:88
  67.9 3.6 %slice-start.3 = ((s8[7864320]{0:T(1024)(128)(4,1)}), s8[3670016]{0:T(1024)(128)(4,1)S(1)}, s32[]{:S(2)}) async-start(s8[7864320]{0:T(1024)(128)(4,1)} %bitcast.69), calls=%async_computation.4 | async-start | bytes 7340032
  69.4 7.4 %collective-permute-start.8 = (bf16[64,1536]{1,0:T(8,128)(2,1)S(1)}, bf16[64,1536]{1,0:T(8,128)(2,1)S(1)}, u32[]{:S(2)}, u32[]{:S(2)}) collective-permute-start(bf16[64,1536]{1,0:T(8,128)(2,1)S(1)} %select_convert_fusion), channel_id=1, source_target_pairs={{0,1},{1,0},{2,3},{3,2},{4,5},{5,4},{6,7},{7,6},{8,9},{9,8},{10,11... | collective-permute-start | bytes 589832 | tf_op jit(solution)/shard_map/ppermute | solution.py:88
  73.0 7.9 %collective-permute-start.4 = (bf16[64,1536]{1,0:T(8,128)(2,1)S(1)}, bf16[64,1536]{1,0:T(8,128)(2,1)S(1)}, u32[]{:S(2)}, u32[]{:S(2)}) collective-permute-start(bf16[64,1536]{1,0:T(8,128)(2,1)S(1)} %select_convert_fusion.1), channel_id=1, source_target_pairs={{0,1},{1,0},{2,3},{3,2},{4,5},{5,4},{6,7},{7,6},{8,9},{9,8},{10,11... | collective-permute-start | bytes 589832 | tf_op jit(solution)/shard_map/ppermute | solution.py:88
  73.5 8.9 %collective-permute-start.7 = (f32[64]{0:T(128)S(1)}, f32[64]{0:T(128)S(1)}, u32[]{:S(2)}, u32[]{:S(2)}) collective-permute-start(f32[64]{0:T(128)S(1)} %add.56), channel_id=1, source_target_pairs={{0,2},{1,3},{2,0},{3,1},{4,6},{5,7},{6,4},{7,5},{8,10},{9,11},{10,... | collective-permute-start | bytes 776 | tf_op jit(solution)/shard_map/ppermute | solution.py:88
  76.9 5.6 %collective-permute-start.9 = (bf16[64,768]{1,0:T(8,128)(2,1)S(1)}, bf16[64,768]{1,0:T(8,128)(2,1)S(1)}, u32[]{:S(2)}, u32[]{:S(2)}) collective-permute-start(bf16[64,768]{1,0:T(8,128)(2,1)S(1)} %select_convert_fusion.2), channel_id=1, source_target_pairs={{0,2},{1,3},{2,0},{3,1},{4,6},{5,7},{6,4},{7,5},{8,10},{9,11},{10,... | collective-permute-start | bytes 294920 | tf_op jit(solution)/shard_map/ppermute | solution.py:88
  81.0 7.0 %collective-permute-start.5 = (bf16[64,768]{1,0:T(8,128)(2,1)S(1)}, bf16[64,768]{1,0:T(8,128)(2,1)S(1)}, u32[]{:S(2)}, u32[]{:S(2)}) collective-permute-start(bf16[64,768]{1,0:T(8,128)(2,1)S(1)} %select_convert_fusion.3), channel_id=1, source_target_pairs={{0,2},{1,3},{2,0},{3,1},{4,6},{5,7},{6,4},{7,5},{8,10},{9,11},{10,... | collective-permute-start | bytes 294920 | tf_op jit(solution)/shard_map/ppermute | solution.py:88
  88.1 6.4 %collective-permute-start.10 = (bf16[64,768]{1,0:T(8,128)(2,1)S(1)}, bf16[64,768]{1,0:T(8,128)(2,1)S(1)}, u32[]{:S(2)}, u32[]{:S(2)}) collective-permute-start(bf16[64,768]{1,0:T(8,128)(2,1)S(1)} %multiply_convert_fusion.1), channel_id=1, source_target_pairs={{0,2},{1,3},{2,0},{3,1},{4,6},{5,7},{6,4},{7,5},{8,10},{9,11},{10,... | collective-permute-start | bytes 294920 | tf_op jit(solution)/shard_map/ppermute | solution.py:88
  94.6 5.7 %collective-permute-start.11 = (bf16[64,1536]{1,0:T(8,128)(2,1)S(1)}, bf16[64,1536]{1,0:T(8,128)(2,1)S(1)}, u32[]{:S(2)}, u32[]{:S(2)}) collective-permute-start(bf16[64,1536]{1,0:T(8,128)(2,1)S(1)} %maximum_select_fusion.2), channel_id=1, source_target_pairs={{0,1},{1,0},{2,3},{3,2},{4,5},{5,4},{6,7},{7,6},{8,9},{9,8},{10,11... | collective-permute-start | bytes 589832 | tf_op jit(solution)/shard_map/ppermute | solution.py:88
  105.1 1.3 %collective-permute-start.12 = (bf16[2,16,1280]{2,1,0:T(8,128)(2,1)S(1)}, bf16[2,16,1280]{2,1,0:T(8,128)(2,1)S(1)}, u32[]{:S(2)}, u32[]{:S(2)}) collective-permute-start(bf16[2,16,1280]{2,1,0:T(8,128)(2,1)S(1)} %fusion.9), channel_id=1, source_target_pairs={{0,4},{4,0},{8,12},{12,8},{1,5},{5,1},{9,13},{13,9},{2,6},{6,2},{1... | collective-permute-start | bytes 245768 | tf_op jit(solution)/shard_map/ppermute | solution.py:88
  106.5 4.1 %collective-permute-start.13 = (bf16[1,16,1280]{2,1,0:T(8,128)(2,1)S(1)}, bf16[1,16,1280]{2,1,0:T(8,128)(2,1)S(1)}, u32[]{:S(2)}, u32[]{:S(2)}) collective-permute-start(bf16[1,16,1280]{2,1,0:T(8,128)(2,1)S(1)} %fusion.13), channel_id=1, source_target_pairs={{0,8},{4,12},{8,0},{12,4},{1,9},{5,13},{9,1},{13,5},{2,10},{6,14},... | collective-permute-start | bytes 122888 | tf_op jit(solution)/shard_map/ppermute | solution.py:88

commit v9 on v8

--- a/solution.py
+++ b/solution.py
@@ -82,6 +82,19 @@
         ],
         compiler_params=pltpu.CompilerParams(vmem_limit_bytes=48 * 1024 * 1024),
     )(page_table, lengths, query_columns, cache_columns)
+
+
+def resident_matmul(rows, weights):
+    def kernel(rows_ref, weights_ref, out_ref):
+        out_ref[...] = jnp.dot(rows_ref[...], weights_ref[...], preferred_element_type=jnp.float32)
+
+    return pl.pallas_call(
+        kernel,
+        out_shape=jax.ShapeDtypeStruct((rows.shape[0], weights.shape[1]), jnp.float32),
+        in_specs=[pl.BlockSpec(memory_space=pltpu.VMEM)] * 2,
+        out_specs=pl.BlockSpec(memory_space=pltpu.VMEM),
+        compiler_params=pltpu.CompilerParams(vmem_limit_bytes=40 * 1024 * 1024),
+    )(rows, weights)
 
 
 def swap_with(x, axis, distance, size):
@@ -225,9 +238,7 @@
     group_values = lax.all_gather(values, "sub", axis=1, tiled=True)
     dp_size = axis_sizes["dp"]
     sub_size = axis_sizes["sub"]
-    attention_all = matched_sum(
-        jnp.dot(group_values, out_proj, preferred_element_type=jnp.float32), "dp", dp_size
-    )
+    attention_all = matched_sum(resident_matmul(group_values, out_proj), "dp", dp_size)
     hidden_all = farthest_first_rows_gather(hidden_in, "dp", dp_size)
     all_residual = hidden_all.astype(jnp.float32) + attention_all
     squares = doubling_sum(jnp.sum(all_residual * all_residual, axis=1), "sub", sub_size)

time: 112 us -> 115 us (1.027)
  local copies, waits for them, and re-layouts: 4.69 us -> 8.65 us
  matrix products: 14 us -> 11.4 us
  Pallas kernels: 9.23 us -> 11.1 us
    dot_general x1 -> x0, matrix products: 6.04 us -> none  [shards(): jnp.dot(group_values, out_proj, preferred_element_type=jnp.float32)]
    unnamed x20 -> x18, local copies, waits for them, and re-layouts: 2.52 us -> 6.49 us
    dot_general x1, matrix products: 1.49 us -> 4.86 us  [shards(): up_part = jnp.dot(gained, up_proj, preferred_element_type=jnp.float32)]
    pallas_call x0 -> x1, Pallas kernels: none -> 1.91 us  [resident_matmul(): pl.pallas_call(kernel, out_shape=jax.ShapeDtypeStruct((rows.shape[0], wei...]
  transfers between devices with their start and end apart: 15 -> 15, of which waited for: 12 -> 11; matrix products, arithmetic and copies ran while one was open for 10% -> 7% of each run, Pallas kernels for 0% -> 2%
where the time goes in v9:
time: 115 us; the launch traced here: 114 us
  waiting for transfers between devices  45.7 us (40%)
  starting transfers between devices  18.8 us (16%)
  blocking collectives  16.2 us (14%)
  matrix products  11.4 us (10%)
  Pallas kernels  11.1 us (10%)
  local copies, waits for them, and re-layouts  8.65 us (8%)
  other arithmetic  1.47 us (1%)
    ppermute x14, waiting for transfers between devices, swap_with(): return lax.ppermute(x, axis, [(i, i ^ distance) for i in range(size)])  37.3 us
    all_gather x1, blocking collectives, shards(): group_values = lax.all_gather(values, 'sub', axis=1, tiled=True)  16.2 us
    ppermute x14, starting transfers between devices, swap_with(): return lax.ppermute(x, axis, [(i, i ^ distance) for i in range(size)])  11.5 us
    pallas_call x1, Pallas kernels, attend_all(): pl.pallas_call(kernel, out_shape=jax.ShapeDtypeStruct((req_dev, head_coun...  9.23 us
    all_to_all x1, waiting for transfers between devices, shards(): lax.all_to_all(contexts[None], ('dp', 'sub'), split_axis=2, concat_axis=0...  8.35 us
    all_to_all x1, starting transfers between devices, shards(): lax.all_to_all(contexts[None], ('dp', 'sub'), split_axis=2, concat_axis=0...  7.35 us
    unnamed x18, local copies, waits for them, and re-layouts  6.49 us
    dot_general x1, matrix products, shards(): up_part = jnp.dot(gained, up_proj, preferred_element_type=jnp.float32)  4.86 us
  transfers between devices with their start and end apart: 15, of which 11 were waited for; matrix products, arithmetic and copies ran while one was open for 7% of the time, Pallas kernels for 2%

profile of v9, /device:TPU:0, one launch (start us, length us, event | category | flops | bytes accessed | tf_op | source)
XLA Modules:
  0.0 114.3 jit_solution(805617731871676685)
XLA Ops:
  0.6 0.0 copy-start
  0.6 0.0 copy-start.2
  0.7 1.1 copy-done.2
  1.8 0.0 copy-start.3
  1.8 0.7 copy-done.3
  2.5 0.0 copy-start.4
  2.5 0.7 copy-done.4
  3.1 0.0 copy-start.5
  3.1 0.0 copy-start.6
  3.1 9.2 %shard_map.122 = bf16[4,128,512]{2,1,0:T(8,128)(2,1)S(1)} custom-call(s32[4,16]{1,0:T(4,128)S(1)} %copy-done.3, s32[4]{0:T(128)S(1)} %copy-done.4, bf16[4,576,128]{2,1,0:T(8,128)(2,1)S(1)} %bitcast.64, bf16[64,576,128]{2,1,0:T(8,128)(2,1)} %bitcast.67), custom_call_target="tpu_custom_call" | custom-call | tf_op jit(solution)/shard_map/pallas_call | solution.py:69
  12.4 1.2 %copy.19 = bf16[1,4,128,512]{3,1,0,2:T(4,128)(2,1)} copy(bf16[1,4,128,512]{3,2,1,0:T(8,128)(2,1)S(1)} %bitcast.63) | data formatting | bytes 1048576 | tf_op jit(solution)/shard_map/broadcast_in_dim | solution.py:232
  13.6 7.4 %all-to-all-start = ((bf16[1,4,128,512]{3,1,0,2:T(4,128)(2,1)}), bf16[1,4,128,512]{3,1,0,2:T(4,128)(2,1)S(1)}, u32[]{:S(2)}, u32[]{:S(2)}) async-start(bf16[1,4,128,512]{3,1,0,2:T(4,128)(2,1)} %copy.19), calls=%async_computation | async-start | bytes 1048576 | tf_op jit(solution)/shard_map/all_to_all | solution.py:231
  20.9 0.0 copy-done.5
  21.0 2.0 %collective-permute-start.2 = (bf16[1,16,1280]{2,1,0:T(8,128)(2,1)S(1)}, bf16[1,16,1280]{2,1,0:T(8,128)(2,1)S(1)}, u32[]{:S(2)}, u32[]{:S(2)}) collective-permute-start(bf16[1,16,1280]{2,1,0:T(8,128)(2,1)S(1)} %bitcast.73), channel_id=1, source_target_pairs={{0,8},{4,12},{8,0},{12,4},{1,9},{5,13},{9,1},{13,5},{2,10},{6,14},... | collective-permute-start | bytes 122888 | tf_op jit(solution)/shard_map/ppermute | solution.py:101
  22.9 0.0 copy-done.6
  23.0 5.2 %collective-permute-done.2 = bf16[1,16,1280]{2,1,0:T(8,128)(2,1)S(1)} collective-permute-done((bf16[1,16,1280]{2,1,0:T(8,128)(2,1)S(1)}, bf16[1,16,1280]{2,1,0:T(8,128)(2,1)S(1)}, u32[]{:S(2)}, u32[]{:S(2)}) %collective-permute-start.2) | collective-permute-done | bytes 40992 | tf_op jit(solution)/shard_map/ppermute | solution.py:101
  28.2 0.1 collective-permute-start.3
  28.3 8.3 %all-to-all-done = bf16[1,4,128,512]{3,1,0,2:T(4,128)(2,1)S(1)} async-done(((bf16[1,4,128,512]{3,1,0,2:T(4,128)(2,1)}), bf16[1,4,128,512]{3,1,0,2:T(4,128)(2,1)S(1)}, u32[]{:S(2)}, u32[]{:S(2)}) %all-to-all-start) | async-done | bytes 524320 | tf_op jit(solution)/shard_map/all_to_all | solution.py:231
  36.6 0.2 copy.29
  36.8 0.1 reshape.157
  37.0 0.0 copy-done
  37.0 0.3 fusion
  37.3 16.2 %all_gather.3.rows_ref = bf16[64,4096]{1,0:T(8,128)(2,1)S(1)} all-gather(bf16[64,1024]{1,0:T(8,128)(2,1)S(1)} %bitcast.72), channel_id=1, replica_groups=mesh['grp'=2,'dp'=4,'sub'=4] {'sub'}, dimensions={1}, use_global_device_ids=true | all-gather | bytes 655360 | tf_op jit(solution)/shard_map/all_gather | solution.py:238
  53.6 0.0 copy-start.1
  53.6 4.0 %copy-done.1 = bf16[4096,1280]{1,0:T(8,128)(2,1)S(1)} copy-done((bf16[4096,1280]{1,0:T(8,128)(2,1)S(1)}, bf16[4096,1280]{1,0:T(8,128)(2,1)}, u32[]{:S(2)}) %copy-start.1) | copy-done | bytes 10485784
  57.5 1.9 %shard_map.123 = f32[64,1280]{1,0:T(8,128)S(1)} custom-call(bf16[64,4096]{1,0:T(8,128)(2,1)S(1)} %all_gather.3.rows_ref, bf16[4096,1280]{1,0:T(8,128)(2,1)S(1)} %copy-done.1), custom_call_target="tpu_custom_call" | custom-call | tf_op jit(solution)/shard_map/pallas_call | solution.py:91
  59.5 0.1 collective-permute-start
  59.6 1.4 %collective-permute-done = bf16[64,1280]{1,0:T(8,128)(2,1)S(1)} collective-permute-done((bf16[64,1280]{1,0:T(8,128)(2,1)S(1)}, bf16[64,1280]{1,0:T(8,128)(2,1)S(1)}, u32[]{:S(2)}, u32[]{:S(2)}) %collective-permute-start) | collective-permute-done | bytes 163872 | tf_op jit(solution)/shard_map/ppermute | solution.py:101
  61.0 0.7 collective-permute-start.1
  61.6 0.0 collective-permute-done.3
  61.7 5.6 %collective-permute-done.1 = bf16[64,1280]{1,0:T(8,128)(2,1)S(1)} collective-permute-done((bf16[64,1280]{1,0:T(8,128)(2,1)S(1)}, bf16[64,1280]{1,0:T(8,128)(2,1)S(1)}, u32[]{:S(2)}, u32[]{:S(2)}) %collective-permute-start.1) | collective-permute-done | bytes 163872 | tf_op jit(solution)/shard_map/ppermute | solution.py:101
  67.3 0.0 slice-start
  67.3 0.2 multiply_reduce_fusion
  67.5 0.1 collective-permute-start.6
  67.6 0.0 slice-start.1
  67.6 4.9 %fusion.11 = f32[64,3072]{1,0:T(8,128)S(1)} fusion(bf16[1280,3072]{1,0:T(8,128)(2,1)} %param.20, f32[64,1280]{1,0:T(8,128)S(1)} %get-tuple-element.3, f32[1280]{0:T(1024)S(1)} %convert_element_type.106), kind=kOutput, calls=%fused_computation.39 | convolution fusion | flops 503480320 | bytes 8983552 | tf_op jit(solution)/shard_map/dot_general | solution.py:247
  72.5 2.1 %collective-permute-start.8 = (bf16[64,1536]{1,0:T(8,128)(2,1)S(1)}, bf16[64,1536]{1,0:T(8,128)(2,1)S(1)}, u32[]{:S(2)}, u32[]{:S(2)}) collective-permute-start(bf16[64,1536]{1,0:T(8,128)(2,1)S(1)} %select_convert_fusion), channel_id=1, source_target_pairs={{0,1},{1,0},{2,3},{3,2},{4,5},{5,4},{6,7},{7,6},{8,9},{9,8},{10,11... | collective-permute-start | bytes 589832 | tf_op jit(solution)/shard_map/ppermute | solution.py:101
  74.5 0.0 slice-done
  74.6 0.0 slice-done.1
  74.6 1.5 %fusion.12 = f32[64,3072]{1,0:T(8,128)S(1)} fusion(bf16[1280,3072]{1,0:T(8,128)(2,1)S(1)} %bitcast.66, f32[64,1280]{1,0:T(8,128)S(1)} %get-tuple-element.3, f32[1280]{0:T(1024)S(1)} %convert_element_type.106), kind=kOutput, calls=%fused_computation.40 | convolution fusion | flops 503480320 | bytes 8983552 | tf_op jit(solution)/shard_map/dot_general | solution.py:246
  76.1 0.1 collective-permute-start.4
  76.2 0.0 collective-permute-done.6
  76.2 1.6 %collective-permute-start.7 = (f32[64]{0:T(128)S(1)}, f32[64]{0:T(128)S(1)}, u32[]{:S(2)}, u32[]{:S(2)}) collective-permute-start(f32[64]{0:T(128)S(1)} %add.56), channel_id=1, source_target_pairs={{0,2},{1,3},{2,0},{3,1},{4,6},{5,7},{6,4},{7,5},{8,10},{9,11},{10,... | collective-permute-start | bytes 776 | tf_op jit(solution)/shard_map/ppermute | solution.py:101
  77.8 2.1 %collective-permute-done.8 = bf16[64,1536]{1,0:T(8,128)(2,1)S(1)} collective-permute-done((bf16[64,1536]{1,0:T(8,128)(2,1)S(1)}, bf16[64,1536]{1,0:T(8,128)(2,1)S(1)}, u32[]{:S(2)}, u32[]{:S(2)}) %collective-permute-start.8) | collective-permute-done | bytes 196640 | tf_op jit(solution)/shard_map/ppermute | solution.py:101
  79.9 0.1 convert_add_fusion
  80.0 2.1 %collective-permute-start.9 = (bf16[64,768]{1,0:T(8,128)(2,1)S(1)}, bf16[64,768]{1,0:T(8,128)(2,1)S(1)}, u32[]{:S(2)}, u32[]{:S(2)}) collective-permute-start(bf16[64,768]{1,0:T(8,128)(2,1)S(1)} %select_convert_fusion.2), channel_id=1, source_target_pairs={{0,2},{1,3},{2,0},{3,1},{4,6},{5,7},{6,4},{7,5},{8,10},{9,11},{10,... | collective-permute-start | bytes 294920 | tf_op jit(solution)/shard_map/ppermute | solution.py:101
  82.1 1.8 %collective-permute-done.4 = bf16[64,1536]{1,0:T(8,128)(2,1)S(1)} collective-permute-done((bf16[64,1536]{1,0:T(8,128)(2,1)S(1)}, bf16[64,1536]{1,0:T(8,128)(2,1)S(1)}, u32[]{:S(2)}, u32[]{:S(2)}) %collective-permute-start.4) | collective-permute-done | bytes 196640 | tf_op jit(solution)/shard_map/ppermute | solution.py:101
  83.9 0.1 convert_add_fusion.1
  84.0 1.6 %collective-permute-start.5 = (bf16[64,768]{1,0:T(8,128)(2,1)S(1)}, bf16[64,768]{1,0:T(8,128)(2,1)S(1)}, u32[]{:S(2)}, u32[]{:S(2)}) collective-permute-start(bf16[64,768]{1,0:T(8,128)(2,1)S(1)} %select_convert_fusion.3), channel_id=1, source_target_pairs={{0,2},{1,3},{2,0},{3,1},{4,6},{5,7},{6,4},{7,5},{8,10},{9,11},{10,... | collective-permute-start | bytes 294920 | tf_op jit(solution)/shard_map/ppermute | solution.py:101
  85.7 0.0 collective-permute-done.7
  85.7 0.0 collective-permute-done.9
  85.7 5.4 %collective-permute-done.5 = bf16[64,768]{1,0:T(8,128)(2,1)S(1)} collective-permute-done((bf16[64,768]{1,0:T(8,128)(2,1)S(1)}, bf16[64,768]{1,0:T(8,128)(2,1)S(1)}, u32[]{:S(2)}, u32[]{:S(2)}) %collective-permute-start.5) | collective-permute-done | bytes 98336 | tf_op jit(solution)/shard_map/ppermute | solution.py:101
  91.1 0.1 multiply_convert_fusion.1
  91.2 0.3 collective-permute-start.10
  91.5 6.2 %collective-permute-done.10 = bf16[64,768]{1,0:T(8,128)(2,1)S(1)} collective-permute-done((bf16[64,768]{1,0:T(8,128)(2,1)S(1)}, bf16[64,768]{1,0:T(8,128)(2,1)S(1)}, u32[]{:S(2)}, u32[]{:S(2)}) %collective-permute-start.10) | collective-permute-done | bytes 98336 | tf_op jit(solution)/shard_map/ppermute | solution.py:101
  97.7 0.1 collective-permute-start.11
  97.8 5.7 %collective-permute-done.11 = bf16[64,1536]{1,0:T(8,128)(2,1)S(1)} collective-permute-done((bf16[64,1536]{1,0:T(8,128)(2,1)S(1)}, bf16[64,1536]{1,0:T(8,128)(2,1)S(1)}, u32[]{:S(2)}, u32[]{:S(2)}) %collective-permute-start.11) | collective-permute-done | bytes 196640 | tf_op jit(solution)/shard_map/ppermute | solution.py:101
  103.4 4.7 %fusion.1 = f32[64,1280]{1,0:T(8,128)S(1)} fusion(bf16[3072,1280]{1,0:T(8,128)(2,1)} %param.21, bf16[64,1536]{1,0:T(8,128)(2,1)S(1)} %maximum_select_fusion.2, bf16[64,1536]{1,0:T(8,128)(2,1)S(1)} %collective-permute-done.11, pred[]{:T(512)S(6)} %ne.18), kind=kOutput, calls=%fused_computation.4 | convolution fusion | flops 505085952 | bytes 8585217 | tf_op jit(solution)/shard_map/dot_general | solution.py:253
  108.2 0.1 collective-permute-start.12
  108.3 1.2 %collective-permute-done.12 = bf16[2,16,1280]{2,1,0:T(8,128)(2,1)S(1)} collective-permute-done((bf16[2,16,1280]{2,1,0:T(8,128)(2,1)S(1)}, bf16[2,16,1280]{2,1,0:T(8,128)(2,1)S(1)}, u32[]{:S(2)}, u32[]{:S(2)}) %collective-permute-start.12) | collective-permute-done | bytes 81952 | tf_op jit(solution)/shard_map/ppermute | solution.py:101
  109.6 0.7 collective-permute-start.13
  110.3 0.6 dynamic-slice_convert_fusion
  110.9 2.7 %collective-permute-done.13 = bf16[1,16,1280]{2,1,0:T(8,128)(2,1)S(1)} collective-permute-done((bf16[1,16,1280]{2,1,0:T(8,128)(2,1)S(1)}, bf16[1,16,1280]{2,1,0:T(8,128)(2,1)S(1)}, u32[]{:S(2)}, u32[]{:S(2)}) %collective-permute-start.13) | collective-permute-done | bytes 40992 | tf_op jit(solution)/shard_map/ppermute | solution.py:101
  113.6 0.6 fusion.10
  (19 shorter events, 0.4 us)
Async XLA Ops:
  0.6 36.3 %copy-start = (bf16[8,512,128]{2,1,0:T(8,128)(2,1)S(1)}, bf16[8,512,128]{2,1,0:T(8,128)(2,1)}, u32[]{:S(2)}) copy-start(bf16[8,512,128]{2,1,0:T(8,128)(2,1)} %param.16) | copy-start | bytes 3145732
  0.6 1.2 %copy-start.2 = (bf16[4,128,576]{1,2,0:T(8,128)(2,1)S(1)}, bf16[4,128,576]{1,2,0:T(8,128)(2,1)}, u32[]{:S(2)}) copy-start(bf16[4,128,576]{1,2,0:T(8,128)(2,1)} %param.12) | copy-start | bytes 1769476
  1.8 0.7 copy-start.3
  2.5 0.7 copy-start.4
  3.1 17.8 %copy-start.5 = (bf16[16,1280]{1,0:T(8,128)(2,1)S(1)}, bf16[16,1280]{1,0:T(8,128)(2,1)}, u32[]{:S(2)}) copy-start(bf16[16,1280]{1,0:T(8,128)(2,1)} %param.11) | copy-start | bytes 122884
  3.1 19.8 %copy-start.6 = (bf16[1280]{0:T(1024)(128)(2,1)S(1)}, bf16[1280]{0:T(1024)(128)(2,1)}, u32[]{:S(2)}) copy-start(bf16[1280]{0:T(1024)(128)(2,1)} %param.18) | copy-start | bytes 7684
  13.6 23.0 %all-to-all-start = ((bf16[1,4,128,512]{3,1,0,2:T(4,128)(2,1)}), bf16[1,4,128,512]{3,1,0,2:T(4,128)(2,1)S(1)}, u32[]{:S(2)}, u32[]{:S(2)}) async-start(bf16[1,4,128,512]{3,1,0,2:T(4,128)(2,1)} %copy.19), calls=%async_computation | async-start | bytes 1048576 | tf_op jit(solution)/shard_map/all_to_all | solution.py:231
  21.0 7.2 %collective-permute-start.2 = (bf16[1,16,1280]{2,1,0:T(8,128)(2,1)S(1)}, bf16[1,16,1280]{2,1,0:T(8,128)(2,1)S(1)}, u32[]{:S(2)}, u32[]{:S(2)}) collective-permute-start(bf16[1,16,1280]{2,1,0:T(8,128)(2,1)S(1)} %bitcast.73), channel_id=1, source_target_pairs={{0,8},{4,12},{8,0},{12,4},{1,9},{5,13},{9,1},{13,5},{2,10},{6,14},... | collective-permute-start | bytes 122888 | tf_op jit(solution)/shard_map/ppermute | solution.py:101
  28.2 33.4 %collective-permute-start.3 = (bf16[2,16,1280]{2,1,0:T(8,128)(2,1)S(1)}, bf16[2,16,1280]{2,1,0:T(8,128)(2,1)S(1)}, u32[]{:S(2)}, u32[]{:S(2)}) collective-permute-start(bf16[2,16,1280]{2,1,0:T(8,128)(2,1)S(1)} %maximum_select_fusion.4), channel_id=1, source_target_pairs={{0,4},{4,0},{8,12},{12,8},{1,5},{5,1},{9,13},{13,9},{2,6},{6,2},{1... | collective-permute-start | bytes 245768 | tf_op jit(solution)/shard_map/ppermute | solution.py:101
  53.6 4.0 %copy-start.1 = (bf16[4096,1280]{1,0:T(8,128)(2,1)S(1)}, bf16[4096,1280]{1,0:T(8,128)(2,1)}, u32[]{:S(2)}) copy-start(bf16[4096,1280]{1,0:T(8,128)(2,1)} %weights_ref.1) | copy-start | bytes 31457284
  59.5 1.5 %collective-permute-start = (bf16[64,1280]{1,0:T(8,128)(2,1)S(1)}, bf16[64,1280]{1,0:T(8,128)(2,1)S(1)}, u32[]{:S(2)}, u32[]{:S(2)}) collective-permute-start(bf16[64,1280]{1,0:T(8,128)(2,1)S(1)} %convert_element_type.97), channel_id=1, source_target_pairs={{0,4},{4,0},{8,12},{12,8},{1,5},{5,1},{9,13},{13,9},{2,6},{6,2},{1... | collective-permute-start | bytes 491528 | tf_op jit(solution)/shard_map/ppermute | solution.py:101
  61.0 6.3 %collective-permute-start.1 = (bf16[64,1280]{1,0:T(8,128)(2,1)S(1)}, bf16[64,1280]{1,0:T(8,128)(2,1)S(1)}, u32[]{:S(2)}, u32[]{:S(2)}) collective-permute-start(bf16[64,1280]{1,0:T(8,128)(2,1)S(1)} %add_convert_fusion), channel_id=1, source_target_pairs={{0,8},{4,12},{8,0},{12,4},{1,9},{5,13},{9,1},{13,5},{2,10},{6,14},... | collective-permute-start | bytes 491528 | tf_op jit(solution)/shard_map/ppermute | solution.py:101
  67.3 7.3 %slice-start = ((s8[7864320]{0:T(1024)(128)(4,1)}), s8[4194304]{0:T(1024)(128)(4,1)S(1)}, s32[]{:S(2)}) async-start(s8[7864320]{0:T(1024)(128)(4,1)} %bitcast.65), calls=%async_computation.1 | async-start | bytes 8388608
  67.5 8.7 %collective-permute-start.6 = (f32[64]{0:T(128)S(1)}, f32[64]{0:T(128)S(1)}, u32[]{:S(2)}, u32[]{:S(2)}) collective-permute-start(f32[64]{0:T(128)S(1)} %get-tuple-element.2), channel_id=1, source_target_pairs={{0,1},{1,0},{2,3},{3,2},{4,5},{5,4},{6,7},{7,6},{8,9},{9,8},{10,11... | collective-permute-start | bytes 776 | tf_op jit(solution)/shard_map/ppermute | solution.py:101
  67.6 7.0 %slice-start.1 = ((s8[7864320]{0:T(1024)(128)(4,1)}), s8[3670016]{0:T(1024)(128)(4,1)S(1)}, s32[]{:S(2)}) async-start(s8[7864320]{0:T(1024)(128)(4,1)} %bitcast.65), calls=%async_computation.2 | async-start | bytes 7340032
  72.5 7.4 %collective-permute-start.8 = (bf16[64,1536]{1,0:T(8,128)(2,1)S(1)}, bf16[64,1536]{1,0:T(8,128)(2,1)S(1)}, u32[]{:S(2)}, u32[]{:S(2)}) collective-permute-start(bf16[64,1536]{1,0:T(8,128)(2,1)S(1)} %select_convert_fusion), channel_id=1, source_target_pairs={{0,1},{1,0},{2,3},{3,2},{4,5},{5,4},{6,7},{7,6},{8,9},{9,8},{10,11... | collective-permute-start | bytes 589832 | tf_op jit(solution)/shard_map/ppermute | solution.py:101
  76.1 7.9 %collective-permute-start.4 = (bf16[64,1536]{1,0:T(8,128)(2,1)S(1)}, bf16[64,1536]{1,0:T(8,128)(2,1)S(1)}, u32[]{:S(2)}, u32[]{:S(2)}) collective-permute-start(bf16[64,1536]{1,0:T(8,128)(2,1)S(1)} %select_convert_fusion.1), channel_id=1, source_target_pairs={{0,1},{1,0},{2,3},{3,2},{4,5},{5,4},{6,7},{7,6},{8,9},{9,8},{10,11... | collective-permute-start | bytes 589832 | tf_op jit(solution)/shard_map/ppermute | solution.py:101
  76.2 9.5 %collective-permute-start.7 = (f32[64]{0:T(128)S(1)}, f32[64]{0:T(128)S(1)}, u32[]{:S(2)}, u32[]{:S(2)}) collective-permute-start(f32[64]{0:T(128)S(1)} %add.56), channel_id=1, source_target_pairs={{0,2},{1,3},{2,0},{3,1},{4,6},{5,7},{6,4},{7,5},{8,10},{9,11},{10,... | collective-permute-start | bytes 776 | tf_op jit(solution)/shard_map/ppermute | solution.py:101
  80.0 5.7 %collective-permute-start.9 = (bf16[64,768]{1,0:T(8,128)(2,1)S(1)}, bf16[64,768]{1,0:T(8,128)(2,1)S(1)}, u32[]{:S(2)}, u32[]{:S(2)}) collective-permute-start(bf16[64,768]{1,0:T(8,128)(2,1)S(1)} %select_convert_fusion.2), channel_id=1, source_target_pairs={{0,2},{1,3},{2,0},{3,1},{4,6},{5,7},{6,4},{7,5},{8,10},{9,11},{10,... | collective-permute-start | bytes 294920 | tf_op jit(solution)/shard_map/ppermute | solution.py:101
  84.0 7.0 %collective-permute-start.5 = (bf16[64,768]{1,0:T(8,128)(2,1)S(1)}, bf16[64,768]{1,0:T(8,128)(2,1)S(1)}, u32[]{:S(2)}, u32[]{:S(2)}) collective-permute-start(bf16[64,768]{1,0:T(8,128)(2,1)S(1)} %select_convert_fusion.3), channel_id=1, source_target_pairs={{0,2},{1,3},{2,0},{3,1},{4,6},{5,7},{6,4},{7,5},{8,10},{9,11},{10,... | collective-permute-start | bytes 294920 | tf_op jit(solution)/shard_map/ppermute | solution.py:101
  91.2 6.4 %collective-permute-start.10 = (bf16[64,768]{1,0:T(8,128)(2,1)S(1)}, bf16[64,768]{1,0:T(8,128)(2,1)S(1)}, u32[]{:S(2)}, u32[]{:S(2)}) collective-permute-start(bf16[64,768]{1,0:T(8,128)(2,1)S(1)} %multiply_convert_fusion.1), channel_id=1, source_target_pairs={{0,2},{1,3},{2,0},{3,1},{4,6},{5,7},{6,4},{7,5},{8,10},{9,11},{10,... | collective-permute-start | bytes 294920 | tf_op jit(solution)/shard_map/ppermute | solution.py:101
  97.7 5.7 %collective-permute-start.11 = (bf16[64,1536]{1,0:T(8,128)(2,1)S(1)}, bf16[64,1536]{1,0:T(8,128)(2,1)S(1)}, u32[]{:S(2)}, u32[]{:S(2)}) collective-permute-start(bf16[64,1536]{1,0:T(8,128)(2,1)S(1)} %maximum_select_fusion.2), channel_id=1, source_target_pairs={{0,1},{1,0},{2,3},{3,2},{4,5},{5,4},{6,7},{7,6},{8,9},{9,8},{10,11... | collective-permute-start | bytes 589832 | tf_op jit(solution)/shard_map/ppermute | solution.py:101
  108.2 1.3 %collective-permute-start.12 = (bf16[2,16,1280]{2,1,0:T(8,128)(2,1)S(1)}, bf16[2,16,1280]{2,1,0:T(8,128)(2,1)S(1)}, u32[]{:S(2)}, u32[]{:S(2)}) collective-permute-start(bf16[2,16,1280]{2,1,0:T(8,128)(2,1)S(1)} %fusion.9), channel_id=1, source_target_pairs={{0,4},{4,0},{8,12},{12,8},{1,5},{5,1},{9,13},{13,9},{2,6},{6,2},{1... | collective-permute-start | bytes 245768 | tf_op jit(solution)/shard_map/ppermute | solution.py:101
  109.6 4.1 %collective-permute-start.13 = (bf16[1,16,1280]{2,1,0:T(8,128)(2,1)S(1)}, bf16[1,16,1280]{2,1,0:T(8,128)(2,1)S(1)}, u32[]{:S(2)}, u32[]{:S(2)}) collective-permute-start(bf16[1,16,1280]{2,1,0:T(8,128)(2,1)S(1)} %fusion.13), channel_id=1, source_target_pairs={{0,8},{4,12},{8,0},{12,4},{1,9},{5,13},{9,1},{13,5},{2,10},{6,14},... | collective-permute-start | bytes 122888 | tf_op jit(solution)/shard_map/ppermute | solution.py:101

commit v10 on v8

--- a/solution.py
+++ b/solution.py
@@ -73,14 +73,14 @@
             pl.BlockSpec(memory_space=pltpu.SMEM),
             pl.BlockSpec(memory_space=pltpu.SMEM),
             pl.BlockSpec(memory_space=pltpu.VMEM),
-            pl.BlockSpec(memory_space=pl.ANY),
+            pl.BlockSpec(memory_space=pltpu.HBM),
         ],
         out_specs=pl.BlockSpec(memory_space=pltpu.VMEM),
         scratch_shapes=[
             pltpu.VMEM((req_dev, width, pages_req * page_size), jnp.bfloat16),
             pltpu.SemaphoreType.DMA((req_dev * pages_req,)),
         ],
-        compiler_params=pltpu.CompilerParams(vmem_limit_bytes=48 * 1024 * 1024),
+        compiler_params=pltpu.CompilerParams(vmem_limit_bytes=20 * 1024 * 1024),
     )(page_table, lengths, query_columns, cache_columns)
 
 

time: 112 us -> 116 us (1.036)
  local copies, waits for them, and re-layouts: 4.69 us -> 8.37 us
  Pallas kernels: 9.23 us -> 10.4 us
    unnamed x20 -> x22, local copies, waits for them, and re-layouts: 2.52 us -> 6.2 us
    pallas_call x1, Pallas kernels: 9.23 us -> 10.4 us  [attend_all(): pl.pallas_call(kernel, out_shape=jax.ShapeDtypeStruct((req_dev, head_coun...]
  transfers between devices with their start and end apart: 15 -> 15, of which waited for: 12 -> 12; matrix products, arithmetic and copies ran while one was open for 10% -> 9% of each run, Pallas kernels for 0% -> 0%
where the time goes in v10:
time: 116 us
  waiting for transfers between devices  46.8 us (40%)
  starting transfers between devices  17.8 us (15%)
  blocking collectives  16.4 us (14%)
  matrix products  14 us (12%)
  Pallas kernels  10.4 us (9%)
  local copies, waits for them, and re-layouts  8.37 us (7%)
  other arithmetic  1.46 us (1%)
    ppermute x14, waiting for transfers between devices, swap_with(): return lax.ppermute(x, axis, [(i, i ^ distance) for i in range(size)])  38.4 us
    all_gather x1, blocking collectives, shards(): group_values = lax.all_gather(values, 'sub', axis=1, tiled=True)  16.4 us
    pallas_call x1, Pallas kernels, attend_all(): pl.pallas_call(kernel, out_shape=jax.ShapeDtypeStruct((req_dev, head_coun...  10.4 us
    ppermute x14, starting transfers between devices, swap_with(): return lax.ppermute(x, axis, [(i, i ^ distance) for i in range(size)])  10.4 us
    all_to_all x1, waiting for transfers between devices, shards(): lax.all_to_all(contexts[None], ('dp', 'sub'), split_axis=2, concat_axis=0...  8.35 us
    all_to_all x1, starting transfers between devices, shards(): lax.all_to_all(contexts[None], ('dp', 'sub'), split_axis=2, concat_axis=0...  7.37 us
    unnamed x22, local copies, waits for them, and re-layouts  6.2 us
    dot_general x1, matrix products, shards(): jnp.dot(group_values, out_proj, preferred_element_type=jnp.float32)  6.04 us
  transfers between devices with their start and end apart: 15, of which 12 were waited for; matrix products, arithmetic and copies ran while one was open for 9% of the time, Pallas kernels for 0%

profile of v10, /device:TPU:0, one launch (start us, length us, event | category | flops | bytes accessed | tf_op | source)
XLA Modules:
  0.0 116.1 jit_solution(2879745191727988994)
XLA Ops:
  0.6 0.0 copy-start
  0.6 0.0 copy-start.1
  0.7 3.8 %copy-done.1 = bf16[64,128,576]{1,2,0:T(8,128)(2,1)S(1)} copy-done((bf16[64,128,576]{1,2,0:T(8,128)(2,1)S(1)}, bf16[64,128,576]{1,2,0:T(8,128)(2,1)}, u32[]{:S(2)}) %copy-start.1) | copy-done | bytes 9437208
  4.4 0.0 copy-start.2
  4.4 1.1 copy-done.2
  5.5 0.0 copy-start.3
  5.5 0.7 copy-done.3
  6.2 0.0 copy-start.4
  6.2 0.7 copy-done.4
  6.8 10.4 %shard_map.122 = bf16[4,128,512]{2,1,0:T(8,128)(2,1)S(1)} custom-call(s32[4,16]{1,0:T(4,128)S(1)} %copy-done.3, s32[4]{0:T(128)S(1)} %copy-done.4, bf16[4,576,128]{2,1,0:T(8,128)(2,1)S(1)} %bitcast.67, bf16[64,576,128]{2,1,0:T(8,128)(2,1)S(1)} %bitcast.65), custom_call_target="tpu_custom_call" | custom-call | tf_op jit(solution)/shard_map/pallas_call | solution.py:69
  17.3 1.2 %copy.18 = bf16[1,4,128,512]{3,1,0,2:T(4,128)(2,1)} copy(bf16[1,4,128,512]{3,2,1,0:T(8,128)(2,1)S(1)} %bitcast.66) | data formatting | bytes 1048576 | tf_op jit(solution)/shard_map/broadcast_in_dim | solution.py:219
  18.5 7.4 %all-to-all-start = ((bf16[1,4,128,512]{3,1,0,2:T(4,128)(2,1)}), bf16[1,4,128,512]{3,1,0,2:T(4,128)(2,1)S(1)}, u32[]{:S(2)}, u32[]{:S(2)}) async-start(bf16[1,4,128,512]{3,1,0,2:T(4,128)(2,1)} %copy.18), calls=%async_computation | async-start | bytes 1048576 | tf_op jit(solution)/shard_map/all_to_all | solution.py:218
  25.9 0.0 copy-done.5
  25.9 2.0 %collective-permute-start.2 = (bf16[1,16,1280]{2,1,0:T(8,128)(2,1)S(1)}, bf16[1,16,1280]{2,1,0:T(8,128)(2,1)S(1)}, u32[]{:S(2)}, u32[]{:S(2)}) collective-permute-start(bf16[1,16,1280]{2,1,0:T(8,128)(2,1)S(1)} %bitcast.77), channel_id=1, source_target_pairs={{0,8},{4,12},{8,0},{12,4},{1,9},{5,13},{9,1},{13,5},{2,10},{6,14},... | collective-permute-start | bytes 122888 | tf_op jit(solution)/shard_map/ppermute | solution.py:88
  27.9 0.0 copy-done.6
  27.9 5.2 %collective-permute-done.2 = bf16[1,16,1280]{2,1,0:T(8,128)(2,1)S(1)} collective-permute-done((bf16[1,16,1280]{2,1,0:T(8,128)(2,1)S(1)}, bf16[1,16,1280]{2,1,0:T(8,128)(2,1)S(1)}, u32[]{:S(2)}, u32[]{:S(2)}) %collective-permute-start.2) | collective-permute-done | bytes 40992 | tf_op jit(solution)/shard_map/ppermute | solution.py:88
  33.1 0.1 collective-permute-start.3
  33.2 8.3 %all-to-all-done = bf16[1,4,128,512]{3,1,0,2:T(4,128)(2,1)S(1)} async-done(((bf16[1,4,128,512]{3,1,0,2:T(4,128)(2,1)}), bf16[1,4,128,512]{3,1,0,2:T(4,128)(2,1)S(1)}, u32[]{:S(2)}, u32[]{:S(2)}) %all-to-all-start) | async-done | bytes 524320 | tf_op jit(solution)/shard_map/all_to_all | solution.py:218
  41.5 0.2 copy.28
  41.7 0.1 reshape.157
  41.9 0.0 copy-done
  41.9 0.3 fusion
  42.2 0.0 slice-start
  42.2 16.4 %all_gather.3 = bf16[64,4096]{1,0:T(8,128)(2,1)S(1)} all-gather(bf16[64,1024]{1,0:T(8,128)(2,1)S(1)} %bitcast.76), channel_id=1, replica_groups=mesh['grp'=2,'dp'=4,'sub'=4] {'sub'}, dimensions={1}, use_global_device_ids=true | all-gather | bytes 655360 | tf_op jit(solution)/shard_map/all_gather | solution.py:225
  58.6 6.0 %convolution_convert_fusion = bf16[64,1280]{1,0:T(8,128)(2,1)S(1)} fusion(bf16[64,4096]{1,0:T(8,128)(2,1)S(1)} %all_gather.3, bf16[4096,1280]{1,0:T(8,128)(2,1)} %param.17), kind=kOutput, calls=%fused_computation | convolution fusion | flops 671170560 | bytes 11173888 | tf_op jit(solution)/shard_map/dot_general | solution.py:229
  64.7 0.1 collective-permute-start
  64.8 1.4 %collective-permute-done = bf16[64,1280]{1,0:T(8,128)(2,1)S(1)} collective-permute-done((bf16[64,1280]{1,0:T(8,128)(2,1)S(1)}, bf16[64,1280]{1,0:T(8,128)(2,1)S(1)}, u32[]{:S(2)}, u32[]{:S(2)}) %collective-permute-start) | collective-permute-done | bytes 163872 | tf_op jit(solution)/shard_map/ppermute | solution.py:88
  66.2 0.7 collective-permute-start.1
  66.8 0.0 collective-permute-done.3
  66.9 5.6 %collective-permute-done.1 = bf16[64,1280]{1,0:T(8,128)(2,1)S(1)} collective-permute-done((bf16[64,1280]{1,0:T(8,128)(2,1)S(1)}, bf16[64,1280]{1,0:T(8,128)(2,1)S(1)}, u32[]{:S(2)}, u32[]{:S(2)}) %collective-permute-start.1) | collective-permute-done | bytes 163872 | tf_op jit(solution)/shard_map/ppermute | solution.py:88
  72.5 0.2 multiply_reduce_fusion
  72.7 0.1 collective-permute-start.6
  72.7 0.0 slice-done
  72.8 0.0 slice-done.1
  72.8 0.0 slice-start.3
  72.8 1.5 %fusion.11 = f32[64,3072]{1,0:T(8,128)S(1)} fusion(bf16[1280,3072]{1,0:T(8,128)(2,1)S(1)} %bitcast.69, f32[64,1280]{1,0:T(8,128)S(1)} %get-tuple-element.3, f32[1280]{0:T(1024)S(1)} %convert_element_type.106), kind=kOutput, calls=%fused_computation.40 | convolution fusion | flops 503480320 | bytes 8983552 | tf_op jit(solution)/shard_map/dot_general | solution.py:236
  74.3 2.0 %collective-permute-start.8 = (bf16[64,1536]{1,0:T(8,128)(2,1)S(1)}, bf16[64,1536]{1,0:T(8,128)(2,1)S(1)}, u32[]{:S(2)}, u32[]{:S(2)}) collective-permute-start(bf16[64,1536]{1,0:T(8,128)(2,1)S(1)} %select_convert_fusion), channel_id=1, source_target_pairs={{0,1},{1,0},{2,3},{3,2},{4,5},{5,4},{6,7},{7,6},{8,9},{9,8},{10,11... | collective-permute-start | bytes 589832 | tf_op jit(solution)/shard_map/ppermute | solution.py:88
  76.4 0.0 slice-done.2
  76.4 0.0 slice-done.3
  76.4 1.5 %fusion.12 = f32[64,3072]{1,0:T(8,128)S(1)} fusion(bf16[1280,3072]{1,0:T(8,128)(2,1)S(1)} %bitcast.71, f32[64,1280]{1,0:T(8,128)S(1)} %get-tuple-element.3, f32[1280]{0:T(1024)S(1)} %convert_element_type.106), kind=kOutput, calls=%fused_computation.41 | convolution fusion | flops 503480320 | bytes 8983552 | tf_op jit(solution)/shard_map/dot_general | solution.py:235
  77.9 0.5 collective-permute-start.4
  78.4 0.0 collective-permute-done.6
  78.4 0.9 collective-permute-start.7
  79.3 2.4 %collective-permute-done.8 = bf16[64,1536]{1,0:T(8,128)(2,1)S(1)} collective-permute-done((bf16[64,1536]{1,0:T(8,128)(2,1)S(1)}, bf16[64,1536]{1,0:T(8,128)(2,1)S(1)}, u32[]{:S(2)}, u32[]{:S(2)}) %collective-permute-start.8) | collective-permute-done | bytes 196640 | tf_op jit(solution)/shard_map/ppermute | solution.py:88
  81.7 0.1 convert_add_fusion
  81.8 1.7 %collective-permute-start.9 = (bf16[64,768]{1,0:T(8,128)(2,1)S(1)}, bf16[64,768]{1,0:T(8,128)(2,1)S(1)}, u32[]{:S(2)}, u32[]{:S(2)}) collective-permute-start(bf16[64,768]{1,0:T(8,128)(2,1)S(1)} %select_convert_fusion.2), channel_id=1, source_target_pairs={{0,2},{1,3},{2,0},{3,1},{4,6},{5,7},{6,4},{7,5},{8,10},{9,11},{10,... | collective-permute-start | bytes 294920 | tf_op jit(solution)/shard_map/ppermute | solution.py:88
  83.6 2.2 %collective-permute-done.4 = bf16[64,1536]{1,0:T(8,128)(2,1)S(1)} collective-permute-done((bf16[64,1536]{1,0:T(8,128)(2,1)S(1)}, bf16[64,1536]{1,0:T(8,128)(2,1)S(1)}, u32[]{:S(2)}, u32[]{:S(2)}) %collective-permute-start.4) | collective-permute-done | bytes 196640 | tf_op jit(solution)/shard_map/ppermute | solution.py:88
  85.8 0.1 convert_add_fusion.1
  85.9 1.4 %collective-permute-start.5 = (bf16[64,768]{1,0:T(8,128)(2,1)S(1)}, bf16[64,768]{1,0:T(8,128)(2,1)S(1)}, u32[]{:S(2)}, u32[]{:S(2)}) collective-permute-start(bf16[64,768]{1,0:T(8,128)(2,1)S(1)} %select_convert_fusion.3), channel_id=1, source_target_pairs={{0,2},{1,3},{2,0},{3,1},{4,6},{5,7},{6,4},{7,5},{8,10},{9,11},{10,... | collective-permute-start | bytes 294920 | tf_op jit(solution)/shard_map/ppermute | solution.py:88
  87.3 0.0 collective-permute-done.7
  87.3 0.1 collective-permute-done.9
  87.4 5.5 %collective-permute-done.5 = bf16[64,768]{1,0:T(8,128)(2,1)S(1)} collective-permute-done((bf16[64,768]{1,0:T(8,128)(2,1)S(1)}, bf16[64,768]{1,0:T(8,128)(2,1)S(1)}, u32[]{:S(2)}, u32[]{:S(2)}) %collective-permute-start.5) | collective-permute-done | bytes 98336 | tf_op jit(solution)/shard_map/ppermute | solution.py:88
  92.9 0.1 multiply_convert_fusion.1
  93.0 0.1 collective-permute-start.10
  93.1 6.4 %collective-permute-done.10 = bf16[64,768]{1,0:T(8,128)(2,1)S(1)} collective-permute-done((bf16[64,768]{1,0:T(8,128)(2,1)S(1)}, bf16[64,768]{1,0:T(8,128)(2,1)S(1)}, u32[]{:S(2)}, u32[]{:S(2)}) %collective-permute-start.10) | collective-permute-done | bytes 98336 | tf_op jit(solution)/shard_map/ppermute | solution.py:88
  99.5 0.1 collective-permute-start.11
  99.6 5.7 %collective-permute-done.11 = bf16[64,1536]{1,0:T(8,128)(2,1)S(1)} collective-permute-done((bf16[64,1536]{1,0:T(8,128)(2,1)S(1)}, bf16[64,1536]{1,0:T(8,128)(2,1)S(1)}, u32[]{:S(2)}, u32[]{:S(2)}) %collective-permute-start.11) | collective-permute-done | bytes 196640 | tf_op jit(solution)/shard_map/ppermute | solution.py:88
  105.3 4.7 %fusion.1 = f32[64,1280]{1,0:T(8,128)S(1)} fusion(bf16[3072,1280]{1,0:T(8,128)(2,1)} %param.21, bf16[64,1536]{1,0:T(8,128)(2,1)S(1)} %maximum_select_fusion.2, bf16[64,1536]{1,0:T(8,128)(2,1)S(1)} %collective-permute-done.11, pred[]{:T(512)S(6)} %ne.18), kind=kOutput, calls=%fused_computation.5 | convolution fusion | flops 505085952 | bytes 8585217 | tf_op jit(solution)/shard_map/dot_general | solution.py:242
  110.0 0.1 collective-permute-start.12
  110.1 1.2 %collective-permute-done.12 = bf16[2,16,1280]{2,1,0:T(8,128)(2,1)S(1)} collective-permute-done((bf16[2,16,1280]{2,1,0:T(8,128)(2,1)S(1)}, bf16[2,16,1280]{2,1,0:T(8,128)(2,1)S(1)}, u32[]{:S(2)}, u32[]{:S(2)}) %collective-permute-start.12) | collective-permute-done | bytes 81952 | tf_op jit(solution)/shard_map/ppermute | solution.py:88
  111.4 0.7 collective-permute-start.13
  112.1 0.6 dynamic-slice_convert_fusion
  112.7 2.7 %collective-permute-done.13 = bf16[1,16,1280]{2,1,0:T(8,128)(2,1)S(1)} collective-permute-done((bf16[1,16,1280]{2,1,0:T(8,128)(2,1)S(1)}, bf16[1,16,1280]{2,1,0:T(8,128)(2,1)S(1)}, u32[]{:S(2)}, u32[]{:S(2)}) %collective-permute-start.13) | collective-permute-done | bytes 40992 | tf_op jit(solution)/shard_map/ppermute | solution.py:88
  115.5 0.6 fusion.10
  (23 shorter events, 0.4 us)
Async XLA Ops:
  0.6 41.2 %copy-start = (bf16[8,512,128]{2,1,0:T(8,128)(2,1)S(1)}, bf16[8,512,128]{2,1,0:T(8,128)(2,1)}, u32[]{:S(2)}) copy-start(bf16[8,512,128]{2,1,0:T(8,128)(2,1)} %param.16) | copy-start | bytes 3145732
  0.6 3.8 %copy-start.1 = (bf16[64,128,576]{1,2,0:T(8,128)(2,1)S(1)}, bf16[64,128,576]{1,2,0:T(8,128)(2,1)}, u32[]{:S(2)}) copy-start(bf16[64,128,576]{1,2,0:T(8,128)(2,1)} %param.13) | copy-start | bytes 28311556
  4.4 1.1 copy-start.2
  5.5 0.7 copy-start.3
  6.2 0.7 copy-start.4
  6.8 19.0 %copy-start.5 = (bf16[16,1280]{1,0:T(8,128)(2,1)S(1)}, bf16[16,1280]{1,0:T(8,128)(2,1)}, u32[]{:S(2)}) copy-start(bf16[16,1280]{1,0:T(8,128)(2,1)} %param.11) | copy-start | bytes 122884
  6.8 21.0 %copy-start.6 = (bf16[1280]{0:T(1024)(128)(2,1)S(1)}, bf16[1280]{0:T(1024)(128)(2,1)}, u32[]{:S(2)}) copy-start(bf16[1280]{0:T(1024)(128)(2,1)} %param.18) | copy-start | bytes 7684
  18.5 23.1 %all-to-all-start = ((bf16[1,4,128,512]{3,1,0,2:T(4,128)(2,1)}), bf16[1,4,128,512]{3,1,0,2:T(4,128)(2,1)S(1)}, u32[]{:S(2)}, u32[]{:S(2)}) async-start(bf16[1,4,128,512]{3,1,0,2:T(4,128)(2,1)} %copy.18), calls=%async_computation | async-start | bytes 1048576 | tf_op jit(solution)/shard_map/all_to_all | solution.py:218
  25.9 7.2 %collective-permute-start.2 = (bf16[1,16,1280]{2,1,0:T(8,128)(2,1)S(1)}, bf16[1,16,1280]{2,1,0:T(8,128)(2,1)S(1)}, u32[]{:S(2)}, u32[]{:S(2)}) collective-permute-start(bf16[1,16,1280]{2,1,0:T(8,128)(2,1)S(1)} %bitcast.77), channel_id=1, source_target_pairs={{0,8},{4,12},{8,0},{12,4},{1,9},{5,13},{9,1},{13,5},{2,10},{6,14},... | collective-permute-start | bytes 122888 | tf_op jit(solution)/shard_map/ppermute | solution.py:88
  33.1 33.7 %collective-permute-start.3 = (bf16[2,16,1280]{2,1,0:T(8,128)(2,1)S(1)}, bf16[2,16,1280]{2,1,0:T(8,128)(2,1)S(1)}, u32[]{:S(2)}, u32[]{:S(2)}) collective-permute-start(bf16[2,16,1280]{2,1,0:T(8,128)(2,1)S(1)} %maximum_select_fusion.4), channel_id=1, source_target_pairs={{0,4},{4,0},{8,12},{12,8},{1,5},{5,1},{9,13},{13,9},{2,6},{6,2},{1... | collective-permute-start | bytes 245768 | tf_op jit(solution)/shard_map/ppermute | solution.py:88
  42.2 30.5 %slice-start = ((s8[7864320]{0:T(1024)(128)(4,1)}), s8[4194304]{0:T(1024)(128)(4,1)S(1)}, s32[]{:S(2)}) async-start(s8[7864320]{0:T(1024)(128)(4,1)} %bitcast.68), calls=%async_computation.1 | async-start | bytes 8388608
  58.6 14.1 %slice-start.1 = ((s8[7864320]{0:T(1024)(128)(4,1)}), s8[3670016]{0:T(1024)(128)(4,1)S(1)}, s32[]{:S(2)}) async-start(s8[7864320]{0:T(1024)(128)(4,1)} %bitcast.68), calls=%async_computation.2 | async-start | bytes 7340032
  64.7 1.5 %collective-permute-start = (bf16[64,1280]{1,0:T(8,128)(2,1)S(1)}, bf16[64,1280]{1,0:T(8,128)(2,1)S(1)}, u32[]{:S(2)}, u32[]{:S(2)}) collective-permute-start(bf16[64,1280]{1,0:T(8,128)(2,1)S(1)} %convolution_convert_fusion), channel_id=1, source_target_pairs={{0,4},{4,0},{8,12},{12,8},{1,5},{5,1},{9,13},{13,9},{2,6},{6,2},{1... | collective-permute-start | bytes 491528 | tf_op jit(solution)/shard_map/ppermute | solution.py:88
  66.2 6.3 %collective-permute-start.1 = (bf16[64,1280]{1,0:T(8,128)(2,1)S(1)}, bf16[64,1280]{1,0:T(8,128)(2,1)S(1)}, u32[]{:S(2)}, u32[]{:S(2)}) collective-permute-start(bf16[64,1280]{1,0:T(8,128)(2,1)S(1)} %add_convert_fusion), channel_id=1, source_target_pairs={{0,8},{4,12},{8,0},{12,4},{1,9},{5,13},{9,1},{13,5},{2,10},{6,14},... | collective-permute-start | bytes 491528 | tf_op jit(solution)/shard_map/ppermute | solution.py:88
  72.5 3.9 %slice-start.2 = ((s8[7864320]{0:T(1024)(128)(4,1)}), s8[4194304]{0:T(1024)(128)(4,1)S(1)}, s32[]{:S(2)}) async-start(s8[7864320]{0:T(1024)(128)(4,1)} %bitcast.70), calls=%async_computation.3 | async-start | bytes 8388608
  72.7 5.7 %collective-permute-start.6 = (f32[64]{0:T(128)S(1)}, f32[64]{0:T(128)S(1)}, u32[]{:S(2)}, u32[]{:S(2)}) collective-permute-start(f32[64]{0:T(128)S(1)} %get-tuple-element.2), channel_id=1, source_target_pairs={{0,1},{1,0},{2,3},{3,2},{4,5},{5,4},{6,7},{7,6},{8,9},{9,8},{10,11... | collective-permute-start | bytes 776 | tf_op jit(solution)/shard_map/ppermute | solution.py:88
  72.8 3.6 %slice-start.3 = ((s8[7864320]{0:T(1024)(128)(4,1)}), s8[3670016]{0:T(1024)(128)(4,1)S(1)}, s32[]{:S(2)}) async-start(s8[7864320]{0:T(1024)(128)(4,1)} %bitcast.70), calls=%async_computation.4 | async-start | bytes 7340032
  74.3 7.4 %collective-permute-start.8 = (bf16[64,1536]{1,0:T(8,128)(2,1)S(1)}, bf16[64,1536]{1,0:T(8,128)(2,1)S(1)}, u32[]{:S(2)}, u32[]{:S(2)}) collective-permute-start(bf16[64,1536]{1,0:T(8,128)(2,1)S(1)} %select_convert_fusion), channel_id=1, source_target_pairs={{0,1},{1,0},{2,3},{3,2},{4,5},{5,4},{6,7},{7,6},{8,9},{9,8},{10,11... | collective-permute-start | bytes 589832 | tf_op jit(solution)/shard_map/ppermute | solution.py:88
  77.9 7.9 %collective-permute-start.4 = (bf16[64,1536]{1,0:T(8,128)(2,1)S(1)}, bf16[64,1536]{1,0:T(8,128)(2,1)S(1)}, u32[]{:S(2)}, u32[]{:S(2)}) collective-permute-start(bf16[64,1536]{1,0:T(8,128)(2,1)S(1)} %select_convert_fusion.1), channel_id=1, source_target_pairs={{0,1},{1,0},{2,3},{3,2},{4,5},{5,4},{6,7},{7,6},{8,9},{9,8},{10,11... | collective-permute-start | bytes 589832 | tf_op jit(solution)/shard_map/ppermute | solution.py:88
  78.4 8.9 %collective-permute-start.7 = (f32[64]{0:T(128)S(1)}, f32[64]{0:T(128)S(1)}, u32[]{:S(2)}, u32[]{:S(2)}) collective-permute-start(f32[64]{0:T(128)S(1)} %add.56), channel_id=1, source_target_pairs={{0,2},{1,3},{2,0},{3,1},{4,6},{5,7},{6,4},{7,5},{8,10},{9,11},{10,... | collective-permute-start | bytes 776 | tf_op jit(solution)/shard_map/ppermute | solution.py:88
  81.8 5.6 %collective-permute-start.9 = (bf16[64,768]{1,0:T(8,128)(2,1)S(1)}, bf16[64,768]{1,0:T(8,128)(2,1)S(1)}, u32[]{:S(2)}, u32[]{:S(2)}) collective-permute-start(bf16[64,768]{1,0:T(8,128)(2,1)S(1)} %select_convert_fusion.2), channel_id=1, source_target_pairs={{0,2},{1,3},{2,0},{3,1},{4,6},{5,7},{6,4},{7,5},{8,10},{9,11},{10,... | collective-permute-start | bytes 294920 | tf_op jit(solution)/shard_map/ppermute | solution.py:88
  85.9 7.0 %collective-permute-start.5 = (bf16[64,768]{1,0:T(8,128)(2,1)S(1)}, bf16[64,768]{1,0:T(8,128)(2,1)S(1)}, u32[]{:S(2)}, u32[]{:S(2)}) collective-permute-start(bf16[64,768]{1,0:T(8,128)(2,1)S(1)} %select_convert_fusion.3), channel_id=1, source_target_pairs={{0,2},{1,3},{2,0},{3,1},{4,6},{5,7},{6,4},{7,5},{8,10},{9,11},{10,... | collective-permute-start | bytes 294920 | tf_op jit(solution)/shard_map/ppermute | solution.py:88
  93.0 6.4 %collective-permute-start.10 = (bf16[64,768]{1,0:T(8,128)(2,1)S(1)}, bf16[64,768]{1,0:T(8,128)(2,1)S(1)}, u32[]{:S(2)}, u32[]{:S(2)}) collective-permute-start(bf16[64,768]{1,0:T(8,128)(2,1)S(1)} %multiply_convert_fusion.1), channel_id=1, source_target_pairs={{0,2},{1,3},{2,0},{3,1},{4,6},{5,7},{6,4},{7,5},{8,10},{9,11},{10,... | collective-permute-start | bytes 294920 | tf_op jit(solution)/shard_map/ppermute | solution.py:88
  99.5 5.7 %collective-permute-start.11 = (bf16[64,1536]{1,0:T(8,128)(2,1)S(1)}, bf16[64,1536]{1,0:T(8,128)(2,1)S(1)}, u32[]{:S(2)}, u32[]{:S(2)}) collective-permute-start(bf16[64,1536]{1,0:T(8,128)(2,1)S(1)} %maximum_select_fusion.2), channel_id=1, source_target_pairs={{0,1},{1,0},{2,3},{3,2},{4,5},{5,4},{6,7},{7,6},{8,9},{9,8},{10,11... | collective-permute-start | bytes 589832 | tf_op jit(solution)/shard_map/ppermute | solution.py:88
  110.0 1.3 %collective-permute-start.12 = (bf16[2,16,1280]{2,1,0:T(8,128)(2,1)S(1)}, bf16[2,16,1280]{2,1,0:T(8,128)(2,1)S(1)}, u32[]{:S(2)}, u32[]{:S(2)}) collective-permute-start(bf16[2,16,1280]{2,1,0:T(8,128)(2,1)S(1)} %fusion.9), channel_id=1, source_target_pairs={{0,4},{4,0},{8,12},{12,8},{1,5},{5,1},{9,13},{13,9},{2,6},{6,2},{1... | collective-permute-start | bytes 245768 | tf_op jit(solution)/shard_map/ppermute | solution.py:88
  111.4 4.1 %collective-permute-start.13 = (bf16[1,16,1280]{2,1,0:T(8,128)(2,1)S(1)}, bf16[1,16,1280]{2,1,0:T(8,128)(2,1)S(1)}, u32[]{:S(2)}, u32[]{:S(2)}) collective-permute-start(bf16[1,16,1280]{2,1,0:T(8,128)(2,1)S(1)} %fusion.13), channel_id=1, source_target_pairs={{0,8},{4,12},{8,0},{12,4},{1,9},{5,13},{9,1},{13,5},{2,10},{6,14},... | collective-permute-start | bytes 122888 | tf_op jit(solution)/shard_map/ppermute | solution.py:88

commit v11 on v8

--- a/solution.py
+++ b/solution.py
@@ -56,10 +56,12 @@
             (((1,), (1,)), ((), ())),
             preferred_element_type=jnp.float32,
         )
-        contexts[slot] = (weighted / denominator).astype(contexts.dtype)
-
-
-def attend_all(queries, page_table, lengths, cache_pool, latent, score_scale):
+        blocks, block_heads = contexts.shape[0], head_count // contexts.shape[0]
+        context = (weighted / denominator).reshape(blocks, block_heads, latent)
+        contexts[:, slot * block_heads:(slot + 1) * block_heads, :] = context.astype(contexts.dtype)
+
+
+def attend_all(queries, page_table, lengths, cache_pool, latent, score_scale, blocks):
     req_dev, head_count, width = queries.shape
     pages_req = page_table.shape[1]
     query_columns = jnp.swapaxes(queries, 1, 2)
@@ -68,7 +70,7 @@
     kernel = functools.partial(attend_kernel, latent=latent, score_scale=score_scale)
     return pl.pallas_call(
         kernel,
-        out_shape=jax.ShapeDtypeStruct((req_dev, head_count, latent), jnp.bfloat16),
+        out_shape=jax.ShapeDtypeStruct((blocks, req_dev * (head_count // blocks), latent), jnp.bfloat16),
         in_specs=[
             pl.BlockSpec(memory_space=pltpu.SMEM),
             pl.BlockSpec(memory_space=pltpu.SMEM),
@@ -214,10 +216,9 @@
     pages_req = page_table.shape[1]
     score_scale = float(VDIM + ROPE) ** (-0.5)
     units_here = gate_proj.shape[1]
-    contexts = attend_all(queries, page_table, lengths, cache_pool, latent, score_scale)
-    received = lax.all_to_all(
-        contexts[None], ("dp", "sub"), split_axis=2, concat_axis=0, tiled=True
-    )
+    blocks = axis_sizes["dp"] * axis_sizes["sub"]
+    contexts = attend_all(queries, page_table, lengths, cache_pool, latent, score_scale, blocks)
+    received = lax.all_to_all(contexts, ("dp", "sub"), split_axis=0, concat_axis=0, tiled=True)
     received = received.reshape(-1, heads_here, latent)
     row_count = received.shape[0]
     values = jnp.einsum("rhc,hcv->rhv", received, value_up, preferred_element_type=jnp.float32)

time: 112 us -> 111 us (level)
  local copies, waits for them, and re-layouts: 4.69 us -> 3.16 us
    broadcast_in_dim x1 -> x0, local copies, waits for them, and re-layouts: 1.22 us -> none  [shards(): contexts[None]]
  transfers between devices with their start and end apart: 15 -> 15, of which waited for: 12 -> 12; matrix products, arithmetic and copies ran while one was open for 10% -> 9% of each run, Pallas kernels for 0% -> 0%
where the time goes in v11:
time: 111 us; the launch traced here: 110 us
  waiting for transfers between devices  46.8 us (42%)
  starting transfers between devices  17.7 us (16%)
  blocking collectives  16.2 us (15%)
  matrix products  14.1 us (13%)
  Pallas kernels  10 us (9%)
  local copies, waits for them, and re-layouts  3.16 us (3%)
  other arithmetic  1.45 us (1%)
    ppermute x14, waiting for transfers between devices, swap_with(): return lax.ppermute(x, axis, [(i, i ^ distance) for i in range(size)])  38.4 us
    all_gather x1, blocking collectives, shards(): group_values = lax.all_gather(values, 'sub', axis=1, tiled=True)  16.2 us
    ppermute x14, starting transfers between devices, swap_with(): return lax.ppermute(x, axis, [(i, i ^ distance) for i in range(size)])  10.4 us
    pallas_call x1, Pallas kernels, attend_all(): pl.pallas_call(kernel, out_shape=jax.ShapeDtypeStruct((blocks, req_dev *...  10 us
    all_to_all x1, waiting for transfers between devices, shards(): lax.all_to_all(contexts, ('dp', 'sub'), split_axis=0, concat_axis=0, tile...  8.35 us
    all_to_all x1, starting transfers between devices, shards(): lax.all_to_all(contexts, ('dp', 'sub'), split_axis=0, concat_axis=0, tile...  7.36 us
    dot_general x1, matrix products, shards(): jnp.dot(group_values, out_proj, preferred_element_type=jnp.float32)  6.04 us
    dot_general x1, matrix products, shards(): jnp.dot(hidden_units, down_proj, preferred_element_type=jnp.float32)  4.7 us
  transfers between devices with their start and end apart: 15, of which 12 were waited for; matrix products, arithmetic and copies ran while one was open for 9% of the time, Pallas kernels for 0%

profile of v11, /device:TPU:0, one launch (start us, length us, event | category | flops | bytes accessed | tf_op | source)
XLA Modules:
  0.0 110.3 jit_solution(17084716164082457169)
XLA Ops:
  0.6 0.0 copy-start
  0.6 0.0 copy-start.1
  0.7 1.1 %copy-done.1 = bf16[4,128,576]{1,2,0:T(8,128)(2,1)S(1)} copy-done((bf16[4,128,576]{1,2,0:T(8,128)(2,1)S(1)}, bf16[4,128,576]{1,2,0:T(8,128)(2,1)}, u32[]{:S(2)}) %copy-start.1) | copy-done | bytes 589848
  1.8 0.0 copy-start.2
  1.8 0.7 copy-done.2
  2.5 0.0 copy-start.3
  2.5 0.7 copy-done.3
  3.1 0.0 copy-start.4
  3.1 0.0 copy-start.5
  3.1 10.0 %shard_map.122 = bf16[16,32,512]{2,1,0:T(8,128)(2,1)} custom-call(s32[4,16]{1,0:T(4,128)S(1)} %copy-done.2, s32[4]{0:T(128)S(1)} %copy-done.3, bf16[4,576,128]{2,1,0:T(8,128)(2,1)S(1)} %bitcast.58, bf16[64,576,128]{2,1,0:T(8,128)(2,1)} %bitcast.63), custom_call_target="tpu_custom_call" | custom-call | tf_op jit(solution)/shard_map/pallas_call | solution.py:71
  13.2 7.4 %all-to-all-start = ((bf16[16,32,512]{2,1,0:T(8,128)(2,1)}), bf16[16,32,512]{2,1,0:T(8,128)(2,1)S(1)}, u32[]{:S(2)}, u32[]{:S(2)}) async-start(bf16[16,32,512]{2,1,0:T(8,128)(2,1)} %shard_map.122), calls=%async_computation | async-start | bytes 1048576 | tf_op jit(solution)/shard_map/all_to_all | solution.py:221
  20.6 0.0 copy-done.4
  20.6 2.0 %collective-permute-start.2 = (bf16[1,16,1280]{2,1,0:T(8,128)(2,1)S(1)}, bf16[1,16,1280]{2,1,0:T(8,128)(2,1)S(1)}, u32[]{:S(2)}, u32[]{:S(2)}) collective-permute-start(bf16[1,16,1280]{2,1,0:T(8,128)(2,1)S(1)} %bitcast.68), channel_id=1, source_target_pairs={{0,8},{4,12},{8,0},{12,4},{1,9},{5,13},{9,1},{13,5},{2,10},{6,14},... | collective-permute-start | bytes 122888 | tf_op jit(solution)/shard_map/ppermute | solution.py:90
  22.6 0.0 copy-done.5
  22.6 5.2 %collective-permute-done.2 = bf16[1,16,1280]{2,1,0:T(8,128)(2,1)S(1)} collective-permute-done((bf16[1,16,1280]{2,1,0:T(8,128)(2,1)S(1)}, bf16[1,16,1280]{2,1,0:T(8,128)(2,1)S(1)}, u32[]{:S(2)}, u32[]{:S(2)}) %collective-permute-start.2) | collective-permute-done | bytes 40992 | tf_op jit(solution)/shard_map/ppermute | solution.py:90
  27.8 0.1 collective-permute-start.3
  27.9 8.3 %all-to-all-done = bf16[16,32,512]{2,1,0:T(8,128)(2,1)S(1)} async-done(((bf16[16,32,512]{2,1,0:T(8,128)(2,1)}), bf16[16,32,512]{2,1,0:T(8,128)(2,1)S(1)}, u32[]{:S(2)}, u32[]{:S(2)}) %all-to-all-start) | async-done | bytes 524320 | tf_op jit(solution)/shard_map/all_to_all | solution.py:221
  36.2 0.0 copy-done
  36.2 0.4 fusion
  36.7 0.0 slice-start
  36.7 16.2 %all_gather.3 = bf16[64,4096]{1,0:T(8,128)(2,1)S(1)} all-gather(bf16[64,1024]{1,0:T(8,128)(2,1)S(1)} %bitcast.67), channel_id=1, replica_groups=mesh['grp'=2,'dp'=4,'sub'=4] {'sub'}, dimensions={1}, use_global_device_ids=true | all-gather | bytes 655360 | tf_op jit(solution)/shard_map/all_gather | solution.py:226
  52.9 0.0 slice-start.1
  52.9 6.0 %convolution_convert_fusion = bf16[64,1280]{1,0:T(8,128)(2,1)S(1)} fusion(bf16[64,4096]{1,0:T(8,128)(2,1)S(1)} %all_gather.3, bf16[4096,1280]{1,0:T(8,128)(2,1)} %param.17), kind=kOutput, calls=%fused_computation | convolution fusion | flops 671170560 | bytes 11173888 | tf_op jit(solution)/shard_map/dot_general | solution.py:230
  58.9 0.1 collective-permute-start
  59.0 1.4 %collective-permute-done = bf16[64,1280]{1,0:T(8,128)(2,1)S(1)} collective-permute-done((bf16[64,1280]{1,0:T(8,128)(2,1)S(1)}, bf16[64,1280]{1,0:T(8,128)(2,1)S(1)}, u32[]{:S(2)}, u32[]{:S(2)}) %collective-permute-start) | collective-permute-done | bytes 163872 | tf_op jit(solution)/shard_map/ppermute | solution.py:90
  60.4 0.7 collective-permute-start.1
  61.1 0.0 collective-permute-done.3
  61.1 5.6 %collective-permute-done.1 = bf16[64,1280]{1,0:T(8,128)(2,1)S(1)} collective-permute-done((bf16[64,1280]{1,0:T(8,128)(2,1)S(1)}, bf16[64,1280]{1,0:T(8,128)(2,1)S(1)}, u32[]{:S(2)}, u32[]{:S(2)}) %collective-permute-start.1) | collective-permute-done | bytes 163872 | tf_op jit(solution)/shard_map/ppermute | solution.py:90
  66.7 0.0 slice-start.2
  66.7 0.2 multiply_reduce_fusion
  66.9 0.1 collective-permute-start.6
  67.0 0.0 slice-done
  67.0 0.0 slice-done.1
  67.0 0.0 slice-start.3
  67.0 1.5 %fusion.12 = f32[64,3072]{1,0:T(8,128)S(1)} fusion(bf16[1280,3072]{1,0:T(8,128)(2,1)S(1)} %bitcast.60, f32[64,1280]{1,0:T(8,128)S(1)} %get-tuple-element.3, f32[1280]{0:T(1024)S(1)} %convert_element_type.106), kind=kOutput, calls=%fused_computation.40 | convolution fusion | flops 503480320 | bytes 8983552 | tf_op jit(solution)/shard_map/dot_general | solution.py:237
  68.6 2.0 %collective-permute-start.8 = (bf16[64,1536]{1,0:T(8,128)(2,1)S(1)}, bf16[64,1536]{1,0:T(8,128)(2,1)S(1)}, u32[]{:S(2)}, u32[]{:S(2)}) collective-permute-start(bf16[64,1536]{1,0:T(8,128)(2,1)S(1)} %select_convert_fusion), channel_id=1, source_target_pairs={{0,1},{1,0},{2,3},{3,2},{4,5},{5,4},{6,7},{7,6},{8,9},{9,8},{10,11... | collective-permute-start | bytes 589832 | tf_op jit(solution)/shard_map/ppermute | solution.py:90
  70.6 0.0 slice-done.2
  70.6 0.0 slice-done.3
  70.6 1.5 %fusion.13 = f32[64,3072]{1,0:T(8,128)S(1)} fusion(bf16[1280,3072]{1,0:T(8,128)(2,1)S(1)} %bitcast.62, f32[64,1280]{1,0:T(8,128)S(1)} %get-tuple-element.3, f32[1280]{0:T(1024)S(1)} %convert_element_type.106), kind=kOutput, calls=%fused_computation.41 | convolution fusion | flops 503480320 | bytes 8983552 | tf_op jit(solution)/shard_map/dot_general | solution.py:236
  72.2 0.5 collective-permute-start.4
  72.7 0.0 collective-permute-done.6
  72.7 0.9 collective-permute-start.7
  73.6 2.4 %collective-permute-done.8 = bf16[64,1536]{1,0:T(8,128)(2,1)S(1)} collective-permute-done((bf16[64,1536]{1,0:T(8,128)(2,1)S(1)}, bf16[64,1536]{1,0:T(8,128)(2,1)S(1)}, u32[]{:S(2)}, u32[]{:S(2)}) %collective-permute-start.8) | collective-permute-done | bytes 196640 | tf_op jit(solution)/shard_map/ppermute | solution.py:90
  76.0 0.1 convert_add_fusion
  76.1 1.7 %collective-permute-start.9 = (bf16[64,768]{1,0:T(8,128)(2,1)S(1)}, bf16[64,768]{1,0:T(8,128)(2,1)S(1)}, u32[]{:S(2)}, u32[]{:S(2)}) collective-permute-start(bf16[64,768]{1,0:T(8,128)(2,1)S(1)} %select_convert_fusion.2), channel_id=1, source_target_pairs={{0,2},{1,3},{2,0},{3,1},{4,6},{5,7},{6,4},{7,5},{8,10},{9,11},{10,... | collective-permute-start | bytes 294920 | tf_op jit(solution)/shard_map/ppermute | solution.py:90
  77.8 2.2 %collective-permute-done.4 = bf16[64,1536]{1,0:T(8,128)(2,1)S(1)} collective-permute-done((bf16[64,1536]{1,0:T(8,128)(2,1)S(1)}, bf16[64,1536]{1,0:T(8,128)(2,1)S(1)}, u32[]{:S(2)}, u32[]{:S(2)}) %collective-permute-start.4) | collective-permute-done | bytes 196640 | tf_op jit(solution)/shard_map/ppermute | solution.py:90
  80.0 0.1 convert_add_fusion.1
  80.1 1.4 %collective-permute-start.5 = (bf16[64,768]{1,0:T(8,128)(2,1)S(1)}, bf16[64,768]{1,0:T(8,128)(2,1)S(1)}, u32[]{:S(2)}, u32[]{:S(2)}) collective-permute-start(bf16[64,768]{1,0:T(8,128)(2,1)S(1)} %select_convert_fusion.3), channel_id=1, source_target_pairs={{0,2},{1,3},{2,0},{3,1},{4,6},{5,7},{6,4},{7,5},{8,10},{9,11},{10,... | collective-permute-start | bytes 294920 | tf_op jit(solution)/shard_map/ppermute | solution.py:90
  81.5 0.0 collective-permute-done.7
  81.5 0.1 collective-permute-done.9
  81.7 5.5 %collective-permute-done.5 = bf16[64,768]{1,0:T(8,128)(2,1)S(1)} collective-permute-done((bf16[64,768]{1,0:T(8,128)(2,1)S(1)}, bf16[64,768]{1,0:T(8,128)(2,1)S(1)}, u32[]{:S(2)}, u32[]{:S(2)}) %collective-permute-start.5) | collective-permute-done | bytes 98336 | tf_op jit(solution)/shard_map/ppermute | solution.py:90
  87.1 0.1 multiply_convert_fusion.1
  87.3 0.1 collective-permute-start.10
  87.4 6.4 %collective-permute-done.10 = bf16[64,768]{1,0:T(8,128)(2,1)S(1)} collective-permute-done((bf16[64,768]{1,0:T(8,128)(2,1)S(1)}, bf16[64,768]{1,0:T(8,128)(2,1)S(1)}, u32[]{:S(2)}, u32[]{:S(2)}) %collective-permute-start.10) | collective-permute-done | bytes 98336 | tf_op jit(solution)/shard_map/ppermute | solution.py:90
  93.8 0.1 collective-permute-start.11
  93.9 5.7 %collective-permute-done.11 = bf16[64,1536]{1,0:T(8,128)(2,1)S(1)} collective-permute-done((bf16[64,1536]{1,0:T(8,128)(2,1)S(1)}, bf16[64,1536]{1,0:T(8,128)(2,1)S(1)}, u32[]{:S(2)}, u32[]{:S(2)}) %collective-permute-start.11) | collective-permute-done | bytes 196640 | tf_op jit(solution)/shard_map/ppermute | solution.py:90
  99.5 4.7 %fusion.2 = f32[64,1280]{1,0:T(8,128)S(1)} fusion(bf16[3072,1280]{1,0:T(8,128)(2,1)} %param.21, bf16[64,1536]{1,0:T(8,128)(2,1)S(1)} %maximum_select_fusion.2, bf16[64,1536]{1,0:T(8,128)(2,1)S(1)} %collective-permute-done.11, pred[]{:T(512)S(6)} %ne.18), kind=kOutput, calls=%fused_computation.5 | convolution fusion | flops 505085952 | bytes 8585217 | tf_op jit(solution)/shard_map/dot_general | solution.py:243
  104.2 0.1 collective-permute-start.12
  104.4 1.2 %collective-permute-done.12 = bf16[2,16,1280]{2,1,0:T(8,128)(2,1)S(1)} collective-permute-done((bf16[2,16,1280]{2,1,0:T(8,128)(2,1)S(1)}, bf16[2,16,1280]{2,1,0:T(8,128)(2,1)S(1)}, u32[]{:S(2)}, u32[]{:S(2)}) %collective-permute-start.12) | collective-permute-done | bytes 81952 | tf_op jit(solution)/shard_map/ppermute | solution.py:90
  105.6 0.7 collective-permute-start.13
  106.4 0.6 dynamic-slice_convert_fusion
  107.0 2.7 %collective-permute-done.13 = bf16[1,16,1280]{2,1,0:T(8,128)(2,1)S(1)} collective-permute-done((bf16[1,16,1280]{2,1,0:T(8,128)(2,1)S(1)}, bf16[1,16,1280]{2,1,0:T(8,128)(2,1)S(1)}, u32[]{:S(2)}, u32[]{:S(2)}) %collective-permute-start.13) | collective-permute-done | bytes 40992 | tf_op jit(solution)/shard_map/ppermute | solution.py:90
  109.7 0.6 fusion.11
  (19 shorter events, 0.4 us)
Async XLA Ops:
  0.6 35.6 %copy-start = (bf16[8,512,128]{2,1,0:T(8,128)(2,1)S(1)}, bf16[8,512,128]{2,1,0:T(8,128)(2,1)}, u32[]{:S(2)}) copy-start(bf16[8,512,128]{2,1,0:T(8,128)(2,1)} %param.16) | copy-start | bytes 3145732
  0.6 1.2 %copy-start.1 = (bf16[4,128,576]{1,2,0:T(8,128)(2,1)S(1)}, bf16[4,128,576]{1,2,0:T(8,128)(2,1)}, u32[]{:S(2)}) copy-start(bf16[4,128,576]{1,2,0:T(8,128)(2,1)} %param.12) | copy-start | bytes 1769476
  1.8 0.7 copy-start.2
  2.5 0.7 copy-start.3
  3.1 17.4 %copy-start.4 = (bf16[16,1280]{1,0:T(8,128)(2,1)S(1)}, bf16[16,1280]{1,0:T(8,128)(2,1)}, u32[]{:S(2)}) copy-start(bf16[16,1280]{1,0:T(8,128)(2,1)} %param.11) | copy-start | bytes 122884
  3.1 19.4 %copy-start.5 = (bf16[1280]{0:T(1024)(128)(2,1)S(1)}, bf16[1280]{0:T(1024)(128)(2,1)}, u32[]{:S(2)}) copy-start(bf16[1280]{0:T(1024)(128)(2,1)} %param.18) | copy-start | bytes 7684
  13.2 23.1 %all-to-all-start = ((bf16[16,32,512]{2,1,0:T(8,128)(2,1)}), bf16[16,32,512]{2,1,0:T(8,128)(2,1)S(1)}, u32[]{:S(2)}, u32[]{:S(2)}) async-start(bf16[16,32,512]{2,1,0:T(8,128)(2,1)} %shard_map.122), calls=%async_computation | async-start | bytes 1048576 | tf_op jit(solution)/shard_map/all_to_all | solution.py:221
  20.6 7.2 %collective-permute-start.2 = (bf16[1,16,1280]{2,1,0:T(8,128)(2,1)S(1)}, bf16[1,16,1280]{2,1,0:T(8,128)(2,1)S(1)}, u32[]{:S(2)}, u32[]{:S(2)}) collective-permute-start(bf16[1,16,1280]{2,1,0:T(8,128)(2,1)S(1)} %bitcast.68), channel_id=1, source_target_pairs={{0,8},{4,12},{8,0},{12,4},{1,9},{5,13},{9,1},{13,5},{2,10},{6,14},... | collective-permute-start | bytes 122888 | tf_op jit(solution)/shard_map/ppermute | solution.py:90
  27.8 33.3 %collective-permute-start.3 = (bf16[2,16,1280]{2,1,0:T(8,128)(2,1)S(1)}, bf16[2,16,1280]{2,1,0:T(8,128)(2,1)S(1)}, u32[]{:S(2)}, u32[]{:S(2)}) collective-permute-start(bf16[2,16,1280]{2,1,0:T(8,128)(2,1)S(1)} %maximum_select_fusion.4), channel_id=1, source_target_pairs={{0,4},{4,0},{8,12},{12,8},{1,5},{5,1},{9,13},{13,9},{2,6},{6,2},{1... | collective-permute-start | bytes 245768 | tf_op jit(solution)/shard_map/ppermute | solution.py:90
  36.7 30.3 %slice-start = ((s8[7864320]{0:T(1024)(128)(4,1)}), s8[4194304]{0:T(1024)(128)(4,1)S(1)}, s32[]{:S(2)}) async-start(s8[7864320]{0:T(1024)(128)(4,1)} %bitcast.59), calls=%async_computation.1 | async-start | bytes 8388608
  52.9 14.1 %slice-start.1 = ((s8[7864320]{0:T(1024)(128)(4,1)}), s8[3670016]{0:T(1024)(128)(4,1)S(1)}, s32[]{:S(2)}) async-start(s8[7864320]{0:T(1024)(128)(4,1)} %bitcast.59), calls=%async_computation.2 | async-start | bytes 7340032
  58.9 1.5 %collective-permute-start = (bf16[64,1280]{1,0:T(8,128)(2,1)S(1)}, bf16[64,1280]{1,0:T(8,128)(2,1)S(1)}, u32[]{:S(2)}, u32[]{:S(2)}) collective-permute-start(bf16[64,1280]{1,0:T(8,128)(2,1)S(1)} %convolution_convert_fusion), channel_id=1, source_target_pairs={{0,4},{4,0},{8,12},{12,8},{1,5},{5,1},{9,13},{13,9},{2,6},{6,2},{1... | collective-permute-start | bytes 491528 | tf_op jit(solution)/shard_map/ppermute | solution.py:90
  60.4 6.3 %collective-permute-start.1 = (bf16[64,1280]{1,0:T(8,128)(2,1)S(1)}, bf16[64,1280]{1,0:T(8,128)(2,1)S(1)}, u32[]{:S(2)}, u32[]{:S(2)}) collective-permute-start(bf16[64,1280]{1,0:T(8,128)(2,1)S(1)} %add_convert_fusion), channel_id=1, source_target_pairs={{0,8},{4,12},{8,0},{12,4},{1,9},{5,13},{9,1},{13,5},{2,10},{6,14},... | collective-permute-start | bytes 491528 | tf_op jit(solution)/shard_map/ppermute | solution.py:90
  66.7 3.9 %slice-start.2 = ((s8[7864320]{0:T(1024)(128)(4,1)}), s8[4194304]{0:T(1024)(128)(4,1)S(1)}, s32[]{:S(2)}) async-start(s8[7864320]{0:T(1024)(128)(4,1)} %bitcast.61), calls=%async_computation.3 | async-start | bytes 8388608
  66.9 5.7 %collective-permute-start.6 = (f32[64]{0:T(128)S(1)}, f32[64]{0:T(128)S(1)}, u32[]{:S(2)}, u32[]{:S(2)}) collective-permute-start(f32[64]{0:T(128)S(1)} %get-tuple-element.2), channel_id=1, source_target_pairs={{0,1},{1,0},{2,3},{3,2},{4,5},{5,4},{6,7},{7,6},{8,9},{9,8},{10,11... | collective-permute-start | bytes 776 | tf_op jit(solution)/shard_map/ppermute | solution.py:90
  67.0 3.6 %slice-start.3 = ((s8[7864320]{0:T(1024)(128)(4,1)}), s8[3670016]{0:T(1024)(128)(4,1)S(1)}, s32[]{:S(2)}) async-start(s8[7864320]{0:T(1024)(128)(4,1)} %bitcast.61), calls=%async_computation.4 | async-start | bytes 7340032
  68.6 7.4 %collective-permute-start.8 = (bf16[64,1536]{1,0:T(8,128)(2,1)S(1)}, bf16[64,1536]{1,0:T(8,128)(2,1)S(1)}, u32[]{:S(2)}, u32[]{:S(2)}) collective-permute-start(bf16[64,1536]{1,0:T(8,128)(2,1)S(1)} %select_convert_fusion), channel_id=1, source_target_pairs={{0,1},{1,0},{2,3},{3,2},{4,5},{5,4},{6,7},{7,6},{8,9},{9,8},{10,11... | collective-permute-start | bytes 589832 | tf_op jit(solution)/shard_map/ppermute | solution.py:90
  72.2 7.9 %collective-permute-start.4 = (bf16[64,1536]{1,0:T(8,128)(2,1)S(1)}, bf16[64,1536]{1,0:T(8,128)(2,1)S(1)}, u32[]{:S(2)}, u32[]{:S(2)}) collective-permute-start(bf16[64,1536]{1,0:T(8,128)(2,1)S(1)} %select_convert_fusion.1), channel_id=1, source_target_pairs={{0,1},{1,0},{2,3},{3,2},{4,5},{5,4},{6,7},{7,6},{8,9},{9,8},{10,11... | collective-permute-start | bytes 589832 | tf_op jit(solution)/shard_map/ppermute | solution.py:90
  72.7 8.9 %collective-permute-start.7 = (f32[64]{0:T(128)S(1)}, f32[64]{0:T(128)S(1)}, u32[]{:S(2)}, u32[]{:S(2)}) collective-permute-start(f32[64]{0:T(128)S(1)} %add.56), channel_id=1, source_target_pairs={{0,2},{1,3},{2,0},{3,1},{4,6},{5,7},{6,4},{7,5},{8,10},{9,11},{10,... | collective-permute-start | bytes 776 | tf_op jit(solution)/shard_map/ppermute | solution.py:90
  76.1 5.6 %collective-permute-start.9 = (bf16[64,768]{1,0:T(8,128)(2,1)S(1)}, bf16[64,768]{1,0:T(8,128)(2,1)S(1)}, u32[]{:S(2)}, u32[]{:S(2)}) collective-permute-start(bf16[64,768]{1,0:T(8,128)(2,1)S(1)} %select_convert_fusion.2), channel_id=1, source_target_pairs={{0,2},{1,3},{2,0},{3,1},{4,6},{5,7},{6,4},{7,5},{8,10},{9,11},{10,... | collective-permute-start | bytes 294920 | tf_op jit(solution)/shard_map/ppermute | solution.py:90
  80.1 7.0 %collective-permute-start.5 = (bf16[64,768]{1,0:T(8,128)(2,1)S(1)}, bf16[64,768]{1,0:T(8,128)(2,1)S(1)}, u32[]{:S(2)}, u32[]{:S(2)}) collective-permute-start(bf16[64,768]{1,0:T(8,128)(2,1)S(1)} %select_convert_fusion.3), channel_id=1, source_target_pairs={{0,2},{1,3},{2,0},{3,1},{4,6},{5,7},{6,4},{7,5},{8,10},{9,11},{10,... | collective-permute-start | bytes 294920 | tf_op jit(solution)/shard_map/ppermute | solution.py:90
  87.3 6.4 %collective-permute-start.10 = (bf16[64,768]{1,0:T(8,128)(2,1)S(1)}, bf16[64,768]{1,0:T(8,128)(2,1)S(1)}, u32[]{:S(2)}, u32[]{:S(2)}) collective-permute-start(bf16[64,768]{1,0:T(8,128)(2,1)S(1)} %multiply_convert_fusion.1), channel_id=1, source_target_pairs={{0,2},{1,3},{2,0},{3,1},{4,6},{5,7},{6,4},{7,5},{8,10},{9,11},{10,... | collective-permute-start | bytes 294920 | tf_op jit(solution)/shard_map/ppermute | solution.py:90
  93.8 5.7 %collective-permute-start.11 = (bf16[64,1536]{1,0:T(8,128)(2,1)S(1)}, bf16[64,1536]{1,0:T(8,128)(2,1)S(1)}, u32[]{:S(2)}, u32[]{:S(2)}) collective-permute-start(bf16[64,1536]{1,0:T(8,128)(2,1)S(1)} %maximum_select_fusion.2), channel_id=1, source_target_pairs={{0,1},{1,0},{2,3},{3,2},{4,5},{5,4},{6,7},{7,6},{8,9},{9,8},{10,11... | collective-permute-start | bytes 589832 | tf_op jit(solution)/shard_map/ppermute | solution.py:90
  104.2 1.3 %collective-permute-start.12 = (bf16[2,16,1280]{2,1,0:T(8,128)(2,1)S(1)}, bf16[2,16,1280]{2,1,0:T(8,128)(2,1)S(1)}, u32[]{:S(2)}, u32[]{:S(2)}) collective-permute-start(bf16[2,16,1280]{2,1,0:T(8,128)(2,1)S(1)} %fusion.10), channel_id=1, source_target_pairs={{0,4},{4,0},{8,12},{12,8},{1,5},{5,1},{9,13},{13,9},{2,6},{6,2},{1... | collective-permute-start | bytes 245768 | tf_op jit(solution)/shard_map/ppermute | solution.py:90
  105.6 4.1 %collective-permute-start.13 = (bf16[1,16,1280]{2,1,0:T(8,128)(2,1)S(1)}, bf16[1,16,1280]{2,1,0:T(8,128)(2,1)S(1)}, u32[]{:S(2)}, u32[]{:S(2)}) collective-permute-start(bf16[1,16,1280]{2,1,0:T(8,128)(2,1)S(1)} %fusion.14), channel_id=1, source_target_pairs={{0,8},{4,12},{8,0},{12,4},{1,9},{5,13},{9,1},{13,5},{2,10},{6,14},... | collective-permute-start | bytes 122888 | tf_op jit(solution)/shard_map/ppermute | solution.py:90

commit v12 on v11

--- a/solution.py
+++ b/solution.py
@@ -84,6 +84,31 @@
         ],
         compiler_params=pltpu.CompilerParams(vmem_limit_bytes=48 * 1024 * 1024),
     )(page_table, lengths, query_columns, cache_columns)
+
+
+def streamed_matmul(rows, weights):
+    row_count, depth = rows.shape
+    width = weights.shape[1]
+    block = next(size for size in (1024, 512, 256, 128, depth) if depth % size == 0)
+
+    def kernel(rows_ref, weights_ref, out_ref):
+        @pl.when(pl.program_id(0) == 0)
+        def _():
+            out_ref[...] = jnp.zeros_like(out_ref)
+
+        out_ref[...] += jnp.dot(rows_ref[...], weights_ref[...], preferred_element_type=jnp.float32)
+
+    return pl.pallas_call(
+        kernel,
+        out_shape=jax.ShapeDtypeStruct((row_count, width), jnp.float32),
+        grid=(depth // block,),
+        in_specs=[
+            pl.BlockSpec((row_count, block), lambda step: (0, step)),
+            pl.BlockSpec((block, width), lambda step: (step, 0)),
+        ],
+        out_specs=pl.BlockSpec((row_count, width), lambda step: (0, 0)),
+        compiler_params=pltpu.CompilerParams(dimension_semantics=("arbitrary",)),
+    )(rows, weights)
 
 
 def swap_with(x, axis, distance, size):
@@ -226,9 +251,7 @@
     group_values = lax.all_gather(values, "sub", axis=1, tiled=True)
     dp_size = axis_sizes["dp"]
     sub_size = axis_sizes["sub"]
-    attention_all = matched_sum(
-        jnp.dot(group_values, out_proj, preferred_element_type=jnp.float32), "dp", dp_size
-    )
+    attention_all = matched_sum(streamed_matmul(group_values, out_proj), "dp", dp_size)
     hidden_all = farthest_first_rows_gather(hidden_in, "dp", dp_size)
     all_residual = hidden_all.astype(jnp.float32) + attention_all
     squares = doubling_sum(jnp.sum(all_residual * all_residual, axis=1), "sub", sub_size)
@@ -240,7 +263,7 @@
     hidden_chunk = (jax.nn.silu(gate_sum * scale_rows) * (up_sum * scale_rows)).astype(jnp.bfloat16)
     hidden_units = farthest_first_gather(hidden_chunk, "sub", sub_size, 1)
     feed_forward = nearest_first_rows_scatter(
-        jnp.dot(hidden_units, down_proj, preferred_element_type=jnp.float32), "dp", axis_sizes["dp"]
+        streamed_matmul(hidden_units, down_proj), "dp", axis_sizes["dp"]
     )
     own_rows = hidden_in.shape[0]
     first_row = lax.axis_index("dp") * own_rows

time: 111 us -> 121 us (1.090)
  Pallas kernels: 10 us -> 22.1 us
  matrix products: 14.1 us -> 6.73 us
  other arithmetic: 1.45 us -> 6.25 us
    pallas_call x0 -> x2, Pallas kernels: none -> 12.1 us  [streamed_matmul(): pl.pallas_call(kernel, out_shape=jax.ShapeDtypeStruct((row_count, width),...]
    dot_general x2 -> x0, matrix products: 10.7 us -> none  [the longest x1 6.04 us: shards(): jnp.dot(group_values, out_proj, preferred_element_type=jnp.float32)]
    dot_general x1, matrix products: 1.48 us -> 4.86 us  [shards(): up_part = jnp.dot(gained, up_proj, preferred_element_type=jnp.float32)]
    convert_element_type x1 -> x2, other arithmetic: 0.04 us -> 2 us  [matched_sum(): mine = x.astype(jnp.bfloat16)]
    unnamed x20 -> x16, local copies, waits for them, and re-layouts: 2.52 us -> 2.51 us
  transfers between devices with their start and end apart: 15 -> 15, of which waited for: 12 -> 12; matrix products, arithmetic and copies ran while one was open for 9% -> 8% of each run, Pallas kernels for 0% -> 5%
where the time goes in v12:
time: 121 us; the launch traced here: 120 us
  waiting for transfers between devices  46.4 us (38%)
  Pallas kernels  22.1 us (18%)
  starting transfers between devices  18.1 us (15%)
  blocking collectives  16.5 us (14%)
  matrix products  6.73 us (6%)
  other arithmetic  6.25 us (5%)
  local copies, waits for them, and re-layouts  3.15 us (3%)
    ppermute x14, waiting for transfers between devices, swap_with(): return lax.ppermute(x, axis, [(i, i ^ distance) for i in range(size)])  38.1 us
    all_gather x1, blocking collectives, shards(): group_values = lax.all_gather(values, 'sub', axis=1, tiled=True)  16.5 us
    pallas_call x2, Pallas kernels, streamed_matmul(): pl.pallas_call(kernel, out_shape=jax.ShapeDtypeStruct((row_count, width),...  12.1 us
    ppermute x14, starting transfers between devices, swap_with(): return lax.ppermute(x, axis, [(i, i ^ distance) for i in range(size)])  10.8 us
    pallas_call x1, Pallas kernels, attend_all(): pl.pallas_call(kernel, out_shape=jax.ShapeDtypeStruct((blocks, req_dev *...  10 us
    all_to_all x1, waiting for transfers between devices, shards(): lax.all_to_all(contexts, ('dp', 'sub'), split_axis=0, concat_axis=0, tile...  8.35 us
    all_to_all x1, starting transfers between devices, shards(): lax.all_to_all(contexts, ('dp', 'sub'), split_axis=0, concat_axis=0, tile...  7.36 us
    dot_general x1, matrix products, shards(): up_part = jnp.dot(gained, up_proj, preferred_element_type=jnp.float32)  4.86 us
  transfers between devices with their start and end apart: 15, of which 12 were waited for; matrix products, arithmetic and copies ran while one was open for 8% of the time, Pallas kernels for 5%

profile of v12, /device:TPU:0, one launch (start us, length us, event | category | flops | bytes accessed | tf_op | source)
XLA Modules:
  0.0 120.2 jit_solution(18182456733512609213)
XLA Ops:
  0.6 0.0 copy-start
  0.6 0.0 copy-start.1
  0.7 1.1 copy-done.1
  1.8 0.0 copy-start.2
  1.8 0.7 copy-done.2
  2.5 0.0 copy-start.3
  2.5 0.7 copy-done.3
  3.1 0.0 copy-start.4
  3.1 0.0 copy-start.5
  3.1 10.0 %shard_map.122 = bf16[16,32,512]{2,1,0:T(8,128)(2,1)} custom-call(s32[4,16]{1,0:T(4,128)S(1)} %copy-done.2, s32[4]{0:T(128)S(1)} %copy-done.3, bf16[4,576,128]{2,1,0:T(8,128)(2,1)S(1)} %bitcast.55, bf16[64,576,128]{2,1,0:T(8,128)(2,1)} %bitcast.58), custom_call_target="tpu_custom_call" | custom-call | tf_op jit(solution)/shard_map/pallas_call | solution.py:71
  13.2 7.4 %all-to-all-start = ((bf16[16,32,512]{2,1,0:T(8,128)(2,1)}), bf16[16,32,512]{2,1,0:T(8,128)(2,1)S(1)}, u32[]{:S(2)}, u32[]{:S(2)}) async-start(bf16[16,32,512]{2,1,0:T(8,128)(2,1)} %shard_map.122), calls=%async_computation | async-start | bytes 1048576 | tf_op jit(solution)/shard_map/all_to_all | solution.py:246
  20.6 0.0 copy-done.4
  20.6 2.0 %collective-permute-start.2 = (bf16[1,16,1280]{2,1,0:T(8,128)(2,1)S(1)}, bf16[1,16,1280]{2,1,0:T(8,128)(2,1)S(1)}, u32[]{:S(2)}, u32[]{:S(2)}) collective-permute-start(bf16[1,16,1280]{2,1,0:T(8,128)(2,1)S(1)} %bitcast.63), channel_id=1, source_target_pairs={{0,8},{4,12},{8,0},{12,4},{1,9},{5,13},{9,1},{13,5},{2,10},{6,14},... | collective-permute-start | bytes 122888 | tf_op jit(solution)/shard_map/ppermute | solution.py:115
  22.6 0.0 copy-done.5
  22.6 5.2 %collective-permute-done.2 = bf16[1,16,1280]{2,1,0:T(8,128)(2,1)S(1)} collective-permute-done((bf16[1,16,1280]{2,1,0:T(8,128)(2,1)S(1)}, bf16[1,16,1280]{2,1,0:T(8,128)(2,1)S(1)}, u32[]{:S(2)}, u32[]{:S(2)}) %collective-permute-start.2) | collective-permute-done | bytes 40992 | tf_op jit(solution)/shard_map/ppermute | solution.py:115
  27.8 0.1 collective-permute-start.3
  27.9 8.3 %all-to-all-done = bf16[16,32,512]{2,1,0:T(8,128)(2,1)S(1)} async-done(((bf16[16,32,512]{2,1,0:T(8,128)(2,1)}), bf16[16,32,512]{2,1,0:T(8,128)(2,1)S(1)}, u32[]{:S(2)}, u32[]{:S(2)}) %all-to-all-start) | async-done | bytes 524320 | tf_op jit(solution)/shard_map/all_to_all | solution.py:246
  36.2 0.0 copy-done
  36.2 0.4 fusion
  36.7 16.5 %all_gather.3.rows_ref = bf16[64,4096]{1,0:T(8,128)(2,1)} all-gather(bf16[64,1024]{1,0:T(8,128)(2,1)S(1)} %bitcast.62), channel_id=1, replica_groups=mesh['grp'=2,'dp'=4,'sub'=4] {'sub'}, dimensions={1}, use_global_device_ids=true | all-gather | bytes 655360 | tf_op jit(solution)/shard_map/all_gather | solution.py:251
  53.2 6.5 %shard_map.123 = f32[64,1280]{1,0:T(8,128)} custom-call(bf16[64,4096]{1,0:T(8,128)(2,1)} %all_gather.3.rows_ref, bf16[4096,1280]{1,0:T(8,128)(2,1)} %weights_ref.2), custom_call_target="tpu_custom_call" | custom-call | tf_op jit(solution)/shard_map/pallas_call | solution.py:101
  59.7 1.0 convert_element_type.97
  60.7 0.1 collective-permute-start
  60.8 1.4 %collective-permute-done = bf16[64,1280]{1,0:T(8,128)(2,1)S(1)} collective-permute-done((bf16[64,1280]{1,0:T(8,128)(2,1)S(1)}, bf16[64,1280]{1,0:T(8,128)(2,1)S(1)}, u32[]{:S(2)}, u32[]{:S(2)}) %collective-permute-start) | collective-permute-done | bytes 163872 | tf_op jit(solution)/shard_map/ppermute | solution.py:115
  62.2 1.0 add_convert_fusion
  63.2 0.7 collective-permute-start.1
  63.9 0.0 collective-permute-done.3
  63.9 5.6 %collective-permute-done.1 = bf16[64,1280]{1,0:T(8,128)(2,1)S(1)} collective-permute-done((bf16[64,1280]{1,0:T(8,128)(2,1)S(1)}, bf16[64,1280]{1,0:T(8,128)(2,1)S(1)}, u32[]{:S(2)}, u32[]{:S(2)}) %collective-permute-start.1) | collective-permute-done | bytes 163872 | tf_op jit(solution)/shard_map/ppermute | solution.py:115
  69.5 0.0 slice-start
  69.5 0.2 multiply_reduce_fusion
  69.7 0.1 collective-permute-start.6
  69.8 0.0 slice-start.1
  69.8 4.9 %fusion.5 = f32[64,3072]{1,0:T(8,128)S(1)} fusion(bf16[1280,3072]{1,0:T(8,128)(2,1)} %param.20, f32[64,1280]{1,0:T(8,128)S(1)} %get-tuple-element.3, f32[1280]{0:T(1024)S(1)} %convert_element_type.106), kind=kOutput, calls=%fused_computation.32 | convolution fusion | flops 503480320 | bytes 8983552 | tf_op jit(solution)/shard_map/dot_general | solution.py:260
  74.7 2.1 %collective-permute-start.8 = (bf16[64,1536]{1,0:T(8,128)(2,1)S(1)}, bf16[64,1536]{1,0:T(8,128)(2,1)S(1)}, u32[]{:S(2)}, u32[]{:S(2)}) collective-permute-start(bf16[64,1536]{1,0:T(8,128)(2,1)S(1)} %select_convert_fusion), channel_id=1, source_target_pairs={{0,1},{1,0},{2,3},{3,2},{4,5},{5,4},{6,7},{7,6},{8,9},{9,8},{10,11... | collective-permute-start | bytes 589832 | tf_op jit(solution)/shard_map/ppermute | solution.py:115
  76.8 0.0 slice-done
  76.8 0.0 slice-done.1
  76.8 1.5 %fusion.6 = f32[64,3072]{1,0:T(8,128)S(1)} fusion(bf16[1280,3072]{1,0:T(8,128)(2,1)S(1)} %bitcast.57, f32[64,1280]{1,0:T(8,128)S(1)} %get-tuple-element.3, f32[1280]{0:T(1024)S(1)} %convert_element_type.106), kind=kOutput, calls=%fused_computation.33 | convolution fusion | flops 503480320 | bytes 8983552 | tf_op jit(solution)/shard_map/dot_general | solution.py:259
  78.3 0.1 collective-permute-start.4
  78.4 0.0 collective-permute-done.6
  78.4 1.4 %collective-permute-start.7 = (f32[64]{0:T(128)S(1)}, f32[64]{0:T(128)S(1)}, u32[]{:S(2)}, u32[]{:S(2)}) collective-permute-start(f32[64]{0:T(128)S(1)} %add.56), channel_id=1, source_target_pairs={{0,2},{1,3},{2,0},{3,1},{4,6},{5,7},{6,4},{7,5},{8,10},{9,11},{10,... | collective-permute-start | bytes 776 | tf_op jit(solution)/shard_map/ppermute | solution.py:115
  79.8 2.3 %collective-permute-done.8 = bf16[64,1536]{1,0:T(8,128)(2,1)S(1)} collective-permute-done((bf16[64,1536]{1,0:T(8,128)(2,1)S(1)}, bf16[64,1536]{1,0:T(8,128)(2,1)S(1)}, u32[]{:S(2)}, u32[]{:S(2)}) %collective-permute-start.8) | collective-permute-done | bytes 196640 | tf_op jit(solution)/shard_map/ppermute | solution.py:115
  82.1 0.1 convert_add_fusion
  82.2 1.9 %collective-permute-start.9 = (bf16[64,768]{1,0:T(8,128)(2,1)S(1)}, bf16[64,768]{1,0:T(8,128)(2,1)S(1)}, u32[]{:S(2)}, u32[]{:S(2)}) collective-permute-start(bf16[64,768]{1,0:T(8,128)(2,1)S(1)} %select_convert_fusion.2), channel_id=1, source_target_pairs={{0,2},{1,3},{2,0},{3,1},{4,6},{5,7},{6,4},{7,5},{8,10},{9,11},{10,... | collective-permute-start | bytes 294920 | tf_op jit(solution)/shard_map/ppermute | solution.py:115
  84.1 2.0 %collective-permute-done.4 = bf16[64,1536]{1,0:T(8,128)(2,1)S(1)} collective-permute-done((bf16[64,1536]{1,0:T(8,128)(2,1)S(1)}, bf16[64,1536]{1,0:T(8,128)(2,1)S(1)}, u32[]{:S(2)}, u32[]{:S(2)}) %collective-permute-start.4) | collective-permute-done | bytes 196640 | tf_op jit(solution)/shard_map/ppermute | solution.py:115
  86.2 0.1 convert_add_fusion.1
  86.2 1.4 %collective-permute-start.5 = (bf16[64,768]{1,0:T(8,128)(2,1)S(1)}, bf16[64,768]{1,0:T(8,128)(2,1)S(1)}, u32[]{:S(2)}, u32[]{:S(2)}) collective-permute-start(bf16[64,768]{1,0:T(8,128)(2,1)S(1)} %select_convert_fusion.3), channel_id=1, source_target_pairs={{0,2},{1,3},{2,0},{3,1},{4,6},{5,7},{6,4},{7,5},{8,10},{9,11},{10,... | collective-permute-start | bytes 294920 | tf_op jit(solution)/shard_map/ppermute | solution.py:115
  87.7 0.0 collective-permute-done.7
  87.7 0.1 collective-permute-done.9
  87.8 5.5 %collective-permute-done.5 = bf16[64,768]{1,0:T(8,128)(2,1)S(1)} collective-permute-done((bf16[64,768]{1,0:T(8,128)(2,1)S(1)}, bf16[64,768]{1,0:T(8,128)(2,1)S(1)}, u32[]{:S(2)}, u32[]{:S(2)}) %collective-permute-start.5) | collective-permute-done | bytes 98336 | tf_op jit(solution)/shard_map/ppermute | solution.py:115
  93.3 0.1 multiply_convert_fusion.1
  93.4 0.1 collective-permute-start.10
  93.5 6.4 %collective-permute-done.10 = bf16[64,768]{1,0:T(8,128)(2,1)S(1)} collective-permute-done((bf16[64,768]{1,0:T(8,128)(2,1)S(1)}, bf16[64,768]{1,0:T(8,128)(2,1)S(1)}, u32[]{:S(2)}, u32[]{:S(2)}) %collective-permute-start.10) | collective-permute-done | bytes 98336 | tf_op jit(solution)/shard_map/ppermute | solution.py:115
  99.9 0.1 collective-permute-start.11
  100.0 5.7 %collective-permute-done.11 = bf16[64,1536]{1,0:T(8,128)(2,1)S(1)} collective-permute-done((bf16[64,1536]{1,0:T(8,128)(2,1)S(1)}, bf16[64,1536]{1,0:T(8,128)(2,1)S(1)}, u32[]{:S(2)}, u32[]{:S(2)}) %collective-permute-start.11) | collective-permute-done | bytes 196640 | tf_op jit(solution)/shard_map/ppermute | solution.py:115
  105.6 0.8 maximum_select_fusion.rows_ref
  106.5 5.6 %shard_map.124 = f32[64,1280]{1,0:T(8,128)} custom-call(bf16[64,3072]{1,0:T(8,128)(2,1)} %maximum_select_fusion.rows_ref, bf16[3072,1280]{1,0:T(8,128)(2,1)} %weights_ref.3), custom_call_target="tpu_custom_call" | custom-call | tf_op jit(solution)/shard_map/pallas_call | solution.py:101
  112.0 1.0 fusion.3
  113.1 0.1 collective-permute-start.12
  113.2 1.2 %collective-permute-done.12 = bf16[2,16,1280]{2,1,0:T(8,128)(2,1)S(1)} collective-permute-done((bf16[2,16,1280]{2,1,0:T(8,128)(2,1)S(1)}, bf16[2,16,1280]{2,1,0:T(8,128)(2,1)S(1)}, u32[]{:S(2)}, u32[]{:S(2)}) %collective-permute-start.12) | collective-permute-done | bytes 81952 | tf_op jit(solution)/shard_map/ppermute | solution.py:115
  114.4 1.0 fusion.2
  115.4 0.7 collective-permute-start.13
  116.2 0.6 dynamic-slice_convert_fusion
  116.8 2.7 %collective-permute-done.13 = bf16[1,16,1280]{2,1,0:T(8,128)(2,1)S(1)} collective-permute-done((bf16[1,16,1280]{2,1,0:T(8,128)(2,1)S(1)}, bf16[1,16,1280]{2,1,0:T(8,128)(2,1)S(1)}, u32[]{:S(2)}, u32[]{:S(2)}) %collective-permute-start.13) | collective-permute-done | bytes 40992 | tf_op jit(solution)/shard_map/ppermute | solution.py:115
  119.5 0.6 fusion.4
  (15 shorter events, 0.3 us)
Async XLA Ops:
  0.6 35.6 %copy-start = (bf16[8,512,128]{2,1,0:T(8,128)(2,1)S(1)}, bf16[8,512,128]{2,1,0:T(8,128)(2,1)}, u32[]{:S(2)}) copy-start(bf16[8,512,128]{2,1,0:T(8,128)(2,1)} %param.16) | copy-start | bytes 3145732
  0.6 1.2 copy-start.1
  1.8 0.7 copy-start.2
  2.5 0.7 copy-start.3
  3.1 17.4 %copy-start.4 = (bf16[16,1280]{1,0:T(8,128)(2,1)S(1)}, bf16[16,1280]{1,0:T(8,128)(2,1)}, u32[]{:S(2)}) copy-start(bf16[16,1280]{1,0:T(8,128)(2,1)} %param.11) | copy-start | bytes 122884
  3.1 19.4 %copy-start.5 = (bf16[1280]{0:T(1024)(128)(2,1)S(1)}, bf16[1280]{0:T(1024)(128)(2,1)}, u32[]{:S(2)}) copy-start(bf16[1280]{0:T(1024)(128)(2,1)} %param.18) | copy-start | bytes 7684
  13.2 23.1 %all-to-all-start = ((bf16[16,32,512]{2,1,0:T(8,128)(2,1)}), bf16[16,32,512]{2,1,0:T(8,128)(2,1)S(1)}, u32[]{:S(2)}, u32[]{:S(2)}) async-start(bf16[16,32,512]{2,1,0:T(8,128)(2,1)} %shard_map.122), calls=%async_computation | async-start | bytes 1048576 | tf_op jit(solution)/shard_map/all_to_all | solution.py:246
  20.6 7.2 %collective-permute-start.2 = (bf16[1,16,1280]{2,1,0:T(8,128)(2,1)S(1)}, bf16[1,16,1280]{2,1,0:T(8,128)(2,1)S(1)}, u32[]{:S(2)}, u32[]{:S(2)}) collective-permute-start(bf16[1,16,1280]{2,1,0:T(8,128)(2,1)S(1)} %bitcast.63), channel_id=1, source_target_pairs={{0,8},{4,12},{8,0},{12,4},{1,9},{5,13},{9,1},{13,5},{2,10},{6,14},... | collective-permute-start | bytes 122888 | tf_op jit(solution)/shard_map/ppermute | solution.py:115
  27.8 36.1 %collective-permute-start.3 = (bf16[2,16,1280]{2,1,0:T(8,128)(2,1)S(1)}, bf16[2,16,1280]{2,1,0:T(8,128)(2,1)S(1)}, u32[]{:S(2)}, u32[]{:S(2)}) collective-permute-start(bf16[2,16,1280]{2,1,0:T(8,128)(2,1)S(1)} %maximum_select_fusion.3), channel_id=1, source_target_pairs={{0,4},{4,0},{8,12},{12,8},{1,5},{5,1},{9,13},{13,9},{2,6},{6,2},{1... | collective-permute-start | bytes 245768 | tf_op jit(solution)/shard_map/ppermute | solution.py:115
  60.7 1.5 %collective-permute-start = (bf16[64,1280]{1,0:T(8,128)(2,1)S(1)}, bf16[64,1280]{1,0:T(8,128)(2,1)S(1)}, u32[]{:S(2)}, u32[]{:S(2)}) collective-permute-start(bf16[64,1280]{1,0:T(8,128)(2,1)S(1)} %convert_element_type.97), channel_id=1, source_target_pairs={{0,4},{4,0},{8,12},{12,8},{1,5},{5,1},{9,13},{13,9},{2,6},{6,2},{1... | collective-permute-start | bytes 491528 | tf_op jit(solution)/shard_map/ppermute | solution.py:115
  63.2 6.3 %collective-permute-start.1 = (bf16[64,1280]{1,0:T(8,128)(2,1)S(1)}, bf16[64,1280]{1,0:T(8,128)(2,1)S(1)}, u32[]{:S(2)}, u32[]{:S(2)}) collective-permute-start(bf16[64,1280]{1,0:T(8,128)(2,1)S(1)} %add_convert_fusion), channel_id=1, source_target_pairs={{0,8},{4,12},{8,0},{12,4},{1,9},{5,13},{9,1},{13,5},{2,10},{6,14},... | collective-permute-start | bytes 491528 | tf_op jit(solution)/shard_map/ppermute | solution.py:115
  69.5 7.3 %slice-start = ((s8[7864320]{0:T(1024)(128)(4,1)}), s8[4194304]{0:T(1024)(128)(4,1)S(1)}, s32[]{:S(2)}) async-start(s8[7864320]{0:T(1024)(128)(4,1)} %bitcast.56), calls=%async_computation.1 | async-start | bytes 8388608
  69.7 8.7 %collective-permute-start.6 = (f32[64]{0:T(128)S(1)}, f32[64]{0:T(128)S(1)}, u32[]{:S(2)}, u32[]{:S(2)}) collective-permute-start(f32[64]{0:T(128)S(1)} %get-tuple-element.2), channel_id=1, source_target_pairs={{0,1},{1,0},{2,3},{3,2},{4,5},{5,4},{6,7},{7,6},{8,9},{9,8},{10,11... | collective-permute-start | bytes 776 | tf_op jit(solution)/shard_map/ppermute | solution.py:115
  69.8 7.0 %slice-start.1 = ((s8[7864320]{0:T(1024)(128)(4,1)}), s8[3670016]{0:T(1024)(128)(4,1)S(1)}, s32[]{:S(2)}) async-start(s8[7864320]{0:T(1024)(128)(4,1)} %bitcast.56), calls=%async_computation.2 | async-start | bytes 7340032
  74.7 7.4 %collective-permute-start.8 = (bf16[64,1536]{1,0:T(8,128)(2,1)S(1)}, bf16[64,1536]{1,0:T(8,128)(2,1)S(1)}, u32[]{:S(2)}, u32[]{:S(2)}) collective-permute-start(bf16[64,1536]{1,0:T(8,128)(2,1)S(1)} %select_convert_fusion), channel_id=1, source_target_pairs={{0,1},{1,0},{2,3},{3,2},{4,5},{5,4},{6,7},{7,6},{8,9},{9,8},{10,11... | collective-permute-start | bytes 589832 | tf_op jit(solution)/shard_map/ppermute | solution.py:115
  78.3 7.9 %collective-permute-start.4 = (bf16[64,1536]{1,0:T(8,128)(2,1)S(1)}, bf16[64,1536]{1,0:T(8,128)(2,1)S(1)}, u32[]{:S(2)}, u32[]{:S(2)}) collective-permute-start(bf16[64,1536]{1,0:T(8,128)(2,1)S(1)} %select_convert_fusion.1), channel_id=1, source_target_pairs={{0,1},{1,0},{2,3},{3,2},{4,5},{5,4},{6,7},{7,6},{8,9},{9,8},{10,11... | collective-permute-start | bytes 589832 | tf_op jit(solution)/shard_map/ppermute | solution.py:115
  78.4 9.3 %collective-permute-start.7 = (f32[64]{0:T(128)S(1)}, f32[64]{0:T(128)S(1)}, u32[]{:S(2)}, u32[]{:S(2)}) collective-permute-start(f32[64]{0:T(128)S(1)} %add.56), channel_id=1, source_target_pairs={{0,2},{1,3},{2,0},{3,1},{4,6},{5,7},{6,4},{7,5},{8,10},{9,11},{10,... | collective-permute-start | bytes 776 | tf_op jit(solution)/shard_map/ppermute | solution.py:115
  82.2 5.6 %collective-permute-start.9 = (bf16[64,768]{1,0:T(8,128)(2,1)S(1)}, bf16[64,768]{1,0:T(8,128)(2,1)S(1)}, u32[]{:S(2)}, u32[]{:S(2)}) collective-permute-start(bf16[64,768]{1,0:T(8,128)(2,1)S(1)} %select_convert_fusion.2), channel_id=1, source_target_pairs={{0,2},{1,3},{2,0},{3,1},{4,6},{5,7},{6,4},{7,5},{8,10},{9,11},{10,... | collective-permute-start | bytes 294920 | tf_op jit(solution)/shard_map/ppermute | solution.py:115
  86.2 7.0 %collective-permute-start.5 = (bf16[64,768]{1,0:T(8,128)(2,1)S(1)}, bf16[64,768]{1,0:T(8,128)(2,1)S(1)}, u32[]{:S(2)}, u32[]{:S(2)}) collective-permute-start(bf16[64,768]{1,0:T(8,128)(2,1)S(1)} %select_convert_fusion.3), channel_id=1, source_target_pairs={{0,2},{1,3},{2,0},{3,1},{4,6},{5,7},{6,4},{7,5},{8,10},{9,11},{10,... | collective-permute-start | bytes 294920 | tf_op jit(solution)/shard_map/ppermute | solution.py:115
  93.4 6.4 %collective-permute-start.10 = (bf16[64,768]{1,0:T(8,128)(2,1)S(1)}, bf16[64,768]{1,0:T(8,128)(2,1)S(1)}, u32[]{:S(2)}, u32[]{:S(2)}) collective-permute-start(bf16[64,768]{1,0:T(8,128)(2,1)S(1)} %multiply_convert_fusion.1), channel_id=1, source_target_pairs={{0,2},{1,3},{2,0},{3,1},{4,6},{5,7},{6,4},{7,5},{8,10},{9,11},{10,... | collective-permute-start | bytes 294920 | tf_op jit(solution)/shard_map/ppermute | solution.py:115
  99.9 5.7 %collective-permute-start.11 = (bf16[64,1536]{1,0:T(8,128)(2,1)S(1)}, bf16[64,1536]{1,0:T(8,128)(2,1)S(1)}, u32[]{:S(2)}, u32[]{:S(2)}) collective-permute-start(bf16[64,1536]{1,0:T(8,128)(2,1)S(1)} %maximum_select_fusion.1), channel_id=1, source_target_pairs={{0,1},{1,0},{2,3},{3,2},{4,5},{5,4},{6,7},{7,6},{8,9},{9,8},{10,11... | collective-permute-start | bytes 589832 | tf_op jit(solution)/shard_map/ppermute | solution.py:115
  113.1 1.3 %collective-permute-start.12 = (bf16[2,16,1280]{2,1,0:T(8,128)(2,1)S(1)}, bf16[2,16,1280]{2,1,0:T(8,128)(2,1)S(1)}, u32[]{:S(2)}, u32[]{:S(2)}) collective-permute-start(bf16[2,16,1280]{2,1,0:T(8,128)(2,1)S(1)} %fusion.3), channel_id=1, source_target_pairs={{0,4},{4,0},{8,12},{12,8},{1,5},{5,1},{9,13},{13,9},{2,6},{6,2},{1... | collective-permute-start | bytes 245768 | tf_op jit(solution)/shard_map/ppermute | solution.py:115
  115.4 4.1 %collective-permute-start.13 = (bf16[1,16,1280]{2,1,0:T(8,128)(2,1)S(1)}, bf16[1,16,1280]{2,1,0:T(8,128)(2,1)S(1)}, u32[]{:S(2)}, u32[]{:S(2)}) collective-permute-start(bf16[1,16,1280]{2,1,0:T(8,128)(2,1)S(1)} %fusion.7), channel_id=1, source_target_pairs={{0,8},{4,12},{8,0},{12,4},{1,9},{5,13},{9,1},{13,5},{2,10},{6,14},... | collective-permute-start | bytes 122888 | tf_op jit(solution)/shard_map/ppermute | solution.py:115

commit v13 on v11

--- a/solution.py
+++ b/solution.py
@@ -15,7 +15,7 @@
 masked_score = -1e30
 
 
-def attend_kernel(page_table, lengths, queries, cache_pool, contexts, keys, copy_sems,
+def attend_kernel(page_table, lengths, queries, cache_pool, contexts, keys, finished, copy_sems,
                   *, latent, score_scale):
     req_dev, pages_req = page_table.shape
     page_size = cache_pool.shape[2]
@@ -56,9 +56,11 @@
             (((1,), (1,)), ((), ())),
             preferred_element_type=jnp.float32,
         )
-        blocks, block_heads = contexts.shape[0], head_count // contexts.shape[0]
-        context = (weighted / denominator).reshape(blocks, block_heads, latent)
-        contexts[:, slot * block_heads:(slot + 1) * block_heads, :] = context.astype(contexts.dtype)
+        finished[slot] = weighted / denominator
+    blocks, block_heads = contexts.shape[0], head_count // contexts.shape[0]
+    for block in range(blocks):
+        rows = finished[:, block * block_heads:(block + 1) * block_heads, :]
+        contexts[block] = rows.reshape(req_dev * block_heads, latent).astype(contexts.dtype)
 
 
 def attend_all(queries, page_table, lengths, cache_pool, latent, score_scale, blocks):
@@ -80,6 +82,7 @@
         out_specs=pl.BlockSpec(memory_space=pltpu.VMEM),
         scratch_shapes=[
             pltpu.VMEM((req_dev, width, pages_req * page_size), jnp.bfloat16),
+            pltpu.VMEM((req_dev, head_count, latent), jnp.float32),
             pltpu.SemaphoreType.DMA((req_dev * pages_req,)),
         ],
         compiler_params=pltpu.CompilerParams(vmem_limit_bytes=48 * 1024 * 1024),

time: 111 us -> 111 us (level)
  no operation moved by 1% of the time
where the time goes in v13:
time: 111 us; the launch traced here: 110 us
  waiting for transfers between devices  46.8 us (42%)
  starting transfers between devices  17.7 us (16%)
  blocking collectives  16.2 us (15%)
  matrix products  14.1 us (13%)
  Pallas kernels  10 us (9%)
  local copies, waits for them, and re-layouts  3.16 us (3%)
  other arithmetic  1.45 us (1%)
    ppermute x14, waiting for transfers between devices, swap_with(): return lax.ppermute(x, axis, [(i, i ^ distance) for i in range(size)])  38.5 us
    all_gather x1, blocking collectives, shards(): group_values = lax.all_gather(values, 'sub', axis=1, tiled=True)  16.2 us
    ppermute x14, starting transfers between devices, swap_with(): return lax.ppermute(x, axis, [(i, i ^ distance) for i in range(size)])  10.4 us
    pallas_call x1, Pallas kernels, attend_all(): pl.pallas_call(kernel, out_shape=jax.ShapeDtypeStruct((blocks, req_dev *...  10 us
    all_to_all x1, waiting for transfers between devices, shards(): lax.all_to_all(contexts, ('dp', 'sub'), split_axis=0, concat_axis=0, tile...  8.35 us
    all_to_all x1, starting transfers between devices, shards(): lax.all_to_all(contexts, ('dp', 'sub'), split_axis=0, concat_axis=0, tile...  7.36 us
    dot_general x1, matrix products, shards(): jnp.dot(group_values, out_proj, preferred_element_type=jnp.float32)  6.04 us
    dot_general x1, matrix products, shards(): jnp.dot(hidden_units, down_proj, preferred_element_type=jnp.float32)  4.7 us
  transfers between devices with their start and end apart: 15, of which 12 were waited for; matrix products, arithmetic and copies ran while one was open for 9% of the time, Pallas kernels for 0%

profile of v13, /device:TPU:0, one launch (start us, length us, event | category | flops | bytes accessed | tf_op | source)
XLA Modules:
  0.0 110.4 jit_solution(10612845508230078900)
XLA Ops:
  0.6 0.0 copy-start
  0.6 0.0 copy-start.1
  0.7 1.1 %copy-done.1 = bf16[4,128,576]{1,2,0:T(8,128)(2,1)S(1)} copy-done((bf16[4,128,576]{1,2,0:T(8,128)(2,1)S(1)}, bf16[4,128,576]{1,2,0:T(8,128)(2,1)}, u32[]{:S(2)}) %copy-start.1) | copy-done | bytes 589848
  1.8 0.0 copy-start.2
  1.8 0.7 copy-done.2
  2.5 0.0 copy-start.3
  2.5 0.7 copy-done.3
  3.1 0.0 copy-start.4
  3.1 0.0 copy-start.5
  3.1 10.0 %shard_map.122 = bf16[16,32,512]{2,1,0:T(8,128)(2,1)} custom-call(s32[4,16]{1,0:T(4,128)S(1)} %copy-done.2, s32[4]{0:T(128)S(1)} %copy-done.3, bf16[4,576,128]{2,1,0:T(8,128)(2,1)S(1)} %bitcast.58, bf16[64,576,128]{2,1,0:T(8,128)(2,1)} %bitcast.63), custom_call_target="tpu_custom_call" | custom-call | tf_op jit(solution)/shard_map/pallas_call | solution.py:73
  13.2 7.4 %all-to-all-start = ((bf16[16,32,512]{2,1,0:T(8,128)(2,1)}), bf16[16,32,512]{2,1,0:T(8,128)(2,1)S(1)}, u32[]{:S(2)}, u32[]{:S(2)}) async-start(bf16[16,32,512]{2,1,0:T(8,128)(2,1)} %shard_map.122), calls=%async_computation | async-start | bytes 1048576 | tf_op jit(solution)/shard_map/all_to_all | solution.py:224
  20.6 0.0 copy-done.4
  20.6 2.0 %collective-permute-start.2 = (bf16[1,16,1280]{2,1,0:T(8,128)(2,1)S(1)}, bf16[1,16,1280]{2,1,0:T(8,128)(2,1)S(1)}, u32[]{:S(2)}, u32[]{:S(2)}) collective-permute-start(bf16[1,16,1280]{2,1,0:T(8,128)(2,1)S(1)} %bitcast.68), channel_id=1, source_target_pairs={{0,8},{4,12},{8,0},{12,4},{1,9},{5,13},{9,1},{13,5},{2,10},{6,14},... | collective-permute-start | bytes 122888 | tf_op jit(solution)/shard_map/ppermute | solution.py:93
  22.6 0.0 copy-done.5
  22.6 5.2 %collective-permute-done.2 = bf16[1,16,1280]{2,1,0:T(8,128)(2,1)S(1)} collective-permute-done((bf16[1,16,1280]{2,1,0:T(8,128)(2,1)S(1)}, bf16[1,16,1280]{2,1,0:T(8,128)(2,1)S(1)}, u32[]{:S(2)}, u32[]{:S(2)}) %collective-permute-start.2) | collective-permute-done | bytes 40992 | tf_op jit(solution)/shard_map/ppermute | solution.py:93
  27.8 0.1 collective-permute-start.3
  27.9 8.3 %all-to-all-done = bf16[16,32,512]{2,1,0:T(8,128)(2,1)S(1)} async-done(((bf16[16,32,512]{2,1,0:T(8,128)(2,1)}), bf16[16,32,512]{2,1,0:T(8,128)(2,1)S(1)}, u32[]{:S(2)}, u32[]{:S(2)}) %all-to-all-start) | async-done | bytes 524320 | tf_op jit(solution)/shard_map/all_to_all | solution.py:224
  36.2 0.0 copy-done
  36.2 0.4 fusion
  36.7 0.0 slice-start
  36.7 16.2 %all_gather.3 = bf16[64,4096]{1,0:T(8,128)(2,1)S(1)} all-gather(bf16[64,1024]{1,0:T(8,128)(2,1)S(1)} %bitcast.67), channel_id=1, replica_groups=mesh['grp'=2,'dp'=4,'sub'=4] {'sub'}, dimensions={1}, use_global_device_ids=true | all-gather | bytes 655360 | tf_op jit(solution)/shard_map/all_gather | solution.py:229
  52.9 0.0 slice-start.1
  52.9 6.0 %convolution_convert_fusion = bf16[64,1280]{1,0:T(8,128)(2,1)S(1)} fusion(bf16[64,4096]{1,0:T(8,128)(2,1)S(1)} %all_gather.3, bf16[4096,1280]{1,0:T(8,128)(2,1)} %param.17), kind=kOutput, calls=%fused_computation | convolution fusion | flops 671170560 | bytes 11173888 | tf_op jit(solution)/shard_map/dot_general | solution.py:233
  58.9 0.1 collective-permute-start
  59.0 1.4 %collective-permute-done = bf16[64,1280]{1,0:T(8,128)(2,1)S(1)} collective-permute-done((bf16[64,1280]{1,0:T(8,128)(2,1)S(1)}, bf16[64,1280]{1,0:T(8,128)(2,1)S(1)}, u32[]{:S(2)}, u32[]{:S(2)}) %collective-permute-start) | collective-permute-done | bytes 163872 | tf_op jit(solution)/shard_map/ppermute | solution.py:93
  60.4 0.7 collective-permute-start.1
  61.1 0.0 collective-permute-done.3
  61.1 5.6 %collective-permute-done.1 = bf16[64,1280]{1,0:T(8,128)(2,1)S(1)} collective-permute-done((bf16[64,1280]{1,0:T(8,128)(2,1)S(1)}, bf16[64,1280]{1,0:T(8,128)(2,1)S(1)}, u32[]{:S(2)}, u32[]{:S(2)}) %collective-permute-start.1) | collective-permute-done | bytes 163872 | tf_op jit(solution)/shard_map/ppermute | solution.py:93
  66.7 0.0 slice-start.2
  66.7 0.2 multiply_reduce_fusion
  66.9 0.1 collective-permute-start.6
  67.0 0.0 slice-done
  67.0 0.0 slice-done.1
  67.0 0.0 slice-start.3
  67.0 1.5 %fusion.12 = f32[64,3072]{1,0:T(8,128)S(1)} fusion(bf16[1280,3072]{1,0:T(8,128)(2,1)S(1)} %bitcast.60, f32[64,1280]{1,0:T(8,128)S(1)} %get-tuple-element.3, f32[1280]{0:T(1024)S(1)} %convert_element_type.106), kind=kOutput, calls=%fused_computation.40 | convolution fusion | flops 503480320 | bytes 8983552 | tf_op jit(solution)/shard_map/dot_general | solution.py:240
  68.6 2.0 %collective-permute-start.8 = (bf16[64,1536]{1,0:T(8,128)(2,1)S(1)}, bf16[64,1536]{1,0:T(8,128)(2,1)S(1)}, u32[]{:S(2)}, u32[]{:S(2)}) collective-permute-start(bf16[64,1536]{1,0:T(8,128)(2,1)S(1)} %select_convert_fusion), channel_id=1, source_target_pairs={{0,1},{1,0},{2,3},{3,2},{4,5},{5,4},{6,7},{7,6},{8,9},{9,8},{10,11... | collective-permute-start | bytes 589832 | tf_op jit(solution)/shard_map/ppermute | solution.py:93
  70.6 0.0 slice-done.2
  70.6 0.0 slice-done.3
  70.6 1.5 %fusion.13 = f32[64,3072]{1,0:T(8,128)S(1)} fusion(bf16[1280,3072]{1,0:T(8,128)(2,1)S(1)} %bitcast.62, f32[64,1280]{1,0:T(8,128)S(1)} %get-tuple-element.3, f32[1280]{0:T(1024)S(1)} %convert_element_type.106), kind=kOutput, calls=%fused_computation.41 | convolution fusion | flops 503480320 | bytes 8983552 | tf_op jit(solution)/shard_map/dot_general | solution.py:239
  72.2 0.5 collective-permute-start.4
  72.7 0.0 collective-permute-done.6
  72.7 0.9 collective-permute-start.7
  73.6 2.4 %collective-permute-done.8 = bf16[64,1536]{1,0:T(8,128)(2,1)S(1)} collective-permute-done((bf16[64,1536]{1,0:T(8,128)(2,1)S(1)}, bf16[64,1536]{1,0:T(8,128)(2,1)S(1)}, u32[]{:S(2)}, u32[]{:S(2)}) %collective-permute-start.8) | collective-permute-done | bytes 196640 | tf_op jit(solution)/shard_map/ppermute | solution.py:93
  76.0 0.1 convert_add_fusion
  76.1 1.7 %collective-permute-start.9 = (bf16[64,768]{1,0:T(8,128)(2,1)S(1)}, bf16[64,768]{1,0:T(8,128)(2,1)S(1)}, u32[]{:S(2)}, u32[]{:S(2)}) collective-permute-start(bf16[64,768]{1,0:T(8,128)(2,1)S(1)} %select_convert_fusion.2), channel_id=1, source_target_pairs={{0,2},{1,3},{2,0},{3,1},{4,6},{5,7},{6,4},{7,5},{8,10},{9,11},{10,... | collective-permute-start | bytes 294920 | tf_op jit(solution)/shard_map/ppermute | solution.py:93
  77.8 2.2 %collective-permute-done.4 = bf16[64,1536]{1,0:T(8,128)(2,1)S(1)} collective-permute-done((bf16[64,1536]{1,0:T(8,128)(2,1)S(1)}, bf16[64,1536]{1,0:T(8,128)(2,1)S(1)}, u32[]{:S(2)}, u32[]{:S(2)}) %collective-permute-start.4) | collective-permute-done | bytes 196640 | tf_op jit(solution)/shard_map/ppermute | solution.py:93
  80.0 0.1 convert_add_fusion.1
  80.1 1.4 %collective-permute-start.5 = (bf16[64,768]{1,0:T(8,128)(2,1)S(1)}, bf16[64,768]{1,0:T(8,128)(2,1)S(1)}, u32[]{:S(2)}, u32[]{:S(2)}) collective-permute-start(bf16[64,768]{1,0:T(8,128)(2,1)S(1)} %select_convert_fusion.3), channel_id=1, source_target_pairs={{0,2},{1,3},{2,0},{3,1},{4,6},{5,7},{6,4},{7,5},{8,10},{9,11},{10,... | collective-permute-start | bytes 294920 | tf_op jit(solution)/shard_map/ppermute | solution.py:93
  81.5 0.0 collective-permute-done.7
  81.5 0.1 collective-permute-done.9
  81.7 5.5 %collective-permute-done.5 = bf16[64,768]{1,0:T(8,128)(2,1)S(1)} collective-permute-done((bf16[64,768]{1,0:T(8,128)(2,1)S(1)}, bf16[64,768]{1,0:T(8,128)(2,1)S(1)}, u32[]{:S(2)}, u32[]{:S(2)}) %collective-permute-start.5) | collective-permute-done | bytes 98336 | tf_op jit(solution)/shard_map/ppermute | solution.py:93
  87.1 0.1 multiply_convert_fusion.1
  87.3 0.1 collective-permute-start.10
  87.4 6.4 %collective-permute-done.10 = bf16[64,768]{1,0:T(8,128)(2,1)S(1)} collective-permute-done((bf16[64,768]{1,0:T(8,128)(2,1)S(1)}, bf16[64,768]{1,0:T(8,128)(2,1)S(1)}, u32[]{:S(2)}, u32[]{:S(2)}) %collective-permute-start.10) | collective-permute-done | bytes 98336 | tf_op jit(solution)/shard_map/ppermute | solution.py:93
  93.8 0.1 collective-permute-start.11
  93.9 5.7 %collective-permute-done.11 = bf16[64,1536]{1,0:T(8,128)(2,1)S(1)} collective-permute-done((bf16[64,1536]{1,0:T(8,128)(2,1)S(1)}, bf16[64,1536]{1,0:T(8,128)(2,1)S(1)}, u32[]{:S(2)}, u32[]{:S(2)}) %collective-permute-start.11) | collective-permute-done | bytes 196640 | tf_op jit(solution)/shard_map/ppermute | solution.py:93
  99.5 4.7 %fusion.2 = f32[64,1280]{1,0:T(8,128)S(1)} fusion(bf16[3072,1280]{1,0:T(8,128)(2,1)} %param.21, bf16[64,1536]{1,0:T(8,128)(2,1)S(1)} %maximum_select_fusion.2, bf16[64,1536]{1,0:T(8,128)(2,1)S(1)} %collective-permute-done.11, pred[]{:T(512)S(6)} %ne.18), kind=kOutput, calls=%fused_computation.5 | convolution fusion | flops 505085952 | bytes 8585217 | tf_op jit(solution)/shard_map/dot_general | solution.py:246
  104.2 0.1 collective-permute-start.12
  104.4 1.2 %collective-permute-done.12 = bf16[2,16,1280]{2,1,0:T(8,128)(2,1)S(1)} collective-permute-done((bf16[2,16,1280]{2,1,0:T(8,128)(2,1)S(1)}, bf16[2,16,1280]{2,1,0:T(8,128)(2,1)S(1)}, u32[]{:S(2)}, u32[]{:S(2)}) %collective-permute-start.12) | collective-permute-done | bytes 81952 | tf_op jit(solution)/shard_map/ppermute | solution.py:93
  105.6 0.7 collective-permute-start.13
  106.4 0.6 dynamic-slice_convert_fusion
  107.0 2.7 %collective-permute-done.13 = bf16[1,16,1280]{2,1,0:T(8,128)(2,1)S(1)} collective-permute-done((bf16[1,16,1280]{2,1,0:T(8,128)(2,1)S(1)}, bf16[1,16,1280]{2,1,0:T(8,128)(2,1)S(1)}, u32[]{:S(2)}, u32[]{:S(2)}) %collective-permute-start.13) | collective-permute-done | bytes 40992 | tf_op jit(solution)/shard_map/ppermute | solution.py:93
  109.7 0.6 fusion.11
  (19 shorter events, 0.4 us)
Async XLA Ops:
  0.6 35.6 %copy-start = (bf16[8,512,128]{2,1,0:T(8,128)(2,1)S(1)}, bf16[8,512,128]{2,1,0:T(8,128)(2,1)}, u32[]{:S(2)}) copy-start(bf16[8,512,128]{2,1,0:T(8,128)(2,1)} %param.16) | copy-start | bytes 3145732
  0.6 1.2 %copy-start.1 = (bf16[4,128,576]{1,2,0:T(8,128)(2,1)S(1)}, bf16[4,128,576]{1,2,0:T(8,128)(2,1)}, u32[]{:S(2)}) copy-start(bf16[4,128,576]{1,2,0:T(8,128)(2,1)} %param.12) | copy-start | bytes 1769476
  1.8 0.7 copy-start.2
  2.5 0.7 copy-start.3
  3.1 17.4 %copy-start.4 = (bf16[16,1280]{1,0:T(8,128)(2,1)S(1)}, bf16[16,1280]{1,0:T(8,128)(2,1)}, u32[]{:S(2)}) copy-start(bf16[16,1280]{1,0:T(8,128)(2,1)} %param.11) | copy-start | bytes 122884
  3.1 19.4 %copy-start.5 = (bf16[1280]{0:T(1024)(128)(2,1)S(1)}, bf16[1280]{0:T(1024)(128)(2,1)}, u32[]{:S(2)}) copy-start(bf16[1280]{0:T(1024)(128)(2,1)} %param.18) | copy-start | bytes 7684
  13.2 23.1 %all-to-all-start = ((bf16[16,32,512]{2,1,0:T(8,128)(2,1)}), bf16[16,32,512]{2,1,0:T(8,128)(2,1)S(1)}, u32[]{:S(2)}, u32[]{:S(2)}) async-start(bf16[16,32,512]{2,1,0:T(8,128)(2,1)} %shard_map.122), calls=%async_computation | async-start | bytes 1048576 | tf_op jit(solution)/shard_map/all_to_all | solution.py:224
  20.6 7.2 %collective-permute-start.2 = (bf16[1,16,1280]{2,1,0:T(8,128)(2,1)S(1)}, bf16[1,16,1280]{2,1,0:T(8,128)(2,1)S(1)}, u32[]{:S(2)}, u32[]{:S(2)}) collective-permute-start(bf16[1,16,1280]{2,1,0:T(8,128)(2,1)S(1)} %bitcast.68), channel_id=1, source_target_pairs={{0,8},{4,12},{8,0},{12,4},{1,9},{5,13},{9,1},{13,5},{2,10},{6,14},... | collective-permute-start | bytes 122888 | tf_op jit(solution)/shard_map/ppermute | solution.py:93
  27.8 33.3 %collective-permute-start.3 = (bf16[2,16,1280]{2,1,0:T(8,128)(2,1)S(1)}, bf16[2,16,1280]{2,1,0:T(8,128)(2,1)S(1)}, u32[]{:S(2)}, u32[]{:S(2)}) collective-permute-start(bf16[2,16,1280]{2,1,0:T(8,128)(2,1)S(1)} %maximum_select_fusion.4), channel_id=1, source_target_pairs={{0,4},{4,0},{8,12},{12,8},{1,5},{5,1},{9,13},{13,9},{2,6},{6,2},{1... | collective-permute-start | bytes 245768 | tf_op jit(solution)/shard_map/ppermute | solution.py:93
  36.7 30.3 %slice-start = ((s8[7864320]{0:T(1024)(128)(4,1)}), s8[4194304]{0:T(1024)(128)(4,1)S(1)}, s32[]{:S(2)}) async-start(s8[7864320]{0:T(1024)(128)(4,1)} %bitcast.59), calls=%async_computation.1 | async-start | bytes 8388608
  52.9 14.1 %slice-start.1 = ((s8[7864320]{0:T(1024)(128)(4,1)}), s8[3670016]{0:T(1024)(128)(4,1)S(1)}, s32[]{:S(2)}) async-start(s8[7864320]{0:T(1024)(128)(4,1)} %bitcast.59), calls=%async_computation.2 | async-start | bytes 7340032
  58.9 1.5 %collective-permute-start = (bf16[64,1280]{1,0:T(8,128)(2,1)S(1)}, bf16[64,1280]{1,0:T(8,128)(2,1)S(1)}, u32[]{:S(2)}, u32[]{:S(2)}) collective-permute-start(bf16[64,1280]{1,0:T(8,128)(2,1)S(1)} %convolution_convert_fusion), channel_id=1, source_target_pairs={{0,4},{4,0},{8,12},{12,8},{1,5},{5,1},{9,13},{13,9},{2,6},{6,2},{1... | collective-permute-start | bytes 491528 | tf_op jit(solution)/shard_map/ppermute | solution.py:93
  60.4 6.3 %collective-permute-start.1 = (bf16[64,1280]{1,0:T(8,128)(2,1)S(1)}, bf16[64,1280]{1,0:T(8,128)(2,1)S(1)}, u32[]{:S(2)}, u32[]{:S(2)}) collective-permute-start(bf16[64,1280]{1,0:T(8,128)(2,1)S(1)} %add_convert_fusion), channel_id=1, source_target_pairs={{0,8},{4,12},{8,0},{12,4},{1,9},{5,13},{9,1},{13,5},{2,10},{6,14},... | collective-permute-start | bytes 491528 | tf_op jit(solution)/shard_map/ppermute | solution.py:93
  66.7 3.9 %slice-start.2 = ((s8[7864320]{0:T(1024)(128)(4,1)}), s8[4194304]{0:T(1024)(128)(4,1)S(1)}, s32[]{:S(2)}) async-start(s8[7864320]{0:T(1024)(128)(4,1)} %bitcast.61), calls=%async_computation.3 | async-start | bytes 8388608
  66.9 5.7 %collective-permute-start.6 = (f32[64]{0:T(128)S(1)}, f32[64]{0:T(128)S(1)}, u32[]{:S(2)}, u32[]{:S(2)}) collective-permute-start(f32[64]{0:T(128)S(1)} %get-tuple-element.2), channel_id=1, source_target_pairs={{0,1},{1,0},{2,3},{3,2},{4,5},{5,4},{6,7},{7,6},{8,9},{9,8},{10,11... | collective-permute-start | bytes 776 | tf_op jit(solution)/shard_map/ppermute | solution.py:93
  67.0 3.6 %slice-start.3 = ((s8[7864320]{0:T(1024)(128)(4,1)}), s8[3670016]{0:T(1024)(128)(4,1)S(1)}, s32[]{:S(2)}) async-start(s8[7864320]{0:T(1024)(128)(4,1)} %bitcast.61), calls=%async_computation.4 | async-start | bytes 7340032
  68.6 7.4 %collective-permute-start.8 = (bf16[64,1536]{1,0:T(8,128)(2,1)S(1)}, bf16[64,1536]{1,0:T(8,128)(2,1)S(1)}, u32[]{:S(2)}, u32[]{:S(2)}) collective-permute-start(bf16[64,1536]{1,0:T(8,128)(2,1)S(1)} %select_convert_fusion), channel_id=1, source_target_pairs={{0,1},{1,0},{2,3},{3,2},{4,5},{5,4},{6,7},{7,6},{8,9},{9,8},{10,11... | collective-permute-start | bytes 589832 | tf_op jit(solution)/shard_map/ppermute | solution.py:93
  72.2 7.9 %collective-permute-start.4 = (bf16[64,1536]{1,0:T(8,128)(2,1)S(1)}, bf16[64,1536]{1,0:T(8,128)(2,1)S(1)}, u32[]{:S(2)}, u32[]{:S(2)}) collective-permute-start(bf16[64,1536]{1,0:T(8,128)(2,1)S(1)} %select_convert_fusion.1), channel_id=1, source_target_pairs={{0,1},{1,0},{2,3},{3,2},{4,5},{5,4},{6,7},{7,6},{8,9},{9,8},{10,11... | collective-permute-start | bytes 589832 | tf_op jit(solution)/shard_map/ppermute | solution.py:93
  72.7 8.9 %collective-permute-start.7 = (f32[64]{0:T(128)S(1)}, f32[64]{0:T(128)S(1)}, u32[]{:S(2)}, u32[]{:S(2)}) collective-permute-start(f32[64]{0:T(128)S(1)} %add.56), channel_id=1, source_target_pairs={{0,2},{1,3},{2,0},{3,1},{4,6},{5,7},{6,4},{7,5},{8,10},{9,11},{10,... | collective-permute-start | bytes 776 | tf_op jit(solution)/shard_map/ppermute | solution.py:93
  76.1 5.6 %collective-permute-start.9 = (bf16[64,768]{1,0:T(8,128)(2,1)S(1)}, bf16[64,768]{1,0:T(8,128)(2,1)S(1)}, u32[]{:S(2)}, u32[]{:S(2)}) collective-permute-start(bf16[64,768]{1,0:T(8,128)(2,1)S(1)} %select_convert_fusion.2), channel_id=1, source_target_pairs={{0,2},{1,3},{2,0},{3,1},{4,6},{5,7},{6,4},{7,5},{8,10},{9,11},{10,... | collective-permute-start | bytes 294920 | tf_op jit(solution)/shard_map/ppermute | solution.py:93
  80.1 7.0 %collective-permute-start.5 = (bf16[64,768]{1,0:T(8,128)(2,1)S(1)}, bf16[64,768]{1,0:T(8,128)(2,1)S(1)}, u32[]{:S(2)}, u32[]{:S(2)}) collective-permute-start(bf16[64,768]{1,0:T(8,128)(2,1)S(1)} %select_convert_fusion.3), channel_id=1, source_target_pairs={{0,2},{1,3},{2,0},{3,1},{4,6},{5,7},{6,4},{7,5},{8,10},{9,11},{10,... | collective-permute-start | bytes 294920 | tf_op jit(solution)/shard_map/ppermute | solution.py:93
  87.3 6.4 %collective-permute-start.10 = (bf16[64,768]{1,0:T(8,128)(2,1)S(1)}, bf16[64,768]{1,0:T(8,128)(2,1)S(1)}, u32[]{:S(2)}, u32[]{:S(2)}) collective-permute-start(bf16[64,768]{1,0:T(8,128)(2,1)S(1)} %multiply_convert_fusion.1), channel_id=1, source_target_pairs={{0,2},{1,3},{2,0},{3,1},{4,6},{5,7},{6,4},{7,5},{8,10},{9,11},{10,... | collective-permute-start | bytes 294920 | tf_op jit(solution)/shard_map/ppermute | solution.py:93
  93.8 5.7 %collective-permute-start.11 = (bf16[64,1536]{1,0:T(8,128)(2,1)S(1)}, bf16[64,1536]{1,0:T(8,128)(2,1)S(1)}, u32[]{:S(2)}, u32[]{:S(2)}) collective-permute-start(bf16[64,1536]{1,0:T(8,128)(2,1)S(1)} %maximum_select_fusion.2), channel_id=1, source_target_pairs={{0,1},{1,0},{2,3},{3,2},{4,5},{5,4},{6,7},{7,6},{8,9},{9,8},{10,11... | collective-permute-start | bytes 589832 | tf_op jit(solution)/shard_map/ppermute | solution.py:93
  104.2 1.3 %collective-permute-start.12 = (bf16[2,16,1280]{2,1,0:T(8,128)(2,1)S(1)}, bf16[2,16,1280]{2,1,0:T(8,128)(2,1)S(1)}, u32[]{:S(2)}, u32[]{:S(2)}) collective-permute-start(bf16[2,16,1280]{2,1,0:T(8,128)(2,1)S(1)} %fusion.10), channel_id=1, source_target_pairs={{0,4},{4,0},{8,12},{12,8},{1,5},{5,1},{9,13},{13,9},{2,6},{6,2},{1... | collective-permute-start | bytes 245768 | tf_op jit(solution)/shard_map/ppermute | solution.py:93
  105.6 4.1 %collective-permute-start.13 = (bf16[1,16,1280]{2,1,0:T(8,128)(2,1)S(1)}, bf16[1,16,1280]{2,1,0:T(8,128)(2,1)S(1)}, u32[]{:S(2)}, u32[]{:S(2)}) collective-permute-start(bf16[1,16,1280]{2,1,0:T(8,128)(2,1)S(1)} %fusion.14), channel_id=1, source_target_pairs={{0,8},{4,12},{8,0},{12,4},{1,9},{5,13},{9,1},{13,5},{2,10},{6,14},... | collective-permute-start | bytes 122888 | tf_op jit(solution)/shard_map/ppermute | solution.py:93

commit v14 on v11

--- a/solution.py
+++ b/solution.py
@@ -36,26 +36,36 @@
         lax.fori_loop(0, pages_req, start, 0)
 
     span = pages_req * page_size
-    positions = lax.broadcasted_iota(jnp.int32, (head_count, span), 1)
+    chunk = min(512, span)
+    positions = lax.broadcasted_iota(jnp.int32, (head_count, chunk), 1)
     for slot in range(req_dev):
         def finish(page, carry, slot=slot):
             page_copy(slot, page).wait()
             return carry
 
         lax.fori_loop(0, pages_req, finish, 0)
-        live = positions < lengths[slot]
+        length = lengths[slot]
         query_rows = jnp.transpose(queries[slot])
-        scores = jnp.dot(query_rows, keys[slot], preferred_element_type=jnp.float32) * score_scale
-        scores = jnp.where(live, scores, masked_score)
-        row_max = jnp.max(scores, axis=1, keepdims=True)
-        exponent = jnp.exp(scores - row_max)
-        denominator = jnp.sum(exponent, axis=1, keepdims=True)
-        weighted = lax.dot_general(
-            exponent.astype(jnp.bfloat16),
-            keys[slot, :latent, :],
-            (((1,), (1,)), ((), ())),
-            preferred_element_type=jnp.float32,
-        )
+        blocks_of_scores = []
+        row_max = jnp.full((head_count, 1), masked_score, jnp.float32)
+        for first in range(0, span, chunk):
+            block = jnp.dot(
+                query_rows, keys[slot, :, first:first + chunk], preferred_element_type=jnp.float32
+            ) * score_scale
+            block = jnp.where(positions + first < length, block, masked_score)
+            blocks_of_scores.append(block)
+            row_max = jnp.maximum(row_max, jnp.max(block, axis=1, keepdims=True))
+        denominator = jnp.zeros((head_count, 1), jnp.float32)
+        weighted = jnp.zeros((head_count, latent), jnp.float32)
+        for first, block in zip(range(0, span, chunk), blocks_of_scores):
+            exponent = jnp.exp(block - row_max)
+            denominator = denominator + jnp.sum(exponent, axis=1, keepdims=True)
+            weighted = weighted + lax.dot_general(
+                exponent.astype(jnp.bfloat16),
+                keys[slot, :latent, first:first + chunk],
+                (((1,), (1,)), ((), ())),
+                preferred_element_type=jnp.float32,
+            )
         blocks, block_heads = contexts.shape[0], head_count // contexts.shape[0]
         context = (weighted / denominator).reshape(blocks, block_heads, latent)
         contexts[:, slot * block_heads:(slot + 1) * block_heads, :] = context.astype(contexts.dtype)

time: 111 us -> 110 us (level)
  no operation moved by 1% of the time
where the time goes in v14:
time: 110 us
  waiting for transfers between devices  46.8 us (43%)
  starting transfers between devices  17.8 us (16%)
  blocking collectives  16.2 us (15%)
  matrix products  14.1 us (13%)
  Pallas kernels  9.73 us (9%)
  local copies, waits for them, and re-layouts  3.16 us (3%)
  other arithmetic  1.45 us (1%)
    ppermute x14, waiting for transfers between devices, swap_with(): return lax.ppermute(x, axis, [(i, i ^ distance) for i in range(size)])  38.4 us
    all_gather x1, blocking collectives, shards(): group_values = lax.all_gather(values, 'sub', axis=1, tiled=True)  16.2 us
    ppermute x14, starting transfers between devices, swap_with(): return lax.ppermute(x, axis, [(i, i ^ distance) for i in range(size)])  10.4 us
    pallas_call x1, Pallas kernels, attend_all(): pl.pallas_call(kernel, out_shape=jax.ShapeDtypeStruct((blocks, req_dev *...  9.73 us
    all_to_all x1, waiting for transfers between devices, shards(): lax.all_to_all(contexts, ('dp', 'sub'), split_axis=0, concat_axis=0, tile...  8.35 us
    all_to_all x1, starting transfers between devices, shards(): lax.all_to_all(contexts, ('dp', 'sub'), split_axis=0, concat_axis=0, tile...  7.37 us
    dot_general x1, matrix products, shards(): jnp.dot(group_values, out_proj, preferred_element_type=jnp.float32)  6.04 us
    dot_general x1, matrix products, shards(): jnp.dot(hidden_units, down_proj, preferred_element_type=jnp.float32)  4.7 us
  transfers between devices with their start and end apart: 15, of which 12 were waited for; matrix products, arithmetic and copies ran while one was open for 9% of the time, Pallas kernels for 0%

profile of v14, /device:TPU:0, one launch (start us, length us, event | category | flops | bytes accessed | tf_op | source)
XLA Modules:
  0.0 110.0 jit_solution(9701306344157185257)
XLA Ops:
  0.6 0.0 copy-start
  0.6 0.0 copy-start.1
  0.7 1.1 %copy-done.1 = bf16[4,128,576]{1,2,0:T(8,128)(2,1)S(1)} copy-done((bf16[4,128,576]{1,2,0:T(8,128)(2,1)S(1)}, bf16[4,128,576]{1,2,0:T(8,128)(2,1)}, u32[]{:S(2)}) %copy-start.1) | copy-done | bytes 589848
  1.8 0.0 copy-start.2
  1.8 0.7 copy-done.2
  2.5 0.0 copy-start.3
  2.5 0.7 copy-done.3
  3.1 0.0 copy-start.4
  3.1 0.0 copy-start.5
  3.1 9.7 %shard_map.122 = bf16[16,32,512]{2,1,0:T(8,128)(2,1)} custom-call(s32[4,16]{1,0:T(4,128)S(1)} %copy-done.2, s32[4]{0:T(128)S(1)} %copy-done.3, bf16[4,576,128]{2,1,0:T(8,128)(2,1)S(1)} %bitcast.58, bf16[64,576,128]{2,1,0:T(8,128)(2,1)} %bitcast.63), custom_call_target="tpu_custom_call" | custom-call | tf_op jit(solution)/shard_map/pallas_call | solution.py:81
  12.9 7.4 %all-to-all-start = ((bf16[16,32,512]{2,1,0:T(8,128)(2,1)}), bf16[16,32,512]{2,1,0:T(8,128)(2,1)S(1)}, u32[]{:S(2)}, u32[]{:S(2)}) async-start(bf16[16,32,512]{2,1,0:T(8,128)(2,1)} %shard_map.122), calls=%async_computation | async-start | bytes 1048576 | tf_op jit(solution)/shard_map/all_to_all | solution.py:231
  20.3 0.0 copy-done.4
  20.3 2.0 %collective-permute-start.2 = (bf16[1,16,1280]{2,1,0:T(8,128)(2,1)S(1)}, bf16[1,16,1280]{2,1,0:T(8,128)(2,1)S(1)}, u32[]{:S(2)}, u32[]{:S(2)}) collective-permute-start(bf16[1,16,1280]{2,1,0:T(8,128)(2,1)S(1)} %bitcast.68), channel_id=1, source_target_pairs={{0,8},{4,12},{8,0},{12,4},{1,9},{5,13},{9,1},{13,5},{2,10},{6,14},... | collective-permute-start | bytes 122888 | tf_op jit(solution)/shard_map/ppermute | solution.py:100
  22.3 0.0 copy-done.5
  22.3 5.2 %collective-permute-done.2 = bf16[1,16,1280]{2,1,0:T(8,128)(2,1)S(1)} collective-permute-done((bf16[1,16,1280]{2,1,0:T(8,128)(2,1)S(1)}, bf16[1,16,1280]{2,1,0:T(8,128)(2,1)S(1)}, u32[]{:S(2)}, u32[]{:S(2)}) %collective-permute-start.2) | collective-permute-done | bytes 40992 | tf_op jit(solution)/shard_map/ppermute | solution.py:100
  27.5 0.1 collective-permute-start.3
  27.6 8.3 %all-to-all-done = bf16[16,32,512]{2,1,0:T(8,128)(2,1)S(1)} async-done(((bf16[16,32,512]{2,1,0:T(8,128)(2,1)}), bf16[16,32,512]{2,1,0:T(8,128)(2,1)S(1)}, u32[]{:S(2)}, u32[]{:S(2)}) %all-to-all-start) | async-done | bytes 524320 | tf_op jit(solution)/shard_map/all_to_all | solution.py:231
  35.9 0.0 copy-done
  35.9 0.4 fusion
  36.4 0.0 slice-start
  36.4 16.2 %all_gather.3 = bf16[64,4096]{1,0:T(8,128)(2,1)S(1)} all-gather(bf16[64,1024]{1,0:T(8,128)(2,1)S(1)} %bitcast.67), channel_id=1, replica_groups=mesh['grp'=2,'dp'=4,'sub'=4] {'sub'}, dimensions={1}, use_global_device_ids=true | all-gather | bytes 655360 | tf_op jit(solution)/shard_map/all_gather | solution.py:236
  52.6 0.0 slice-start.1
  52.6 6.0 %convolution_convert_fusion = bf16[64,1280]{1,0:T(8,128)(2,1)S(1)} fusion(bf16[64,4096]{1,0:T(8,128)(2,1)S(1)} %all_gather.3, bf16[4096,1280]{1,0:T(8,128)(2,1)} %param.17), kind=kOutput, calls=%fused_computation | convolution fusion | flops 671170560 | bytes 11173888 | tf_op jit(solution)/shard_map/dot_general | solution.py:240
  58.6 0.1 collective-permute-start
  58.7 1.4 %collective-permute-done = bf16[64,1280]{1,0:T(8,128)(2,1)S(1)} collective-permute-done((bf16[64,1280]{1,0:T(8,128)(2,1)S(1)}, bf16[64,1280]{1,0:T(8,128)(2,1)S(1)}, u32[]{:S(2)}, u32[]{:S(2)}) %collective-permute-start) | collective-permute-done | bytes 163872 | tf_op jit(solution)/shard_map/ppermute | solution.py:100
  60.1 0.7 collective-permute-start.1
  60.8 0.0 collective-permute-done.3
  60.8 5.6 %collective-permute-done.1 = bf16[64,1280]{1,0:T(8,128)(2,1)S(1)} collective-permute-done((bf16[64,1280]{1,0:T(8,128)(2,1)S(1)}, bf16[64,1280]{1,0:T(8,128)(2,1)S(1)}, u32[]{:S(2)}, u32[]{:S(2)}) %collective-permute-start.1) | collective-permute-done | bytes 163872 | tf_op jit(solution)/shard_map/ppermute | solution.py:100
  66.4 0.0 slice-start.2
  66.4 0.2 multiply_reduce_fusion
  66.6 0.1 collective-permute-start.6
  66.7 0.0 slice-done
  66.7 0.0 slice-done.1
  66.7 0.0 slice-start.3
  66.7 1.5 %fusion.12 = f32[64,3072]{1,0:T(8,128)S(1)} fusion(bf16[1280,3072]{1,0:T(8,128)(2,1)S(1)} %bitcast.60, f32[64,1280]{1,0:T(8,128)S(1)} %get-tuple-element.3, f32[1280]{0:T(1024)S(1)} %convert_element_type.106), kind=kOutput, calls=%fused_computation.40 | convolution fusion | flops 503480320 | bytes 8983552 | tf_op jit(solution)/shard_map/dot_general | solution.py:247
  68.3 2.0 %collective-permute-start.8 = (bf16[64,1536]{1,0:T(8,128)(2,1)S(1)}, bf16[64,1536]{1,0:T(8,128)(2,1)S(1)}, u32[]{:S(2)}, u32[]{:S(2)}) collective-permute-start(bf16[64,1536]{1,0:T(8,128)(2,1)S(1)} %select_convert_fusion), channel_id=1, source_target_pairs={{0,1},{1,0},{2,3},{3,2},{4,5},{5,4},{6,7},{7,6},{8,9},{9,8},{10,11... | collective-permute-start | bytes 589832 | tf_op jit(solution)/shard_map/ppermute | solution.py:100
  70.3 0.0 slice-done.2
  70.3 0.0 slice-done.3
  70.3 1.5 %fusion.13 = f32[64,3072]{1,0:T(8,128)S(1)} fusion(bf16[1280,3072]{1,0:T(8,128)(2,1)S(1)} %bitcast.62, f32[64,1280]{1,0:T(8,128)S(1)} %get-tuple-element.3, f32[1280]{0:T(1024)S(1)} %convert_element_type.106), kind=kOutput, calls=%fused_computation.41 | convolution fusion | flops 503480320 | bytes 8983552 | tf_op jit(solution)/shard_map/dot_general | solution.py:246
  71.9 0.5 collective-permute-start.4
  72.4 0.0 collective-permute-done.6
  72.4 0.9 collective-permute-start.7
  73.3 2.4 %collective-permute-done.8 = bf16[64,1536]{1,0:T(8,128)(2,1)S(1)} collective-permute-done((bf16[64,1536]{1,0:T(8,128)(2,1)S(1)}, bf16[64,1536]{1,0:T(8,128)(2,1)S(1)}, u32[]{:S(2)}, u32[]{:S(2)}) %collective-permute-start.8) | collective-permute-done | bytes 196640 | tf_op jit(solution)/shard_map/ppermute | solution.py:100
  75.7 0.1 convert_add_fusion
  75.8 1.7 %collective-permute-start.9 = (bf16[64,768]{1,0:T(8,128)(2,1)S(1)}, bf16[64,768]{1,0:T(8,128)(2,1)S(1)}, u32[]{:S(2)}, u32[]{:S(2)}) collective-permute-start(bf16[64,768]{1,0:T(8,128)(2,1)S(1)} %select_convert_fusion.2), channel_id=1, source_target_pairs={{0,2},{1,3},{2,0},{3,1},{4,6},{5,7},{6,4},{7,5},{8,10},{9,11},{10,... | collective-permute-start | bytes 294920 | tf_op jit(solution)/shard_map/ppermute | solution.py:100
  77.5 2.2 %collective-permute-done.4 = bf16[64,1536]{1,0:T(8,128)(2,1)S(1)} collective-permute-done((bf16[64,1536]{1,0:T(8,128)(2,1)S(1)}, bf16[64,1536]{1,0:T(8,128)(2,1)S(1)}, u32[]{:S(2)}, u32[]{:S(2)}) %collective-permute-start.4) | collective-permute-done | bytes 196640 | tf_op jit(solution)/shard_map/ppermute | solution.py:100
  79.7 0.1 convert_add_fusion.1
  79.8 1.4 %collective-permute-start.5 = (bf16[64,768]{1,0:T(8,128)(2,1)S(1)}, bf16[64,768]{1,0:T(8,128)(2,1)S(1)}, u32[]{:S(2)}, u32[]{:S(2)}) collective-permute-start(bf16[64,768]{1,0:T(8,128)(2,1)S(1)} %select_convert_fusion.3), channel_id=1, source_target_pairs={{0,2},{1,3},{2,0},{3,1},{4,6},{5,7},{6,4},{7,5},{8,10},{9,11},{10,... | collective-permute-start | bytes 294920 | tf_op jit(solution)/shard_map/ppermute | solution.py:100
  81.2 0.0 collective-permute-done.7
  81.2 0.1 collective-permute-done.9
  81.3 5.5 %collective-permute-done.5 = bf16[64,768]{1,0:T(8,128)(2,1)S(1)} collective-permute-done((bf16[64,768]{1,0:T(8,128)(2,1)S(1)}, bf16[64,768]{1,0:T(8,128)(2,1)S(1)}, u32[]{:S(2)}, u32[]{:S(2)}) %collective-permute-start.5) | collective-permute-done | bytes 98336 | tf_op jit(solution)/shard_map/ppermute | solution.py:100
  86.8 0.1 multiply_convert_fusion.1
  87.0 0.1 collective-permute-start.10
  87.1 6.4 %collective-permute-done.10 = bf16[64,768]{1,0:T(8,128)(2,1)S(1)} collective-permute-done((bf16[64,768]{1,0:T(8,128)(2,1)S(1)}, bf16[64,768]{1,0:T(8,128)(2,1)S(1)}, u32[]{:S(2)}, u32[]{:S(2)}) %collective-permute-start.10) | collective-permute-done | bytes 98336 | tf_op jit(solution)/shard_map/ppermute | solution.py:100
  93.5 0.1 collective-permute-start.11
  93.6 5.7 %collective-permute-done.11 = bf16[64,1536]{1,0:T(8,128)(2,1)S(1)} collective-permute-done((bf16[64,1536]{1,0:T(8,128)(2,1)S(1)}, bf16[64,1536]{1,0:T(8,128)(2,1)S(1)}, u32[]{:S(2)}, u32[]{:S(2)}) %collective-permute-start.11) | collective-permute-done | bytes 196640 | tf_op jit(solution)/shard_map/ppermute | solution.py:100
  99.2 4.7 %fusion.2 = f32[64,1280]{1,0:T(8,128)S(1)} fusion(bf16[3072,1280]{1,0:T(8,128)(2,1)} %param.21, bf16[64,1536]{1,0:T(8,128)(2,1)S(1)} %maximum_select_fusion.2, bf16[64,1536]{1,0:T(8,128)(2,1)S(1)} %collective-permute-done.11, pred[]{:T(512)S(6)} %ne.18), kind=kOutput, calls=%fused_computation.5 | convolution fusion | flops 505085952 | bytes 8585217 | tf_op jit(solution)/shard_map/dot_general | solution.py:253
  103.9 0.1 collective-permute-start.12
  104.1 1.2 %collective-permute-done.12 = bf16[2,16,1280]{2,1,0:T(8,128)(2,1)S(1)} collective-permute-done((bf16[2,16,1280]{2,1,0:T(8,128)(2,1)S(1)}, bf16[2,16,1280]{2,1,0:T(8,128)(2,1)S(1)}, u32[]{:S(2)}, u32[]{:S(2)}) %collective-permute-start.12) | collective-permute-done | bytes 81952 | tf_op jit(solution)/shard_map/ppermute | solution.py:100
  105.3 0.7 collective-permute-start.13
  106.0 0.6 dynamic-slice_convert_fusion
  106.7 2.7 %collective-permute-done.13 = bf16[1,16,1280]{2,1,0:T(8,128)(2,1)S(1)} collective-permute-done((bf16[1,16,1280]{2,1,0:T(8,128)(2,1)S(1)}, bf16[1,16,1280]{2,1,0:T(8,128)(2,1)S(1)}, u32[]{:S(2)}, u32[]{:S(2)}) %collective-permute-start.13) | collective-permute-done | bytes 40992 | tf_op jit(solution)/shard_map/ppermute | solution.py:100
  109.4 0.6 fusion.11
  (19 shorter events, 0.4 us)
Async XLA Ops:
  0.6 35.3 %copy-start = (bf16[8,512,128]{2,1,0:T(8,128)(2,1)S(1)}, bf16[8,512,128]{2,1,0:T(8,128)(2,1)}, u32[]{:S(2)}) copy-start(bf16[8,512,128]{2,1,0:T(8,128)(2,1)} %param.16) | copy-start | bytes 3145732
  0.6 1.2 %copy-start.1 = (bf16[4,128,576]{1,2,0:T(8,128)(2,1)S(1)}, bf16[4,128,576]{1,2,0:T(8,128)(2,1)}, u32[]{:S(2)}) copy-start(bf16[4,128,576]{1,2,0:T(8,128)(2,1)} %param.12) | copy-start | bytes 1769476
  1.8 0.7 copy-start.2
  2.5 0.7 copy-start.3
  3.1 17.1 %copy-start.4 = (bf16[16,1280]{1,0:T(8,128)(2,1)S(1)}, bf16[16,1280]{1,0:T(8,128)(2,1)}, u32[]{:S(2)}) copy-start(bf16[16,1280]{1,0:T(8,128)(2,1)} %param.11) | copy-start | bytes 122884
  3.1 19.1 %copy-start.5 = (bf16[1280]{0:T(1024)(128)(2,1)S(1)}, bf16[1280]{0:T(1024)(128)(2,1)}, u32[]{:S(2)}) copy-start(bf16[1280]{0:T(1024)(128)(2,1)} %param.18) | copy-start | bytes 7684
  12.9 23.1 %all-to-all-start = ((bf16[16,32,512]{2,1,0:T(8,128)(2,1)}), bf16[16,32,512]{2,1,0:T(8,128)(2,1)S(1)}, u32[]{:S(2)}, u32[]{:S(2)}) async-start(bf16[16,32,512]{2,1,0:T(8,128)(2,1)} %shard_map.122), calls=%async_computation | async-start | bytes 1048576 | tf_op jit(solution)/shard_map/all_to_all | solution.py:231
  20.3 7.2 %collective-permute-start.2 = (bf16[1,16,1280]{2,1,0:T(8,128)(2,1)S(1)}, bf16[1,16,1280]{2,1,0:T(8,128)(2,1)S(1)}, u32[]{:S(2)}, u32[]{:S(2)}) collective-permute-start(bf16[1,16,1280]{2,1,0:T(8,128)(2,1)S(1)} %bitcast.68), channel_id=1, source_target_pairs={{0,8},{4,12},{8,0},{12,4},{1,9},{5,13},{9,1},{13,5},{2,10},{6,14},... | collective-permute-start | bytes 122888 | tf_op jit(solution)/shard_map/ppermute | solution.py:100
  27.5 33.3 %collective-permute-start.3 = (bf16[2,16,1280]{2,1,0:T(8,128)(2,1)S(1)}, bf16[2,16,1280]{2,1,0:T(8,128)(2,1)S(1)}, u32[]{:S(2)}, u32[]{:S(2)}) collective-permute-start(bf16[2,16,1280]{2,1,0:T(8,128)(2,1)S(1)} %maximum_select_fusion.4), channel_id=1, source_target_pairs={{0,4},{4,0},{8,12},{12,8},{1,5},{5,1},{9,13},{13,9},{2,6},{6,2},{1... | collective-permute-start | bytes 245768 | tf_op jit(solution)/shard_map/ppermute | solution.py:100
  36.4 30.3 %slice-start = ((s8[7864320]{0:T(1024)(128)(4,1)}), s8[4194304]{0:T(1024)(128)(4,1)S(1)}, s32[]{:S(2)}) async-start(s8[7864320]{0:T(1024)(128)(4,1)} %bitcast.59), calls=%async_computation.1 | async-start | bytes 8388608
  52.6 14.1 %slice-start.1 = ((s8[7864320]{0:T(1024)(128)(4,1)}), s8[3670016]{0:T(1024)(128)(4,1)S(1)}, s32[]{:S(2)}) async-start(s8[7864320]{0:T(1024)(128)(4,1)} %bitcast.59), calls=%async_computation.2 | async-start | bytes 7340032
  58.6 1.5 %collective-permute-start = (bf16[64,1280]{1,0:T(8,128)(2,1)S(1)}, bf16[64,1280]{1,0:T(8,128)(2,1)S(1)}, u32[]{:S(2)}, u32[]{:S(2)}) collective-permute-start(bf16[64,1280]{1,0:T(8,128)(2,1)S(1)} %convolution_convert_fusion), channel_id=1, source_target_pairs={{0,4},{4,0},{8,12},{12,8},{1,5},{5,1},{9,13},{13,9},{2,6},{6,2},{1... | collective-permute-start | bytes 491528 | tf_op jit(solution)/shard_map/ppermute | solution.py:100
  60.1 6.3 %collective-permute-start.1 = (bf16[64,1280]{1,0:T(8,128)(2,1)S(1)}, bf16[64,1280]{1,0:T(8,128)(2,1)S(1)}, u32[]{:S(2)}, u32[]{:S(2)}) collective-permute-start(bf16[64,1280]{1,0:T(8,128)(2,1)S(1)} %add_convert_fusion), channel_id=1, source_target_pairs={{0,8},{4,12},{8,0},{12,4},{1,9},{5,13},{9,1},{13,5},{2,10},{6,14},... | collective-permute-start | bytes 491528 | tf_op jit(solution)/shard_map/ppermute | solution.py:100
  66.4 3.9 %slice-start.2 = ((s8[7864320]{0:T(1024)(128)(4,1)}), s8[4194304]{0:T(1024)(128)(4,1)S(1)}, s32[]{:S(2)}) async-start(s8[7864320]{0:T(1024)(128)(4,1)} %bitcast.61), calls=%async_computation.3 | async-start | bytes 8388608
  66.6 5.7 %collective-permute-start.6 = (f32[64]{0:T(128)S(1)}, f32[64]{0:T(128)S(1)}, u32[]{:S(2)}, u32[]{:S(2)}) collective-permute-start(f32[64]{0:T(128)S(1)} %get-tuple-element.2), channel_id=1, source_target_pairs={{0,1},{1,0},{2,3},{3,2},{4,5},{5,4},{6,7},{7,6},{8,9},{9,8},{10,11... | collective-permute-start | bytes 776 | tf_op jit(solution)/shard_map/ppermute | solution.py:100
  66.7 3.6 %slice-start.3 = ((s8[7864320]{0:T(1024)(128)(4,1)}), s8[3670016]{0:T(1024)(128)(4,1)S(1)}, s32[]{:S(2)}) async-start(s8[7864320]{0:T(1024)(128)(4,1)} %bitcast.61), calls=%async_computation.4 | async-start | bytes 7340032
  68.3 7.4 %collective-permute-start.8 = (bf16[64,1536]{1,0:T(8,128)(2,1)S(1)}, bf16[64,1536]{1,0:T(8,128)(2,1)S(1)}, u32[]{:S(2)}, u32[]{:S(2)}) collective-permute-start(bf16[64,1536]{1,0:T(8,128)(2,1)S(1)} %select_convert_fusion), channel_id=1, source_target_pairs={{0,1},{1,0},{2,3},{3,2},{4,5},{5,4},{6,7},{7,6},{8,9},{9,8},{10,11... | collective-permute-start | bytes 589832 | tf_op jit(solution)/shard_map/ppermute | solution.py:100
  71.9 7.9 %collective-permute-start.4 = (bf16[64,1536]{1,0:T(8,128)(2,1)S(1)}, bf16[64,1536]{1,0:T(8,128)(2,1)S(1)}, u32[]{:S(2)}, u32[]{:S(2)}) collective-permute-start(bf16[64,1536]{1,0:T(8,128)(2,1)S(1)} %select_convert_fusion.1), channel_id=1, source_target_pairs={{0,1},{1,0},{2,3},{3,2},{4,5},{5,4},{6,7},{7,6},{8,9},{9,8},{10,11... | collective-permute-start | bytes 589832 | tf_op jit(solution)/shard_map/ppermute | solution.py:100
  72.4 8.9 %collective-permute-start.7 = (f32[64]{0:T(128)S(1)}, f32[64]{0:T(128)S(1)}, u32[]{:S(2)}, u32[]{:S(2)}) collective-permute-start(f32[64]{0:T(128)S(1)} %add.56), channel_id=1, source_target_pairs={{0,2},{1,3},{2,0},{3,1},{4,6},{5,7},{6,4},{7,5},{8,10},{9,11},{10,... | collective-permute-start | bytes 776 | tf_op jit(solution)/shard_map/ppermute | solution.py:100
  75.8 5.6 %collective-permute-start.9 = (bf16[64,768]{1,0:T(8,128)(2,1)S(1)}, bf16[64,768]{1,0:T(8,128)(2,1)S(1)}, u32[]{:S(2)}, u32[]{:S(2)}) collective-permute-start(bf16[64,768]{1,0:T(8,128)(2,1)S(1)} %select_convert_fusion.2), channel_id=1, source_target_pairs={{0,2},{1,3},{2,0},{3,1},{4,6},{5,7},{6,4},{7,5},{8,10},{9,11},{10,... | collective-permute-start | bytes 294920 | tf_op jit(solution)/shard_map/ppermute | solution.py:100
  79.8 7.0 %collective-permute-start.5 = (bf16[64,768]{1,0:T(8,128)(2,1)S(1)}, bf16[64,768]{1,0:T(8,128)(2,1)S(1)}, u32[]{:S(2)}, u32[]{:S(2)}) collective-permute-start(bf16[64,768]{1,0:T(8,128)(2,1)S(1)} %select_convert_fusion.3), channel_id=1, source_target_pairs={{0,2},{1,3},{2,0},{3,1},{4,6},{5,7},{6,4},{7,5},{8,10},{9,11},{10,... | collective-permute-start | bytes 294920 | tf_op jit(solution)/shard_map/ppermute | solution.py:100
  87.0 6.4 %collective-permute-start.10 = (bf16[64,768]{1,0:T(8,128)(2,1)S(1)}, bf16[64,768]{1,0:T(8,128)(2,1)S(1)}, u32[]{:S(2)}, u32[]{:S(2)}) collective-permute-start(bf16[64,768]{1,0:T(8,128)(2,1)S(1)} %multiply_convert_fusion.1), channel_id=1, source_target_pairs={{0,2},{1,3},{2,0},{3,1},{4,6},{5,7},{6,4},{7,5},{8,10},{9,11},{10,... | collective-permute-start | bytes 294920 | tf_op jit(solution)/shard_map/ppermute | solution.py:100
  93.5 5.7 %collective-permute-start.11 = (bf16[64,1536]{1,0:T(8,128)(2,1)S(1)}, bf16[64,1536]{1,0:T(8,128)(2,1)S(1)}, u32[]{:S(2)}, u32[]{:S(2)}) collective-permute-start(bf16[64,1536]{1,0:T(8,128)(2,1)S(1)} %maximum_select_fusion.2), channel_id=1, source_target_pairs={{0,1},{1,0},{2,3},{3,2},{4,5},{5,4},{6,7},{7,6},{8,9},{9,8},{10,11... | collective-permute-start | bytes 589832 | tf_op jit(solution)/shard_map/ppermute | solution.py:100
  103.9 1.3 %collective-permute-start.12 = (bf16[2,16,1280]{2,1,0:T(8,128)(2,1)S(1)}, bf16[2,16,1280]{2,1,0:T(8,128)(2,1)S(1)}, u32[]{:S(2)}, u32[]{:S(2)}) collective-permute-start(bf16[2,16,1280]{2,1,0:T(8,128)(2,1)S(1)} %fusion.10), channel_id=1, source_target_pairs={{0,4},{4,0},{8,12},{12,8},{1,5},{5,1},{9,13},{13,9},{2,6},{6,2},{1... | collective-permute-start | bytes 245768 | tf_op jit(solution)/shard_map/ppermute | solution.py:100
  105.3 4.1 %collective-permute-start.13 = (bf16[1,16,1280]{2,1,0:T(8,128)(2,1)S(1)}, bf16[1,16,1280]{2,1,0:T(8,128)(2,1)S(1)}, u32[]{:S(2)}, u32[]{:S(2)}) collective-permute-start(bf16[1,16,1280]{2,1,0:T(8,128)(2,1)S(1)} %fusion.14), channel_id=1, source_target_pairs={{0,8},{4,12},{8,0},{12,4},{1,9},{5,13},{9,1},{13,5},{2,10},{6,14},... | collective-permute-start | bytes 122888 | tf_op jit(solution)/shard_map/ppermute | solution.py:100

commit v15 on v14

--- a/solution.py
+++ b/solution.py
@@ -36,7 +36,7 @@
         lax.fori_loop(0, pages_req, start, 0)
 
     span = pages_req * page_size
-    chunk = min(512, span)
+    chunk = min(256, span)
     positions = lax.broadcasted_iota(jnp.int32, (head_count, chunk), 1)
     for slot in range(req_dev):
         def finish(page, carry, slot=slot):

time: 110 us -> 110 us (level)
  no operation moved by 1% of the time
where the time goes in v15:
time: 110 us
  waiting for transfers between devices  46.8 us (43%)
  starting transfers between devices  17.8 us (16%)
  blocking collectives  16.2 us (15%)
  matrix products  14.1 us (13%)
  Pallas kernels  9.76 us (9%)
  local copies, waits for them, and re-layouts  3.16 us (3%)
  other arithmetic  1.45 us (1%)
    ppermute x14, waiting for transfers between devices, swap_with(): return lax.ppermute(x, axis, [(i, i ^ distance) for i in range(size)])  38.4 us
    all_gather x1, blocking collectives, shards(): group_values = lax.all_gather(values, 'sub', axis=1, tiled=True)  16.2 us
    ppermute x14, starting transfers between devices, swap_with(): return lax.ppermute(x, axis, [(i, i ^ distance) for i in range(size)])  10.4 us
    pallas_call x1, Pallas kernels, attend_all(): pl.pallas_call(kernel, out_shape=jax.ShapeDtypeStruct((blocks, req_dev *...  9.76 us
    all_to_all x1, waiting for transfers between devices, shards(): lax.all_to_all(contexts, ('dp', 'sub'), split_axis=0, concat_axis=0, tile...  8.35 us
    all_to_all x1, starting transfers between devices, shards(): lax.all_to_all(contexts, ('dp', 'sub'), split_axis=0, concat_axis=0, tile...  7.37 us
    dot_general x1, matrix products, shards(): jnp.dot(group_values, out_proj, preferred_element_type=jnp.float32)  6.04 us
    dot_general x1, matrix products, shards(): jnp.dot(hidden_units, down_proj, preferred_element_type=jnp.float32)  4.7 us
  transfers between devices with their start and end apart: 15, of which 12 were waited for; matrix products, arithmetic and copies ran while one was open for 9% of the time, Pallas kernels for 0%

profile of v15, /device:TPU:0, one launch (start us, length us, event | category | flops | bytes accessed | tf_op | source)
XLA Modules:
  0.0 110.1 jit_solution(7256056301098236738)
XLA Ops:
  0.6 0.0 copy-start
  0.6 0.0 copy-start.1
  0.7 1.1 %copy-done.1 = bf16[4,128,576]{1,2,0:T(8,128)(2,1)S(1)} copy-done((bf16[4,128,576]{1,2,0:T(8,128)(2,1)S(1)}, bf16[4,128,576]{1,2,0:T(8,128)(2,1)}, u32[]{:S(2)}) %copy-start.1) | copy-done | bytes 589848
  1.8 0.0 copy-start.2
  1.8 0.7 copy-done.2
  2.5 0.0 copy-start.3
  2.5 0.7 copy-done.3
  3.1 0.0 copy-start.4
  3.1 0.0 copy-start.5
  3.1 9.8 %shard_map.122 = bf16[16,32,512]{2,1,0:T(8,128)(2,1)} custom-call(s32[4,16]{1,0:T(4,128)S(1)} %copy-done.2, s32[4]{0:T(128)S(1)} %copy-done.3, bf16[4,576,128]{2,1,0:T(8,128)(2,1)S(1)} %bitcast.58, bf16[64,576,128]{2,1,0:T(8,128)(2,1)} %bitcast.63), custom_call_target="tpu_custom_call" | custom-call | tf_op jit(solution)/shard_map/pallas_call | solution.py:81
  12.9 7.4 %all-to-all-start = ((bf16[16,32,512]{2,1,0:T(8,128)(2,1)}), bf16[16,32,512]{2,1,0:T(8,128)(2,1)S(1)}, u32[]{:S(2)}, u32[]{:S(2)}) async-start(bf16[16,32,512]{2,1,0:T(8,128)(2,1)} %shard_map.122), calls=%async_computation | async-start | bytes 1048576 | tf_op jit(solution)/shard_map/all_to_all | solution.py:231
  20.3 0.0 copy-done.4
  20.3 2.0 %collective-permute-start.2 = (bf16[1,16,1280]{2,1,0:T(8,128)(2,1)S(1)}, bf16[1,16,1280]{2,1,0:T(8,128)(2,1)S(1)}, u32[]{:S(2)}, u32[]{:S(2)}) collective-permute-start(bf16[1,16,1280]{2,1,0:T(8,128)(2,1)S(1)} %bitcast.68), channel_id=1, source_target_pairs={{0,8},{4,12},{8,0},{12,4},{1,9},{5,13},{9,1},{13,5},{2,10},{6,14},... | collective-permute-start | bytes 122888 | tf_op jit(solution)/shard_map/ppermute | solution.py:100
  22.3 0.0 copy-done.5
  22.3 5.2 %collective-permute-done.2 = bf16[1,16,1280]{2,1,0:T(8,128)(2,1)S(1)} collective-permute-done((bf16[1,16,1280]{2,1,0:T(8,128)(2,1)S(1)}, bf16[1,16,1280]{2,1,0:T(8,128)(2,1)S(1)}, u32[]{:S(2)}, u32[]{:S(2)}) %collective-permute-start.2) | collective-permute-done | bytes 40992 | tf_op jit(solution)/shard_map/ppermute | solution.py:100
  27.5 0.1 collective-permute-start.3
  27.6 8.3 %all-to-all-done = bf16[16,32,512]{2,1,0:T(8,128)(2,1)S(1)} async-done(((bf16[16,32,512]{2,1,0:T(8,128)(2,1)}), bf16[16,32,512]{2,1,0:T(8,128)(2,1)S(1)}, u32[]{:S(2)}, u32[]{:S(2)}) %all-to-all-start) | async-done | bytes 524320 | tf_op jit(solution)/shard_map/all_to_all | solution.py:231
  36.0 0.0 copy-done
  36.0 0.4 fusion
  36.4 0.0 slice-start
  36.4 16.2 %all_gather.3 = bf16[64,4096]{1,0:T(8,128)(2,1)S(1)} all-gather(bf16[64,1024]{1,0:T(8,128)(2,1)S(1)} %bitcast.67), channel_id=1, replica_groups=mesh['grp'=2,'dp'=4,'sub'=4] {'sub'}, dimensions={1}, use_global_device_ids=true | all-gather | bytes 655360 | tf_op jit(solution)/shard_map/all_gather | solution.py:236
  52.6 0.0 slice-start.1
  52.6 6.0 %convolution_convert_fusion = bf16[64,1280]{1,0:T(8,128)(2,1)S(1)} fusion(bf16[64,4096]{1,0:T(8,128)(2,1)S(1)} %all_gather.3, bf16[4096,1280]{1,0:T(8,128)(2,1)} %param.17), kind=kOutput, calls=%fused_computation | convolution fusion | flops 671170560 | bytes 11173888 | tf_op jit(solution)/shard_map/dot_general | solution.py:240
  58.6 0.1 collective-permute-start
  58.7 1.4 %collective-permute-done = bf16[64,1280]{1,0:T(8,128)(2,1)S(1)} collective-permute-done((bf16[64,1280]{1,0:T(8,128)(2,1)S(1)}, bf16[64,1280]{1,0:T(8,128)(2,1)S(1)}, u32[]{:S(2)}, u32[]{:S(2)}) %collective-permute-start) | collective-permute-done | bytes 163872 | tf_op jit(solution)/shard_map/ppermute | solution.py:100
  60.1 0.7 collective-permute-start.1
  60.8 0.0 collective-permute-done.3
  60.8 5.6 %collective-permute-done.1 = bf16[64,1280]{1,0:T(8,128)(2,1)S(1)} collective-permute-done((bf16[64,1280]{1,0:T(8,128)(2,1)S(1)}, bf16[64,1280]{1,0:T(8,128)(2,1)S(1)}, u32[]{:S(2)}, u32[]{:S(2)}) %collective-permute-start.1) | collective-permute-done | bytes 163872 | tf_op jit(solution)/shard_map/ppermute | solution.py:100
  66.5 0.0 slice-start.2
  66.5 0.2 multiply_reduce_fusion
  66.6 0.1 collective-permute-start.6
  66.7 0.0 slice-done
  66.7 0.0 slice-done.1
  66.8 0.0 slice-start.3
  66.8 1.5 %fusion.12 = f32[64,3072]{1,0:T(8,128)S(1)} fusion(bf16[1280,3072]{1,0:T(8,128)(2,1)S(1)} %bitcast.60, f32[64,1280]{1,0:T(8,128)S(1)} %get-tuple-element.3, f32[1280]{0:T(1024)S(1)} %convert_element_type.106), kind=kOutput, calls=%fused_computation.40 | convolution fusion | flops 503480320 | bytes 8983552 | tf_op jit(solution)/shard_map/dot_general | solution.py:247
  68.3 2.0 %collective-permute-start.8 = (bf16[64,1536]{1,0:T(8,128)(2,1)S(1)}, bf16[64,1536]{1,0:T(8,128)(2,1)S(1)}, u32[]{:S(2)}, u32[]{:S(2)}) collective-permute-start(bf16[64,1536]{1,0:T(8,128)(2,1)S(1)} %select_convert_fusion), channel_id=1, source_target_pairs={{0,1},{1,0},{2,3},{3,2},{4,5},{5,4},{6,7},{7,6},{8,9},{9,8},{10,11... | collective-permute-start | bytes 589832 | tf_op jit(solution)/shard_map/ppermute | solution.py:100
  70.4 0.0 slice-done.2
  70.4 0.0 slice-done.3
  70.4 1.5 %fusion.13 = f32[64,3072]{1,0:T(8,128)S(1)} fusion(bf16[1280,3072]{1,0:T(8,128)(2,1)S(1)} %bitcast.62, f32[64,1280]{1,0:T(8,128)S(1)} %get-tuple-element.3, f32[1280]{0:T(1024)S(1)} %convert_element_type.106), kind=kOutput, calls=%fused_computation.41 | convolution fusion | flops 503480320 | bytes 8983552 | tf_op jit(solution)/shard_map/dot_general | solution.py:246
  71.9 0.5 collective-permute-start.4
  72.4 0.0 collective-permute-done.6
  72.4 0.9 collective-permute-start.7
  73.3 2.4 %collective-permute-done.8 = bf16[64,1536]{1,0:T(8,128)(2,1)S(1)} collective-permute-done((bf16[64,1536]{1,0:T(8,128)(2,1)S(1)}, bf16[64,1536]{1,0:T(8,128)(2,1)S(1)}, u32[]{:S(2)}, u32[]{:S(2)}) %collective-permute-start.8) | collective-permute-done | bytes 196640 | tf_op jit(solution)/shard_map/ppermute | solution.py:100
  75.7 0.1 convert_add_fusion
  75.8 1.7 %collective-permute-start.9 = (bf16[64,768]{1,0:T(8,128)(2,1)S(1)}, bf16[64,768]{1,0:T(8,128)(2,1)S(1)}, u32[]{:S(2)}, u32[]{:S(2)}) collective-permute-start(bf16[64,768]{1,0:T(8,128)(2,1)S(1)} %select_convert_fusion.2), channel_id=1, source_target_pairs={{0,2},{1,3},{2,0},{3,1},{4,6},{5,7},{6,4},{7,5},{8,10},{9,11},{10,... | collective-permute-start | bytes 294920 | tf_op jit(solution)/shard_map/ppermute | solution.py:100
  77.5 2.2 %collective-permute-done.4 = bf16[64,1536]{1,0:T(8,128)(2,1)S(1)} collective-permute-done((bf16[64,1536]{1,0:T(8,128)(2,1)S(1)}, bf16[64,1536]{1,0:T(8,128)(2,1)S(1)}, u32[]{:S(2)}, u32[]{:S(2)}) %collective-permute-start.4) | collective-permute-done | bytes 196640 | tf_op jit(solution)/shard_map/ppermute | solution.py:100
  79.8 0.1 convert_add_fusion.1
  79.9 1.4 %collective-permute-start.5 = (bf16[64,768]{1,0:T(8,128)(2,1)S(1)}, bf16[64,768]{1,0:T(8,128)(2,1)S(1)}, u32[]{:S(2)}, u32[]{:S(2)}) collective-permute-start(bf16[64,768]{1,0:T(8,128)(2,1)S(1)} %select_convert_fusion.3), channel_id=1, source_target_pairs={{0,2},{1,3},{2,0},{3,1},{4,6},{5,7},{6,4},{7,5},{8,10},{9,11},{10,... | collective-permute-start | bytes 294920 | tf_op jit(solution)/shard_map/ppermute | solution.py:100
  81.3 0.0 collective-permute-done.7
  81.3 0.1 collective-permute-done.9
  81.4 5.5 %collective-permute-done.5 = bf16[64,768]{1,0:T(8,128)(2,1)S(1)} collective-permute-done((bf16[64,768]{1,0:T(8,128)(2,1)S(1)}, bf16[64,768]{1,0:T(8,128)(2,1)S(1)}, u32[]{:S(2)}, u32[]{:S(2)}) %collective-permute-start.5) | collective-permute-done | bytes 98336 | tf_op jit(solution)/shard_map/ppermute | solution.py:100
  86.9 0.1 multiply_convert_fusion.1
  87.0 0.1 collective-permute-start.10
  87.1 6.4 %collective-permute-done.10 = bf16[64,768]{1,0:T(8,128)(2,1)S(1)} collective-permute-done((bf16[64,768]{1,0:T(8,128)(2,1)S(1)}, bf16[64,768]{1,0:T(8,128)(2,1)S(1)}, u32[]{:S(2)}, u32[]{:S(2)}) %collective-permute-start.10) | collective-permute-done | bytes 98336 | tf_op jit(solution)/shard_map/ppermute | solution.py:100
  93.5 0.1 collective-permute-start.11
  93.6 5.7 %collective-permute-done.11 = bf16[64,1536]{1,0:T(8,128)(2,1)S(1)} collective-permute-done((bf16[64,1536]{1,0:T(8,128)(2,1)S(1)}, bf16[64,1536]{1,0:T(8,128)(2,1)S(1)}, u32[]{:S(2)}, u32[]{:S(2)}) %collective-permute-start.11) | collective-permute-done | bytes 196640 | tf_op jit(solution)/shard_map/ppermute | solution.py:100
  99.2 4.7 %fusion.2 = f32[64,1280]{1,0:T(8,128)S(1)} fusion(bf16[3072,1280]{1,0:T(8,128)(2,1)} %param.21, bf16[64,1536]{1,0:T(8,128)(2,1)S(1)} %maximum_select_fusion.2, bf16[64,1536]{1,0:T(8,128)(2,1)S(1)} %collective-permute-done.11, pred[]{:T(512)S(6)} %ne.18), kind=kOutput, calls=%fused_computation.5 | convolution fusion | flops 505085952 | bytes 8585217 | tf_op jit(solution)/shard_map/dot_general | solution.py:253
  104.0 0.1 collective-permute-start.12
  104.1 1.2 %collective-permute-done.12 = bf16[2,16,1280]{2,1,0:T(8,128)(2,1)S(1)} collective-permute-done((bf16[2,16,1280]{2,1,0:T(8,128)(2,1)S(1)}, bf16[2,16,1280]{2,1,0:T(8,128)(2,1)S(1)}, u32[]{:S(2)}, u32[]{:S(2)}) %collective-permute-start.12) | collective-permute-done | bytes 81952 | tf_op jit(solution)/shard_map/ppermute | solution.py:100
  105.4 0.7 collective-permute-start.13
  106.1 0.6 dynamic-slice_convert_fusion
  106.7 2.7 %collective-permute-done.13 = bf16[1,16,1280]{2,1,0:T(8,128)(2,1)S(1)} collective-permute-done((bf16[1,16,1280]{2,1,0:T(8,128)(2,1)S(1)}, bf16[1,16,1280]{2,1,0:T(8,128)(2,1)S(1)}, u32[]{:S(2)}, u32[]{:S(2)}) %collective-permute-start.13) | collective-permute-done | bytes 40992 | tf_op jit(solution)/shard_map/ppermute | solution.py:100
  109.4 0.6 fusion.11
  (19 shorter events, 0.4 us)
Async XLA Ops:
  0.6 35.3 %copy-start = (bf16[8,512,128]{2,1,0:T(8,128)(2,1)S(1)}, bf16[8,512,128]{2,1,0:T(8,128)(2,1)}, u32[]{:S(2)}) copy-start(bf16[8,512,128]{2,1,0:T(8,128)(2,1)} %param.16) | copy-start | bytes 3145732
  0.6 1.2 %copy-start.1 = (bf16[4,128,576]{1,2,0:T(8,128)(2,1)S(1)}, bf16[4,128,576]{1,2,0:T(8,128)(2,1)}, u32[]{:S(2)}) copy-start(bf16[4,128,576]{1,2,0:T(8,128)(2,1)} %param.12) | copy-start | bytes 1769476
  1.8 0.7 copy-start.2
  2.5 0.7 copy-start.3
  3.1 17.2 %copy-start.4 = (bf16[16,1280]{1,0:T(8,128)(2,1)S(1)}, bf16[16,1280]{1,0:T(8,128)(2,1)}, u32[]{:S(2)}) copy-start(bf16[16,1280]{1,0:T(8,128)(2,1)} %param.11) | copy-start | bytes 122884
  3.1 19.1 %copy-start.5 = (bf16[1280]{0:T(1024)(128)(2,1)S(1)}, bf16[1280]{0:T(1024)(128)(2,1)}, u32[]{:S(2)}) copy-start(bf16[1280]{0:T(1024)(128)(2,1)} %param.18) | copy-start | bytes 7684
  12.9 23.1 %all-to-all-start = ((bf16[16,32,512]{2,1,0:T(8,128)(2,1)}), bf16[16,32,512]{2,1,0:T(8,128)(2,1)S(1)}, u32[]{:S(2)}, u32[]{:S(2)}) async-start(bf16[16,32,512]{2,1,0:T(8,128)(2,1)} %shard_map.122), calls=%async_computation | async-start | bytes 1048576 | tf_op jit(solution)/shard_map/all_to_all | solution.py:231
  20.3 7.2 %collective-permute-start.2 = (bf16[1,16,1280]{2,1,0:T(8,128)(2,1)S(1)}, bf16[1,16,1280]{2,1,0:T(8,128)(2,1)S(1)}, u32[]{:S(2)}, u32[]{:S(2)}) collective-permute-start(bf16[1,16,1280]{2,1,0:T(8,128)(2,1)S(1)} %bitcast.68), channel_id=1, source_target_pairs={{0,8},{4,12},{8,0},{12,4},{1,9},{5,13},{9,1},{13,5},{2,10},{6,14},... | collective-permute-start | bytes 122888 | tf_op jit(solution)/shard_map/ppermute | solution.py:100
  27.5 33.3 %collective-permute-start.3 = (bf16[2,16,1280]{2,1,0:T(8,128)(2,1)S(1)}, bf16[2,16,1280]{2,1,0:T(8,128)(2,1)S(1)}, u32[]{:S(2)}, u32[]{:S(2)}) collective-permute-start(bf16[2,16,1280]{2,1,0:T(8,128)(2,1)S(1)} %maximum_select_fusion.4), channel_id=1, source_target_pairs={{0,4},{4,0},{8,12},{12,8},{1,5},{5,1},{9,13},{13,9},{2,6},{6,2},{1... | collective-permute-start | bytes 245768 | tf_op jit(solution)/shard_map/ppermute | solution.py:100
  36.4 30.3 %slice-start = ((s8[7864320]{0:T(1024)(128)(4,1)}), s8[4194304]{0:T(1024)(128)(4,1)S(1)}, s32[]{:S(2)}) async-start(s8[7864320]{0:T(1024)(128)(4,1)} %bitcast.59), calls=%async_computation.1 | async-start | bytes 8388608
  52.6 14.1 %slice-start.1 = ((s8[7864320]{0:T(1024)(128)(4,1)}), s8[3670016]{0:T(1024)(128)(4,1)S(1)}, s32[]{:S(2)}) async-start(s8[7864320]{0:T(1024)(128)(4,1)} %bitcast.59), calls=%async_computation.2 | async-start | bytes 7340032
  58.6 1.5 %collective-permute-start = (bf16[64,1280]{1,0:T(8,128)(2,1)S(1)}, bf16[64,1280]{1,0:T(8,128)(2,1)S(1)}, u32[]{:S(2)}, u32[]{:S(2)}) collective-permute-start(bf16[64,1280]{1,0:T(8,128)(2,1)S(1)} %convolution_convert_fusion), channel_id=1, source_target_pairs={{0,4},{4,0},{8,12},{12,8},{1,5},{5,1},{9,13},{13,9},{2,6},{6,2},{1... | collective-permute-start | bytes 491528 | tf_op jit(solution)/shard_map/ppermute | solution.py:100
  60.1 6.3 %collective-permute-start.1 = (bf16[64,1280]{1,0:T(8,128)(2,1)S(1)}, bf16[64,1280]{1,0:T(8,128)(2,1)S(1)}, u32[]{:S(2)}, u32[]{:S(2)}) collective-permute-start(bf16[64,1280]{1,0:T(8,128)(2,1)S(1)} %add_convert_fusion), channel_id=1, source_target_pairs={{0,8},{4,12},{8,0},{12,4},{1,9},{5,13},{9,1},{13,5},{2,10},{6,14},... | collective-permute-start | bytes 491528 | tf_op jit(solution)/shard_map/ppermute | solution.py:100
  66.5 3.9 %slice-start.2 = ((s8[7864320]{0:T(1024)(128)(4,1)}), s8[4194304]{0:T(1024)(128)(4,1)S(1)}, s32[]{:S(2)}) async-start(s8[7864320]{0:T(1024)(128)(4,1)} %bitcast.61), calls=%async_computation.3 | async-start | bytes 8388608
  66.6 5.7 %collective-permute-start.6 = (f32[64]{0:T(128)S(1)}, f32[64]{0:T(128)S(1)}, u32[]{:S(2)}, u32[]{:S(2)}) collective-permute-start(f32[64]{0:T(128)S(1)} %get-tuple-element.2), channel_id=1, source_target_pairs={{0,1},{1,0},{2,3},{3,2},{4,5},{5,4},{6,7},{7,6},{8,9},{9,8},{10,11... | collective-permute-start | bytes 776 | tf_op jit(solution)/shard_map/ppermute | solution.py:100
  66.8 3.6 %slice-start.3 = ((s8[7864320]{0:T(1024)(128)(4,1)}), s8[3670016]{0:T(1024)(128)(4,1)S(1)}, s32[]{:S(2)}) async-start(s8[7864320]{0:T(1024)(128)(4,1)} %bitcast.61), calls=%async_computation.4 | async-start | bytes 7340032
  68.3 7.4 %collective-permute-start.8 = (bf16[64,1536]{1,0:T(8,128)(2,1)S(1)}, bf16[64,1536]{1,0:T(8,128)(2,1)S(1)}, u32[]{:S(2)}, u32[]{:S(2)}) collective-permute-start(bf16[64,1536]{1,0:T(8,128)(2,1)S(1)} %select_convert_fusion), channel_id=1, source_target_pairs={{0,1},{1,0},{2,3},{3,2},{4,5},{5,4},{6,7},{7,6},{8,9},{9,8},{10,11... | collective-permute-start | bytes 589832 | tf_op jit(solution)/shard_map/ppermute | solution.py:100
  71.9 7.9 %collective-permute-start.4 = (bf16[64,1536]{1,0:T(8,128)(2,1)S(1)}, bf16[64,1536]{1,0:T(8,128)(2,1)S(1)}, u32[]{:S(2)}, u32[]{:S(2)}) collective-permute-start(bf16[64,1536]{1,0:T(8,128)(2,1)S(1)} %select_convert_fusion.1), channel_id=1, source_target_pairs={{0,1},{1,0},{2,3},{3,2},{4,5},{5,4},{6,7},{7,6},{8,9},{9,8},{10,11... | collective-permute-start | bytes 589832 | tf_op jit(solution)/shard_map/ppermute | solution.py:100
  72.4 8.9 %collective-permute-start.7 = (f32[64]{0:T(128)S(1)}, f32[64]{0:T(128)S(1)}, u32[]{:S(2)}, u32[]{:S(2)}) collective-permute-start(f32[64]{0:T(128)S(1)} %add.56), channel_id=1, source_target_pairs={{0,2},{1,3},{2,0},{3,1},{4,6},{5,7},{6,4},{7,5},{8,10},{9,11},{10,... | collective-permute-start | bytes 776 | tf_op jit(solution)/shard_map/ppermute | solution.py:100
  75.8 5.6 %collective-permute-start.9 = (bf16[64,768]{1,0:T(8,128)(2,1)S(1)}, bf16[64,768]{1,0:T(8,128)(2,1)S(1)}, u32[]{:S(2)}, u32[]{:S(2)}) collective-permute-start(bf16[64,768]{1,0:T(8,128)(2,1)S(1)} %select_convert_fusion.2), channel_id=1, source_target_pairs={{0,2},{1,3},{2,0},{3,1},{4,6},{5,7},{6,4},{7,5},{8,10},{9,11},{10,... | collective-permute-start | bytes 294920 | tf_op jit(solution)/shard_map/ppermute | solution.py:100
  79.9 7.0 %collective-permute-start.5 = (bf16[64,768]{1,0:T(8,128)(2,1)S(1)}, bf16[64,768]{1,0:T(8,128)(2,1)S(1)}, u32[]{:S(2)}, u32[]{:S(2)}) collective-permute-start(bf16[64,768]{1,0:T(8,128)(2,1)S(1)} %select_convert_fusion.3), channel_id=1, source_target_pairs={{0,2},{1,3},{2,0},{3,1},{4,6},{5,7},{6,4},{7,5},{8,10},{9,11},{10,... | collective-permute-start | bytes 294920 | tf_op jit(solution)/shard_map/ppermute | solution.py:100
  87.0 6.4 %collective-permute-start.10 = (bf16[64,768]{1,0:T(8,128)(2,1)S(1)}, bf16[64,768]{1,0:T(8,128)(2,1)S(1)}, u32[]{:S(2)}, u32[]{:S(2)}) collective-permute-start(bf16[64,768]{1,0:T(8,128)(2,1)S(1)} %multiply_convert_fusion.1), channel_id=1, source_target_pairs={{0,2},{1,3},{2,0},{3,1},{4,6},{5,7},{6,4},{7,5},{8,10},{9,11},{10,... | collective-permute-start | bytes 294920 | tf_op jit(solution)/shard_map/ppermute | solution.py:100
  93.5 5.7 %collective-permute-start.11 = (bf16[64,1536]{1,0:T(8,128)(2,1)S(1)}, bf16[64,1536]{1,0:T(8,128)(2,1)S(1)}, u32[]{:S(2)}, u32[]{:S(2)}) collective-permute-start(bf16[64,1536]{1,0:T(8,128)(2,1)S(1)} %maximum_select_fusion.2), channel_id=1, source_target_pairs={{0,1},{1,0},{2,3},{3,2},{4,5},{5,4},{6,7},{7,6},{8,9},{9,8},{10,11... | collective-permute-start | bytes 589832 | tf_op jit(solution)/shard_map/ppermute | solution.py:100
  104.0 1.3 %collective-permute-start.12 = (bf16[2,16,1280]{2,1,0:T(8,128)(2,1)S(1)}, bf16[2,16,1280]{2,1,0:T(8,128)(2,1)S(1)}, u32[]{:S(2)}, u32[]{:S(2)}) collective-permute-start(bf16[2,16,1280]{2,1,0:T(8,128)(2,1)S(1)} %fusion.10), channel_id=1, source_target_pairs={{0,4},{4,0},{8,12},{12,8},{1,5},{5,1},{9,13},{13,9},{2,6},{6,2},{1... | collective-permute-start | bytes 245768 | tf_op jit(solution)/shard_map/ppermute | solution.py:100
  105.4 4.1 %collective-permute-start.13 = (bf16[1,16,1280]{2,1,0:T(8,128)(2,1)S(1)}, bf16[1,16,1280]{2,1,0:T(8,128)(2,1)S(1)}, u32[]{:S(2)}, u32[]{:S(2)}) collective-permute-start(bf16[1,16,1280]{2,1,0:T(8,128)(2,1)S(1)} %fusion.14), channel_id=1, source_target_pairs={{0,8},{4,12},{8,0},{12,4},{1,9},{5,13},{9,1},{13,5},{2,10},{6,14},... | collective-permute-start | bytes 122888 | tf_op jit(solution)/shard_map/ppermute | solution.py:100

commit v16 on v11

--- a/solution.py
+++ b/solution.py
@@ -15,8 +15,8 @@
 masked_score = -1e30
 
 
-def attend_kernel(page_table, lengths, queries, cache_pool, contexts, keys, copy_sems,
-                  *, latent, score_scale):
+def attend_kernel(page_table, lengths, queries, cache_pool, contexts, keys, score_ref, row_max_ref,
+                  denominator_ref, weighted_ref, copy_sems, *, latent, score_scale, chunk):
     req_dev, pages_req = page_table.shape
     page_size = cache_pool.shape[2]
     head_count = queries.shape[2]
@@ -36,26 +36,43 @@
         lax.fori_loop(0, pages_req, start, 0)
 
     span = pages_req * page_size
-    positions = lax.broadcasted_iota(jnp.int32, (head_count, span), 1)
+    positions = lax.broadcasted_iota(jnp.int32, (head_count, chunk), 1)
     for slot in range(req_dev):
         def finish(page, carry, slot=slot):
             page_copy(slot, page).wait()
             return carry
 
         lax.fori_loop(0, pages_req, finish, 0)
-        live = positions < lengths[slot]
+        length = lengths[slot]
         query_rows = jnp.transpose(queries[slot])
-        scores = jnp.dot(query_rows, keys[slot], preferred_element_type=jnp.float32) * score_scale
-        scores = jnp.where(live, scores, masked_score)
-        row_max = jnp.max(scores, axis=1, keepdims=True)
-        exponent = jnp.exp(scores - row_max)
-        denominator = jnp.sum(exponent, axis=1, keepdims=True)
-        weighted = lax.dot_general(
-            exponent.astype(jnp.bfloat16),
-            keys[slot, :latent, :],
-            (((1,), (1,)), ((), ())),
-            preferred_element_type=jnp.float32,
-        )
+        row_max_ref[...] = jnp.full(row_max_ref.shape, masked_score, jnp.float32)
+        for index, first in enumerate(range(0, span, chunk)):
+            @pl.when(first < length)
+            def _(index=index, first=first):
+                block = jnp.dot(
+                    query_rows, keys[slot, :, first:first + chunk], preferred_element_type=jnp.float32
+                ) * score_scale
+                block = jnp.where(positions + first < length, block, masked_score)
+                score_ref[index] = block
+                row_max_ref[...] = jnp.maximum(row_max_ref[...], jnp.max(block, axis=1, keepdims=True))
+
+        row_max = row_max_ref[...]
+        denominator_ref[...] = jnp.zeros_like(denominator_ref)
+        weighted_ref[...] = jnp.zeros_like(weighted_ref)
+        for index, first in enumerate(range(0, span, chunk)):
+            @pl.when(first < length)
+            def _(index=index, first=first):
+                exponent = jnp.exp(score_ref[index] - row_max)
+                denominator_ref[...] += jnp.sum(exponent, axis=1, keepdims=True)
+                weighted_ref[...] += lax.dot_general(
+                    exponent.astype(jnp.bfloat16),
+                    keys[slot, :latent, first:first + chunk],
+                    (((1,), (1,)), ((), ())),
+                    preferred_element_type=jnp.float32,
+                )
+
+        weighted = weighted_ref[...]
+        denominator = denominator_ref[...]
         blocks, block_heads = contexts.shape[0], head_count // contexts.shape[0]
         context = (weighted / denominator).reshape(blocks, block_heads, latent)
         contexts[:, slot * block_heads:(slot + 1) * block_heads, :] = context.astype(contexts.dtype)
@@ -67,7 +84,9 @@
     query_columns = jnp.swapaxes(queries, 1, 2)
     page_size = cache_pool.shape[1]
     cache_columns = jnp.swapaxes(cache_pool, 1, 2)
-    kernel = functools.partial(attend_kernel, latent=latent, score_scale=score_scale)
+    span = pages_req * page_size
+    chunk = min(512, span)
+    kernel = functools.partial(attend_kernel, latent=latent, score_scale=score_scale, chunk=chunk)
     return pl.pallas_call(
         kernel,
         out_shape=jax.ShapeDtypeStruct((blocks, req_dev * (head_count // blocks), latent), jnp.bfloat16),
@@ -79,7 +98,11 @@
         ],
         out_specs=pl.BlockSpec(memory_space=pltpu.VMEM),
         scratch_shapes=[
-            pltpu.VMEM((req_dev, width, pages_req * page_size), jnp.bfloat16),
+            pltpu.VMEM((req_dev, width, span), jnp.bfloat16),
+            pltpu.VMEM((span // chunk, head_count, chunk), jnp.float32),
+            pltpu.VMEM((head_count, 1), jnp.float32),
+            pltpu.VMEM((head_count, 1), jnp.float32),
+            pltpu.VMEM((head_count, latent), jnp.float32),
             pltpu.SemaphoreType.DMA((req_dev * pages_req,)),
         ],
         compiler_params=pltpu.CompilerParams(vmem_limit_bytes=48 * 1024 * 1024),

time: 111 us -> 114 us (1.027)
  starting transfers between devices: 17.7 us -> 19.8 us
    all_to_all x1, starting transfers between devices: 7.36 us -> 9.4 us  [shards(): lax.all_to_all(contexts, ('dp', 'sub'), split_axis=0, concat_axis=0, tile...]
where the time goes in v16:
time: 114 us; the launch traced here: 113 us
  waiting for transfers between devices  46.8 us (41%)
  starting transfers between devices  19.8 us (17%)
  blocking collectives  16.4 us (14%)
  matrix products  14.1 us (12%)
  Pallas kernels  10.1 us (9%)
  local copies, waits for them, and re-layouts  3.16 us (3%)
  other arithmetic  1.45 us (1%)
    ppermute x14, waiting for transfers between devices, swap_with(): return lax.ppermute(x, axis, [(i, i ^ distance) for i in range(size)])  38.4 us
    all_gather x1, blocking collectives, shards(): group_values = lax.all_gather(values, 'sub', axis=1, tiled=True)  16.4 us
    ppermute x14, starting transfers between devices, swap_with(): return lax.ppermute(x, axis, [(i, i ^ distance) for i in range(size)])  10.4 us
    pallas_call x1, Pallas kernels, attend_all(): pl.pallas_call(kernel, out_shape=jax.ShapeDtypeStruct((blocks, req_dev *...  10.1 us
    all_to_all x1, starting transfers between devices, shards(): lax.all_to_all(contexts, ('dp', 'sub'), split_axis=0, concat_axis=0, tile...  9.4 us
    all_to_all x1, waiting for transfers between devices, shards(): lax.all_to_all(contexts, ('dp', 'sub'), split_axis=0, concat_axis=0, tile...  8.35 us
    dot_general x1, matrix products, shards(): jnp.dot(group_values, out_proj, preferred_element_type=jnp.float32)  6.04 us
    dot_general x1, matrix products, shards(): jnp.dot(hidden_units, down_proj, preferred_element_type=jnp.float32)  4.7 us
  transfers between devices with their start and end apart: 15, of which 12 were waited for; matrix products, arithmetic and copies ran while one was open for 9% of the time, Pallas kernels for 0%

profile of v16, /device:TPU:0, one launch (start us, length us, event | category | flops | bytes accessed | tf_op | source)
XLA Modules:
  0.0 112.6 jit_solution(4151920047344458413)
XLA Ops:
  0.6 0.0 copy-start
  0.6 0.0 copy-start.1
  0.7 1.1 %copy-done.1 = bf16[4,128,576]{1,2,0:T(8,128)(2,1)S(1)} copy-done((bf16[4,128,576]{1,2,0:T(8,128)(2,1)S(1)}, bf16[4,128,576]{1,2,0:T(8,128)(2,1)}, u32[]{:S(2)}) %copy-start.1) | copy-done | bytes 589848
  1.8 0.0 copy-start.2
  1.8 0.7 copy-done.2
  2.5 0.0 copy-start.3
  2.5 0.7 copy-done.3
  3.1 0.0 copy-start.4
  3.1 0.0 copy-start.5
  3.1 10.1 %shard_map.122 = bf16[16,32,512]{2,1,0:T(8,128)(2,1)} custom-call(s32[4,16]{1,0:T(4,128)S(1)} %copy-done.2, s32[4]{0:T(128)S(1)} %copy-done.3, bf16[4,576,128]{2,1,0:T(8,128)(2,1)S(1)} %bitcast.58, bf16[64,576,128]{2,1,0:T(8,128)(2,1)} %bitcast.63), custom_call_target="tpu_custom_call" | custom-call | tf_op jit(solution)/shard_map/pallas_call | solution.py:90
  13.2 9.4 %all-to-all-start = ((bf16[16,32,512]{2,1,0:T(8,128)(2,1)}), bf16[16,32,512]{2,1,0:T(8,128)(2,1)S(1)}, u32[]{:S(2)}, u32[]{:S(2)}) async-start(bf16[16,32,512]{2,1,0:T(8,128)(2,1)} %shard_map.122), calls=%async_computation | async-start | bytes 1048576 | tf_op jit(solution)/shard_map/all_to_all | solution.py:244
  22.6 0.0 copy-done.4
  22.7 2.0 %collective-permute-start.2 = (bf16[1,16,1280]{2,1,0:T(8,128)(2,1)S(1)}, bf16[1,16,1280]{2,1,0:T(8,128)(2,1)S(1)}, u32[]{:S(2)}, u32[]{:S(2)}) collective-permute-start(bf16[1,16,1280]{2,1,0:T(8,128)(2,1)S(1)} %bitcast.68), channel_id=1, source_target_pairs={{0,8},{4,12},{8,0},{12,4},{1,9},{5,13},{9,1},{13,5},{2,10},{6,14},... | collective-permute-start | bytes 122888 | tf_op jit(solution)/shard_map/ppermute | solution.py:113
  24.6 0.0 copy-done.5
  24.6 5.2 %collective-permute-done.2 = bf16[1,16,1280]{2,1,0:T(8,128)(2,1)S(1)} collective-permute-done((bf16[1,16,1280]{2,1,0:T(8,128)(2,1)S(1)}, bf16[1,16,1280]{2,1,0:T(8,128)(2,1)S(1)}, u32[]{:S(2)}, u32[]{:S(2)}) %collective-permute-start.2) | collective-permute-done | bytes 40992 | tf_op jit(solution)/shard_map/ppermute | solution.py:113
  29.9 0.1 collective-permute-start.3
  30.0 8.3 %all-to-all-done = bf16[16,32,512]{2,1,0:T(8,128)(2,1)S(1)} async-done(((bf16[16,32,512]{2,1,0:T(8,128)(2,1)}), bf16[16,32,512]{2,1,0:T(8,128)(2,1)S(1)}, u32[]{:S(2)}, u32[]{:S(2)}) %all-to-all-start) | async-done | bytes 524320 | tf_op jit(solution)/shard_map/all_to_all | solution.py:244
  38.3 0.0 copy-done
  38.3 0.4 fusion
  38.7 0.0 slice-start
  38.8 16.4 %all_gather.3 = bf16[64,4096]{1,0:T(8,128)(2,1)S(1)} all-gather(bf16[64,1024]{1,0:T(8,128)(2,1)S(1)} %bitcast.67), channel_id=1, replica_groups=mesh['grp'=2,'dp'=4,'sub'=4] {'sub'}, dimensions={1}, use_global_device_ids=true | all-gather | bytes 655360 | tf_op jit(solution)/shard_map/all_gather | solution.py:249
  55.1 0.0 slice-start.1
  55.1 6.0 %convolution_convert_fusion = bf16[64,1280]{1,0:T(8,128)(2,1)S(1)} fusion(bf16[64,4096]{1,0:T(8,128)(2,1)S(1)} %all_gather.3, bf16[4096,1280]{1,0:T(8,128)(2,1)} %param.17), kind=kOutput, calls=%fused_computation | convolution fusion | flops 671170560 | bytes 11173888 | tf_op jit(solution)/shard_map/dot_general | solution.py:253
  61.2 0.1 collective-permute-start
  61.3 1.4 %collective-permute-done = bf16[64,1280]{1,0:T(8,128)(2,1)S(1)} collective-permute-done((bf16[64,1280]{1,0:T(8,128)(2,1)S(1)}, bf16[64,1280]{1,0:T(8,128)(2,1)S(1)}, u32[]{:S(2)}, u32[]{:S(2)}) %collective-permute-start) | collective-permute-done | bytes 163872 | tf_op jit(solution)/shard_map/ppermute | solution.py:113
  62.7 0.7 collective-permute-start.1
  63.3 0.0 collective-permute-done.3
  63.4 5.6 %collective-permute-done.1 = bf16[64,1280]{1,0:T(8,128)(2,1)S(1)} collective-permute-done((bf16[64,1280]{1,0:T(8,128)(2,1)S(1)}, bf16[64,1280]{1,0:T(8,128)(2,1)S(1)}, u32[]{:S(2)}, u32[]{:S(2)}) %collective-permute-start.1) | collective-permute-done | bytes 163872 | tf_op jit(solution)/shard_map/ppermute | solution.py:113
  69.0 0.0 slice-start.2
  69.0 0.2 multiply_reduce_fusion
  69.2 0.1 collective-permute-start.6
  69.3 0.0 slice-done
  69.3 0.0 slice-done.1
  69.3 0.0 slice-start.3
  69.3 1.5 %fusion.12 = f32[64,3072]{1,0:T(8,128)S(1)} fusion(bf16[1280,3072]{1,0:T(8,128)(2,1)S(1)} %bitcast.60, f32[64,1280]{1,0:T(8,128)S(1)} %get-tuple-element.3, f32[1280]{0:T(1024)S(1)} %convert_element_type.106), kind=kOutput, calls=%fused_computation.40 | convolution fusion | flops 503480320 | bytes 8983552 | tf_op jit(solution)/shard_map/dot_general | solution.py:260
  70.8 2.0 %collective-permute-start.8 = (bf16[64,1536]{1,0:T(8,128)(2,1)S(1)}, bf16[64,1536]{1,0:T(8,128)(2,1)S(1)}, u32[]{:S(2)}, u32[]{:S(2)}) collective-permute-start(bf16[64,1536]{1,0:T(8,128)(2,1)S(1)} %select_convert_fusion), channel_id=1, source_target_pairs={{0,1},{1,0},{2,3},{3,2},{4,5},{5,4},{6,7},{7,6},{8,9},{9,8},{10,11... | collective-permute-start | bytes 589832 | tf_op jit(solution)/shard_map/ppermute | solution.py:113
  72.9 0.0 slice-done.2
  72.9 0.0 slice-done.3
  72.9 1.5 %fusion.13 = f32[64,3072]{1,0:T(8,128)S(1)} fusion(bf16[1280,3072]{1,0:T(8,128)(2,1)S(1)} %bitcast.62, f32[64,1280]{1,0:T(8,128)S(1)} %get-tuple-element.3, f32[1280]{0:T(1024)S(1)} %convert_element_type.106), kind=kOutput, calls=%fused_computation.41 | convolution fusion | flops 503480320 | bytes 8983552 | tf_op jit(solution)/shard_map/dot_general | solution.py:259
  74.4 0.5 collective-permute-start.4
  74.9 0.0 collective-permute-done.6
  74.9 0.9 collective-permute-start.7
  75.8 2.4 %collective-permute-done.8 = bf16[64,1536]{1,0:T(8,128)(2,1)S(1)} collective-permute-done((bf16[64,1536]{1,0:T(8,128)(2,1)S(1)}, bf16[64,1536]{1,0:T(8,128)(2,1)S(1)}, u32[]{:S(2)}, u32[]{:S(2)}) %collective-permute-start.8) | collective-permute-done | bytes 196640 | tf_op jit(solution)/shard_map/ppermute | solution.py:113
  78.2 0.1 convert_add_fusion
  78.3 1.7 %collective-permute-start.9 = (bf16[64,768]{1,0:T(8,128)(2,1)S(1)}, bf16[64,768]{1,0:T(8,128)(2,1)S(1)}, u32[]{:S(2)}, u32[]{:S(2)}) collective-permute-start(bf16[64,768]{1,0:T(8,128)(2,1)S(1)} %select_convert_fusion.2), channel_id=1, source_target_pairs={{0,2},{1,3},{2,0},{3,1},{4,6},{5,7},{6,4},{7,5},{8,10},{9,11},{10,... | collective-permute-start | bytes 294920 | tf_op jit(solution)/shard_map/ppermute | solution.py:113
  80.1 2.2 %collective-permute-done.4 = bf16[64,1536]{1,0:T(8,128)(2,1)S(1)} collective-permute-done((bf16[64,1536]{1,0:T(8,128)(2,1)S(1)}, bf16[64,1536]{1,0:T(8,128)(2,1)S(1)}, u32[]{:S(2)}, u32[]{:S(2)}) %collective-permute-start.4) | collective-permute-done | bytes 196640 | tf_op jit(solution)/shard_map/ppermute | solution.py:113
  82.3 0.1 convert_add_fusion.1
  82.4 1.4 %collective-permute-start.5 = (bf16[64,768]{1,0:T(8,128)(2,1)S(1)}, bf16[64,768]{1,0:T(8,128)(2,1)S(1)}, u32[]{:S(2)}, u32[]{:S(2)}) collective-permute-start(bf16[64,768]{1,0:T(8,128)(2,1)S(1)} %select_convert_fusion.3), channel_id=1, source_target_pairs={{0,2},{1,3},{2,0},{3,1},{4,6},{5,7},{6,4},{7,5},{8,10},{9,11},{10,... | collective-permute-start | bytes 294920 | tf_op jit(solution)/shard_map/ppermute | solution.py:113
  83.8 0.0 collective-permute-done.7
  83.8 0.1 collective-permute-done.9
  83.9 5.5 %collective-permute-done.5 = bf16[64,768]{1,0:T(8,128)(2,1)S(1)} collective-permute-done((bf16[64,768]{1,0:T(8,128)(2,1)S(1)}, bf16[64,768]{1,0:T(8,128)(2,1)S(1)}, u32[]{:S(2)}, u32[]{:S(2)}) %collective-permute-start.5) | collective-permute-done | bytes 98336 | tf_op jit(solution)/shard_map/ppermute | solution.py:113
  89.4 0.1 multiply_convert_fusion.1
  89.6 0.1 collective-permute-start.10
  89.6 6.4 %collective-permute-done.10 = bf16[64,768]{1,0:T(8,128)(2,1)S(1)} collective-permute-done((bf16[64,768]{1,0:T(8,128)(2,1)S(1)}, bf16[64,768]{1,0:T(8,128)(2,1)S(1)}, u32[]{:S(2)}, u32[]{:S(2)}) %collective-permute-start.10) | collective-permute-done | bytes 98336 | tf_op jit(solution)/shard_map/ppermute | solution.py:113
  96.0 0.1 collective-permute-start.11
  96.1 5.7 %collective-permute-done.11 = bf16[64,1536]{1,0:T(8,128)(2,1)S(1)} collective-permute-done((bf16[64,1536]{1,0:T(8,128)(2,1)S(1)}, bf16[64,1536]{1,0:T(8,128)(2,1)S(1)}, u32[]{:S(2)}, u32[]{:S(2)}) %collective-permute-start.11) | collective-permute-done | bytes 196640 | tf_op jit(solution)/shard_map/ppermute | solution.py:113
  101.8 4.7 %fusion.2 = f32[64,1280]{1,0:T(8,128)S(1)} fusion(bf16[3072,1280]{1,0:T(8,128)(2,1)} %param.21, bf16[64,1536]{1,0:T(8,128)(2,1)S(1)} %maximum_select_fusion.2, bf16[64,1536]{1,0:T(8,128)(2,1)S(1)} %collective-permute-done.11, pred[]{:T(512)S(6)} %ne.18), kind=kOutput, calls=%fused_computation.5 | convolution fusion | flops 505085952 | bytes 8585217 | tf_op jit(solution)/shard_map/dot_general | solution.py:266
  106.5 0.1 collective-permute-start.12
  106.6 1.2 %collective-permute-done.12 = bf16[2,16,1280]{2,1,0:T(8,128)(2,1)S(1)} collective-permute-done((bf16[2,16,1280]{2,1,0:T(8,128)(2,1)S(1)}, bf16[2,16,1280]{2,1,0:T(8,128)(2,1)S(1)}, u32[]{:S(2)}, u32[]{:S(2)}) %collective-permute-start.12) | collective-permute-done | bytes 81952 | tf_op jit(solution)/shard_map/ppermute | solution.py:113
  107.9 0.7 collective-permute-start.13
  108.6 0.6 dynamic-slice_convert_fusion
  109.2 2.7 %collective-permute-done.13 = bf16[1,16,1280]{2,1,0:T(8,128)(2,1)S(1)} collective-permute-done((bf16[1,16,1280]{2,1,0:T(8,128)(2,1)S(1)}, bf16[1,16,1280]{2,1,0:T(8,128)(2,1)S(1)}, u32[]{:S(2)}, u32[]{:S(2)}) %collective-permute-start.13) | collective-permute-done | bytes 40992 | tf_op jit(solution)/shard_map/ppermute | solution.py:113
  112.0 0.6 fusion.11
  (19 shorter events, 0.4 us)
Async XLA Ops:
  0.6 37.7 %copy-start = (bf16[8,512,128]{2,1,0:T(8,128)(2,1)S(1)}, bf16[8,512,128]{2,1,0:T(8,128)(2,1)}, u32[]{:S(2)}) copy-start(bf16[8,512,128]{2,1,0:T(8,128)(2,1)} %param.16) | copy-start | bytes 3145732
  0.6 1.2 %copy-start.1 = (bf16[4,128,576]{1,2,0:T(8,128)(2,1)S(1)}, bf16[4,128,576]{1,2,0:T(8,128)(2,1)}, u32[]{:S(2)}) copy-start(bf16[4,128,576]{1,2,0:T(8,128)(2,1)} %param.12) | copy-start | bytes 1769476
  1.8 0.7 copy-start.2
  2.5 0.7 copy-start.3
  3.1 19.5 %copy-start.4 = (bf16[16,1280]{1,0:T(8,128)(2,1)S(1)}, bf16[16,1280]{1,0:T(8,128)(2,1)}, u32[]{:S(2)}) copy-start(bf16[16,1280]{1,0:T(8,128)(2,1)} %param.11) | copy-start | bytes 122884
  3.1 21.5 %copy-start.5 = (bf16[1280]{0:T(1024)(128)(2,1)S(1)}, bf16[1280]{0:T(1024)(128)(2,1)}, u32[]{:S(2)}) copy-start(bf16[1280]{0:T(1024)(128)(2,1)} %param.18) | copy-start | bytes 7684
  13.2 25.1 %all-to-all-start = ((bf16[16,32,512]{2,1,0:T(8,128)(2,1)}), bf16[16,32,512]{2,1,0:T(8,128)(2,1)S(1)}, u32[]{:S(2)}, u32[]{:S(2)}) async-start(bf16[16,32,512]{2,1,0:T(8,128)(2,1)} %shard_map.122), calls=%async_computation | async-start | bytes 1048576 | tf_op jit(solution)/shard_map/all_to_all | solution.py:244
  22.7 7.2 %collective-permute-start.2 = (bf16[1,16,1280]{2,1,0:T(8,128)(2,1)S(1)}, bf16[1,16,1280]{2,1,0:T(8,128)(2,1)S(1)}, u32[]{:S(2)}, u32[]{:S(2)}) collective-permute-start(bf16[1,16,1280]{2,1,0:T(8,128)(2,1)S(1)} %bitcast.68), channel_id=1, source_target_pairs={{0,8},{4,12},{8,0},{12,4},{1,9},{5,13},{9,1},{13,5},{2,10},{6,14},... | collective-permute-start | bytes 122888 | tf_op jit(solution)/shard_map/ppermute | solution.py:113
  29.9 33.4 %collective-permute-start.3 = (bf16[2,16,1280]{2,1,0:T(8,128)(2,1)S(1)}, bf16[2,16,1280]{2,1,0:T(8,128)(2,1)S(1)}, u32[]{:S(2)}, u32[]{:S(2)}) collective-permute-start(bf16[2,16,1280]{2,1,0:T(8,128)(2,1)S(1)} %maximum_select_fusion.4), channel_id=1, source_target_pairs={{0,4},{4,0},{8,12},{12,8},{1,5},{5,1},{9,13},{13,9},{2,6},{6,2},{1... | collective-permute-start | bytes 245768 | tf_op jit(solution)/shard_map/ppermute | solution.py:113
  38.7 30.5 %slice-start = ((s8[7864320]{0:T(1024)(128)(4,1)}), s8[4194304]{0:T(1024)(128)(4,1)S(1)}, s32[]{:S(2)}) async-start(s8[7864320]{0:T(1024)(128)(4,1)} %bitcast.59), calls=%async_computation.1 | async-start | bytes 8388608
  55.1 14.1 %slice-start.1 = ((s8[7864320]{0:T(1024)(128)(4,1)}), s8[3670016]{0:T(1024)(128)(4,1)S(1)}, s32[]{:S(2)}) async-start(s8[7864320]{0:T(1024)(128)(4,1)} %bitcast.59), calls=%async_computation.2 | async-start | bytes 7340032
  61.2 1.5 %collective-permute-start = (bf16[64,1280]{1,0:T(8,128)(2,1)S(1)}, bf16[64,1280]{1,0:T(8,128)(2,1)S(1)}, u32[]{:S(2)}, u32[]{:S(2)}) collective-permute-start(bf16[64,1280]{1,0:T(8,128)(2,1)S(1)} %convolution_convert_fusion), channel_id=1, source_target_pairs={{0,4},{4,0},{8,12},{12,8},{1,5},{5,1},{9,13},{13,9},{2,6},{6,2},{1... | collective-permute-start | bytes 491528 | tf_op jit(solution)/shard_map/ppermute | solution.py:113
  62.7 6.3 %collective-permute-start.1 = (bf16[64,1280]{1,0:T(8,128)(2,1)S(1)}, bf16[64,1280]{1,0:T(8,128)(2,1)S(1)}, u32[]{:S(2)}, u32[]{:S(2)}) collective-permute-start(bf16[64,1280]{1,0:T(8,128)(2,1)S(1)} %add_convert_fusion), channel_id=1, source_target_pairs={{0,8},{4,12},{8,0},{12,4},{1,9},{5,13},{9,1},{13,5},{2,10},{6,14},... | collective-permute-start | bytes 491528 | tf_op jit(solution)/shard_map/ppermute | solution.py:113
  69.0 3.9 %slice-start.2 = ((s8[7864320]{0:T(1024)(128)(4,1)}), s8[4194304]{0:T(1024)(128)(4,1)S(1)}, s32[]{:S(2)}) async-start(s8[7864320]{0:T(1024)(128)(4,1)} %bitcast.61), calls=%async_computation.3 | async-start | bytes 8388608
  69.2 5.7 %collective-permute-start.6 = (f32[64]{0:T(128)S(1)}, f32[64]{0:T(128)S(1)}, u32[]{:S(2)}, u32[]{:S(2)}) collective-permute-start(f32[64]{0:T(128)S(1)} %get-tuple-element.2), channel_id=1, source_target_pairs={{0,1},{1,0},{2,3},{3,2},{4,5},{5,4},{6,7},{7,6},{8,9},{9,8},{10,11... | collective-permute-start | bytes 776 | tf_op jit(solution)/shard_map/ppermute | solution.py:113
  69.3 3.6 %slice-start.3 = ((s8[7864320]{0:T(1024)(128)(4,1)}), s8[3670016]{0:T(1024)(128)(4,1)S(1)}, s32[]{:S(2)}) async-start(s8[7864320]{0:T(1024)(128)(4,1)} %bitcast.61), calls=%async_computation.4 | async-start | bytes 7340032
  70.8 7.4 %collective-permute-start.8 = (bf16[64,1536]{1,0:T(8,128)(2,1)S(1)}, bf16[64,1536]{1,0:T(8,128)(2,1)S(1)}, u32[]{:S(2)}, u32[]{:S(2)}) collective-permute-start(bf16[64,1536]{1,0:T(8,128)(2,1)S(1)} %select_convert_fusion), channel_id=1, source_target_pairs={{0,1},{1,0},{2,3},{3,2},{4,5},{5,4},{6,7},{7,6},{8,9},{9,8},{10,11... | collective-permute-start | bytes 589832 | tf_op jit(solution)/shard_map/ppermute | solution.py:113
  74.4 7.9 %collective-permute-start.4 = (bf16[64,1536]{1,0:T(8,128)(2,1)S(1)}, bf16[64,1536]{1,0:T(8,128)(2,1)S(1)}, u32[]{:S(2)}, u32[]{:S(2)}) collective-permute-start(bf16[64,1536]{1,0:T(8,128)(2,1)S(1)} %select_convert_fusion.1), channel_id=1, source_target_pairs={{0,1},{1,0},{2,3},{3,2},{4,5},{5,4},{6,7},{7,6},{8,9},{9,8},{10,11... | collective-permute-start | bytes 589832 | tf_op jit(solution)/shard_map/ppermute | solution.py:113
  74.9 8.9 %collective-permute-start.7 = (f32[64]{0:T(128)S(1)}, f32[64]{0:T(128)S(1)}, u32[]{:S(2)}, u32[]{:S(2)}) collective-permute-start(f32[64]{0:T(128)S(1)} %add.56), channel_id=1, source_target_pairs={{0,2},{1,3},{2,0},{3,1},{4,6},{5,7},{6,4},{7,5},{8,10},{9,11},{10,... | collective-permute-start | bytes 776 | tf_op jit(solution)/shard_map/ppermute | solution.py:113
  78.3 5.6 %collective-permute-start.9 = (bf16[64,768]{1,0:T(8,128)(2,1)S(1)}, bf16[64,768]{1,0:T(8,128)(2,1)S(1)}, u32[]{:S(2)}, u32[]{:S(2)}) collective-permute-start(bf16[64,768]{1,0:T(8,128)(2,1)S(1)} %select_convert_fusion.2), channel_id=1, source_target_pairs={{0,2},{1,3},{2,0},{3,1},{4,6},{5,7},{6,4},{7,5},{8,10},{9,11},{10,... | collective-permute-start | bytes 294920 | tf_op jit(solution)/shard_map/ppermute | solution.py:113
  82.4 7.0 %collective-permute-start.5 = (bf16[64,768]{1,0:T(8,128)(2,1)S(1)}, bf16[64,768]{1,0:T(8,128)(2,1)S(1)}, u32[]{:S(2)}, u32[]{:S(2)}) collective-permute-start(bf16[64,768]{1,0:T(8,128)(2,1)S(1)} %select_convert_fusion.3), channel_id=1, source_target_pairs={{0,2},{1,3},{2,0},{3,1},{4,6},{5,7},{6,4},{7,5},{8,10},{9,11},{10,... | collective-permute-start | bytes 294920 | tf_op jit(solution)/shard_map/ppermute | solution.py:113
  89.6 6.4 %collective-permute-start.10 = (bf16[64,768]{1,0:T(8,128)(2,1)S(1)}, bf16[64,768]{1,0:T(8,128)(2,1)S(1)}, u32[]{:S(2)}, u32[]{:S(2)}) collective-permute-start(bf16[64,768]{1,0:T(8,128)(2,1)S(1)} %multiply_convert_fusion.1), channel_id=1, source_target_pairs={{0,2},{1,3},{2,0},{3,1},{4,6},{5,7},{6,4},{7,5},{8,10},{9,11},{10,... | collective-permute-start | bytes 294920 | tf_op jit(solution)/shard_map/ppermute | solution.py:113
  96.0 5.7 %collective-permute-start.11 = (bf16[64,1536]{1,0:T(8,128)(2,1)S(1)}, bf16[64,1536]{1,0:T(8,128)(2,1)S(1)}, u32[]{:S(2)}, u32[]{:S(2)}) collective-permute-start(bf16[64,1536]{1,0:T(8,128)(2,1)S(1)} %maximum_select_fusion.2), channel_id=1, source_target_pairs={{0,1},{1,0},{2,3},{3,2},{4,5},{5,4},{6,7},{7,6},{8,9},{9,8},{10,11... | collective-permute-start | bytes 589832 | tf_op jit(solution)/shard_map/ppermute | solution.py:113
  106.5 1.3 %collective-permute-start.12 = (bf16[2,16,1280]{2,1,0:T(8,128)(2,1)S(1)}, bf16[2,16,1280]{2,1,0:T(8,128)(2,1)S(1)}, u32[]{:S(2)}, u32[]{:S(2)}) collective-permute-start(bf16[2,16,1280]{2,1,0:T(8,128)(2,1)S(1)} %fusion.10), channel_id=1, source_target_pairs={{0,4},{4,0},{8,12},{12,8},{1,5},{5,1},{9,13},{13,9},{2,6},{6,2},{1... | collective-permute-start | bytes 245768 | tf_op jit(solution)/shard_map/ppermute | solution.py:113
  107.9 4.1 %collective-permute-start.13 = (bf16[1,16,1280]{2,1,0:T(8,128)(2,1)S(1)}, bf16[1,16,1280]{2,1,0:T(8,128)(2,1)S(1)}, u32[]{:S(2)}, u32[]{:S(2)}) collective-permute-start(bf16[1,16,1280]{2,1,0:T(8,128)(2,1)S(1)} %fusion.14), channel_id=1, source_target_pairs={{0,8},{4,12},{8,0},{12,4},{1,9},{5,13},{9,1},{13,5},{2,10},{6,14},... | collective-permute-start | bytes 122888 | tf_op jit(solution)/shard_map/ppermute | solution.py:113

commit v17 on v15

--- a/solution.py
+++ b/solution.py
@@ -36,7 +36,7 @@
         lax.fori_loop(0, pages_req, start, 0)
 
     span = pages_req * page_size
-    chunk = min(256, span)
+    chunk = min(1024, span)
     positions = lax.broadcasted_iota(jnp.int32, (head_count, chunk), 1)
     for slot in range(req_dev):
         def finish(page, carry, slot=slot):

time: 110 us -> 111 us (level)
  no operation moved by 1% of the time
where the time goes in v17:
time: 111 us; the launch traced here: 110 us
  waiting for transfers between devices  46.8 us (42%)
  starting transfers between devices  17.7 us (16%)
  blocking collectives  16.2 us (15%)
  matrix products  14.1 us (13%)
  Pallas kernels  9.9 us (9%)
  local copies, waits for them, and re-layouts  3.16 us (3%)
  other arithmetic  1.45 us (1%)
    ppermute x14, waiting for transfers between devices, swap_with(): return lax.ppermute(x, axis, [(i, i ^ distance) for i in range(size)])  38.5 us
    all_gather x1, blocking collectives, shards(): group_values = lax.all_gather(values, 'sub', axis=1, tiled=True)  16.2 us
    ppermute x14, starting transfers between devices, swap_with(): return lax.ppermute(x, axis, [(i, i ^ distance) for i in range(size)])  10.3 us
    pallas_call x1, Pallas kernels, attend_all(): pl.pallas_call(kernel, out_shape=jax.ShapeDtypeStruct((blocks, req_dev *...  9.9 us
    all_to_all x1, waiting for transfers between devices, shards(): lax.all_to_all(contexts, ('dp', 'sub'), split_axis=0, concat_axis=0, tile...  8.35 us
    all_to_all x1, starting transfers between devices, shards(): lax.all_to_all(contexts, ('dp', 'sub'), split_axis=0, concat_axis=0, tile...  7.36 us
    dot_general x1, matrix products, shards(): jnp.dot(group_values, out_proj, preferred_element_type=jnp.float32)  6.04 us
    dot_general x1, matrix products, shards(): jnp.dot(hidden_units, down_proj, preferred_element_type=jnp.float32)  4.7 us
  transfers between devices with their start and end apart: 15, of which 12 were waited for; matrix products, arithmetic and copies ran while one was open for 9% of the time, Pallas kernels for 0%

profile of v17, /device:TPU:0, one launch (start us, length us, event | category | flops | bytes accessed | tf_op | source)
XLA Modules:
  0.0 110.2 jit_solution(5129830235269780625)
XLA Ops:
  0.6 0.0 copy-start
  0.6 0.0 copy-start.1
  0.7 1.1 %copy-done.1 = bf16[4,128,576]{1,2,0:T(8,128)(2,1)S(1)} copy-done((bf16[4,128,576]{1,2,0:T(8,128)(2,1)S(1)}, bf16[4,128,576]{1,2,0:T(8,128)(2,1)}, u32[]{:S(2)}) %copy-start.1) | copy-done | bytes 589848
  1.8 0.0 copy-start.2
  1.8 0.7 copy-done.2
  2.5 0.0 copy-start.3
  2.5 0.7 copy-done.3
  3.1 0.0 copy-start.4
  3.1 0.0 copy-start.5
  3.1 9.9 %shard_map.122 = bf16[16,32,512]{2,1,0:T(8,128)(2,1)} custom-call(s32[4,16]{1,0:T(4,128)S(1)} %copy-done.2, s32[4]{0:T(128)S(1)} %copy-done.3, bf16[4,576,128]{2,1,0:T(8,128)(2,1)S(1)} %bitcast.58, bf16[64,576,128]{2,1,0:T(8,128)(2,1)} %bitcast.63), custom_call_target="tpu_custom_call" | custom-call | tf_op jit(solution)/shard_map/pallas_call | solution.py:81
  13.1 7.4 %all-to-all-start = ((bf16[16,32,512]{2,1,0:T(8,128)(2,1)}), bf16[16,32,512]{2,1,0:T(8,128)(2,1)S(1)}, u32[]{:S(2)}, u32[]{:S(2)}) async-start(bf16[16,32,512]{2,1,0:T(8,128)(2,1)} %shard_map.122), calls=%async_computation | async-start | bytes 1048576 | tf_op jit(solution)/shard_map/all_to_all | solution.py:231
  20.4 0.0 copy-done.4
  20.4 2.0 %collective-permute-start.2 = (bf16[1,16,1280]{2,1,0:T(8,128)(2,1)S(1)}, bf16[1,16,1280]{2,1,0:T(8,128)(2,1)S(1)}, u32[]{:S(2)}, u32[]{:S(2)}) collective-permute-start(bf16[1,16,1280]{2,1,0:T(8,128)(2,1)S(1)} %bitcast.68), channel_id=1, source_target_pairs={{0,8},{4,12},{8,0},{12,4},{1,9},{5,13},{9,1},{13,5},{2,10},{6,14},... | collective-permute-start | bytes 122888 | tf_op jit(solution)/shard_map/ppermute | solution.py:100
  22.4 0.0 copy-done.5
  22.4 5.2 %collective-permute-done.2 = bf16[1,16,1280]{2,1,0:T(8,128)(2,1)S(1)} collective-permute-done((bf16[1,16,1280]{2,1,0:T(8,128)(2,1)S(1)}, bf16[1,16,1280]{2,1,0:T(8,128)(2,1)S(1)}, u32[]{:S(2)}, u32[]{:S(2)}) %collective-permute-start.2) | collective-permute-done | bytes 40992 | tf_op jit(solution)/shard_map/ppermute | solution.py:100
  27.7 0.1 collective-permute-start.3
  27.8 8.3 %all-to-all-done = bf16[16,32,512]{2,1,0:T(8,128)(2,1)S(1)} async-done(((bf16[16,32,512]{2,1,0:T(8,128)(2,1)}), bf16[16,32,512]{2,1,0:T(8,128)(2,1)S(1)}, u32[]{:S(2)}, u32[]{:S(2)}) %all-to-all-start) | async-done | bytes 524320 | tf_op jit(solution)/shard_map/all_to_all | solution.py:231
  36.1 0.0 copy-done
  36.1 0.4 fusion
  36.5 0.0 slice-start
  36.5 16.2 %all_gather.3 = bf16[64,4096]{1,0:T(8,128)(2,1)S(1)} all-gather(bf16[64,1024]{1,0:T(8,128)(2,1)S(1)} %bitcast.67), channel_id=1, replica_groups=mesh['grp'=2,'dp'=4,'sub'=4] {'sub'}, dimensions={1}, use_global_device_ids=true | all-gather | bytes 655360 | tf_op jit(solution)/shard_map/all_gather | solution.py:236
  52.7 0.0 slice-start.1
  52.7 6.0 %convolution_convert_fusion = bf16[64,1280]{1,0:T(8,128)(2,1)S(1)} fusion(bf16[64,4096]{1,0:T(8,128)(2,1)S(1)} %all_gather.3, bf16[4096,1280]{1,0:T(8,128)(2,1)} %param.17), kind=kOutput, calls=%fused_computation | convolution fusion | flops 671170560 | bytes 11173888 | tf_op jit(solution)/shard_map/dot_general | solution.py:240
  58.8 0.1 collective-permute-start
  58.9 1.4 %collective-permute-done = bf16[64,1280]{1,0:T(8,128)(2,1)S(1)} collective-permute-done((bf16[64,1280]{1,0:T(8,128)(2,1)S(1)}, bf16[64,1280]{1,0:T(8,128)(2,1)S(1)}, u32[]{:S(2)}, u32[]{:S(2)}) %collective-permute-start) | collective-permute-done | bytes 163872 | tf_op jit(solution)/shard_map/ppermute | solution.py:100
  60.3 0.7 collective-permute-start.1
  61.0 0.0 collective-permute-done.3
  61.0 5.6 %collective-permute-done.1 = bf16[64,1280]{1,0:T(8,128)(2,1)S(1)} collective-permute-done((bf16[64,1280]{1,0:T(8,128)(2,1)S(1)}, bf16[64,1280]{1,0:T(8,128)(2,1)S(1)}, u32[]{:S(2)}, u32[]{:S(2)}) %collective-permute-start.1) | collective-permute-done | bytes 163872 | tf_op jit(solution)/shard_map/ppermute | solution.py:100
  66.6 0.0 slice-start.2
  66.6 0.2 multiply_reduce_fusion
  66.8 0.1 collective-permute-start.6
  66.9 0.0 slice-done
  66.9 0.0 slice-done.1
  66.9 0.0 slice-start.3
  66.9 1.5 %fusion.12 = f32[64,3072]{1,0:T(8,128)S(1)} fusion(bf16[1280,3072]{1,0:T(8,128)(2,1)S(1)} %bitcast.60, f32[64,1280]{1,0:T(8,128)S(1)} %get-tuple-element.3, f32[1280]{0:T(1024)S(1)} %convert_element_type.106), kind=kOutput, calls=%fused_computation.40 | convolution fusion | flops 503480320 | bytes 8983552 | tf_op jit(solution)/shard_map/dot_general | solution.py:247
  68.4 2.0 %collective-permute-start.8 = (bf16[64,1536]{1,0:T(8,128)(2,1)S(1)}, bf16[64,1536]{1,0:T(8,128)(2,1)S(1)}, u32[]{:S(2)}, u32[]{:S(2)}) collective-permute-start(bf16[64,1536]{1,0:T(8,128)(2,1)S(1)} %select_convert_fusion), channel_id=1, source_target_pairs={{0,1},{1,0},{2,3},{3,2},{4,5},{5,4},{6,7},{7,6},{8,9},{9,8},{10,11... | collective-permute-start | bytes 589832 | tf_op jit(solution)/shard_map/ppermute | solution.py:100
  70.5 0.0 slice-done.2
  70.5 0.0 slice-done.3
  70.5 1.5 %fusion.13 = f32[64,3072]{1,0:T(8,128)S(1)} fusion(bf16[1280,3072]{1,0:T(8,128)(2,1)S(1)} %bitcast.62, f32[64,1280]{1,0:T(8,128)S(1)} %get-tuple-element.3, f32[1280]{0:T(1024)S(1)} %convert_element_type.106), kind=kOutput, calls=%fused_computation.41 | convolution fusion | flops 503480320 | bytes 8983552 | tf_op jit(solution)/shard_map/dot_general | solution.py:246
  72.0 0.5 collective-permute-start.4
  72.5 0.0 collective-permute-done.6
  72.5 0.9 collective-permute-start.7
  73.4 2.4 %collective-permute-done.8 = bf16[64,1536]{1,0:T(8,128)(2,1)S(1)} collective-permute-done((bf16[64,1536]{1,0:T(8,128)(2,1)S(1)}, bf16[64,1536]{1,0:T(8,128)(2,1)S(1)}, u32[]{:S(2)}, u32[]{:S(2)}) %collective-permute-start.8) | collective-permute-done | bytes 196640 | tf_op jit(solution)/shard_map/ppermute | solution.py:100
  75.8 0.1 convert_add_fusion
  75.9 1.7 %collective-permute-start.9 = (bf16[64,768]{1,0:T(8,128)(2,1)S(1)}, bf16[64,768]{1,0:T(8,128)(2,1)S(1)}, u32[]{:S(2)}, u32[]{:S(2)}) collective-permute-start(bf16[64,768]{1,0:T(8,128)(2,1)S(1)} %select_convert_fusion.2), channel_id=1, source_target_pairs={{0,2},{1,3},{2,0},{3,1},{4,6},{5,7},{6,4},{7,5},{8,10},{9,11},{10,... | collective-permute-start | bytes 294920 | tf_op jit(solution)/shard_map/ppermute | solution.py:100
  77.6 2.3 %collective-permute-done.4 = bf16[64,1536]{1,0:T(8,128)(2,1)S(1)} collective-permute-done((bf16[64,1536]{1,0:T(8,128)(2,1)S(1)}, bf16[64,1536]{1,0:T(8,128)(2,1)S(1)}, u32[]{:S(2)}, u32[]{:S(2)}) %collective-permute-start.4) | collective-permute-done | bytes 196640 | tf_op jit(solution)/shard_map/ppermute | solution.py:100
  79.9 0.1 convert_add_fusion.1
  80.0 1.4 %collective-permute-start.5 = (bf16[64,768]{1,0:T(8,128)(2,1)S(1)}, bf16[64,768]{1,0:T(8,128)(2,1)S(1)}, u32[]{:S(2)}, u32[]{:S(2)}) collective-permute-start(bf16[64,768]{1,0:T(8,128)(2,1)S(1)} %select_convert_fusion.3), channel_id=1, source_target_pairs={{0,2},{1,3},{2,0},{3,1},{4,6},{5,7},{6,4},{7,5},{8,10},{9,11},{10,... | collective-permute-start | bytes 294920 | tf_op jit(solution)/shard_map/ppermute | solution.py:100
  81.4 0.0 collective-permute-done.7
  81.4 0.1 collective-permute-done.9
  81.5 5.5 %collective-permute-done.5 = bf16[64,768]{1,0:T(8,128)(2,1)S(1)} collective-permute-done((bf16[64,768]{1,0:T(8,128)(2,1)S(1)}, bf16[64,768]{1,0:T(8,128)(2,1)S(1)}, u32[]{:S(2)}, u32[]{:S(2)}) %collective-permute-start.5) | collective-permute-done | bytes 98336 | tf_op jit(solution)/shard_map/ppermute | solution.py:100
  87.0 0.1 multiply_convert_fusion.1
  87.2 0.1 collective-permute-start.10
  87.2 6.4 %collective-permute-done.10 = bf16[64,768]{1,0:T(8,128)(2,1)S(1)} collective-permute-done((bf16[64,768]{1,0:T(8,128)(2,1)S(1)}, bf16[64,768]{1,0:T(8,128)(2,1)S(1)}, u32[]{:S(2)}, u32[]{:S(2)}) %collective-permute-start.10) | collective-permute-done | bytes 98336 | tf_op jit(solution)/shard_map/ppermute | solution.py:100
  93.6 0.1 collective-permute-start.11
  93.7 5.7 %collective-permute-done.11 = bf16[64,1536]{1,0:T(8,128)(2,1)S(1)} collective-permute-done((bf16[64,1536]{1,0:T(8,128)(2,1)S(1)}, bf16[64,1536]{1,0:T(8,128)(2,1)S(1)}, u32[]{:S(2)}, u32[]{:S(2)}) %collective-permute-start.11) | collective-permute-done | bytes 196640 | tf_op jit(solution)/shard_map/ppermute | solution.py:100
  99.4 4.7 %fusion.2 = f32[64,1280]{1,0:T(8,128)S(1)} fusion(bf16[3072,1280]{1,0:T(8,128)(2,1)} %param.21, bf16[64,1536]{1,0:T(8,128)(2,1)S(1)} %maximum_select_fusion.2, bf16[64,1536]{1,0:T(8,128)(2,1)S(1)} %collective-permute-done.11, pred[]{:T(512)S(6)} %ne.18), kind=kOutput, calls=%fused_computation.5 | convolution fusion | flops 505085952 | bytes 8585217 | tf_op jit(solution)/shard_map/dot_general | solution.py:253
  104.1 0.1 collective-permute-start.12
  104.2 1.2 %collective-permute-done.12 = bf16[2,16,1280]{2,1,0:T(8,128)(2,1)S(1)} collective-permute-done((bf16[2,16,1280]{2,1,0:T(8,128)(2,1)S(1)}, bf16[2,16,1280]{2,1,0:T(8,128)(2,1)S(1)}, u32[]{:S(2)}, u32[]{:S(2)}) %collective-permute-start.12) | collective-permute-done | bytes 81952 | tf_op jit(solution)/shard_map/ppermute | solution.py:100
  105.5 0.7 collective-permute-start.13
  106.2 0.6 dynamic-slice_convert_fusion
  106.8 2.7 %collective-permute-done.13 = bf16[1,16,1280]{2,1,0:T(8,128)(2,1)S(1)} collective-permute-done((bf16[1,16,1280]{2,1,0:T(8,128)(2,1)S(1)}, bf16[1,16,1280]{2,1,0:T(8,128)(2,1)S(1)}, u32[]{:S(2)}, u32[]{:S(2)}) %collective-permute-start.13) | collective-permute-done | bytes 40992 | tf_op jit(solution)/shard_map/ppermute | solution.py:100
  109.6 0.6 fusion.11
  (19 shorter events, 0.4 us)
Async XLA Ops:
  0.6 35.5 %copy-start = (bf16[8,512,128]{2,1,0:T(8,128)(2,1)S(1)}, bf16[8,512,128]{2,1,0:T(8,128)(2,1)}, u32[]{:S(2)}) copy-start(bf16[8,512,128]{2,1,0:T(8,128)(2,1)} %param.16) | copy-start | bytes 3145732
  0.6 1.2 %copy-start.1 = (bf16[4,128,576]{1,2,0:T(8,128)(2,1)S(1)}, bf16[4,128,576]{1,2,0:T(8,128)(2,1)}, u32[]{:S(2)}) copy-start(bf16[4,128,576]{1,2,0:T(8,128)(2,1)} %param.12) | copy-start | bytes 1769476
  1.8 0.7 copy-start.2
  2.5 0.7 copy-start.3
  3.1 17.3 %copy-start.4 = (bf16[16,1280]{1,0:T(8,128)(2,1)S(1)}, bf16[16,1280]{1,0:T(8,128)(2,1)}, u32[]{:S(2)}) copy-start(bf16[16,1280]{1,0:T(8,128)(2,1)} %param.11) | copy-start | bytes 122884
  3.1 19.3 %copy-start.5 = (bf16[1280]{0:T(1024)(128)(2,1)S(1)}, bf16[1280]{0:T(1024)(128)(2,1)}, u32[]{:S(2)}) copy-start(bf16[1280]{0:T(1024)(128)(2,1)} %param.18) | copy-start | bytes 7684
  13.1 23.1 %all-to-all-start = ((bf16[16,32,512]{2,1,0:T(8,128)(2,1)}), bf16[16,32,512]{2,1,0:T(8,128)(2,1)S(1)}, u32[]{:S(2)}, u32[]{:S(2)}) async-start(bf16[16,32,512]{2,1,0:T(8,128)(2,1)} %shard_map.122), calls=%async_computation | async-start | bytes 1048576 | tf_op jit(solution)/shard_map/all_to_all | solution.py:231
  20.4 7.2 %collective-permute-start.2 = (bf16[1,16,1280]{2,1,0:T(8,128)(2,1)S(1)}, bf16[1,16,1280]{2,1,0:T(8,128)(2,1)S(1)}, u32[]{:S(2)}, u32[]{:S(2)}) collective-permute-start(bf16[1,16,1280]{2,1,0:T(8,128)(2,1)S(1)} %bitcast.68), channel_id=1, source_target_pairs={{0,8},{4,12},{8,0},{12,4},{1,9},{5,13},{9,1},{13,5},{2,10},{6,14},... | collective-permute-start | bytes 122888 | tf_op jit(solution)/shard_map/ppermute | solution.py:100
  27.7 33.3 %collective-permute-start.3 = (bf16[2,16,1280]{2,1,0:T(8,128)(2,1)S(1)}, bf16[2,16,1280]{2,1,0:T(8,128)(2,1)S(1)}, u32[]{:S(2)}, u32[]{:S(2)}) collective-permute-start(bf16[2,16,1280]{2,1,0:T(8,128)(2,1)S(1)} %maximum_select_fusion.4), channel_id=1, source_target_pairs={{0,4},{4,0},{8,12},{12,8},{1,5},{5,1},{9,13},{13,9},{2,6},{6,2},{1... | collective-permute-start | bytes 245768 | tf_op jit(solution)/shard_map/ppermute | solution.py:100
  36.5 30.3 %slice-start = ((s8[7864320]{0:T(1024)(128)(4,1)}), s8[4194304]{0:T(1024)(128)(4,1)S(1)}, s32[]{:S(2)}) async-start(s8[7864320]{0:T(1024)(128)(4,1)} %bitcast.59), calls=%async_computation.1 | async-start | bytes 8388608
  52.7 14.1 %slice-start.1 = ((s8[7864320]{0:T(1024)(128)(4,1)}), s8[3670016]{0:T(1024)(128)(4,1)S(1)}, s32[]{:S(2)}) async-start(s8[7864320]{0:T(1024)(128)(4,1)} %bitcast.59), calls=%async_computation.2 | async-start | bytes 7340032
  58.8 1.5 %collective-permute-start = (bf16[64,1280]{1,0:T(8,128)(2,1)S(1)}, bf16[64,1280]{1,0:T(8,128)(2,1)S(1)}, u32[]{:S(2)}, u32[]{:S(2)}) collective-permute-start(bf16[64,1280]{1,0:T(8,128)(2,1)S(1)} %convolution_convert_fusion), channel_id=1, source_target_pairs={{0,4},{4,0},{8,12},{12,8},{1,5},{5,1},{9,13},{13,9},{2,6},{6,2},{1... | collective-permute-start | bytes 491528 | tf_op jit(solution)/shard_map/ppermute | solution.py:100
  60.3 6.3 %collective-permute-start.1 = (bf16[64,1280]{1,0:T(8,128)(2,1)S(1)}, bf16[64,1280]{1,0:T(8,128)(2,1)S(1)}, u32[]{:S(2)}, u32[]{:S(2)}) collective-permute-start(bf16[64,1280]{1,0:T(8,128)(2,1)S(1)} %add_convert_fusion), channel_id=1, source_target_pairs={{0,8},{4,12},{8,0},{12,4},{1,9},{5,13},{9,1},{13,5},{2,10},{6,14},... | collective-permute-start | bytes 491528 | tf_op jit(solution)/shard_map/ppermute | solution.py:100
  66.6 3.9 %slice-start.2 = ((s8[7864320]{0:T(1024)(128)(4,1)}), s8[4194304]{0:T(1024)(128)(4,1)S(1)}, s32[]{:S(2)}) async-start(s8[7864320]{0:T(1024)(128)(4,1)} %bitcast.61), calls=%async_computation.3 | async-start | bytes 8388608
  66.8 5.7 %collective-permute-start.6 = (f32[64]{0:T(128)S(1)}, f32[64]{0:T(128)S(1)}, u32[]{:S(2)}, u32[]{:S(2)}) collective-permute-start(f32[64]{0:T(128)S(1)} %get-tuple-element.2), channel_id=1, source_target_pairs={{0,1},{1,0},{2,3},{3,2},{4,5},{5,4},{6,7},{7,6},{8,9},{9,8},{10,11... | collective-permute-start | bytes 776 | tf_op jit(solution)/shard_map/ppermute | solution.py:100
  66.9 3.6 %slice-start.3 = ((s8[7864320]{0:T(1024)(128)(4,1)}), s8[3670016]{0:T(1024)(128)(4,1)S(1)}, s32[]{:S(2)}) async-start(s8[7864320]{0:T(1024)(128)(4,1)} %bitcast.61), calls=%async_computation.4 | async-start | bytes 7340032
  68.4 7.4 %collective-permute-start.8 = (bf16[64,1536]{1,0:T(8,128)(2,1)S(1)}, bf16[64,1536]{1,0:T(8,128)(2,1)S(1)}, u32[]{:S(2)}, u32[]{:S(2)}) collective-permute-start(bf16[64,1536]{1,0:T(8,128)(2,1)S(1)} %select_convert_fusion), channel_id=1, source_target_pairs={{0,1},{1,0},{2,3},{3,2},{4,5},{5,4},{6,7},{7,6},{8,9},{9,8},{10,11... | collective-permute-start | bytes 589832 | tf_op jit(solution)/shard_map/ppermute | solution.py:100
  72.0 7.9 %collective-permute-start.4 = (bf16[64,1536]{1,0:T(8,128)(2,1)S(1)}, bf16[64,1536]{1,0:T(8,128)(2,1)S(1)}, u32[]{:S(2)}, u32[]{:S(2)}) collective-permute-start(bf16[64,1536]{1,0:T(8,128)(2,1)S(1)} %select_convert_fusion.1), channel_id=1, source_target_pairs={{0,1},{1,0},{2,3},{3,2},{4,5},{5,4},{6,7},{7,6},{8,9},{9,8},{10,11... | collective-permute-start | bytes 589832 | tf_op jit(solution)/shard_map/ppermute | solution.py:100
  72.5 8.8 %collective-permute-start.7 = (f32[64]{0:T(128)S(1)}, f32[64]{0:T(128)S(1)}, u32[]{:S(2)}, u32[]{:S(2)}) collective-permute-start(f32[64]{0:T(128)S(1)} %add.56), channel_id=1, source_target_pairs={{0,2},{1,3},{2,0},{3,1},{4,6},{5,7},{6,4},{7,5},{8,10},{9,11},{10,... | collective-permute-start | bytes 776 | tf_op jit(solution)/shard_map/ppermute | solution.py:100
  75.9 5.6 %collective-permute-start.9 = (bf16[64,768]{1,0:T(8,128)(2,1)S(1)}, bf16[64,768]{1,0:T(8,128)(2,1)S(1)}, u32[]{:S(2)}, u32[]{:S(2)}) collective-permute-start(bf16[64,768]{1,0:T(8,128)(2,1)S(1)} %select_convert_fusion.2), channel_id=1, source_target_pairs={{0,2},{1,3},{2,0},{3,1},{4,6},{5,7},{6,4},{7,5},{8,10},{9,11},{10,... | collective-permute-start | bytes 294920 | tf_op jit(solution)/shard_map/ppermute | solution.py:100
  80.0 7.0 %collective-permute-start.5 = (bf16[64,768]{1,0:T(8,128)(2,1)S(1)}, bf16[64,768]{1,0:T(8,128)(2,1)S(1)}, u32[]{:S(2)}, u32[]{:S(2)}) collective-permute-start(bf16[64,768]{1,0:T(8,128)(2,1)S(1)} %select_convert_fusion.3), channel_id=1, source_target_pairs={{0,2},{1,3},{2,0},{3,1},{4,6},{5,7},{6,4},{7,5},{8,10},{9,11},{10,... | collective-permute-start | bytes 294920 | tf_op jit(solution)/shard_map/ppermute | solution.py:100
  87.2 6.4 %collective-permute-start.10 = (bf16[64,768]{1,0:T(8,128)(2,1)S(1)}, bf16[64,768]{1,0:T(8,128)(2,1)S(1)}, u32[]{:S(2)}, u32[]{:S(2)}) collective-permute-start(bf16[64,768]{1,0:T(8,128)(2,1)S(1)} %multiply_convert_fusion.1), channel_id=1, source_target_pairs={{0,2},{1,3},{2,0},{3,1},{4,6},{5,7},{6,4},{7,5},{8,10},{9,11},{10,... | collective-permute-start | bytes 294920 | tf_op jit(solution)/shard_map/ppermute | solution.py:100
  93.6 5.7 %collective-permute-start.11 = (bf16[64,1536]{1,0:T(8,128)(2,1)S(1)}, bf16[64,1536]{1,0:T(8,128)(2,1)S(1)}, u32[]{:S(2)}, u32[]{:S(2)}) collective-permute-start(bf16[64,1536]{1,0:T(8,128)(2,1)S(1)} %maximum_select_fusion.2), channel_id=1, source_target_pairs={{0,1},{1,0},{2,3},{3,2},{4,5},{5,4},{6,7},{7,6},{8,9},{9,8},{10,11... | collective-permute-start | bytes 589832 | tf_op jit(solution)/shard_map/ppermute | solution.py:100
  104.1 1.3 %collective-permute-start.12 = (bf16[2,16,1280]{2,1,0:T(8,128)(2,1)S(1)}, bf16[2,16,1280]{2,1,0:T(8,128)(2,1)S(1)}, u32[]{:S(2)}, u32[]{:S(2)}) collective-permute-start(bf16[2,16,1280]{2,1,0:T(8,128)(2,1)S(1)} %fusion.10), channel_id=1, source_target_pairs={{0,4},{4,0},{8,12},{12,8},{1,5},{5,1},{9,13},{13,9},{2,6},{6,2},{1... | collective-permute-start | bytes 245768 | tf_op jit(solution)/shard_map/ppermute | solution.py:100
  105.5 4.1 %collective-permute-start.13 = (bf16[1,16,1280]{2,1,0:T(8,128)(2,1)S(1)}, bf16[1,16,1280]{2,1,0:T(8,128)(2,1)S(1)}, u32[]{:S(2)}, u32[]{:S(2)}) collective-permute-start(bf16[1,16,1280]{2,1,0:T(8,128)(2,1)S(1)} %fusion.14), channel_id=1, source_target_pairs={{0,8},{4,12},{8,0},{12,4},{1,9},{5,13},{9,1},{13,5},{2,10},{6,14},... | collective-permute-start | bytes 122888 | tf_op jit(solution)/shard_map/ppermute | solution.py:100

commit v18 on v14

--- a/solution.py
+++ b/solution.py
@@ -127,7 +127,8 @@
         sends = tuple(
             jnp.where(upper, part[:, :half], part[:, half:]).astype(jnp.bfloat16) for part in parts
         )
-        got = swap_with(sends, axis, distance, size)
+        joined = swap_with(jnp.concatenate(sends, axis=1), axis, distance, size)
+        got = jnp.split(joined, len(parts), axis=1)
         parts = tuple(keep + more.astype(jnp.float32) for keep, more in zip(keeps, got))
         distance *= 2
     return parts

time: 110 us -> 119 us (1.082)
  waiting for transfers between devices: 46.8 us -> 53.5 us
  other arithmetic: 1.45 us -> 3.26 us
  local copies, waits for them, and re-layouts: 3.16 us -> 4.95 us
  starting transfers between devices: 17.8 us -> 16.1 us
    ppermute x14 -> x12, waiting for transfers between devices: 38.4 us -> 45.2 us  [swap_with(): return lax.ppermute(x, axis, [(i, i ^ distance) for i in range(size)])]
    unnamed x20, local copies, waits for them, and re-layouts: 2.52 us -> 4.3 us
    ppermute x14 -> x12, starting transfers between devices: 10.4 us -> 8.72 us  [swap_with(): return lax.ppermute(x, axis, [(i, i ^ distance) for i in range(size)])]
  transfers between devices with their start and end apart: 15 -> 13, of which waited for: 12 -> 11; matrix products, arithmetic and copies ran while one was open for 9% -> 7% of each run, Pallas kernels for 0% -> 0%
where the time goes in v18:
time: 119 us
  waiting for transfers between devices  53.5 us (45%)
  blocking collectives  16.2 us (14%)
  starting transfers between devices  16.1 us (14%)
  matrix products  14.1 us (12%)
  Pallas kernels  9.73 us (8%)
  local copies, waits for them, and re-layouts  4.95 us (4%)
  other arithmetic  3.26 us (3%)
    ppermute x12, waiting for transfers between devices, swap_with(): return lax.ppermute(x, axis, [(i, i ^ distance) for i in range(size)])  45.2 us
    all_gather x1, blocking collectives, shards(): group_values = lax.all_gather(values, 'sub', axis=1, tiled=True)  16.2 us
    pallas_call x1, Pallas kernels, attend_all(): pl.pallas_call(kernel, out_shape=jax.ShapeDtypeStruct((blocks, req_dev *...  9.73 us
    ppermute x12, starting transfers between devices, swap_with(): return lax.ppermute(x, axis, [(i, i ^ distance) for i in range(size)])  8.72 us
    all_to_all x1, waiting for transfers between devices, shards(): lax.all_to_all(contexts, ('dp', 'sub'), split_axis=0, concat_axis=0, tile...  8.35 us
    all_to_all x1, starting transfers between devices, shards(): lax.all_to_all(contexts, ('dp', 'sub'), split_axis=0, concat_axis=0, tile...  7.37 us
    dot_general x1, matrix products, shards(): jnp.dot(group_values, out_proj, preferred_element_type=jnp.float32)  6.04 us
    dot_general x1, matrix products, shards(): jnp.dot(hidden_units, down_proj, preferred_element_type=jnp.float32)  4.7 us
  transfers between devices with their start and end apart: 13, of which 11 were waited for; matrix products, arithmetic and copies ran while one was open for 7% of the time, Pallas kernels for 0%

profile of v18, /device:TPU:0, one launch (start us, length us, event | category | flops | bytes accessed | tf_op | source)
XLA Modules:
  0.0 118.7 jit_solution(1278145608636503730)
XLA Ops:
  0.6 0.0 copy-start
  0.6 0.0 copy-start.1
  0.7 1.1 copy-done.1
  1.8 0.0 copy-start.2
  1.8 0.7 copy-done.2
  2.5 0.0 copy-start.3
  2.5 0.7 copy-done.3
  3.1 0.0 copy-start.4
  3.1 0.0 copy-start.5
  3.1 9.7 %shard_map.122 = bf16[16,32,512]{2,1,0:T(8,128)(2,1)} custom-call(s32[4,16]{1,0:T(4,128)S(1)} %copy-done.2, s32[4]{0:T(128)S(1)} %copy-done.3, bf16[4,576,128]{2,1,0:T(8,128)(2,1)S(1)} %bitcast.58, bf16[64,576,128]{2,1,0:T(8,128)(2,1)} %bitcast.63), custom_call_target="tpu_custom_call" | custom-call | tf_op jit(solution)/shard_map/pallas_call | solution.py:81
  12.9 7.4 %all-to-all-start = ((bf16[16,32,512]{2,1,0:T(8,128)(2,1)}), bf16[16,32,512]{2,1,0:T(8,128)(2,1)S(1)}, u32[]{:S(2)}, u32[]{:S(2)}) async-start(bf16[16,32,512]{2,1,0:T(8,128)(2,1)} %shard_map.122), calls=%async_computation | async-start | bytes 1048576 | tf_op jit(solution)/shard_map/all_to_all | solution.py:232
  20.3 0.0 copy-done.4
  20.3 2.0 %collective-permute-start.2 = (bf16[1,16,1280]{2,1,0:T(8,128)(2,1)S(1)}, bf16[1,16,1280]{2,1,0:T(8,128)(2,1)S(1)}, u32[]{:S(2)}, u32[]{:S(2)}) collective-permute-start(bf16[1,16,1280]{2,1,0:T(8,128)(2,1)S(1)} %bitcast.68), channel_id=1, source_target_pairs={{0,8},{4,12},{8,0},{12,4},{1,9},{5,13},{9,1},{13,5},{2,10},{6,14},... | collective-permute-start | bytes 122888 | tf_op jit(solution)/shard_map/ppermute | solution.py:100
  22.3 0.0 copy-done.5
  22.3 5.2 %collective-permute-done.2 = bf16[1,16,1280]{2,1,0:T(8,128)(2,1)S(1)} collective-permute-done((bf16[1,16,1280]{2,1,0:T(8,128)(2,1)S(1)}, bf16[1,16,1280]{2,1,0:T(8,128)(2,1)S(1)}, u32[]{:S(2)}, u32[]{:S(2)}) %collective-permute-start.2) | collective-permute-done | bytes 40992 | tf_op jit(solution)/shard_map/ppermute | solution.py:100
  27.5 0.1 collective-permute-start.3
  27.6 8.3 %all-to-all-done = bf16[16,32,512]{2,1,0:T(8,128)(2,1)S(1)} async-done(((bf16[16,32,512]{2,1,0:T(8,128)(2,1)}), bf16[16,32,512]{2,1,0:T(8,128)(2,1)S(1)}, u32[]{:S(2)}, u32[]{:S(2)}) %all-to-all-start) | async-done | bytes 524320 | tf_op jit(solution)/shard_map/all_to_all | solution.py:232
  35.9 0.0 copy-done
  35.9 0.4 fusion
  36.4 0.0 slice-start
  36.4 16.2 %all_gather.3 = bf16[64,4096]{1,0:T(8,128)(2,1)S(1)} all-gather(bf16[64,1024]{1,0:T(8,128)(2,1)S(1)} %bitcast.67), channel_id=1, replica_groups=mesh['grp'=2,'dp'=4,'sub'=4] {'sub'}, dimensions={1}, use_global_device_ids=true | all-gather | bytes 655360 | tf_op jit(solution)/shard_map/all_gather | solution.py:237
  52.6 0.0 slice-start.1
  52.6 6.0 %convolution_convert_fusion = bf16[64,1280]{1,0:T(8,128)(2,1)S(1)} fusion(bf16[64,4096]{1,0:T(8,128)(2,1)S(1)} %all_gather.3, bf16[4096,1280]{1,0:T(8,128)(2,1)} %param.17), kind=kOutput, calls=%fused_computation | convolution fusion | flops 671170560 | bytes 11173888 | tf_op jit(solution)/shard_map/dot_general | solution.py:241
  58.6 0.1 collective-permute-start
  58.7 1.4 %collective-permute-done = bf16[64,1280]{1,0:T(8,128)(2,1)S(1)} collective-permute-done((bf16[64,1280]{1,0:T(8,128)(2,1)S(1)}, bf16[64,1280]{1,0:T(8,128)(2,1)S(1)}, u32[]{:S(2)}, u32[]{:S(2)}) %collective-permute-start) | collective-permute-done | bytes 163872 | tf_op jit(solution)/shard_map/ppermute | solution.py:100
  60.1 0.7 collective-permute-start.1
  60.8 0.0 collective-permute-done.3
  60.8 5.6 %collective-permute-done.1 = bf16[64,1280]{1,0:T(8,128)(2,1)S(1)} collective-permute-done((bf16[64,1280]{1,0:T(8,128)(2,1)S(1)}, bf16[64,1280]{1,0:T(8,128)(2,1)S(1)}, u32[]{:S(2)}, u32[]{:S(2)}) %collective-permute-start.1) | collective-permute-done | bytes 163872 | tf_op jit(solution)/shard_map/ppermute | solution.py:100
  66.4 0.2 multiply_reduce_fusion
  66.6 0.0 slice-start.2
  66.6 0.0 slice-done
  66.6 0.0 slice-done.1
  66.6 0.0 slice-start.3
  66.7 1.5 %fusion.12 = f32[64,3072]{1,0:T(8,128)S(1)} fusion(bf16[1280,3072]{1,0:T(8,128)(2,1)S(1)} %bitcast.60, f32[64,1280]{1,0:T(8,128)S(1)} %get-tuple-element.3, f32[1280]{0:T(1024)S(1)} %convert_element_type.106), kind=kOutput, calls=%fused_computation.42 | convolution fusion | flops 503480320 | bytes 8983552 | tf_op jit(solution)/shard_map/dot_general | solution.py:248
  68.2 0.7 slice-done.2
  68.8 1.1 slice-done.3
  69.9 1.5 %fusion.13 = f32[64,3072]{1,0:T(8,128)S(1)} fusion(bf16[1280,3072]{1,0:T(8,128)(2,1)S(1)} %bitcast.62, f32[64,1280]{1,0:T(8,128)S(1)} %get-tuple-element.3, f32[1280]{0:T(1024)S(1)} %convert_element_type.106), kind=kOutput, calls=%fused_computation.43 | convolution fusion | flops 503480320 | bytes 8983552 | tf_op jit(solution)/shard_map/dot_general | solution.py:247
  71.4 0.1 select_convert_fusion
  71.5 0.8 pad_maximum_fusion
  72.3 0.0 collective-permute-start.4
  72.3 2.0 %collective-permute-start.6 = (f32[64]{0:T(128)S(1)}, f32[64]{0:T(128)S(1)}, u32[]{:S(2)}, u32[]{:S(2)}) collective-permute-start(f32[64]{0:T(128)S(1)} %get-tuple-element.2), channel_id=1, source_target_pairs={{0,1},{1,0},{2,3},{3,2},{4,5},{5,4},{6,7},{7,6},{8,9},{9,8},{10,11... | collective-permute-start | bytes 776 | tf_op jit(solution)/shard_map/ppermute | solution.py:100
  74.3 8.6 %collective-permute-done.6 = f32[64]{0:T(128)S(1)} collective-permute-done((f32[64]{0:T(128)S(1)}, f32[64]{0:T(128)S(1)}, u32[]{:S(2)}, u32[]{:S(2)}) %collective-permute-start.6) | collective-permute-done | bytes 288 | tf_op jit(solution)/shard_map/ppermute | solution.py:100
  83.0 0.7 collective-permute-start.7
  83.7 0.0 collective-permute-done.4
  83.7 1.1 convert_add_fusion.1
  84.9 2.3 %collective-permute-start.5 = (bf16[64,1536]{1,0:T(8,128)(2,1)S(1)}, bf16[64,1536]{1,0:T(8,128)(2,1)S(1)}, u32[]{:S(2)}, u32[]{:S(2)}) collective-permute-start(bf16[64,1536]{1,0:T(8,128)(2,1)S(1)} %pad_maximum_fusion.1), channel_id=1, source_target_pairs={{0,2},{1,3},{2,0},{3,1},{4,6},{5,7},{6,4},{7,5},{8,10},{9,11},{10,... | collective-permute-start | bytes 589832 | tf_op jit(solution)/shard_map/ppermute | solution.py:100
  87.2 2.3 %collective-permute-done.7 = f32[64]{0:T(128)S(1)} collective-permute-done((f32[64]{0:T(128)S(1)}, f32[64]{0:T(128)S(1)}, u32[]{:S(2)}, u32[]{:S(2)}) %collective-permute-start.7) | collective-permute-done | bytes 288 | tf_op jit(solution)/shard_map/ppermute | solution.py:100
  89.5 5.6 %collective-permute-done.5 = bf16[64,1536]{1,0:T(8,128)(2,1)S(1)} collective-permute-done((bf16[64,1536]{1,0:T(8,128)(2,1)S(1)}, bf16[64,1536]{1,0:T(8,128)(2,1)S(1)}, u32[]{:S(2)}, u32[]{:S(2)}) %collective-permute-start.5) | collective-permute-done | bytes 196640 | tf_op jit(solution)/shard_map/ppermute | solution.py:100
  95.0 0.1 multiply_convert_fusion.1
  95.2 0.1 collective-permute-start.8
  95.3 6.3 %collective-permute-done.8 = bf16[64,768]{1,0:T(8,128)(2,1)S(1)} collective-permute-done((bf16[64,768]{1,0:T(8,128)(2,1)S(1)}, bf16[64,768]{1,0:T(8,128)(2,1)S(1)}, u32[]{:S(2)}, u32[]{:S(2)}) %collective-permute-start.8) | collective-permute-done | bytes 98336 | tf_op jit(solution)/shard_map/ppermute | solution.py:100
  101.6 0.1 collective-permute-start.9
  101.7 6.2 %collective-permute-done.9 = bf16[64,1536]{1,0:T(8,128)(2,1)S(1)} collective-permute-done((bf16[64,1536]{1,0:T(8,128)(2,1)S(1)}, bf16[64,1536]{1,0:T(8,128)(2,1)S(1)}, u32[]{:S(2)}, u32[]{:S(2)}) %collective-permute-start.9) | collective-permute-done | bytes 196640 | tf_op jit(solution)/shard_map/ppermute | solution.py:100
  107.9 4.7 %fusion.2 = f32[64,1280]{1,0:T(8,128)S(1)} fusion(bf16[3072,1280]{1,0:T(8,128)(2,1)} %param.21, bf16[64,1536]{1,0:T(8,128)(2,1)S(1)} %maximum_select_fusion.2, bf16[64,1536]{1,0:T(8,128)(2,1)S(1)} %collective-permute-done.9, pred[]{:T(512)S(6)} %ne.18), kind=kOutput, calls=%fused_computation.6 | convolution fusion | flops 505085952 | bytes 8585217 | tf_op jit(solution)/shard_map/dot_general | solution.py:254
  112.6 0.1 collective-permute-start.10
  112.7 1.2 %collective-permute-done.10 = bf16[2,16,1280]{2,1,0:T(8,128)(2,1)S(1)} collective-permute-done((bf16[2,16,1280]{2,1,0:T(8,128)(2,1)S(1)}, bf16[2,16,1280]{2,1,0:T(8,128)(2,1)S(1)}, u32[]{:S(2)}, u32[]{:S(2)}) %collective-permute-start.10) | collective-permute-done | bytes 81952 | tf_op jit(solution)/shard_map/ppermute | solution.py:100
  114.0 0.7 collective-permute-start.11
  114.7 0.6 dynamic-slice_convert_fusion
  115.3 2.8 %collective-permute-done.11 = bf16[1,16,1280]{2,1,0:T(8,128)(2,1)S(1)} collective-permute-done((bf16[1,16,1280]{2,1,0:T(8,128)(2,1)S(1)}, bf16[1,16,1280]{2,1,0:T(8,128)(2,1)S(1)}, u32[]{:S(2)}, u32[]{:S(2)}) %collective-permute-start.11) | collective-permute-done | bytes 40992 | tf_op jit(solution)/shard_map/ppermute | solution.py:100
  118.1 0.6 fusion.11
  (18 shorter events, 0.3 us)
Async XLA Ops:
  0.6 35.3 %copy-start = (bf16[8,512,128]{2,1,0:T(8,128)(2,1)S(1)}, bf16[8,512,128]{2,1,0:T(8,128)(2,1)}, u32[]{:S(2)}) copy-start(bf16[8,512,128]{2,1,0:T(8,128)(2,1)} %param.16) | copy-start | bytes 3145732
  0.6 1.2 copy-start.1
  1.8 0.7 copy-start.2
  2.5 0.7 copy-start.3
  3.1 17.1 %copy-start.4 = (bf16[16,1280]{1,0:T(8,128)(2,1)S(1)}, bf16[16,1280]{1,0:T(8,128)(2,1)}, u32[]{:S(2)}) copy-start(bf16[16,1280]{1,0:T(8,128)(2,1)} %param.11) | copy-start | bytes 122884
  3.1 19.1 %copy-start.5 = (bf16[1280]{0:T(1024)(128)(2,1)S(1)}, bf16[1280]{0:T(1024)(128)(2,1)}, u32[]{:S(2)}) copy-start(bf16[1280]{0:T(1024)(128)(2,1)} %param.18) | copy-start | bytes 7684
  12.9 23.1 %all-to-all-start = ((bf16[16,32,512]{2,1,0:T(8,128)(2,1)}), bf16[16,32,512]{2,1,0:T(8,128)(2,1)S(1)}, u32[]{:S(2)}, u32[]{:S(2)}) async-start(bf16[16,32,512]{2,1,0:T(8,128)(2,1)} %shard_map.122), calls=%async_computation | async-start | bytes 1048576 | tf_op jit(solution)/shard_map/all_to_all | solution.py:232
  20.3 7.2 %collective-permute-start.2 = (bf16[1,16,1280]{2,1,0:T(8,128)(2,1)S(1)}, bf16[1,16,1280]{2,1,0:T(8,128)(2,1)S(1)}, u32[]{:S(2)}, u32[]{:S(2)}) collective-permute-start(bf16[1,16,1280]{2,1,0:T(8,128)(2,1)S(1)} %bitcast.68), channel_id=1, source_target_pairs={{0,8},{4,12},{8,0},{12,4},{1,9},{5,13},{9,1},{13,5},{2,10},{6,14},... | collective-permute-start | bytes 122888 | tf_op jit(solution)/shard_map/ppermute | solution.py:100
  27.5 33.3 %collective-permute-start.3 = (bf16[2,16,1280]{2,1,0:T(8,128)(2,1)S(1)}, bf16[2,16,1280]{2,1,0:T(8,128)(2,1)S(1)}, u32[]{:S(2)}, u32[]{:S(2)}) collective-permute-start(bf16[2,16,1280]{2,1,0:T(8,128)(2,1)S(1)} %maximum_select_fusion.4), channel_id=1, source_target_pairs={{0,4},{4,0},{8,12},{12,8},{1,5},{5,1},{9,13},{13,9},{2,6},{6,2},{1... | collective-permute-start | bytes 245768 | tf_op jit(solution)/shard_map/ppermute | solution.py:100
  36.4 30.3 %slice-start = ((s8[7864320]{0:T(1024)(128)(4,1)}), s8[4194304]{0:T(1024)(128)(4,1)S(1)}, s32[]{:S(2)}) async-start(s8[7864320]{0:T(1024)(128)(4,1)} %bitcast.59), calls=%async_computation.1 | async-start | bytes 8388608
  52.6 14.1 %slice-start.1 = ((s8[7864320]{0:T(1024)(128)(4,1)}), s8[3670016]{0:T(1024)(128)(4,1)S(1)}, s32[]{:S(2)}) async-start(s8[7864320]{0:T(1024)(128)(4,1)} %bitcast.59), calls=%async_computation.2 | async-start | bytes 7340032
  58.6 1.5 %collective-permute-start = (bf16[64,1280]{1,0:T(8,128)(2,1)S(1)}, bf16[64,1280]{1,0:T(8,128)(2,1)S(1)}, u32[]{:S(2)}, u32[]{:S(2)}) collective-permute-start(bf16[64,1280]{1,0:T(8,128)(2,1)S(1)} %convolution_convert_fusion), channel_id=1, source_target_pairs={{0,4},{4,0},{8,12},{12,8},{1,5},{5,1},{9,13},{13,9},{2,6},{6,2},{1... | collective-permute-start | bytes 491528 | tf_op jit(solution)/shard_map/ppermute | solution.py:100
  60.1 6.3 %collective-permute-start.1 = (bf16[64,1280]{1,0:T(8,128)(2,1)S(1)}, bf16[64,1280]{1,0:T(8,128)(2,1)S(1)}, u32[]{:S(2)}, u32[]{:S(2)}) collective-permute-start(bf16[64,1280]{1,0:T(8,128)(2,1)S(1)} %add_convert_fusion), channel_id=1, source_target_pairs={{0,8},{4,12},{8,0},{12,4},{1,9},{5,13},{9,1},{13,5},{2,10},{6,14},... | collective-permute-start | bytes 491528 | tf_op jit(solution)/shard_map/ppermute | solution.py:100
  66.6 2.2 %slice-start.2 = ((s8[7864320]{0:T(1024)(128)(4,1)}), s8[4194304]{0:T(1024)(128)(4,1)S(1)}, s32[]{:S(2)}) async-start(s8[7864320]{0:T(1024)(128)(4,1)} %bitcast.61), calls=%async_computation.3 | async-start | bytes 8388608
  66.6 3.3 %slice-start.3 = ((s8[7864320]{0:T(1024)(128)(4,1)}), s8[3670016]{0:T(1024)(128)(4,1)S(1)}, s32[]{:S(2)}) async-start(s8[7864320]{0:T(1024)(128)(4,1)} %bitcast.61), calls=%async_computation.4 | async-start | bytes 7340032
  72.3 11.4 %collective-permute-start.4 = (bf16[64,3072]{1,0:T(8,128)(2,1)}, bf16[64,3072]{1,0:T(8,128)(2,1)}, u32[]{:S(2)}, u32[]{:S(2)}) collective-permute-start(bf16[64,3072]{1,0:T(8,128)(2,1)} %pad_maximum_fusion), channel_id=1, source_target_pairs={{0,1},{1,0},{2,3},{3,2},{4,5},{5,4},{6,7},{7,6},{8,9},{9,8},{10,11... | collective-permute-start | bytes 1179656 | tf_op jit(solution)/shard_map/ppermute | solution.py:100
  72.3 10.7 %collective-permute-start.6 = (f32[64]{0:T(128)S(1)}, f32[64]{0:T(128)S(1)}, u32[]{:S(2)}, u32[]{:S(2)}) collective-permute-start(f32[64]{0:T(128)S(1)} %get-tuple-element.2), channel_id=1, source_target_pairs={{0,1},{1,0},{2,3},{3,2},{4,5},{5,4},{6,7},{7,6},{8,9},{9,8},{10,11... | collective-permute-start | bytes 776 | tf_op jit(solution)/shard_map/ppermute | solution.py:100
  83.0 6.5 %collective-permute-start.7 = (f32[64]{0:T(128)S(1)}, f32[64]{0:T(128)S(1)}, u32[]{:S(2)}, u32[]{:S(2)}) collective-permute-start(f32[64]{0:T(128)S(1)} %add.57), channel_id=1, source_target_pairs={{0,2},{1,3},{2,0},{3,1},{4,6},{5,7},{6,4},{7,5},{8,10},{9,11},{10,... | collective-permute-start | bytes 776 | tf_op jit(solution)/shard_map/ppermute | solution.py:100
  84.9 10.1 %collective-permute-start.5 = (bf16[64,1536]{1,0:T(8,128)(2,1)S(1)}, bf16[64,1536]{1,0:T(8,128)(2,1)S(1)}, u32[]{:S(2)}, u32[]{:S(2)}) collective-permute-start(bf16[64,1536]{1,0:T(8,128)(2,1)S(1)} %pad_maximum_fusion.1), channel_id=1, source_target_pairs={{0,2},{1,3},{2,0},{3,1},{4,6},{5,7},{6,4},{7,5},{8,10},{9,11},{10,... | collective-permute-start | bytes 589832 | tf_op jit(solution)/shard_map/ppermute | solution.py:100
  95.2 6.4 %collective-permute-start.8 = (bf16[64,768]{1,0:T(8,128)(2,1)S(1)}, bf16[64,768]{1,0:T(8,128)(2,1)S(1)}, u32[]{:S(2)}, u32[]{:S(2)}) collective-permute-start(bf16[64,768]{1,0:T(8,128)(2,1)S(1)} %multiply_convert_fusion.1), channel_id=1, source_target_pairs={{0,2},{1,3},{2,0},{3,1},{4,6},{5,7},{6,4},{7,5},{8,10},{9,11},{10,... | collective-permute-start | bytes 294920 | tf_op jit(solution)/shard_map/ppermute | solution.py:100
  101.6 6.3 %collective-permute-start.9 = (bf16[64,1536]{1,0:T(8,128)(2,1)S(1)}, bf16[64,1536]{1,0:T(8,128)(2,1)S(1)}, u32[]{:S(2)}, u32[]{:S(2)}) collective-permute-start(bf16[64,1536]{1,0:T(8,128)(2,1)S(1)} %maximum_select_fusion.2), channel_id=1, source_target_pairs={{0,1},{1,0},{2,3},{3,2},{4,5},{5,4},{6,7},{7,6},{8,9},{9,8},{10,11... | collective-permute-start | bytes 589832 | tf_op jit(solution)/shard_map/ppermute | solution.py:100
  112.6 1.3 %collective-permute-start.10 = (bf16[2,16,1280]{2,1,0:T(8,128)(2,1)S(1)}, bf16[2,16,1280]{2,1,0:T(8,128)(2,1)S(1)}, u32[]{:S(2)}, u32[]{:S(2)}) collective-permute-start(bf16[2,16,1280]{2,1,0:T(8,128)(2,1)S(1)} %fusion.10), channel_id=1, source_target_pairs={{0,4},{4,0},{8,12},{12,8},{1,5},{5,1},{9,13},{13,9},{2,6},{6,2},{1... | collective-permute-start | bytes 245768 | tf_op jit(solution)/shard_map/ppermute | solution.py:100
  114.0 4.1 %collective-permute-start.11 = (bf16[1,16,1280]{2,1,0:T(8,128)(2,1)S(1)}, bf16[1,16,1280]{2,1,0:T(8,128)(2,1)S(1)}, u32[]{:S(2)}, u32[]{:S(2)}) collective-permute-start(bf16[1,16,1280]{2,1,0:T(8,128)(2,1)S(1)} %fusion.14), channel_id=1, source_target_pairs={{0,8},{4,12},{8,0},{12,4},{1,9},{5,13},{9,1},{13,5},{2,10},{6,14},... | collective-permute-start | bytes 122888 | tf_op jit(solution)/shard_map/ppermute | solution.py:100

commit v19 on v14

--- a/solution.py
+++ b/solution.py
@@ -38,12 +38,8 @@
     span = pages_req * page_size
     chunk = min(512, span)
     positions = lax.broadcasted_iota(jnp.int32, (head_count, chunk), 1)
-    for slot in range(req_dev):
-        def finish(page, carry, slot=slot):
-            page_copy(slot, page).wait()
-            return carry
-
-        lax.fori_loop(0, pages_req, finish, 0)
+
+    def score_pass(slot):
         length = lengths[slot]
         query_rows = jnp.transpose(queries[slot])
         blocks_of_scores = []
@@ -55,6 +51,9 @@
             block = jnp.where(positions + first < length, block, masked_score)
             blocks_of_scores.append(block)
             row_max = jnp.maximum(row_max, jnp.max(block, axis=1, keepdims=True))
+        return slot, blocks_of_scores, row_max
+
+    def weight_pass(slot, blocks_of_scores, row_max):
         denominator = jnp.zeros((head_count, 1), jnp.float32)
         weighted = jnp.zeros((head_count, latent), jnp.float32)
         for first, block in zip(range(0, span, chunk), blocks_of_scores):
@@ -69,6 +68,19 @@
         blocks, block_heads = contexts.shape[0], head_count // contexts.shape[0]
         context = (weighted / denominator).reshape(blocks, block_heads, latent)
         contexts[:, slot * block_heads:(slot + 1) * block_heads, :] = context.astype(contexts.dtype)
+
+    pending = None
+    for slot in range(req_dev):
+        def finish(page, carry, slot=slot):
+            page_copy(slot, page).wait()
+            return carry
+
+        lax.fori_loop(0, pages_req, finish, 0)
+        scored = score_pass(slot)
+        if pending is not None:
+            weight_pass(*pending)
+        pending = scored
+    weight_pass(*pending)
 
 
 def attend_all(queries, page_table, lengths, cache_pool, latent, score_scale, blocks):

time: 110 us -> 110 us (level)
  no operation moved by 1% of the time
where the time goes in v19:
time: 110 us
  waiting for transfers between devices  46.8 us (43%)
  starting transfers between devices  17.7 us (16%)
  blocking collectives  16.2 us (15%)
  matrix products  14.1 us (13%)
  Pallas kernels  9.28 us (8%)
  local copies, waits for them, and re-layouts  3.16 us (3%)
  other arithmetic  1.45 us (1%)
    ppermute x14, waiting for transfers between devices, swap_with(): return lax.ppermute(x, axis, [(i, i ^ distance) for i in range(size)])  38.4 us
    all_gather x1, blocking collectives, shards(): group_values = lax.all_gather(values, 'sub', axis=1, tiled=True)  16.2 us
    ppermute x14, starting transfers between devices, swap_with(): return lax.ppermute(x, axis, [(i, i ^ distance) for i in range(size)])  10.4 us
    pallas_call x1, Pallas kernels, attend_all(): pl.pallas_call(kernel, out_shape=jax.ShapeDtypeStruct((blocks, req_dev *...  9.28 us
    all_to_all x1, waiting for transfers between devices, shards(): lax.all_to_all(contexts, ('dp', 'sub'), split_axis=0, concat_axis=0, tile...  8.35 us
    all_to_all x1, starting transfers between devices, shards(): lax.all_to_all(contexts, ('dp', 'sub'), split_axis=0, concat_axis=0, tile...  7.37 us
    dot_general x1, matrix products, shards(): jnp.dot(group_values, out_proj, preferred_element_type=jnp.float32)  6.04 us
    dot_general x1, matrix products, shards(): jnp.dot(hidden_units, down_proj, preferred_element_type=jnp.float32)  4.7 us
  transfers between devices with their start and end apart: 15, of which 12 were waited for; matrix products, arithmetic and copies ran while one was open for 9% of the time, Pallas kernels for 0%

profile of v19, /device:TPU:0, one launch (start us, length us, event | category | flops | bytes accessed | tf_op | source)
XLA Modules:
  0.0 109.6 jit_solution(18301038006439058569)
XLA Ops:
  0.6 0.0 copy-start
  0.6 0.0 copy-start.1
  0.7 1.1 %copy-done.1 = bf16[4,128,576]{1,2,0:T(8,128)(2,1)S(1)} copy-done((bf16[4,128,576]{1,2,0:T(8,128)(2,1)S(1)}, bf16[4,128,576]{1,2,0:T(8,128)(2,1)}, u32[]{:S(2)}) %copy-start.1) | copy-done | bytes 589848
  1.8 0.0 copy-start.2
  1.8 0.7 copy-done.2
  2.5 0.0 copy-start.3
  2.5 0.7 copy-done.3
  3.1 0.0 copy-start.4
  3.1 0.0 copy-start.5
  3.1 9.3 %shard_map.122 = bf16[16,32,512]{2,1,0:T(8,128)(2,1)} custom-call(s32[4,16]{1,0:T(4,128)S(1)} %copy-done.2, s32[4]{0:T(128)S(1)} %copy-done.3, bf16[4,576,128]{2,1,0:T(8,128)(2,1)S(1)} %bitcast.58, bf16[64,576,128]{2,1,0:T(8,128)(2,1)} %bitcast.63), custom_call_target="tpu_custom_call" | custom-call | tf_op jit(solution)/shard_map/pallas_call | solution.py:93
  12.4 7.4 %all-to-all-start = ((bf16[16,32,512]{2,1,0:T(8,128)(2,1)}), bf16[16,32,512]{2,1,0:T(8,128)(2,1)S(1)}, u32[]{:S(2)}, u32[]{:S(2)}) async-start(bf16[16,32,512]{2,1,0:T(8,128)(2,1)} %shard_map.122), calls=%async_computation | async-start | bytes 1048576 | tf_op jit(solution)/shard_map/all_to_all | solution.py:243
  19.8 0.0 copy-done.4
  19.8 2.0 %collective-permute-start.2 = (bf16[1,16,1280]{2,1,0:T(8,128)(2,1)S(1)}, bf16[1,16,1280]{2,1,0:T(8,128)(2,1)S(1)}, u32[]{:S(2)}, u32[]{:S(2)}) collective-permute-start(bf16[1,16,1280]{2,1,0:T(8,128)(2,1)S(1)} %bitcast.68), channel_id=1, source_target_pairs={{0,8},{4,12},{8,0},{12,4},{1,9},{5,13},{9,1},{13,5},{2,10},{6,14},... | collective-permute-start | bytes 122888 | tf_op jit(solution)/shard_map/ppermute | solution.py:112
  21.8 0.0 copy-done.5
  21.8 5.2 %collective-permute-done.2 = bf16[1,16,1280]{2,1,0:T(8,128)(2,1)S(1)} collective-permute-done((bf16[1,16,1280]{2,1,0:T(8,128)(2,1)S(1)}, bf16[1,16,1280]{2,1,0:T(8,128)(2,1)S(1)}, u32[]{:S(2)}, u32[]{:S(2)}) %collective-permute-start.2) | collective-permute-done | bytes 40992 | tf_op jit(solution)/shard_map/ppermute | solution.py:112
  27.1 0.1 collective-permute-start.3
  27.1 8.3 %all-to-all-done = bf16[16,32,512]{2,1,0:T(8,128)(2,1)S(1)} async-done(((bf16[16,32,512]{2,1,0:T(8,128)(2,1)}), bf16[16,32,512]{2,1,0:T(8,128)(2,1)S(1)}, u32[]{:S(2)}, u32[]{:S(2)}) %all-to-all-start) | async-done | bytes 524320 | tf_op jit(solution)/shard_map/all_to_all | solution.py:243
  35.5 0.0 copy-done
  35.5 0.4 fusion
  35.9 0.0 slice-start
  35.9 16.2 %all_gather.3 = bf16[64,4096]{1,0:T(8,128)(2,1)S(1)} all-gather(bf16[64,1024]{1,0:T(8,128)(2,1)S(1)} %bitcast.67), channel_id=1, replica_groups=mesh['grp'=2,'dp'=4,'sub'=4] {'sub'}, dimensions={1}, use_global_device_ids=true | all-gather | bytes 655360 | tf_op jit(solution)/shard_map/all_gather | solution.py:248
  52.1 0.0 slice-start.1
  52.1 6.0 %convolution_convert_fusion = bf16[64,1280]{1,0:T(8,128)(2,1)S(1)} fusion(bf16[64,4096]{1,0:T(8,128)(2,1)S(1)} %all_gather.3, bf16[4096,1280]{1,0:T(8,128)(2,1)} %param.17), kind=kOutput, calls=%fused_computation | convolution fusion | flops 671170560 | bytes 11173888 | tf_op jit(solution)/shard_map/dot_general | solution.py:252
  58.2 0.1 collective-permute-start
  58.3 1.4 %collective-permute-done = bf16[64,1280]{1,0:T(8,128)(2,1)S(1)} collective-permute-done((bf16[64,1280]{1,0:T(8,128)(2,1)S(1)}, bf16[64,1280]{1,0:T(8,128)(2,1)S(1)}, u32[]{:S(2)}, u32[]{:S(2)}) %collective-permute-start) | collective-permute-done | bytes 163872 | tf_op jit(solution)/shard_map/ppermute | solution.py:112
  59.7 0.7 collective-permute-start.1
  60.3 0.0 collective-permute-done.3
  60.4 5.6 %collective-permute-done.1 = bf16[64,1280]{1,0:T(8,128)(2,1)S(1)} collective-permute-done((bf16[64,1280]{1,0:T(8,128)(2,1)S(1)}, bf16[64,1280]{1,0:T(8,128)(2,1)S(1)}, u32[]{:S(2)}, u32[]{:S(2)}) %collective-permute-start.1) | collective-permute-done | bytes 163872 | tf_op jit(solution)/shard_map/ppermute | solution.py:112
  66.0 0.0 slice-start.2
  66.0 0.2 multiply_reduce_fusion
  66.2 0.1 collective-permute-start.6
  66.2 0.0 slice-done
  66.3 0.0 slice-done.1
  66.3 0.0 slice-start.3
  66.3 1.5 %fusion.12 = f32[64,3072]{1,0:T(8,128)S(1)} fusion(bf16[1280,3072]{1,0:T(8,128)(2,1)S(1)} %bitcast.60, f32[64,1280]{1,0:T(8,128)S(1)} %get-tuple-element.3, f32[1280]{0:T(1024)S(1)} %convert_element_type.106), kind=kOutput, calls=%fused_computation.40 | convolution fusion | flops 503480320 | bytes 8983552 | tf_op jit(solution)/shard_map/dot_general | solution.py:259
  67.8 2.0 %collective-permute-start.8 = (bf16[64,1536]{1,0:T(8,128)(2,1)S(1)}, bf16[64,1536]{1,0:T(8,128)(2,1)S(1)}, u32[]{:S(2)}, u32[]{:S(2)}) collective-permute-start(bf16[64,1536]{1,0:T(8,128)(2,1)S(1)} %select_convert_fusion), channel_id=1, source_target_pairs={{0,1},{1,0},{2,3},{3,2},{4,5},{5,4},{6,7},{7,6},{8,9},{9,8},{10,11... | collective-permute-start | bytes 589832 | tf_op jit(solution)/shard_map/ppermute | solution.py:112
  69.9 0.0 slice-done.2
  69.9 0.0 slice-done.3
  69.9 1.5 %fusion.13 = f32[64,3072]{1,0:T(8,128)S(1)} fusion(bf16[1280,3072]{1,0:T(8,128)(2,1)S(1)} %bitcast.62, f32[64,1280]{1,0:T(8,128)S(1)} %get-tuple-element.3, f32[1280]{0:T(1024)S(1)} %convert_element_type.106), kind=kOutput, calls=%fused_computation.41 | convolution fusion | flops 503480320 | bytes 8983552 | tf_op jit(solution)/shard_map/dot_general | solution.py:258
  71.4 0.5 collective-permute-start.4
  71.9 0.0 collective-permute-done.6
  71.9 0.9 collective-permute-start.7
  72.8 2.4 %collective-permute-done.8 = bf16[64,1536]{1,0:T(8,128)(2,1)S(1)} collective-permute-done((bf16[64,1536]{1,0:T(8,128)(2,1)S(1)}, bf16[64,1536]{1,0:T(8,128)(2,1)S(1)}, u32[]{:S(2)}, u32[]{:S(2)}) %collective-permute-start.8) | collective-permute-done | bytes 196640 | tf_op jit(solution)/shard_map/ppermute | solution.py:112
  75.2 0.1 convert_add_fusion
  75.3 1.7 %collective-permute-start.9 = (bf16[64,768]{1,0:T(8,128)(2,1)S(1)}, bf16[64,768]{1,0:T(8,128)(2,1)S(1)}, u32[]{:S(2)}, u32[]{:S(2)}) collective-permute-start(bf16[64,768]{1,0:T(8,128)(2,1)S(1)} %select_convert_fusion.2), channel_id=1, source_target_pairs={{0,2},{1,3},{2,0},{3,1},{4,6},{5,7},{6,4},{7,5},{8,10},{9,11},{10,... | collective-permute-start | bytes 294920 | tf_op jit(solution)/shard_map/ppermute | solution.py:112
  77.1 2.2 %collective-permute-done.4 = bf16[64,1536]{1,0:T(8,128)(2,1)S(1)} collective-permute-done((bf16[64,1536]{1,0:T(8,128)(2,1)S(1)}, bf16[64,1536]{1,0:T(8,128)(2,1)S(1)}, u32[]{:S(2)}, u32[]{:S(2)}) %collective-permute-start.4) | collective-permute-done | bytes 196640 | tf_op jit(solution)/shard_map/ppermute | solution.py:112
  79.3 0.1 convert_add_fusion.1
  79.4 1.4 %collective-permute-start.5 = (bf16[64,768]{1,0:T(8,128)(2,1)S(1)}, bf16[64,768]{1,0:T(8,128)(2,1)S(1)}, u32[]{:S(2)}, u32[]{:S(2)}) collective-permute-start(bf16[64,768]{1,0:T(8,128)(2,1)S(1)} %select_convert_fusion.3), channel_id=1, source_target_pairs={{0,2},{1,3},{2,0},{3,1},{4,6},{5,7},{6,4},{7,5},{8,10},{9,11},{10,... | collective-permute-start | bytes 294920 | tf_op jit(solution)/shard_map/ppermute | solution.py:112
  80.8 0.0 collective-permute-done.7
  80.8 0.1 collective-permute-done.9
  80.9 5.5 %collective-permute-done.5 = bf16[64,768]{1,0:T(8,128)(2,1)S(1)} collective-permute-done((bf16[64,768]{1,0:T(8,128)(2,1)S(1)}, bf16[64,768]{1,0:T(8,128)(2,1)S(1)}, u32[]{:S(2)}, u32[]{:S(2)}) %collective-permute-start.5) | collective-permute-done | bytes 98336 | tf_op jit(solution)/shard_map/ppermute | solution.py:112
  86.4 0.1 multiply_convert_fusion.1
  86.5 0.1 collective-permute-start.10
  86.6 6.4 %collective-permute-done.10 = bf16[64,768]{1,0:T(8,128)(2,1)S(1)} collective-permute-done((bf16[64,768]{1,0:T(8,128)(2,1)S(1)}, bf16[64,768]{1,0:T(8,128)(2,1)S(1)}, u32[]{:S(2)}, u32[]{:S(2)}) %collective-permute-start.10) | collective-permute-done | bytes 98336 | tf_op jit(solution)/shard_map/ppermute | solution.py:112
  93.0 0.1 collective-permute-start.11
  93.1 5.7 %collective-permute-done.11 = bf16[64,1536]{1,0:T(8,128)(2,1)S(1)} collective-permute-done((bf16[64,1536]{1,0:T(8,128)(2,1)S(1)}, bf16[64,1536]{1,0:T(8,128)(2,1)S(1)}, u32[]{:S(2)}, u32[]{:S(2)}) %collective-permute-start.11) | collective-permute-done | bytes 196640 | tf_op jit(solution)/shard_map/ppermute | solution.py:112
  98.8 4.7 %fusion.2 = f32[64,1280]{1,0:T(8,128)S(1)} fusion(bf16[3072,1280]{1,0:T(8,128)(2,1)} %param.21, bf16[64,1536]{1,0:T(8,128)(2,1)S(1)} %maximum_select_fusion.2, bf16[64,1536]{1,0:T(8,128)(2,1)S(1)} %collective-permute-done.11, pred[]{:T(512)S(6)} %ne.18), kind=kOutput, calls=%fused_computation.5 | convolution fusion | flops 505085952 | bytes 8585217 | tf_op jit(solution)/shard_map/dot_general | solution.py:265
  103.5 0.1 collective-permute-start.12
  103.6 1.2 %collective-permute-done.12 = bf16[2,16,1280]{2,1,0:T(8,128)(2,1)S(1)} collective-permute-done((bf16[2,16,1280]{2,1,0:T(8,128)(2,1)S(1)}, bf16[2,16,1280]{2,1,0:T(8,128)(2,1)S(1)}, u32[]{:S(2)}, u32[]{:S(2)}) %collective-permute-start.12) | collective-permute-done | bytes 81952 | tf_op jit(solution)/shard_map/ppermute | solution.py:112
  104.9 0.7 collective-permute-start.13
  105.6 0.6 dynamic-slice_convert_fusion
  106.2 2.7 %collective-permute-done.13 = bf16[1,16,1280]{2,1,0:T(8,128)(2,1)S(1)} collective-permute-done((bf16[1,16,1280]{2,1,0:T(8,128)(2,1)S(1)}, bf16[1,16,1280]{2,1,0:T(8,128)(2,1)S(1)}, u32[]{:S(2)}, u32[]{:S(2)}) %collective-permute-start.13) | collective-permute-done | bytes 40992 | tf_op jit(solution)/shard_map/ppermute | solution.py:112
  109.0 0.6 fusion.11
  (19 shorter events, 0.4 us)
Async XLA Ops:
  0.6 34.9 %copy-start = (bf16[8,512,128]{2,1,0:T(8,128)(2,1)S(1)}, bf16[8,512,128]{2,1,0:T(8,128)(2,1)}, u32[]{:S(2)}) copy-start(bf16[8,512,128]{2,1,0:T(8,128)(2,1)} %param.16) | copy-start | bytes 3145732
  0.6 1.2 %copy-start.1 = (bf16[4,128,576]{1,2,0:T(8,128)(2,1)S(1)}, bf16[4,128,576]{1,2,0:T(8,128)(2,1)}, u32[]{:S(2)}) copy-start(bf16[4,128,576]{1,2,0:T(8,128)(2,1)} %param.12) | copy-start | bytes 1769476
  1.8 0.7 copy-start.2
  2.5 0.7 copy-start.3
  3.1 16.7 %copy-start.4 = (bf16[16,1280]{1,0:T(8,128)(2,1)S(1)}, bf16[16,1280]{1,0:T(8,128)(2,1)}, u32[]{:S(2)}) copy-start(bf16[16,1280]{1,0:T(8,128)(2,1)} %param.11) | copy-start | bytes 122884
  3.1 18.7 %copy-start.5 = (bf16[1280]{0:T(1024)(128)(2,1)S(1)}, bf16[1280]{0:T(1024)(128)(2,1)}, u32[]{:S(2)}) copy-start(bf16[1280]{0:T(1024)(128)(2,1)} %param.18) | copy-start | bytes 7684
  12.4 23.1 %all-to-all-start = ((bf16[16,32,512]{2,1,0:T(8,128)(2,1)}), bf16[16,32,512]{2,1,0:T(8,128)(2,1)S(1)}, u32[]{:S(2)}, u32[]{:S(2)}) async-start(bf16[16,32,512]{2,1,0:T(8,128)(2,1)} %shard_map.122), calls=%async_computation | async-start | bytes 1048576 | tf_op jit(solution)/shard_map/all_to_all | solution.py:243
  19.8 7.2 %collective-permute-start.2 = (bf16[1,16,1280]{2,1,0:T(8,128)(2,1)S(1)}, bf16[1,16,1280]{2,1,0:T(8,128)(2,1)S(1)}, u32[]{:S(2)}, u32[]{:S(2)}) collective-permute-start(bf16[1,16,1280]{2,1,0:T(8,128)(2,1)S(1)} %bitcast.68), channel_id=1, source_target_pairs={{0,8},{4,12},{8,0},{12,4},{1,9},{5,13},{9,1},{13,5},{2,10},{6,14},... | collective-permute-start | bytes 122888 | tf_op jit(solution)/shard_map/ppermute | solution.py:112
  27.1 33.3 %collective-permute-start.3 = (bf16[2,16,1280]{2,1,0:T(8,128)(2,1)S(1)}, bf16[2,16,1280]{2,1,0:T(8,128)(2,1)S(1)}, u32[]{:S(2)}, u32[]{:S(2)}) collective-permute-start(bf16[2,16,1280]{2,1,0:T(8,128)(2,1)S(1)} %maximum_select_fusion.4), channel_id=1, source_target_pairs={{0,4},{4,0},{8,12},{12,8},{1,5},{5,1},{9,13},{13,9},{2,6},{6,2},{1... | collective-permute-start | bytes 245768 | tf_op jit(solution)/shard_map/ppermute | solution.py:112
  35.9 30.3 %slice-start = ((s8[7864320]{0:T(1024)(128)(4,1)}), s8[4194304]{0:T(1024)(128)(4,1)S(1)}, s32[]{:S(2)}) async-start(s8[7864320]{0:T(1024)(128)(4,1)} %bitcast.59), calls=%async_computation.1 | async-start | bytes 8388608
  52.1 14.1 %slice-start.1 = ((s8[7864320]{0:T(1024)(128)(4,1)}), s8[3670016]{0:T(1024)(128)(4,1)S(1)}, s32[]{:S(2)}) async-start(s8[7864320]{0:T(1024)(128)(4,1)} %bitcast.59), calls=%async_computation.2 | async-start | bytes 7340032
  58.2 1.5 %collective-permute-start = (bf16[64,1280]{1,0:T(8,128)(2,1)S(1)}, bf16[64,1280]{1,0:T(8,128)(2,1)S(1)}, u32[]{:S(2)}, u32[]{:S(2)}) collective-permute-start(bf16[64,1280]{1,0:T(8,128)(2,1)S(1)} %convolution_convert_fusion), channel_id=1, source_target_pairs={{0,4},{4,0},{8,12},{12,8},{1,5},{5,1},{9,13},{13,9},{2,6},{6,2},{1... | collective-permute-start | bytes 491528 | tf_op jit(solution)/shard_map/ppermute | solution.py:112
  59.7 6.3 %collective-permute-start.1 = (bf16[64,1280]{1,0:T(8,128)(2,1)S(1)}, bf16[64,1280]{1,0:T(8,128)(2,1)S(1)}, u32[]{:S(2)}, u32[]{:S(2)}) collective-permute-start(bf16[64,1280]{1,0:T(8,128)(2,1)S(1)} %add_convert_fusion), channel_id=1, source_target_pairs={{0,8},{4,12},{8,0},{12,4},{1,9},{5,13},{9,1},{13,5},{2,10},{6,14},... | collective-permute-start | bytes 491528 | tf_op jit(solution)/shard_map/ppermute | solution.py:112
  66.0 3.9 %slice-start.2 = ((s8[7864320]{0:T(1024)(128)(4,1)}), s8[4194304]{0:T(1024)(128)(4,1)S(1)}, s32[]{:S(2)}) async-start(s8[7864320]{0:T(1024)(128)(4,1)} %bitcast.61), calls=%async_computation.3 | async-start | bytes 8388608
  66.2 5.7 %collective-permute-start.6 = (f32[64]{0:T(128)S(1)}, f32[64]{0:T(128)S(1)}, u32[]{:S(2)}, u32[]{:S(2)}) collective-permute-start(f32[64]{0:T(128)S(1)} %get-tuple-element.2), channel_id=1, source_target_pairs={{0,1},{1,0},{2,3},{3,2},{4,5},{5,4},{6,7},{7,6},{8,9},{9,8},{10,11... | collective-permute-start | bytes 776 | tf_op jit(solution)/shard_map/ppermute | solution.py:112
  66.3 3.6 %slice-start.3 = ((s8[7864320]{0:T(1024)(128)(4,1)}), s8[3670016]{0:T(1024)(128)(4,1)S(1)}, s32[]{:S(2)}) async-start(s8[7864320]{0:T(1024)(128)(4,1)} %bitcast.61), calls=%async_computation.4 | async-start | bytes 7340032
  67.8 7.4 %collective-permute-start.8 = (bf16[64,1536]{1,0:T(8,128)(2,1)S(1)}, bf16[64,1536]{1,0:T(8,128)(2,1)S(1)}, u32[]{:S(2)}, u32[]{:S(2)}) collective-permute-start(bf16[64,1536]{1,0:T(8,128)(2,1)S(1)} %select_convert_fusion), channel_id=1, source_target_pairs={{0,1},{1,0},{2,3},{3,2},{4,5},{5,4},{6,7},{7,6},{8,9},{9,8},{10,11... | collective-permute-start | bytes 589832 | tf_op jit(solution)/shard_map/ppermute | solution.py:112
  71.4 7.9 %collective-permute-start.4 = (bf16[64,1536]{1,0:T(8,128)(2,1)S(1)}, bf16[64,1536]{1,0:T(8,128)(2,1)S(1)}, u32[]{:S(2)}, u32[]{:S(2)}) collective-permute-start(bf16[64,1536]{1,0:T(8,128)(2,1)S(1)} %select_convert_fusion.1), channel_id=1, source_target_pairs={{0,1},{1,0},{2,3},{3,2},{4,5},{5,4},{6,7},{7,6},{8,9},{9,8},{10,11... | collective-permute-start | bytes 589832 | tf_op jit(solution)/shard_map/ppermute | solution.py:112
  71.9 8.9 %collective-permute-start.7 = (f32[64]{0:T(128)S(1)}, f32[64]{0:T(128)S(1)}, u32[]{:S(2)}, u32[]{:S(2)}) collective-permute-start(f32[64]{0:T(128)S(1)} %add.56), channel_id=1, source_target_pairs={{0,2},{1,3},{2,0},{3,1},{4,6},{5,7},{6,4},{7,5},{8,10},{9,11},{10,... | collective-permute-start | bytes 776 | tf_op jit(solution)/shard_map/ppermute | solution.py:112
  75.3 5.6 %collective-permute-start.9 = (bf16[64,768]{1,0:T(8,128)(2,1)S(1)}, bf16[64,768]{1,0:T(8,128)(2,1)S(1)}, u32[]{:S(2)}, u32[]{:S(2)}) collective-permute-start(bf16[64,768]{1,0:T(8,128)(2,1)S(1)} %select_convert_fusion.2), channel_id=1, source_target_pairs={{0,2},{1,3},{2,0},{3,1},{4,6},{5,7},{6,4},{7,5},{8,10},{9,11},{10,... | collective-permute-start | bytes 294920 | tf_op jit(solution)/shard_map/ppermute | solution.py:112
  79.4 7.0 %collective-permute-start.5 = (bf16[64,768]{1,0:T(8,128)(2,1)S(1)}, bf16[64,768]{1,0:T(8,128)(2,1)S(1)}, u32[]{:S(2)}, u32[]{:S(2)}) collective-permute-start(bf16[64,768]{1,0:T(8,128)(2,1)S(1)} %select_convert_fusion.3), channel_id=1, source_target_pairs={{0,2},{1,3},{2,0},{3,1},{4,6},{5,7},{6,4},{7,5},{8,10},{9,11},{10,... | collective-permute-start | bytes 294920 | tf_op jit(solution)/shard_map/ppermute | solution.py:112
  86.5 6.4 %collective-permute-start.10 = (bf16[64,768]{1,0:T(8,128)(2,1)S(1)}, bf16[64,768]{1,0:T(8,128)(2,1)S(1)}, u32[]{:S(2)}, u32[]{:S(2)}) collective-permute-start(bf16[64,768]{1,0:T(8,128)(2,1)S(1)} %multiply_convert_fusion.1), channel_id=1, source_target_pairs={{0,2},{1,3},{2,0},{3,1},{4,6},{5,7},{6,4},{7,5},{8,10},{9,11},{10,... | collective-permute-start | bytes 294920 | tf_op jit(solution)/shard_map/ppermute | solution.py:112
  93.0 5.7 %collective-permute-start.11 = (bf16[64,1536]{1,0:T(8,128)(2,1)S(1)}, bf16[64,1536]{1,0:T(8,128)(2,1)S(1)}, u32[]{:S(2)}, u32[]{:S(2)}) collective-permute-start(bf16[64,1536]{1,0:T(8,128)(2,1)S(1)} %maximum_select_fusion.2), channel_id=1, source_target_pairs={{0,1},{1,0},{2,3},{3,2},{4,5},{5,4},{6,7},{7,6},{8,9},{9,8},{10,11... | collective-permute-start | bytes 589832 | tf_op jit(solution)/shard_map/ppermute | solution.py:112
  103.5 1.3 %collective-permute-start.12 = (bf16[2,16,1280]{2,1,0:T(8,128)(2,1)S(1)}, bf16[2,16,1280]{2,1,0:T(8,128)(2,1)S(1)}, u32[]{:S(2)}, u32[]{:S(2)}) collective-permute-start(bf16[2,16,1280]{2,1,0:T(8,128)(2,1)S(1)} %fusion.10), channel_id=1, source_target_pairs={{0,4},{4,0},{8,12},{12,8},{1,5},{5,1},{9,13},{13,9},{2,6},{6,2},{1... | collective-permute-start | bytes 245768 | tf_op jit(solution)/shard_map/ppermute | solution.py:112
  104.9 4.1 %collective-permute-start.13 = (bf16[1,16,1280]{2,1,0:T(8,128)(2,1)S(1)}, bf16[1,16,1280]{2,1,0:T(8,128)(2,1)S(1)}, u32[]{:S(2)}, u32[]{:S(2)}) collective-permute-start(bf16[1,16,1280]{2,1,0:T(8,128)(2,1)S(1)} %fusion.14), channel_id=1, source_target_pairs={{0,8},{4,12},{8,0},{12,4},{1,9},{5,13},{9,1},{13,5},{2,10},{6,14},... | collective-permute-start | bytes 122888 | tf_op jit(solution)/shard_map/ppermute | solution.py:112
